TPU v7x, 32 devices: a whole 2x2x4 slice. The times are simulated.
32 devices in a mesh: groups: 2 (over y), seq: 4 (over z), dp: 2 (over x), head: 2 (over core).
Axes of the slice: x: 2, y: 2, z: 4, core: 2. Of those that a mesh axis runs over, the one named last changes fastest.
Arguments:
- queries: bfloat16 [4, 512, 2048], P(('groups', 'dp'), 'seq', 'head'), parts along dimension 0, may hold values from -8 to 8
- keys: bfloat16 [4, 512, 2048], P(('groups', 'dp'), 'seq', 'head'), parts along dimension 0, may hold values from -8 to 8
- values: bfloat16 [4, 512, 2048], P(('groups', 'dp'), 'seq', 'head'), parts along dimension 0, may hold values from -12 to 12
- pattern: int32 [4, 8, 2], P(('groups', 'dp'), 'seq'), parts along dimension 0, may hold values from -2 to 2, as said below
- out_weight: bfloat16 [4096, 2048], P('seq', 'head'), may hold values from -0.125 to 0.125
- cotangent: bfloat16 [4, 512, 4096], P(('groups', 'dp'), 'seq'), parts along dimension 0, may hold values from -6 to 6
Outputs:
- attention: bfloat16 [4, 512, 2048], P(('groups', 'dp'), 'seq', 'head'), parts along dimension 0
- query_grad: bfloat16 [4, 512, 2048], P(('groups', 'dp'), 'seq', 'head'), parts along dimension 0
- key_grad: bfloat16 [4, 512, 2048], P(('groups', 'dp'), 'seq', 'head'), parts along dimension 0
- value_grad: bfloat16 [4, 512, 2048], P(('groups', 'dp'), 'seq', 'head'), parts along dimension 0
- weight_grad: float32 [8192, 2048], P(('groups', 'seq'), 'head'), parts along dimension 0
There are 2 independent parts, one for each index of `groups`. A program takes and returns all parts, laid end to end along the dimension named above; an argument that names none is the same for every part. Nothing has to cross between parts.
Inputs may be any that keep to these rules, and one draw needn't show every extreme that they name: `pattern`: each row holds 2 different block offsets from -2, -1, 1, 2, each keeping the block inside its document.
All inputs are finite; a program needn't handle non-finite values.
Results may differ from a plain program's by a relative error of at most 0.0099.
Values may be sent and summed in bfloat16 or wider, within the bound.
No kernel may reach another device: no remote copies, remote signals or barrier semaphores. Data moves between devices by JAX's collectives and lax.ppermute only.
A program may use at most 128 MiB of HBM per device.

v0:
```python
import math

import jax
import jax.numpy as jnp
from jax import lax
from jax.sharding import PartitionSpec as P

HEAD_DIM = 128
NEAR = 2


def extended(cells, sides, width):
    for axis, dim in sides:
        count = lax.axis_size(axis)
        ends = count - 1
        head = lax.slice_in_dim(cells, 0, width, axis=dim)
        tail = lax.slice_in_dim(cells, cells.shape[dim] - width, cells.shape[dim], axis=dim)
        cells = jnp.concatenate(
            [
                lax.ppermute(tail, axis, [(i, (i + 1) % count) for i in range(ends)]),
                cells,
                lax.ppermute(head, axis, [((i + 1) % count, i) for i in range(ends)]),
            ],
            axis=dim,
        )
    return cells


def swapped(shard, axis, stride):
    return lax.ppermute(shard, axis, [(i, i ^ 1 << stride) for i in range(lax.axis_size(axis))])


def pool_pairs(source):
    shaped = source.reshape(
        source.shape[0], source.shape[1], source.shape[2] // 2, 2, source.shape[3]
    )
    return jnp.sum(shaped, axis=3) * 0.5


def pick_blocks(blocks_doc, chosen_doc):
    return blocks_doc[:, chosen_doc]


def place_blocks(grad_doc, chosen_doc):
    holder = jnp.zeros((grad_doc.shape[0], 6, grad_doc.shape[3], grad_doc.shape[4]), jnp.float32)
    return holder.at[:, chosen_doc].add(grad_doc)


def shards(queries, keys, values, pattern, out_weight, cotangent):
    doc_count, tok_count, head_cols = queries.shape
    block = tok_count // 2
    heads = head_cols // HEAD_DIM
    seq_count = lax.axis_size("seq")
    levels = seq_count.bit_length() - 1
    position = lax.axis_index("seq")
    score_scale = 1.0 / math.sqrt(HEAD_DIM)
    near_width = (NEAR + 1) * block
    key_value = jnp.stack([keys, values])
    padded = extended(key_value, (("seq", 2),), tok_count)
    blocks_six = padded.reshape(2, doc_count, 6, block, head_cols)
    local_ids = jnp.arange(2, dtype=jnp.int32)[None, :, None]
    chosen = jnp.concatenate([local_ids, local_ids + pattern], axis=2) + 2
    near_pair = jax.vmap(pick_blocks, in_axes=(1, 0), out_axes=1)(blocks_six, chosen)
    near_pair = near_pair.reshape(2, doc_count, 2, near_width, head_cols)
    pooled = pool_pairs(key_value.astype(jnp.float32))
    siblings = []
    own_level = pooled
    for level_no in range(levels):
        other = swapped(own_level, "seq", level_no)
        siblings.append(other)
        if level_no + 1 < levels:
            upper = position >> level_no & 1 == 1
            joined = jnp.where(
                upper,
                jnp.concatenate([other, own_level], axis=2),
                jnp.concatenate([own_level, other], axis=2),
            )
            own_level = pool_pairs(joined)
    far_pair = jnp.concatenate(siblings, axis=2).astype(jnp.bfloat16)
    query_heads = queries.reshape(doc_count, 2, block, heads, HEAD_DIM)
    near_k = near_pair[0].reshape(doc_count, 2, near_width, heads, HEAD_DIM)
    near_v = near_pair[1].reshape(doc_count, 2, near_width, heads, HEAD_DIM)
    far_k = far_pair[0].reshape(doc_count, levels * block, heads, HEAD_DIM)
    far_v = far_pair[1].reshape(doc_count, levels * block, heads, HEAD_DIM)
    score_near = (
        jnp.einsum("dbqhe,dbkhe->dbhqk", query_heads, near_k, preferred_element_type=jnp.float32)
        * score_scale
    )
    score_far = (
        jnp.einsum("dbqhe,dkhe->dbhqk", query_heads, far_k, preferred_element_type=jnp.float32)
        * score_scale
    )
    top = jnp.maximum(
        jnp.max(score_near, axis=-1, keepdims=True), jnp.max(score_far, axis=-1, keepdims=True)
    )
    exp_near = jnp.exp(score_near - top)
    exp_far = jnp.exp(score_far - top)
    total = jnp.sum(exp_near, axis=-1, keepdims=True) + jnp.sum(exp_far, axis=-1, keepdims=True)
    weight_near = exp_near / total
    weight_far = exp_far / total
    rounded_near = weight_near.astype(jnp.bfloat16)
    rounded_far = weight_far.astype(jnp.bfloat16)
    output = jnp.einsum(
        "dbhqk,dbkhe->dbqhe", rounded_near, near_v, preferred_element_type=jnp.float32
    )
    output = output + jnp.einsum(
        "dbhqk,dkhe->dbqhe", rounded_far, far_v, preferred_element_type=jnp.float32
    )
    attention = output.reshape(doc_count, tok_count, head_cols).astype(jnp.bfloat16)
    cot_rows = cotangent.reshape(doc_count * tok_count, cotangent.shape[2])
    whole_weight = lax.all_gather(out_weight, "seq", axis=0, tiled=True)
    attn_grad = jnp.dot(cot_rows, whole_weight, preferred_element_type=jnp.float32).astype(
        jnp.bfloat16
    )
    by_feature = lax.all_to_all(cotangent, "seq", split_axis=2, concat_axis=1, tiled=True)
    whole_output = lax.all_gather(attention, "seq", axis=1, tiled=True)
    weight_part = jnp.einsum(
        "dtc,dtw->cw", by_feature, whole_output, preferred_element_type=jnp.float32
    )
    weight_grad = lax.psum(weight_part, "dp")
    grad_heads = attn_grad.reshape(doc_count, 2, block, heads, HEAD_DIM)
    prob_near = jnp.einsum(
        "dbqhe,dbkhe->dbhqk", grad_heads, near_v, preferred_element_type=jnp.float32
    )
    prob_far = jnp.einsum(
        "dbqhe,dkhe->dbhqk", grad_heads, far_v, preferred_element_type=jnp.float32
    )
    row_dot = jnp.sum(weight_near * prob_near, axis=-1, keepdims=True) + jnp.sum(
        weight_far * prob_far, axis=-1, keepdims=True
    )
    grad_near = (weight_near * (prob_near - row_dot)).astype(jnp.bfloat16)
    grad_far = (weight_far * (prob_far - row_dot)).astype(jnp.bfloat16)
    query_sum = jnp.einsum(
        "dbhqk,dbkhe->dbqhe", grad_near, near_k, preferred_element_type=jnp.float32
    )
    query_sum = query_sum + jnp.einsum(
        "dbhqk,dkhe->dbqhe", grad_far, far_k, preferred_element_type=jnp.float32
    )
    query_grad = (
        (query_sum * score_scale).reshape(doc_count, tok_count, head_cols).astype(jnp.bfloat16)
    )
    near_key_rows = (
        jnp.einsum("dbhqk,dbqhe->dbkhe", grad_near, query_heads, preferred_element_type=jnp.float32)
        * score_scale
    )
    near_value_rows = jnp.einsum(
        "dbhqk,dbqhe->dbkhe", rounded_near, grad_heads, preferred_element_type=jnp.float32
    )
    far_key_rows = (
        jnp.einsum("dbhqk,dbqhe->dkhe", grad_far, query_heads, preferred_element_type=jnp.float32)
        * score_scale
    )
    far_value_rows = jnp.einsum(
        "dbhqk,dbqhe->dkhe", rounded_far, grad_heads, preferred_element_type=jnp.float32
    )
    near_rows = jnp.stack([near_key_rows, near_value_rows]).reshape(
        2, doc_count, 2, NEAR + 1, block, head_cols
    )
    back_six = jax.vmap(place_blocks, in_axes=(1, 0), out_axes=1)(near_rows, chosen)
    rims = jnp.concatenate([back_six[:, :, 0:2], back_six[:, :, 4:6]], axis=2).reshape(
        2, doc_count, 2 * tok_count, head_cols
    )
    beside_all = extended(rims, (("seq", 2),), tok_count)
    token_grad = back_six[:, :, 2:4].reshape(2, doc_count, tok_count, head_cols)
    token_grad = token_grad + beside_all[:, :, :tok_count] + beside_all[:, :, 3 * tok_count :]
    far_rows = jnp.stack([far_key_rows, far_value_rows]).reshape(
        2, doc_count, levels, block, head_cols
    )
    carried = jnp.zeros((2, doc_count, block, head_cols), jnp.float32)
    for level_no in reversed(range(levels)):
        message = far_rows[:, :, level_no]
        mine = jnp.zeros_like(message)
        if level_no + 1 < levels:
            upper = position >> level_no & 1 == 1
            spread = jnp.repeat(carried, 2, axis=2) * 0.5
            lower_half = spread[:, :, :block]
            upper_half = spread[:, :, block:]
            mine = jnp.where(upper, upper_half, lower_half)
            message = message + jnp.where(upper, lower_half, upper_half)
        returned = swapped(message, "seq", level_no)
        carried = returned + mine
    token_grad = token_grad + jnp.repeat(carried, 2, axis=2) * 0.5
    key_grad = token_grad[0].astype(jnp.bfloat16)
    value_grad = token_grad[1].astype(jnp.bfloat16)
    return (attention, query_grad, key_grad, value_grad, weight_grad)


def solution(mesh):
    in_specs = (
        P(("groups", "dp"), "seq", "head"),
        P(("groups", "dp"), "seq", "head"),
        P(("groups", "dp"), "seq", "head"),
        P(("groups", "dp"), "seq", None),
        P("seq", "head"),
        P(("groups", "dp"), "seq", None),
    )
    out_specs = (
        P(("groups", "dp"), "seq", "head"),
        P(("groups", "dp"), "seq", "head"),
        P(("groups", "dp"), "seq", "head"),
        P(("groups", "dp"), "seq", "head"),
        P(("groups", "seq"), "head"),
    )
    return jax.shard_map(shards, mesh=mesh, in_specs=in_specs, out_specs=out_specs, check_vma=False)
```

profile of v0, /device:TPU:6, one launch (start us, length us, event | category | flops | bytes accessed | tf_op | source)
XLA Modules:
  0.0 358.8 jit_solution(15132520901967970496)
XLA Ops:
  9.0 1.4 collective-permute-start.1
  10.5 5.3 %collective-permute-start = (bf16[2,1,128,1024]{3,2,1,0:T(8,128)(2,1)}, bf16[2,1,128,1024]{3,2,1,0:T(8,128)(2,1)}, u32[]{:S(2)}, u32[]{:S(2)}) collective-permute-start(bf16[2,1,128,1024]{3,2,1,0:T(8,128)(2,1)} %pad_maximum_fusion.4), channel_id=1, source_target_pairs={{0,4},{4,8},{8,12},{1,5},{5,9},{9,13},{2,6},{6,10},{10,14},{3,7},{... | collective-permute-start | bytes 1572872 | tf_op jit(solution)/shard_map/ppermute | solution.py:20
  16.0 1.4 convert_reduce_fusion
  19.4 2.8 copy.237
  22.7 23.4 %reduce.20 = bf16[4096,128]{1,0:T(8,128)(2,1)} reduce(bf16[4096,1,128]{2,1,0:T(2,128)(2,1)S(1)} %bitcast.213, bf16[]{:T(256)} %broadcast.178), dimensions={1}, to_apply=%bitcast.190.reduce_sub_computation | reduce | bytes 2097154
  46.1 3.5 reshape.524
  49.6 4.7 %all-to-all-start = ((bf16[4,2,65536]{2,1,0:T(2,128)(2,1)}), bf16[4,2,65536]{2,1,0:T(2,128)(2,1)}, u32[]{:S(2)}, u32[]{:S(2)}) async-start(bf16[4,2,65536]{2,1,0:T(2,128)(2,1)} %reshape.524), calls=%async_computation | async-start | bytes 2097152 | tf_op jit(solution)/shard_map/all_to_all | solution.py:115
  56.7 1.8 gather_fusion
  58.5 1.6 copy.193
  61.6 24.7 %collective-permute-done.2 = f32[2,1,64,1024]{3,2,1,0:T(8,128)} collective-permute-done((f32[2,1,64,1024]{3,2,1,0:T(8,128)}, f32[2,1,64,1024]{3,2,1,0:T(8,128)}, u32[]{:S(2)}, u32[]{:S(2)}) %collective-permute-start.2) | collective-permute-done | bytes 524320 | tf_op jit(solution)/shard_map/ppermute | solution.py:30
  88.5 1.8 reduce_sum.55
  91.4 8.3 %collective-permute-start.3 = (bf16[2,1,64,1024]{3,2,1,0:T(8,128)(2,1)S(1)}, bf16[2,1,64,1024]{3,2,1,0:T(8,128)(2,1)S(1)}, u32[]{:S(2)}, u32[]{:S(2)}) collective-permute-start(bf16[2,1,64,1024]{3,2,1,0:T(8,128)(2,1)S(1)} %fusion.23), channel_id=1, source_target_pairs={{0,8},{4,12},{8,0},{12,4},{1,9},{5,13},{9,1},{13,5},{2,10},{6,14},... | collective-permute-start | bytes 786440 | tf_op jit(solution)/shard_map/ppermute | solution.py:30
  101.6 35.1 %collective-permute-done.3 = bf16[2,1,64,1024]{3,2,1,0:T(8,128)(2,1)S(1)} collective-permute-done((bf16[2,1,64,1024]{3,2,1,0:T(8,128)(2,1)S(1)}, bf16[2,1,64,1024]{3,2,1,0:T(8,128)(2,1)S(1)}, u32[]{:S(2)}, u32[]{:S(2)}) %collective-permute-start.3) | collective-permute-done | bytes 262176 | tf_op jit(solution)/shard_map/ppermute | solution.py:30
  140.9 2.4 convolution_bitcast_fusion.3
  143.3 51.9 %all-gather.3.cloned.1.call-done = bf16[4096,1024]{1,0:T(8,128)(2,1)} async-done(((bf16[1024,1024]{1,0:T(8,128)(2,1)}), bf16[4096,1024]{1,0:T(8,128)(2,1)}) %all-gather.3.cloned.1.call-update) | async-done | bytes 8388624 | tf_op jit(solution)/shard_map/all_gather | solution.py:111
  195.2 4.7 %fusion.8 = bf16[16,8,8,128]{3,1,2,0:T(8,128)(2,1)S(1)} fusion(bf16[4096,1024]{1,0:T(8,128)(2,1)} %all-gather.3.cloned.1.call-done, bf16[1,128,4096]{2,1,0:T(8,128)(2,1)S(1)} %copy-done), kind=kOutput, calls=%fused_computation.24 | convolution fusion | flops 1073872896 | bytes 9699328 | tf_op jit(solution)/shard_map/dot_general | solution.py:112
  200.1 1.6 multiply_reduce_fusion
  205.3 2.6 reshape.525
  209.1 1.5 copy.238
  211.2 24.5 %all-gather.5.cloned.1.call-done = bf16[1,512,1024]{2,1,0:T(8,128)(2,1)} async-done(((bf16[1,128,1024]{2,1,0:T(8,128)(2,1)}), bf16[1,512,1024]{2,1,0:T(8,128)(2,1)}) %all-gather.5.cloned.1.call-update) | async-done | bytes 1048592 | tf_op jit(solution)/shard_map/all_gather | solution.py:116
  235.8 4.5 %convolution_bitcast_fusion = f32[1024,1024]{0,1:T(8,128)} fusion(bf16[512,1024]{1,0:T(8,128)(2,1)S(1)} %bitcast.233, bf16[1,512,1024]{2,1,0:T(8,128)(2,1)} %all-gather.5.cloned.1.call-done), kind=kOutput, calls=%fused_computation.3 | convolution fusion | flops 1073741824 | bytes 6291456 | tf_op jit(solution)/shard_map/dtc,dtw->cw/dot_general | solution.py:117
  243.1 1.9 collective-permute-start.6
  249.3 3.1 pad_maximum_fusion
  252.4 2.4 copy.255
  255.2 5.5 %scatter_fusion = f32[2,6,64,1024]{3,2,1,0:T(8,128)S(1)} fusion(f32[2,6,64,1024]{3,2,1,0:T(8,128)S(1)} %broadcast.159, s32[6]{0:T(128)S(1)} %reshape.496, f32[6,2,64,1024]{3,2,1,0:T(8,128)} %bitcast.208), kind=kCustom, calls=%fused_computation.1 | custom fusion | flops 786432 | bytes 9437208 | tf_op jit(solution)/shard_map/vmap()/scatter-add | solution.py:46
  262.2 1.6 fusion.42
  263.7 1.4 collective-permute-start.5
  265.1 5.5 %collective-permute-start.4 = (f32[2,1,128,1024]{3,2,1,0:T(8,128)}, f32[2,1,128,1024]{3,2,1,0:T(8,128)}, u32[]{:S(2)}, u32[]{:S(2)}) collective-permute-start(f32[2,1,128,1024]{3,2,1,0:T(8,128)} %get-tuple-element.40), channel_id=1, source_target_pairs={{0,4},{4,8},{8,12},{1,5},{5,9},{9,13},{2,6},{6,10},{10,14},{3,7},{... | collective-permute-start | bytes 3145736 | tf_op jit(solution)/shard_map/ppermute | solution.py:20
  275.0 28.2 %collective-permute-done.7 = f32[2,1,64,1024]{3,0,2,1:T(2,128)S(1)} collective-permute-done((f32[2,1,64,1024]{3,0,2,1:T(2,128)S(1)}, f32[2,1,64,1024]{3,0,2,1:T(2,128)S(1)}, u32[]{:S(2)}, u32[]{:S(2)}) %collective-permute-start.7) | collective-permute-done | bytes 524320 | tf_op jit(solution)/shard_map/ppermute | solution.py:30
  305.0 1.9 add_convert_fusion
  307.7 39.2 %all-reduce.2.cloned.1.call-done = f32[1024,1024]{0,1:T(8,128)} async-done(((f32[1024,1024]{0,1:T(8,128)}), f32[1024,1024]{0,1:T(8,128)}) %all-reduce.2.cloned.1.call-update) | async-done | bytes 4194320 | tf_op jit(solution)/shard_map/psum | solution.py:120
  346.9 5.3 %copy.239 = f32[1024,1024]{1,0:T(8,128)} copy(f32[1024,1024]{0,1:T(8,128)} %all-reduce.2.cloned.1.call-done) | data formatting | bytes 8388608
  (144 shorter events, 38.6 us)
Async XLA Ops:
  7.2 188.0 %all-gather.3.cloned.1.call-start = ((), (), s32[]{:S(2)}) async-start(), calls=%async_computation.1 | async-start | bytes 10485760 | tf_op jit(solution)/shard_map/all_gather | solution.py:111
  9.0 10.4 %copy-start = (bf16[1,128,4096]{2,1,0:T(8,128)(2,1)S(1)}, bf16[1,128,4096]{2,1,0:T(8,128)(2,1)}, u32[]{:S(2)}) copy-start(bf16[1,128,4096]{2,1,0:T(8,128)(2,1)} %param.11) | copy-start | bytes 3145732
  9.0 46.3 %collective-permute-start.1 = (bf16[2,1,128,1024]{3,2,1,0:T(8,128)(2,1)}, bf16[2,1,128,1024]{3,2,1,0:T(8,128)(2,1)}, u32[]{:S(2)}, u32[]{:S(2)}) collective-permute-start(bf16[2,1,128,1024]{3,2,1,0:T(8,128)(2,1)} %pad_maximum_fusion.4), channel_id=1, source_target_pairs={{4,0},{8,4},{12,8},{5,1},{9,5},{13,9},{6,2},{10,6},{14,10},{7,3},{... | collective-permute-start | bytes 1572872 | tf_op jit(solution)/shard_map/ppermute | solution.py:22
  10.5 44.9 %collective-permute-start = (bf16[2,1,128,1024]{3,2,1,0:T(8,128)(2,1)}, bf16[2,1,128,1024]{3,2,1,0:T(8,128)(2,1)}, u32[]{:S(2)}, u32[]{:S(2)}) collective-permute-start(bf16[2,1,128,1024]{3,2,1,0:T(8,128)(2,1)} %pad_maximum_fusion.4), channel_id=1, source_target_pairs={{0,4},{4,8},{8,12},{1,5},{5,9},{9,13},{2,6},{6,10},{10,14},{3,7},{... | collective-permute-start | bytes 1572872 | tf_op jit(solution)/shard_map/ppermute | solution.py:20
  18.6 67.7 %collective-permute-start.2 = (f32[2,1,64,1024]{3,2,1,0:T(8,128)}, f32[2,1,64,1024]{3,2,1,0:T(8,128)}, u32[]{:S(2)}, u32[]{:S(2)}) collective-permute-start(f32[2,1,64,1024]{3,2,1,0:T(8,128)} %get-tuple-element.51), channel_id=1, source_target_pairs={{0,4},{4,0},{8,12},{12,8},{1,5},{5,1},{9,13},{13,9},{2,6},{6,2},{1... | collective-permute-start | bytes 1572872 | tf_op jit(solution)/shard_map/ppermute | solution.py:30
  46.1 8.2 %copy-start.29 = (s32[1,2,2]{2,1,0:T(2,128)S(1)}, s32[1,2,2]{2,1,0:T(2,128)}, u32[]{:S(2)}) copy-start(s32[1,2,2]{2,1,0:T(2,128)} %param.9) | copy-start | bytes 52
  46.1 8.4 %copy-start.28 = (bf16[1,128,1024]{2,1,0:T(8,128)(2,1)S(1)}, bf16[1,128,1024]{2,1,0:T(8,128)(2,1)}, u32[]{:S(2)}) copy-start(bf16[1,128,1024]{2,1,0:T(8,128)(2,1)} %param.6) | copy-start | bytes 786436
  49.6 5.8 %copy-start.15 = (bf16[1,128,1024]{2,1,0:T(8,128)(2,1)S(1)}, bf16[1,128,1024]{2,1,0:T(8,128)(2,1)}, u32[]{:S(2)}) copy-start(bf16[1,128,1024]{2,1,0:T(8,128)(2,1)} %param.8) | copy-start | bytes 786436
  49.6 5.8 %copy-start.17 = (bf16[1,128,1024]{2,1,0:T(8,128)(2,1)S(1)}, bf16[1,128,1024]{2,1,0:T(8,128)(2,1)}, u32[]{:S(2)}) copy-start(bf16[1,128,1024]{2,1,0:T(8,128)(2,1)} %param.7) | copy-start | bytes 786436
  49.6 155.7 %all-to-all-start = ((bf16[4,2,65536]{2,1,0:T(2,128)(2,1)}), bf16[4,2,65536]{2,1,0:T(2,128)(2,1)}, u32[]{:S(2)}, u32[]{:S(2)}) async-start(bf16[4,2,65536]{2,1,0:T(2,128)(2,1)} %reshape.524), calls=%async_computation | async-start | bytes 2097152 | tf_op jit(solution)/shard_map/all_to_all | solution.py:115
  54.3 181.5 %all-gather.5.cloned.1.call-start = ((), (), s32[]{:S(2)}) async-start(), calls=%async_computation.2 | async-start | bytes 1310720 | tf_op jit(solution)/shard_map/all_gather | solution.py:116
  60.3 26.0 %copy-start.23 = (f32[2,1,64,1024]{3,2,0,1:T(8,128)S(1)}, f32[2,1,64,1024]{3,2,0,1:T(8,128)}, u32[]{:S(2)}) copy-start(f32[2,1,64,1024]{3,2,0,1:T(8,128)} %get-tuple-element.50) | copy-start | bytes 1572868
  61.6 39.3 %copy-start.1 = (bf16[48,8,8,128]{3,2,1,0:T(8,128)(2,1)}, bf16[48,8,8,128]{3,2,1,0:T(8,128)(2,1)S(1)}, u32[]{:S(2)}) copy-start(bf16[48,8,8,128]{3,2,1,0:T(8,128)(2,1)S(1)} %copy.256) | copy-start | bytes 2359300
  91.4 45.3 %collective-permute-start.3 = (bf16[2,1,64,1024]{3,2,1,0:T(8,128)(2,1)S(1)}, bf16[2,1,64,1024]{3,2,1,0:T(8,128)(2,1)S(1)}, u32[]{:S(2)}, u32[]{:S(2)}) collective-permute-start(bf16[2,1,64,1024]{3,2,1,0:T(8,128)(2,1)S(1)} %fusion.23), channel_id=1, source_target_pairs={{0,8},{4,12},{8,0},{12,4},{1,9},{5,13},{9,1},{13,5},{2,10},{6,14},... | collective-permute-start | bytes 786440 | tf_op jit(solution)/shard_map/ppermute | solution.py:30
  137.5 1.7 copy-start.25
  137.6 5.6 %copy-start.18 = (bf16[1,1,128,1024]{2,3,1,0:T(8,128)(2,1)}, bf16[1,1,128,1024]{2,3,1,0:T(8,128)(2,1)S(1)}, u32[]{:S(2)}) copy-start(bf16[1,1,128,1024]{2,3,1,0:T(8,128)(2,1)S(1)} %copy.202) | copy-start | bytes 786436
  195.2 4.8 %copy-start.26 = (bf16[48,8,8,128]{3,2,1,0:T(8,128)(2,1)S(1)}, bf16[48,8,8,128]{3,2,1,0:T(8,128)(2,1)}, u32[]{:S(2)}) copy-start(bf16[48,8,8,128]{3,2,1,0:T(8,128)(2,1)} %copy.258) | copy-start | bytes 2359300
  200.0 1.7 copy-start.21
  200.0 1.6 copy-start.20
  201.7 2.0 copy-start.27
  203.7 1.7 copy-start.12
  205.0 141.9 %all-reduce.2.cloned.1.call-start = ((), (), s32[]{:S(2)}) async-start(), calls=%async_computation.3 | async-start | bytes 8388608 | tf_op jit(solution)/shard_map/psum | solution.py:120
  209.1 1.5 copy-start.10
  211.2 30.6 %copy-start.5 = (f32[1,128,8,128]{3,2,0,1:T(8,128)}, f32[1,128,8,128]{3,2,0,1:T(8,128)S(1)}, u32[]{:S(2)}) copy-start(f32[1,128,8,128]{3,2,0,1:T(8,128)S(1)} %copy.233) | copy-start | bytes 1572868
  241.8 3.2 copy-start.7
  243.1 27.5 %collective-permute-start.6 = (f32[2,1,64,1024]{3,0,2,1:T(2,128)}, f32[2,1,64,1024]{3,0,2,1:T(2,128)}, u32[]{:S(2)}, u32[]{:S(2)}) collective-permute-start(f32[2,1,64,1024]{3,0,2,1:T(2,128)} %fusion.21), channel_id=1, source_target_pairs={{0,8},{4,12},{8,0},{12,4},{1,9},{5,13},{9,1},{13,5},{2,10},{6,14},... | collective-permute-start | bytes 1572872 | tf_op jit(solution)/shard_map/ppermute | solution.py:30
  248.0 1.4 copy-start.3
  263.7 8.6 %copy-start.6 = (f32[1,128,8,128]{3,2,0,1:T(8,128)S(1)}, f32[1,128,8,128]{3,2,0,1:T(8,128)}, u32[]{:S(2)}) copy-start(f32[1,128,8,128]{3,2,0,1:T(8,128)} %copy-done.5) | copy-start | bytes 1572868
  263.7 8.6 %copy-start.8 = (f32[1,128,8,128]{3,2,0,1:T(8,128)S(1)}, f32[1,128,8,128]{3,2,0,1:T(8,128)}, u32[]{:S(2)}) copy-start(f32[1,128,8,128]{3,2,0,1:T(8,128)} %copy-done.7) | copy-start | bytes 1572868
  263.7 41.2 %collective-permute-start.5 = (f32[2,1,128,1024]{3,2,1,0:T(8,128)}, f32[2,1,128,1024]{3,2,1,0:T(8,128)}, u32[]{:S(2)}, u32[]{:S(2)}) collective-permute-start(f32[2,1,128,1024]{3,2,1,0:T(8,128)} %get-tuple-element.41), channel_id=1, source_target_pairs={{4,0},{8,4},{12,8},{5,1},{9,5},{13,9},{6,2},{10,6},{14,10},{7,3},{... | collective-permute-start | bytes 3145736 | tf_op jit(solution)/shard_map/ppermute | solution.py:22
  265.1 39.8 %collective-permute-start.4 = (f32[2,1,128,1024]{3,2,1,0:T(8,128)}, f32[2,1,128,1024]{3,2,1,0:T(8,128)}, u32[]{:S(2)}, u32[]{:S(2)}) collective-permute-start(f32[2,1,128,1024]{3,2,1,0:T(8,128)} %get-tuple-element.40), channel_id=1, source_target_pairs={{0,4},{4,8},{8,12},{1,5},{5,9},{9,13},{2,6},{6,10},{10,14},{3,7},{... | collective-permute-start | bytes 3145736 | tf_op jit(solution)/shard_map/ppermute | solution.py:20
  273.1 30.1 %collective-permute-start.7 = (f32[2,1,64,1024]{3,0,2,1:T(2,128)S(1)}, f32[2,1,64,1024]{3,0,2,1:T(2,128)S(1)}, u32[]{:S(2)}, u32[]{:S(2)}) collective-permute-start(f32[2,1,64,1024]{3,0,2,1:T(2,128)S(1)} %fusion.20), channel_id=1, source_target_pairs={{0,4},{4,0},{8,12},{12,8},{1,5},{5,1},{9,13},{13,9},{2,6},{6,2},{1... | collective-permute-start | bytes 1572872 | tf_op jit(solution)/shard_map/ppermute | solution.py:30
  (10 other events, 11.6 us)
Sparse Core Ops, SparseCore 0:
  9.6 185.5 all-gather.2
  205.1 30.6 all-gather.4
  240.4 106.4 all-reduce.1
where the time goes:
time: 362 us; the launch traced here: 359 us
  waiting for transfers between devices  204 us (56%)
  other arithmetic  52 us (14%)
  local copies, waits for them, and re-layouts  39.6 us (11%)
  starting transfers between devices  29.8 us (8%)
  matrix products  18.6 us (5%)
  between operations  14.4 us (4%)
    ppermute x4, waiting for transfers between devices, swapped(): lax.ppermute(shard, axis, [(i, i ^ 1 << stride) for i in range(lax.axis_s...  88.1 us
    all_gather x1, waiting for transfers between devices, shards(): whole_weight = lax.all_gather(out_weight, 'seq', axis=0, tiled=True)  51.9 us
    psum x1, waiting for transfers between devices, shards(): weight_grad = lax.psum(weight_part, 'dp')  39.2 us
    all_gather x1, waiting for transfers between devices, shards(): whole_output = lax.all_gather(attention, 'seq', axis=1, tiled=True)  24.5 us
    unnamed x1, other arithmetic  23.4 us
    unnamed x70, local copies, waits for them, and re-layouts  19.1 us
    ppermute x4, starting transfers between devices, swapped(): lax.ppermute(shard, axis, [(i, i ^ 1 << stride) for i in range(lax.axis_s...  11.1 us
    ppermute x2, starting transfers between devices, extended(): lax.ppermute(tail, axis, [(i, (i + 1) % count) for i in range(ends)])  10.9 us
  transfers between devices with their start and end apart: 12, of which 6 were waited for; matrix products, arithmetic and copies ran while one was open for 27% of the time, Pallas kernels for 0%

commit v1 on v0

--- a/solution.py
+++ b/solution.py
@@ -107,17 +107,30 @@
         "dbhqk,dkhe->dbqhe", rounded_far, far_v, preferred_element_type=jnp.float32
     )
     attention = output.reshape(doc_count, tok_count, head_cols).astype(jnp.bfloat16)
-    cot_rows = cotangent.reshape(doc_count * tok_count, cotangent.shape[2])
-    whole_weight = lax.all_gather(out_weight, "seq", axis=0, tiled=True)
-    attn_grad = jnp.dot(cot_rows, whole_weight, preferred_element_type=jnp.float32).astype(
-        jnp.bfloat16
-    )
-    by_feature = lax.all_to_all(cotangent, "seq", split_axis=2, concat_axis=1, tiled=True)
+    feat_count = cotangent.shape[2] // seq_count
+    cot_split = jnp.transpose(
+        cotangent.reshape(doc_count, tok_count, seq_count, feat_count), (2, 0, 1, 3)
+    )
+    by_feature = lax.all_to_all(cot_split, "seq", 0, 0, tiled=True)
+    grad_part = jnp.einsum(
+        "sdtf,fc->sdtc", by_feature, out_weight, preferred_element_type=jnp.float32
+    )
+    attn_grad = lax.psum_scatter(grad_part, "seq", scatter_dimension=0, tiled=True)
+    attn_grad = attn_grad.reshape(doc_count * tok_count, head_cols).astype(jnp.bfloat16)
+    feat_docs = jnp.transpose(by_feature, (1, 0, 2, 3)).reshape(
+        doc_count, seq_count * tok_count, feat_count
+    )
     whole_output = lax.all_gather(attention, "seq", axis=1, tiled=True)
-    weight_part = jnp.einsum(
-        "dtc,dtw->cw", by_feature, whole_output, preferred_element_type=jnp.float32
-    )
-    weight_grad = lax.psum(weight_part, "dp")
+    dp_count = lax.axis_size("dp")
+    if dp_count == 2:
+        feat_docs = jnp.concatenate([feat_docs, swapped(feat_docs, "dp", 0)], axis=0)
+        whole_output = jnp.concatenate([whole_output, swapped(whole_output, "dp", 0)], axis=0)
+    else:
+        feat_docs = lax.all_gather(feat_docs, "dp", axis=0, tiled=True)
+        whole_output = lax.all_gather(whole_output, "dp", axis=0, tiled=True)
+    weight_grad = jnp.einsum(
+        "dtc,dtw->cw", feat_docs, whole_output, preferred_element_type=jnp.float32
+    )
     grad_heads = attn_grad.reshape(doc_count, 2, block, heads, HEAD_DIM)
     prob_near = jnp.einsum(
         "dbqhe,dbkhe->dbhqk", grad_heads, near_v, preferred_element_type=jnp.float32

time: 362 us -> 243 us (0.67)
  waiting for transfers between devices: 204 us -> 103 us
  blocking collectives: 0 us -> 30.4 us
  other arithmetic: 52 us -> 28.7 us
  local copies, waits for them, and re-layouts: 39.6 us -> 27.1 us
  starting transfers between devices: 29.8 us -> 17.3 us
    all_gather x1 -> x0, waiting for transfers between devices: 51.9 us -> none  [shards(): whole_weight = lax.all_gather(out_weight, 'seq', axis=0, tiled=True)]
    psum x1 -> x0, waiting for transfers between devices: 39.2 us -> none  [shards(): weight_grad = lax.psum(weight_part, 'dp')]
    all_to_all x0 -> x1, blocking collectives: none -> 30.4 us  [shards(): by_feature = lax.all_to_all(cot_split, 'seq', 0, 0, tiled=True)]
    ppermute x2, waiting for transfers between devices: 0.01 us -> 24.9 us  [extended(): lax.ppermute(head, axis, [((i + 1) % count, i) for i in range(ends)])]
    all_gather x1, waiting for transfers between devices: 24.5 us -> 0.02 us  [shards(): whole_output = lax.all_gather(attention, 'seq', axis=1, tiled=True)]
    unnamed x1, other arithmetic: 23.4 us -> 1.08 us
    unnamed x70 -> x53, local copies, waits for them, and re-layouts: 19.1 us -> 6.77 us
    ppermute x4 -> x6, waiting for transfers between devices: 88.1 us -> 77.7 us  [swapped(): lax.ppermute(shard, axis, [(i, i ^ 1 << stride) for i in range(lax.axis_s...]
  transfers between devices with their start and end apart: 12 -> 12, of which waited for: 6 -> 6; matrix products, arithmetic and copies ran while one was open for 27% -> 20% of each run, Pallas kernels for 0% -> 0%
where the time goes in v1:
time: 243 us; the launch traced here: 241 us
  waiting for transfers between devices  103 us (42%)
  blocking collectives  30.4 us (13%)
  other arithmetic  28.7 us (12%)
  local copies, waits for them, and re-layouts  27.1 us (11%)
  matrix products  20 us (8%)
  starting transfers between devices  17.3 us (7%)
  between operations  14.7 us (6%)
    ppermute x6, waiting for transfers between devices, swapped(): lax.ppermute(shard, axis, [(i, i ^ 1 << stride) for i in range(lax.axis_s...  77.7 us
    all_to_all x1, blocking collectives, shards(): by_feature = lax.all_to_all(cot_split, 'seq', 0, 0, tiled=True)  30.4 us
    ppermute x2, waiting for transfers between devices, extended(): lax.ppermute(head, axis, [((i + 1) % count, i) for i in range(ends)])  24.9 us
    ppermute x2, starting transfers between devices, extended(): lax.ppermute(tail, axis, [(i, (i + 1) % count) for i in range(ends)])  12.2 us
    unnamed x53, local copies, waits for them, and re-layouts  6.77 us
    dot_general x1, matrix products, shards(): jnp.einsum('dtc,dtw->cw', feat_docs, whole_output, preferred_element_type...  6.03 us
    scatter-add x1, other arithmetic, place_blocks(): return holder.at[:, chosen_doc].add(grad_doc)  5.44 us
  transfers between devices with their start and end apart: 12, of which 6 were waited for; matrix products, arithmetic and copies ran while one was open for 20% of the time, Pallas kernels for 0%

profile of v1, /device:TPU:6, one launch (start us, length us, event | category | flops | bytes accessed | tf_op | source)
XLA Modules:
  0.0 240.7 jit_solution(1201552216872492738)
XLA Ops:
  7.2 2.4 copy.219
  9.6 1.5 copy.220
  11.1 30.4 %all_to_all.5 = bf16[4,1,128,1024]{3,2,1,0:T(8,128)(2,1)S(1)} all-to-all(bf16[4,1,128,1024]{3,2,1,0:T(8,128)(2,1)S(1)} %copy.220), channel_id=1, replica_groups=mesh['groups'=2,'seq'=4,'dp'=2,'head'=2] {'seq'}, dimensions={0} | all-to-all | bytes 2097152 | tf_op jit(solution)/shard_map/all_to_all | solution.py:114
  42.5 2.6 %fusion.8 = f32[4,1,128,1024]{3,2,0,1:T(8,128)} fusion(bf16[1024,1024]{1,0:T(8,128)(2,1)S(1)} %copy-done, bf16[4,1,128,1024]{3,2,1,0:T(8,128)(2,1)S(1)} %all_to_all.5), kind=kOutput, calls=%fused_computation.13 | convolution fusion | flops 1073741824 | bytes 5242880 | tf_op jit(solution)/shard_map/sdtf,fc->sdtc/dot_general | solution.py:115
  46.2 1.4 collective-permute-start.1
  47.6 5.4 %collective-permute-start = (bf16[2,1,128,1024]{3,2,1,0:T(8,128)(2,1)S(1)}, bf16[2,1,128,1024]{3,2,1,0:T(8,128)(2,1)}, u32[]{:S(2)}, u32[]{:S(2)}) collective-permute-start(bf16[2,1,128,1024]{3,2,1,0:T(8,128)(2,1)S(1)} %pad_maximum_fusion.4), channel_id=1, source_target_pairs={{0,4},{4,8},{8,12},{1,5},{5,9},{9,13},{2,6},{6,10},{10,14},{3,7},{... | collective-permute-start | bytes 1572872 | tf_op jit(solution)/shard_map/ppermute | solution.py:20
  53.2 1.4 convert_reduce_fusion
  55.9 24.9 %collective-permute-done.1 = bf16[2,1,128,1024]{3,2,1,0:T(8,128)(2,1)S(1)} collective-permute-done((bf16[2,1,128,1024]{3,2,1,0:T(8,128)(2,1)S(1)}, bf16[2,1,128,1024]{3,2,1,0:T(8,128)(2,1)S(1)}, u32[]{:S(2)}, u32[]{:S(2)}) %collective-permute-start.1) | collective-permute-done | bytes 524320 | tf_op jit(solution)/shard_map/ppermute | solution.py:22
  83.0 1.9 gather_fusion
  84.8 1.6 copy.198
  87.9 17.9 %collective-permute-done.2 = f32[2,1,64,1024]{3,2,1,0:T(8,128)} collective-permute-done((f32[2,1,64,1024]{3,2,1,0:T(8,128)}, f32[2,1,64,1024]{3,2,1,0:T(8,128)}, u32[]{:S(2)}, u32[]{:S(2)}) %collective-permute-start.2) | collective-permute-done | bytes 524320 | tf_op jit(solution)/shard_map/ppermute | solution.py:30
  110.9 8.2 %collective-permute-done.3 = bf16[2,1,64,1024]{3,2,1,0:T(8,128)(2,1)S(1)} collective-permute-done((bf16[2,1,64,1024]{3,2,1,0:T(8,128)(2,1)S(1)}, bf16[2,1,64,1024]{3,2,1,0:T(8,128)(2,1)S(1)}, u32[]{:S(2)}, u32[]{:S(2)}) %collective-permute-start.3) | collective-permute-done | bytes 262176 | tf_op jit(solution)/shard_map/ppermute | solution.py:30
  120.9 2.4 %convolution_bitcast_fusion.3 = f32[1,2,64,8,128]{4,2,3,1,0:T(8,128)} fusion(bf16[2,192,8,128]{3,2,1,0:T(8,128)(2,1)} %bitcast.251, f32[2,8,64,192]{3,2,1,0:T(8,128)S(1)} %get-tuple-element.23, f32[2,8,64]{2,1,0:T(8,128)S(1)} %copy_add_fusion.1, f32[2,8,64]{2,1,0:T(8,128)S(1)} %copy_maximum_fusion), kind=kOutput, calls=%fused_computation.20 | convolution fusion | flops 50921472 | bytes 2105344 | tf_op jit(solution)/shard_map/dbhqk,dbkhe->dbqhe/dot_general | solution.py:103
  124.5 2.8 %multiply_reduce_fusion = (f32[2,8,64]{2,1,0:T(8,128)S(1)}, f32[2,8,64,192]{3,2,1,0:T(8,128)}) fusion(f32[2,8,64]{2,1,0:T(8,128)S(1)} %copy_add_fusion.1, f32[2,8,64,192]{3,2,1,0:T(8,128)S(1)} %get-tuple-element.23, f32[2,8,64]{2,1,0:T(8,128)S(1)} %copy_maximum_fusion, bf16[2,192,8,128]{3,2,1,0:T(8,128)(2,1)} %bitcast.252, ...), kind=kOutput, calls=%fused_computation.38 | convolution fusion | flops 51117056 | bytes 2633728 | tf_op jit(solution)/shard_map/dbqhe,dbkhe->dbhqk/dot_general | solution.py:135
  127.3 2.1 convolution_bitcast_fusion.1
  132.2 1.7 multiply_convert_fusion
  134.8 1.5 fusion.30
  138.7 3.1 %pad_maximum_fusion = f32[1,2,2,3,64,1024]{5,0,4,3,2,1:T(1,128)S(1)} fusion(f32[1,1,2,3,64,1024]{5,0,4,3,2,1:T(1,128)S(1)} %bitcast.223, f32[1,1,2,3,64,1024]{5,0,4,3,2,1:T(1,128)S(1)} %bitcast.224), kind=kLoop, calls=%fused_computation.2 | loop fusion | flops 786432 | bytes 6291456 | tf_op jit(solution)/shard_map/stack | solution.py:169
  141.8 2.4 copy.260
  144.6 5.4 %scatter_fusion = f32[2,6,64,1024]{3,2,1,0:T(8,128)S(1)} fusion(f32[2,6,64,1024]{3,2,1,0:T(8,128)S(1)} %broadcast.159, s32[6]{0:T(128)S(1)} %reshape.493, f32[6,2,64,1024]{3,2,1,0:T(8,128)} %bitcast.211), kind=kCustom, calls=%fused_computation.1 | custom fusion | flops 786432 | bytes 9437208 | tf_op jit(solution)/shard_map/vmap()/scatter-add | solution.py:46
  151.5 1.5 fusion.52
  153.0 1.4 collective-permute-start.5
  154.4 6.8 %collective-permute-start.4 = (f32[2,1,128,1024]{3,2,1,0:T(8,128)}, f32[2,1,128,1024]{3,2,1,0:T(8,128)}, u32[]{:S(2)}, u32[]{:S(2)}) collective-permute-start(f32[2,1,128,1024]{3,2,1,0:T(8,128)} %get-tuple-element.10), channel_id=1, source_target_pairs={{0,4},{4,8},{8,12},{1,5},{5,9},{9,13},{2,6},{6,10},{10,14},{3,7},{... | collective-permute-start | bytes 3145736 | tf_op jit(solution)/shard_map/ppermute | solution.py:20
  161.2 17.7 %collective-permute-done.6 = f32[2,1,64,1024]{3,0,2,1:T(2,128)} collective-permute-done((f32[2,1,64,1024]{3,0,2,1:T(2,128)}, f32[2,1,64,1024]{3,0,2,1:T(2,128)}, u32[]{:S(2)}, u32[]{:S(2)}) %collective-permute-start.6) | collective-permute-done | bytes 524320 | tf_op jit(solution)/shard_map/ppermute | solution.py:30
  180.6 1.5 fusion.29
  184.5 1.5 collective-permute-start.9
  186.0 1.3 fusion.17
  188.3 22.2 %collective-permute-done.7 = f32[2,1,64,1024]{3,0,2,1:T(2,128)} collective-permute-done((f32[2,1,64,1024]{3,0,2,1:T(2,128)}, f32[2,1,64,1024]{3,0,2,1:T(2,128)}, u32[]{:S(2)}, u32[]{:S(2)}) %collective-permute-start.7) | collective-permute-done | bytes 524320 | tf_op jit(solution)/shard_map/ppermute | solution.py:30
  210.5 1.5 multiply_bitcast_fusion.1
  213.4 2.0 add_convert_fusion
  216.3 11.5 %collective-permute-done.9 = bf16[1,512,1024]{2,1,0:T(8,128)(2,1)} collective-permute-done((bf16[1,512,1024]{2,1,0:T(8,128)(2,1)}, bf16[1,512,1024]{2,1,0:T(8,128)(2,1)}, u32[]{:S(2)}, u32[]{:S(2)}) %collective-permute-start.9) | collective-permute-done | bytes 1048608 | tf_op jit(solution)/shard_map/ppermute | solution.py:30
  227.8 6.0 %convolution_bitcast_fusion = f32[1024,1024]{1,0:T(8,128)} fusion(bf16[1,512,1024]{1,2,0:T(8,128)(2,1)} %collective-permute-done.8, bf16[1,512,1024]{1,2,0:T(8,128)(2,1)S(1)} %copy-done.18, bf16[1,512,1024]{2,1,0:T(8,128)(2,1)} %collective-permute-done.9, bf16[1,512,1024]{2,1,0:T(8,128)(2,1)S(1)} %copy-done.23), kind=kOutput, calls=%fused_computation.3 | convolution fusion | flops 2149580800 | bytes 8388608 | tf_op jit(solution)/shard_map/dtc,dtw->cw/dot_general | solution.py:131
  (128 shorter events, 30.2 us)
Async XLA Ops:
  7.2 35.3 %copy-start = (bf16[1024,1024]{1,0:T(8,128)(2,1)S(1)}, bf16[1024,1024]{1,0:T(8,128)(2,1)}, u32[]{:S(2)}) copy-start(bf16[1024,1024]{1,0:T(8,128)(2,1)} %param.10) | copy-start | bytes 6291460
  7.2 116.2 %reduce-scatter.2.cloned.1.call-start = ((), (), s32[]{:S(2)}) async-start(), calls=%async_computation.2 | async-start | bytes 2621440 | tf_op jit(solution)/shard_map/reduce_scatter | solution.py:118
  45.1 139.4 %all-gather.2.cloned.1.call-start = ((), (), s32[]{:S(2)}) async-start(), calls=%async_computation.3 | async-start | bytes 1310720 | tf_op jit(solution)/shard_map/all_gather | solution.py:123
  46.1 9.4 %copy-start.22 = (s32[1,2,2]{2,1,0:T(2,128)S(1)}, s32[1,2,2]{2,1,0:T(2,128)}, u32[]{:S(2)}) copy-start(s32[1,2,2]{2,1,0:T(2,128)} %param.9) | copy-start | bytes 52
  46.2 9.6 %copy-start.21 = (bf16[1,128,1024]{2,1,0:T(8,128)(2,1)S(1)}, bf16[1,128,1024]{2,1,0:T(8,128)(2,1)}, u32[]{:S(2)}) copy-start(bf16[1,128,1024]{2,1,0:T(8,128)(2,1)} %param.6) | copy-start | bytes 786436
  46.2 34.7 %collective-permute-start.1 = (bf16[2,1,128,1024]{3,2,1,0:T(8,128)(2,1)S(1)}, bf16[2,1,128,1024]{3,2,1,0:T(8,128)(2,1)S(1)}, u32[]{:S(2)}, u32[]{:S(2)}) collective-permute-start(bf16[2,1,128,1024]{3,2,1,0:T(8,128)(2,1)S(1)} %pad_maximum_fusion.4), channel_id=1, source_target_pairs={{4,0},{8,4},{12,8},{5,1},{9,5},{13,9},{6,2},{10,6},{14,10},{7,3},{... | collective-permute-start | bytes 1572872 | tf_op jit(solution)/shard_map/ppermute | solution.py:22
  47.6 34.1 %collective-permute-start = (bf16[2,1,128,1024]{3,2,1,0:T(8,128)(2,1)S(1)}, bf16[2,1,128,1024]{3,2,1,0:T(8,128)(2,1)}, u32[]{:S(2)}, u32[]{:S(2)}) collective-permute-start(bf16[2,1,128,1024]{3,2,1,0:T(8,128)(2,1)S(1)} %pad_maximum_fusion.4), channel_id=1, source_target_pairs={{0,4},{4,8},{8,12},{1,5},{5,9},{9,13},{2,6},{6,10},{10,14},{3,7},{... | collective-permute-start | bytes 1572872 | tf_op jit(solution)/shard_map/ppermute | solution.py:20
  55.5 50.3 %collective-permute-start.2 = (f32[2,1,64,1024]{3,2,1,0:T(8,128)}, f32[2,1,64,1024]{3,2,1,0:T(8,128)}, u32[]{:S(2)}, u32[]{:S(2)}) collective-permute-start(f32[2,1,64,1024]{3,2,1,0:T(8,128)} %get-tuple-element.21), channel_id=1, source_target_pairs={{0,4},{4,0},{8,12},{12,8},{1,5},{5,1},{9,13},{13,9},{2,6},{6,2},{1... | collective-permute-start | bytes 1572872 | tf_op jit(solution)/shard_map/ppermute | solution.py:30
  87.9 22.4 %copy-start.2 = (bf16[48,8,8,128]{3,2,1,0:T(8,128)(2,1)}, bf16[48,8,8,128]{3,2,1,0:T(8,128)(2,1)S(1)}, u32[]{:S(2)}) copy-start(bf16[48,8,8,128]{3,2,1,0:T(8,128)(2,1)S(1)} %copy.261) | copy-start | bytes 2359300
  109.1 10.1 %collective-permute-start.3 = (bf16[2,1,64,1024]{3,2,1,0:T(8,128)(2,1)S(1)}, bf16[2,1,64,1024]{3,2,1,0:T(8,128)(2,1)S(1)}, u32[]{:S(2)}, u32[]{:S(2)}) collective-permute-start(bf16[2,1,64,1024]{3,2,1,0:T(8,128)(2,1)S(1)} %fusion.32), channel_id=1, source_target_pairs={{0,8},{4,12},{8,0},{12,4},{1,9},{5,13},{9,1},{13,5},{2,10},{6,14},... | collective-permute-start | bytes 786440 | tf_op jit(solution)/shard_map/ppermute | solution.py:30
  119.4 4.0 %copy-start.16 = (bf16[1,1,128,1024]{2,3,1,0:T(8,128)(2,1)}, bf16[1,1,128,1024]{2,3,1,0:T(8,128)(2,1)S(1)}, u32[]{:S(2)}) copy-start(bf16[1,1,128,1024]{2,3,1,0:T(8,128)(2,1)S(1)} %copy.207) | copy-start | bytes 786436
  129.6 1.4 copy-start.19
  130.6 6.7 %copy-start.13 = (bf16[2,8,64,128]{3,2,0,1:T(8,128)(2,1)}, bf16[2,8,64,128]{3,2,0,1:T(8,128)(2,1)S(1)}, u32[]{:S(2)}) copy-start(bf16[2,8,64,128]{3,2,0,1:T(8,128)(2,1)S(1)} %get-tuple-element.14) | copy-start | bytes 786436
  133.9 3.4 %copy-start.4 = (bf16[2,8,64,192]{3,2,1,0:T(8,128)(2,1)}, bf16[2,8,64,192]{3,2,1,0:T(8,128)(2,1)S(1)}, u32[]{:S(2)}) copy-start(bf16[2,8,64,192]{3,2,1,0:T(8,128)(2,1)S(1)} %multiply_convert_fusion) | copy-start | bytes 1179652
  134.5 1.7 copy-start.6
  134.8 1.5 copy-start.8
  134.8 1.6 copy-start.17
  136.3 42.7 %collective-permute-start.6 = (f32[2,1,64,1024]{3,0,2,1:T(2,128)}, f32[2,1,64,1024]{3,0,2,1:T(2,128)}, u32[]{:S(2)}, u32[]{:S(2)}) collective-permute-start(f32[2,1,64,1024]{3,0,2,1:T(2,128)} %fusion.30), channel_id=1, source_target_pairs={{0,8},{4,12},{8,0},{12,4},{1,9},{5,13},{9,1},{13,5},{2,10},{6,14},... | collective-permute-start | bytes 1572872 | tf_op jit(solution)/shard_map/ppermute | solution.py:30
  152.9 27.6 %copy-start.7 = (f32[1,128,8,128]{3,2,0,1:T(8,128)S(1)}, f32[1,128,8,128]{3,2,0,1:T(8,128)}, u32[]{:S(2)}) copy-start(f32[1,128,8,128]{3,2,0,1:T(8,128)} %copy-done.6) | copy-start | bytes 1572868
  152.9 27.6 %copy-start.9 = (f32[1,128,8,128]{3,2,0,1:T(8,128)S(1)}, f32[1,128,8,128]{3,2,0,1:T(8,128)}, u32[]{:S(2)}) copy-start(f32[1,128,8,128]{3,2,0,1:T(8,128)} %copy-done.8) | copy-start | bytes 1572868
  153.0 60.4 %collective-permute-start.5 = (f32[2,1,128,1024]{3,2,1,0:T(8,128)}, f32[2,1,128,1024]{3,2,1,0:T(8,128)}, u32[]{:S(2)}, u32[]{:S(2)}) collective-permute-start(f32[2,1,128,1024]{3,2,1,0:T(8,128)} %get-tuple-element.11), channel_id=1, source_target_pairs={{4,0},{8,4},{12,8},{5,1},{9,5},{13,9},{6,2},{10,6},{14,10},{7,3},{... | collective-permute-start | bytes 3145736 | tf_op jit(solution)/shard_map/ppermute | solution.py:22
  154.4 59.0 %collective-permute-start.4 = (f32[2,1,128,1024]{3,2,1,0:T(8,128)}, f32[2,1,128,1024]{3,2,1,0:T(8,128)}, u32[]{:S(2)}, u32[]{:S(2)}) collective-permute-start(f32[2,1,128,1024]{3,2,1,0:T(8,128)} %get-tuple-element.10), channel_id=1, source_target_pairs={{0,4},{4,8},{8,12},{1,5},{5,9},{9,13},{2,6},{6,10},{10,14},{3,7},{... | collective-permute-start | bytes 3145736 | tf_op jit(solution)/shard_map/ppermute | solution.py:20
  180.2 1.9 copy-start.11
  180.6 3.5 %copy-start.3 = (bf16[48,8,8,128]{3,2,1,0:T(8,128)(2,1)S(1)}, bf16[48,8,8,128]{3,2,1,0:T(8,128)(2,1)}, u32[]{:S(2)}) copy-start(bf16[48,8,8,128]{3,2,1,0:T(8,128)(2,1)} %copy-done.2) | copy-start | bytes 2359300
  180.6 3.5 %copy-start.5 = (bf16[2,8,64,192]{3,2,1,0:T(8,128)(2,1)S(1)}, bf16[2,8,64,192]{3,2,1,0:T(8,128)(2,1)}, u32[]{:S(2)}) copy-start(bf16[2,8,64,192]{3,2,1,0:T(8,128)(2,1)} %copy-done.4) | copy-start | bytes 1179652
  182.1 28.4 %collective-permute-start.7 = (f32[2,1,64,1024]{3,0,2,1:T(2,128)}, f32[2,1,64,1024]{3,0,2,1:T(2,128)}, u32[]{:S(2)}, u32[]{:S(2)}) collective-permute-start(f32[2,1,64,1024]{3,0,2,1:T(2,128)} %fusion.29), channel_id=1, source_target_pairs={{0,4},{4,0},{8,12},{12,8},{1,5},{5,1},{9,13},{13,9},{2,6},{6,2},{1... | collective-permute-start | bytes 1572872 | tf_op jit(solution)/shard_map/ppermute | solution.py:30
  183.4 32.9 %collective-permute-start.8 = (bf16[1,512,1024]{1,2,0:T(8,128)(2,1)}, bf16[1,512,1024]{1,2,0:T(8,128)(2,1)}, u32[]{:S(2)}, u32[]{:S(2)}) collective-permute-start(bf16[1,512,1024]{1,2,0:T(8,128)(2,1)} %copy.257), channel_id=1, source_target_pairs={{0,2},{2,0},{1,3},{3,1},{4,6},{6,4},{5,7},{7,5},{8,10},{10,8},{9,1... | collective-permute-start | bytes 3145736 | tf_op jit(solution)/shard_map/ppermute | solution.py:30
  184.5 43.3 %collective-permute-start.9 = (bf16[1,512,1024]{2,1,0:T(8,128)(2,1)}, bf16[1,512,1024]{2,1,0:T(8,128)(2,1)}, u32[]{:S(2)}, u32[]{:S(2)}) collective-permute-start(bf16[1,512,1024]{2,1,0:T(8,128)(2,1)} %all-gather.2.cloned.1.call-done), channel_id=1, source_target_pairs={{0,2},{2,0},{1,3},{3,1},{4,6},{6,4},{5,7},{7,5},{8,10},{10,8},{9,1... | collective-permute-start | bytes 3145736 | tf_op jit(solution)/shard_map/ppermute | solution.py:30
  212.2 1.2 copy-start.12
  213.4 14.4 %copy-start.18 = (bf16[1,512,1024]{1,2,0:T(8,128)(2,1)S(1)}, bf16[1,512,1024]{1,2,0:T(8,128)(2,1)}, u32[]{:S(2)}) copy-start(bf16[1,512,1024]{1,2,0:T(8,128)(2,1)} %copy.257) | copy-start | bytes 3145732
  213.4 14.4 %copy-start.23 = (bf16[1,512,1024]{2,1,0:T(8,128)(2,1)S(1)}, bf16[1,512,1024]{2,1,0:T(8,128)(2,1)}, u32[]{:S(2)}) copy-start(bf16[1,512,1024]{2,1,0:T(8,128)(2,1)} %all-gather.2.cloned.1.call-done) | copy-start | bytes 3145732
  227.8 6.0 %copy-start.1 = (bf16[1024,1024]{1,0:T(8,128)(2,1)S(1)}, bf16[1024,1024]{1,0:T(8,128)(2,1)}, u32[]{:S(2)}) copy-start(bf16[1024,1024]{1,0:T(8,128)(2,1)} %param.10) | copy-start | bytes 6291460
  (4 other events, 3.7 us)
Sparse Core Ops, SparseCore 0:
  45.2 62.6 reduce-scatter.1
  138.8 42.5 all-gather.1

commit v2 on v1

--- a/solution.py
+++ b/solution.py
@@ -108,19 +108,26 @@
     )
     attention = output.reshape(doc_count, tok_count, head_cols).astype(jnp.bfloat16)
     feat_count = cotangent.shape[2] // seq_count
-    cot_split = jnp.transpose(
-        cotangent.reshape(doc_count, tok_count, seq_count, feat_count), (2, 0, 1, 3)
-    )
-    by_feature = lax.all_to_all(cot_split, "seq", 0, 0, tiled=True)
-    grad_part = jnp.einsum(
-        "sdtf,fc->sdtc", by_feature, out_weight, preferred_element_type=jnp.float32
-    )
-    attn_grad = lax.psum_scatter(grad_part, "seq", scatter_dimension=0, tiled=True)
-    attn_grad = attn_grad.reshape(doc_count * tok_count, head_cols).astype(jnp.bfloat16)
-    feat_docs = jnp.transpose(by_feature, (1, 0, 2, 3)).reshape(
-        doc_count, seq_count * tok_count, feat_count
-    )
-    whole_output = lax.all_gather(attention, "seq", axis=1, tiled=True)
+    cot_rows = cotangent.reshape(doc_count * tok_count, cotangent.shape[2])
+    out_rows = attention.reshape(doc_count * tok_count, head_cols)
+    own_cols = lax.dynamic_slice_in_dim(cot_rows, position * feat_count, feat_count, axis=1)
+    grad_sum = jnp.dot(own_cols, out_weight, preferred_element_type=jnp.float32)
+    feat_list = [own_cols]
+    out_list = [out_rows]
+    for step in range(1, seq_count):
+        pairs = [(i, i ^ step) for i in range(seq_count)]
+        sent = lax.dynamic_slice_in_dim(
+            cot_rows, (position ^ step) * feat_count, feat_count, axis=1
+        )
+        got = lax.ppermute(sent, "seq", pairs)
+        part = jnp.dot(got, out_weight, preferred_element_type=jnp.float32)
+        back = lax.ppermute(part.astype(jnp.bfloat16), "seq", pairs)
+        grad_sum = grad_sum + back.astype(jnp.float32)
+        feat_list.append(got)
+        out_list.append(lax.ppermute(out_rows, "seq", pairs))
+    attn_grad = grad_sum.astype(jnp.bfloat16)
+    feat_docs = jnp.concatenate(feat_list, axis=0)
+    whole_output = jnp.concatenate(out_list, axis=0)
     dp_count = lax.axis_size("dp")
     if dp_count == 2:
         feat_docs = jnp.concatenate([feat_docs, swapped(feat_docs, "dp", 0)], axis=0)
@@ -129,7 +136,7 @@
         feat_docs = lax.all_gather(feat_docs, "dp", axis=0, tiled=True)
         whole_output = lax.all_gather(whole_output, "dp", axis=0, tiled=True)
     weight_grad = jnp.einsum(
-        "dtc,dtw->cw", feat_docs, whole_output, preferred_element_type=jnp.float32
+        "tc,tw->cw", feat_docs, whole_output, preferred_element_type=jnp.float32
     )
     grad_heads = attn_grad.reshape(doc_count, 2, block, heads, HEAD_DIM)
     prob_near = jnp.einsum(
@@ -173,7 +180,9 @@
     rims = jnp.concatenate([back_six[:, :, 0:2], back_six[:, :, 4:6]], axis=2).reshape(
         2, doc_count, 2 * tok_count, head_cols
     )
-    beside_all = extended(rims, (("seq", 2),), tok_count)
+    beside_all = extended(rims.astype(jnp.bfloat16), (("seq", 2),), tok_count).astype(
+        jnp.float32
+    )
     token_grad = back_six[:, :, 2:4].reshape(2, doc_count, tok_count, head_cols)
     token_grad = token_grad + beside_all[:, :, :tok_count] + beside_all[:, :, 3 * tok_count :]
     far_rows = jnp.stack([far_key_rows, far_value_rows]).reshape(
@@ -190,7 +199,7 @@
             upper_half = spread[:, :, block:]
             mine = jnp.where(upper, upper_half, lower_half)
             message = message + jnp.where(upper, lower_half, upper_half)
-        returned = swapped(message, "seq", level_no)
+        returned = swapped(message.astype(jnp.bfloat16), "seq", level_no).astype(jnp.float32)
         carried = returned + mine
     token_grad = token_grad + jnp.repeat(carried, 2, axis=2) * 0.5
     key_grad = token_grad[0].astype(jnp.bfloat16)

time: 243 us -> 185 us (0.76)
  waiting for transfers between devices: 103 us -> 59.8 us
  blocking collectives: 30.4 us -> 0 us
  starting transfers between devices: 17.3 us -> 33.6 us
  between operations: 14.7 us -> 1.36 us
  local copies, waits for them, and re-layouts: 27.1 us -> 38.8 us
  other arithmetic: 28.7 us -> 31.8 us
    ppermute x6, waiting for transfers between devices: 77.7 us -> 40.1 us  [swapped(): lax.ppermute(shard, axis, [(i, i ^ 1 << stride) for i in range(lax.axis_s...]
    all_to_all x1 -> x0, blocking collectives: 30.4 us -> none  [shards(): by_feature = lax.all_to_all(cot_split, 'seq', 0, 0, tiled=True)]
    ppermute x2, waiting for transfers between devices: 24.9 us -> 0.01 us  [extended(): lax.ppermute(head, axis, [((i + 1) % count, i) for i in range(ends)])]
    ppermute x0 -> x9, waiting for transfers between devices: none -> 19.8 us  [the longest x3 19.8 us: shards(): got = lax.ppermute(sent, 'seq', pairs)]
    ppermute x0 -> x9, starting transfers between devices: none -> 18.5 us  [the longest x3 10.8 us: shards(): back = lax.ppermute(part.astype(jnp.bfloat16), 'seq', pairs)]
    unnamed x53 -> x75, local copies, waits for them, and re-layouts: 6.77 us -> 13.8 us
    concatenate x0 -> x2, local copies, waits for them, and re-layouts: none -> 3.63 us  [the longest x1 2.33 us: shards(): jnp.concatenate([feat_docs, swapped(feat_docs, 'dp', 0)], axis=0)]
    concatenate x1 -> x2, other arithmetic: 0.24 us -> 3.3 us  [the longest x1 2.24 us: shards(): whole_output = jnp.concatenate(out_list, axis=0)]
  transfers between devices with their start and end apart: 12 -> 19, of which waited for: 6 -> 7; matrix products, arithmetic and copies ran while one was open for 20% -> 44% of each run, Pallas kernels for 0% -> 0%
where the time goes in v2:
time: 185 us
  waiting for transfers between devices  59.8 us (32%)
  local copies, waits for them, and re-layouts  38.8 us (21%)
  starting transfers between devices  33.6 us (18%)
  other arithmetic  31.8 us (17%)
  matrix products  19.2 us (10%)
    ppermute x6, waiting for transfers between devices, swapped(): lax.ppermute(shard, axis, [(i, i ^ 1 << stride) for i in range(lax.axis_s...  40.1 us
    ppermute x3, waiting for transfers between devices, shards(): got = lax.ppermute(sent, 'seq', pairs)  19.8 us
    unnamed x75, local copies, waits for them, and re-layouts  13.8 us
    ppermute x3, starting transfers between devices, shards(): back = lax.ppermute(part.astype(jnp.bfloat16), 'seq', pairs)  10.8 us
    ppermute x2, starting transfers between devices, extended(): lax.ppermute(tail, axis, [(i, (i + 1) % count) for i in range(ends)])  10.7 us
    scatter-add x1, other arithmetic, place_blocks(): return holder.at[:, chosen_doc].add(grad_doc)  5.37 us
    dot_general x1, matrix products, shards(): jnp.einsum('tc,tw->cw', feat_docs, whole_output, preferred_element_type=j...  4.47 us
    ppermute x3, starting transfers between devices, shards(): out_list.append(lax.ppermute(out_rows, 'seq', pairs))  4.39 us
  transfers between devices with their start and end apart: 19, of which 7 were waited for; matrix products, arithmetic and copies ran while one was open for 44% of the time, Pallas kernels for 0%

profile of v2, /device:TPU:6, one launch (start us, length us, event | category | flops | bytes accessed | tf_op | source)
XLA Modules:
  0.0 184.6 jit_solution(9776718707405893607)
XLA Ops:
  0.6 2.0 %pad_maximum_fusion.7 = bf16[2,1,128,1024]{3,2,1,0:T(8,128)(2,1)} fusion(bf16[1,1,128,1024]{3,2,1,0:T(8,128)(2,1)} %bitcast.249, bf16[1,1,128,1024]{3,2,1,0:T(8,128)(2,1)} %bitcast.251), kind=kLoop, calls=%fused_computation.52 | loop fusion | flops 262144 | bytes 1048576 | tf_op jit(solution)/shard_map/stack | solution.py:58
  4.1 5.4 %collective-permute-start = (bf16[2,1,128,1024]{3,2,1,0:T(8,128)(2,1)}, bf16[2,1,128,1024]{3,2,1,0:T(8,128)(2,1)}, u32[]{:S(2)}, u32[]{:S(2)}) collective-permute-start(bf16[2,1,128,1024]{3,2,1,0:T(8,128)(2,1)} %pad_maximum_fusion.7), channel_id=1, source_target_pairs={{0,4},{4,8},{8,12},{1,5},{5,9},{9,13},{2,6},{6,10},{10,14},{3,7},{... | collective-permute-start | bytes 1572872 | tf_op jit(solution)/shard_map/ppermute | solution.py:20
  10.5 1.8 stack.36
  12.3 2.4 %convert_reduce_fusion = f32[2,64,1024]{2,1,0:T(8,128)S(1)} fusion(bf16[1,1,64,2,1024]{4,3,2,1,0:T(2,128)(2,1)S(1)} %stack.37, bf16[1,1,64,2,1024]{4,3,2,1,0:T(2,128)(2,1)} %stack.36), kind=kLoop, calls=%fused_computation.37 | loop fusion | flops 655360 | bytes 1048576 | tf_op jit(solution)/shard_map/reduce_sum | solution.py:37
  17.5 3.3 %collective-permute-start.8 = (bf16[128,1024]{1,0:T(8,128)(2,1)}, bf16[128,1024]{1,0:T(8,128)(2,1)S(1)}, u32[]{:S(2)}, u32[]{:S(2)}) collective-permute-start(bf16[128,1024]{1,0:T(8,128)(2,1)} %get-tuple-element.16), channel_id=1, source_target_pairs={{0,12},{4,8},{8,4},{12,0},{1,13},{5,9},{9,5},{13,1},{2,14},{6,10},... | collective-permute-start | bytes 786440 | tf_op jit(solution)/shard_map/ppermute | solution.py:122
  22.8 1.7 constant_dynamic-update-slice_fusion.4
  25.8 12.7 %collective-permute-done.8 = bf16[128,1024]{1,0:T(8,128)(2,1)S(1)} collective-permute-done((bf16[128,1024]{1,0:T(8,128)(2,1)}, bf16[128,1024]{1,0:T(8,128)(2,1)S(1)}, u32[]{:S(2)}, u32[]{:S(2)}) %collective-permute-start.8) | collective-permute-done | bytes 262176 | tf_op jit(solution)/shard_map/ppermute | solution.py:122
  39.7 4.1 %collective-permute-done.6 = bf16[128,1024]{1,0:T(8,128)(2,1)S(1)} collective-permute-done((bf16[128,1024]{1,0:T(8,128)(2,1)}, bf16[128,1024]{1,0:T(8,128)(2,1)S(1)}, u32[]{:S(2)}, u32[]{:S(2)}) %collective-permute-start.6) | collective-permute-done | bytes 262176 | tf_op jit(solution)/shard_map/ppermute | solution.py:122
  46.5 2.9 %collective-permute-done.4 = bf16[128,1024]{1,0:T(8,128)(2,1)S(1)} collective-permute-done((bf16[128,1024]{1,0:T(8,128)(2,1)S(1)}, bf16[128,1024]{1,0:T(8,128)(2,1)S(1)}, u32[]{:S(2)}, u32[]{:S(2)}) %collective-permute-start.4) | collective-permute-done | bytes 262176 | tf_op jit(solution)/shard_map/ppermute | solution.py:122
  49.3 6.7 %collective-permute-start.7 = (bf16[128,1024]{1,0:T(8,128)(2,1)}, bf16[128,1024]{1,0:T(8,128)(2,1)}, u32[]{:S(2)}, u32[]{:S(2)}) collective-permute-start(bf16[128,1024]{1,0:T(8,128)(2,1)} %convolution_convert_fusion.1), channel_id=1, source_target_pairs={{0,8},{4,12},{8,0},{12,4},{1,9},{5,13},{9,1},{13,5},{2,10},{6,14},... | collective-permute-start | bytes 786440 | tf_op jit(solution)/shard_map/ppermute | solution.py:124
  60.5 2.6 %collective-permute-start.5 = (bf16[128,1024]{1,0:T(8,128)(2,1)}, bf16[128,1024]{1,0:T(8,128)(2,1)}, u32[]{:S(2)}, u32[]{:S(2)}) collective-permute-start(bf16[128,1024]{1,0:T(8,128)(2,1)} %convolution_convert_fusion.2), channel_id=1, source_target_pairs={{0,4},{4,0},{8,12},{12,8},{1,5},{5,1},{9,13},{13,9},{2,6},{6,2},{1... | collective-permute-start | bytes 786440 | tf_op jit(solution)/shard_map/ppermute | solution.py:124
  75.5 5.6 %collective-permute-done.3 = bf16[2,1,64,1024]{3,2,1,0:T(8,128)(2,1)S(1)} collective-permute-done((bf16[2,1,64,1024]{3,2,1,0:T(8,128)(2,1)S(1)}, bf16[2,1,64,1024]{3,2,1,0:T(8,128)(2,1)S(1)}, u32[]{:S(2)}, u32[]{:S(2)}) %collective-permute-start.3) | collective-permute-done | bytes 262176 | tf_op jit(solution)/shard_map/ppermute | solution.py:30
  84.7 1.6 multiply_reduce_fusion
  86.3 2.1 %convolution_bitcast_fusion = f32[1,2,192,8,128]{4,2,3,1,0:T(8,128)} fusion(bf16[2,64,8,128]{3,2,1,0:T(8,128)(2,1)S(1)} %bitcast.259, f32[2,8,64,192]{3,2,1,0:T(8,128)S(1)} %get-tuple-element.27, f32[2,8,64]{2,1,0:T(8,128)S(1)} %copy_add_fusion.1, f32[2,8,64]{2,1,0:T(8,128)S(1)} %copy_maximum_fusion), kind=kOutput, calls=%fused_computation.6 | convolution fusion | flops 50921472 | bytes 2629632 | tf_op jit(solution)/shard_map/dbhqk,dbqhe->dbkhe/dot_general | solution.py:166
  94.7 3.1 %pad_maximum_fusion = f32[1,2,2,3,64,1024]{5,0,4,3,2,1:T(1,128)S(1)} fusion(f32[1,1,2,3,64,1024]{5,0,4,3,2,1:T(1,128)S(1)} %bitcast.235, f32[1,1,2,3,64,1024]{5,0,4,3,2,1:T(1,128)S(1)} %bitcast.236), kind=kLoop, calls=%fused_computation.2 | loop fusion | flops 786432 | bytes 6291456 | tf_op jit(solution)/shard_map/stack | solution.py:176
  97.8 2.4 %copy.260 = f32[1,2,2,3,64,1024]{5,4,1,3,2,0:T(8,128)} copy(f32[1,2,2,3,64,1024]{5,0,4,3,2,1:T(1,128)S(1)} %pad_maximum_fusion) | data formatting | bytes 6291456 | tf_op jit(solution)/shard_map/stack | solution.py:176
  100.5 5.4 %scatter_fusion = f32[2,6,64,1024]{3,2,1,0:T(8,128)S(1)} fusion(f32[2,6,64,1024]{3,2,1,0:T(8,128)S(1)} %broadcast.159, s32[6]{0:T(128)S(1)} %reshape.559, f32[6,2,64,1024]{3,2,1,0:T(8,128)} %bitcast.222), kind=kCustom, calls=%fused_computation.1 | custom fusion | flops 786432 | bytes 9437208 | tf_op jit(solution)/shard_map/vmap()/scatter-add | solution.py:46
  111.8 1.7 collective-permute-start.16
  113.5 2.7 %collective-permute-start.17 = (bf16[128,1024]{1,0:T(8,128)(2,1)}, bf16[128,1024]{1,0:T(8,128)(2,1)}, u32[]{:S(2)}, u32[]{:S(2)}) collective-permute-start(bf16[128,1024]{1,0:T(8,128)(2,1)} %bitcast.216), channel_id=1, source_target_pairs={{0,12},{4,8},{8,4},{12,0},{1,13},{5,9},{9,5},{13,1},{2,14},{6,10},... | collective-permute-start | bytes 786440 | tf_op jit(solution)/shard_map/ppermute | solution.py:127
  121.2 25.1 %collective-permute-done.12 = bf16[2,1,64,1024]{3,0,2,1:T(2,128)(2,1)S(1)} collective-permute-done((bf16[2,1,64,1024]{3,0,2,1:T(2,128)(2,1)S(1)}, bf16[2,1,64,1024]{3,0,2,1:T(2,128)(2,1)S(1)}, u32[]{:S(2)}, u32[]{:S(2)}) %collective-permute-start.12) | collective-permute-done | bytes 262176 | tf_op jit(solution)/shard_map/ppermute | solution.py:30
  146.4 1.5 collective-permute-start.11
  149.2 5.3 %collective-permute-start.10 = (bf16[2,1,128,1024]{3,2,1,0:T(8,128)(2,1)}, bf16[2,1,128,1024]{3,2,1,0:T(8,128)(2,1)}, u32[]{:S(2)}, u32[]{:S(2)}) collective-permute-start(bf16[2,1,128,1024]{3,2,1,0:T(8,128)(2,1)} %get-tuple-element.13), channel_id=1, source_target_pairs={{0,4},{4,8},{8,12},{1,5},{5,9},{9,13},{2,6},{6,10},{10,14},{3,7},{... | collective-permute-start | bytes 1572872 | tf_op jit(solution)/shard_map/ppermute | solution.py:20
  154.6 2.2 %pad_maximum_fusion.3 = bf16[512,1024]{1,0:T(8,128)(2,1)} fusion(bf16[128,1024]{1,0:T(8,128)(2,1)} %collective-permute-done.17, bf16[128,1024]{1,0:T(8,128)(2,1)} %collective-permute-done.16, bf16[128,1024]{1,0:T(8,128)(2,1)} %collective-permute-done.15, bf16[128,1024]{1,0:T(8,128)(2,1)} %bitcast.216), kind=kLoop, calls=%fused_computation.33 | loop fusion | flops 4194304 | bytes 2097152 | tf_op jit(solution)/shard_map/concatenate | solution.py:130
  156.8 1.7 constant_dynamic-update-slice_fusion.8
  158.5 1.7 constant_dynamic-update-slice_fusion.7
  160.1 1.7 constant_dynamic-update-slice_fusion.6
  161.8 5.3 %collective-permute-done.13 = bf16[2,1,64,1024]{3,0,2,1:T(2,128)(2,1)S(1)} collective-permute-done((bf16[2,1,64,1024]{3,0,2,1:T(2,128)(2,1)S(1)}, bf16[2,1,64,1024]{3,0,2,1:T(2,128)(2,1)S(1)}, u32[]{:S(2)}, u32[]{:S(2)}) %collective-permute-start.13) | collective-permute-done | bytes 262176 | tf_op jit(solution)/shard_map/ppermute | solution.py:30
  168.1 1.8 mul.187
  169.9 2.3 %constant_dynamic-update-slice_fusion = bf16[1024,1024]{1,0:T(8,128)(2,1)} fusion(bf16[1024,1024]{1,0:T(8,128)(2,1)} %constant_dynamic-update-slice_fusion.1, bf16[512,1024]{1,0:T(8,128)(2,1)} %collective-permute-done.14), kind=kLoop, calls=%fused_computation.91 | loop fusion | bytes 2097152 | tf_op jit(solution)/shard_map/concatenate | solution.py:133
  172.3 1.7 fusion.10
  174.8 4.0 %collective-permute-done.18 = bf16[512,1024]{1,0:T(8,128)(2,1)} collective-permute-done((bf16[512,1024]{1,0:T(8,128)(2,1)}, bf16[512,1024]{1,0:T(8,128)(2,1)}, u32[]{:S(2)}, u32[]{:S(2)}) %collective-permute-start.18) | collective-permute-done | bytes 1048608 | tf_op jit(solution)/shard_map/ppermute | solution.py:30
  180.1 4.5 %fusion.49 = f32[1024,1024]{1,0:T(8,128)} fusion(bf16[1024,1024]{1,0:T(8,128)(2,1)S(1)} %copy-done.29, bf16[1024,1024]{1,0:T(8,128)(2,1)S(1)} %constant_dynamic-update-slice_fusion.5), kind=kOutput, calls=%fused_computation.118 | convolution fusion | flops 2147483648 | bytes 8388608 | tf_op jit(solution)/shard_map/tc,tw->cw/dot_general | solution.py:138
  (168 shorter events, 54.3 us)
Async XLA Ops:
  0.6 23.9 %copy-start = (bf16[1024,1024]{1,0:T(8,128)(2,1)S(1)}, bf16[1024,1024]{1,0:T(8,128)(2,1)}, u32[]{:S(2)}) copy-start(bf16[1024,1024]{1,0:T(8,128)(2,1)} %param.10) | copy-start | bytes 6291460
  2.7 13.9 %copy-start.21 = (bf16[1,128,4096]{2,1,0:T(8,128)(2,1)S(1)}, bf16[1,128,4096]{2,1,0:T(8,128)(2,1)}, u32[]{:S(2)}) copy-start(bf16[1,128,4096]{2,1,0:T(8,128)(2,1)} %param.11) | copy-start | bytes 3145732
  2.7 57.8 %collective-permute-start.1 = (bf16[2,1,128,1024]{3,2,1,0:T(8,128)(2,1)}, bf16[2,1,128,1024]{3,2,1,0:T(8,128)(2,1)}, u32[]{:S(2)}, u32[]{:S(2)}) collective-permute-start(bf16[2,1,128,1024]{3,2,1,0:T(8,128)(2,1)} %pad_maximum_fusion.7), channel_id=1, source_target_pairs={{4,0},{8,4},{12,8},{5,1},{9,5},{13,9},{6,2},{10,6},{14,10},{7,3},{... | collective-permute-start | bytes 1572872 | tf_op jit(solution)/shard_map/ppermute | solution.py:22
  4.1 59.0 %collective-permute-start = (bf16[2,1,128,1024]{3,2,1,0:T(8,128)(2,1)}, bf16[2,1,128,1024]{3,2,1,0:T(8,128)(2,1)}, u32[]{:S(2)}, u32[]{:S(2)}) collective-permute-start(bf16[2,1,128,1024]{3,2,1,0:T(8,128)(2,1)} %pad_maximum_fusion.7), channel_id=1, source_target_pairs={{0,4},{4,8},{8,12},{1,5},{5,9},{9,13},{2,6},{6,10},{10,14},{3,7},{... | collective-permute-start | bytes 1572872 | tf_op jit(solution)/shard_map/ppermute | solution.py:20
  12.3 8.5 %copy-start.30 = (s32[1,2,2]{2,1,0:T(2,128)S(1)}, s32[1,2,2]{2,1,0:T(2,128)}, u32[]{:S(2)}) copy-start(s32[1,2,2]{2,1,0:T(2,128)} %param.9) | copy-start | bytes 52
  15.8 50.2 %collective-permute-start.2 = (f32[2,1,64,1024]{3,2,1,0:T(8,128)}, f32[2,1,64,1024]{3,2,1,0:T(8,128)}, u32[]{:S(2)}, u32[]{:S(2)}) collective-permute-start(f32[2,1,64,1024]{3,2,1,0:T(8,128)} %get-tuple-element.25), channel_id=1, source_target_pairs={{0,4},{4,0},{8,12},{12,8},{1,5},{5,1},{9,13},{13,9},{2,6},{6,2},{1... | collective-permute-start | bytes 1572872 | tf_op jit(solution)/shard_map/ppermute | solution.py:30
  17.5 21.0 %collective-permute-start.8 = (bf16[128,1024]{1,0:T(8,128)(2,1)}, bf16[128,1024]{1,0:T(8,128)(2,1)S(1)}, u32[]{:S(2)}, u32[]{:S(2)}) collective-permute-start(bf16[128,1024]{1,0:T(8,128)(2,1)} %get-tuple-element.16), channel_id=1, source_target_pairs={{0,12},{4,8},{8,4},{12,0},{1,13},{5,9},{9,5},{13,1},{2,14},{6,10},... | collective-permute-start | bytes 786440 | tf_op jit(solution)/shard_map/ppermute | solution.py:122
  20.8 23.1 %collective-permute-start.6 = (bf16[128,1024]{1,0:T(8,128)(2,1)}, bf16[128,1024]{1,0:T(8,128)(2,1)S(1)}, u32[]{:S(2)}, u32[]{:S(2)}) collective-permute-start(bf16[128,1024]{1,0:T(8,128)(2,1)} %get-tuple-element.17), channel_id=1, source_target_pairs={{0,8},{4,12},{8,0},{12,4},{1,9},{5,13},{9,1},{13,5},{2,10},{6,14},... | collective-permute-start | bytes 786440 | tf_op jit(solution)/shard_map/ppermute | solution.py:122
  22.0 16.5 %copy-start.27 = (bf16[128,1024]{1,0:T(8,128)(2,1)S(1)}, bf16[128,1024]{1,0:T(8,128)(2,1)}, u32[]{:S(2)}) copy-start(bf16[128,1024]{1,0:T(8,128)(2,1)} %get-tuple-element.15) | copy-start | bytes 786436
  38.5 10.8 %collective-permute-start.4 = (bf16[128,1024]{1,0:T(8,128)(2,1)S(1)}, bf16[128,1024]{1,0:T(8,128)(2,1)S(1)}, u32[]{:S(2)}, u32[]{:S(2)}) collective-permute-start(bf16[128,1024]{1,0:T(8,128)(2,1)S(1)} %copy-done.27), channel_id=1, source_target_pairs={{0,4},{4,0},{8,12},{12,8},{1,5},{5,1},{9,13},{13,9},{2,6},{6,2},{1... | collective-permute-start | bytes 786440 | tf_op jit(solution)/shard_map/ppermute | solution.py:122
  43.8 27.7 %collective-permute-start.9 = (bf16[128,1024]{1,0:T(8,128)(2,1)}, bf16[128,1024]{1,0:T(8,128)(2,1)}, u32[]{:S(2)}, u32[]{:S(2)}) collective-permute-start(bf16[128,1024]{1,0:T(8,128)(2,1)} %convolution_convert_fusion), channel_id=1, source_target_pairs={{0,12},{4,8},{8,4},{12,0},{1,13},{5,9},{9,5},{13,1},{2,14},{6,10},... | collective-permute-start | bytes 786440 | tf_op jit(solution)/shard_map/ppermute | solution.py:124
  49.3 22.2 %collective-permute-start.7 = (bf16[128,1024]{1,0:T(8,128)(2,1)}, bf16[128,1024]{1,0:T(8,128)(2,1)}, u32[]{:S(2)}, u32[]{:S(2)}) collective-permute-start(bf16[128,1024]{1,0:T(8,128)(2,1)} %convolution_convert_fusion.1), channel_id=1, source_target_pairs={{0,8},{4,12},{8,0},{12,4},{1,9},{5,13},{9,1},{13,5},{2,10},{6,14},... | collective-permute-start | bytes 786440 | tf_op jit(solution)/shard_map/ppermute | solution.py:124
  57.1 6.5 %copy-start.8 = (bf16[1,128,1024]{2,1,0:T(8,128)(2,1)S(1)}, bf16[1,128,1024]{2,1,0:T(8,128)(2,1)}, u32[]{:S(2)}) copy-start(bf16[1,128,1024]{2,1,0:T(8,128)(2,1)} %param.8) | copy-start | bytes 786436
  57.1 6.5 %copy-start.9 = (bf16[1,128,1024]{2,1,0:T(8,128)(2,1)S(1)}, bf16[1,128,1024]{2,1,0:T(8,128)(2,1)}, u32[]{:S(2)}) copy-start(bf16[1,128,1024]{2,1,0:T(8,128)(2,1)} %param.7) | copy-start | bytes 786436
  60.5 11.0 %collective-permute-start.5 = (bf16[128,1024]{1,0:T(8,128)(2,1)}, bf16[128,1024]{1,0:T(8,128)(2,1)}, u32[]{:S(2)}, u32[]{:S(2)}) collective-permute-start(bf16[128,1024]{1,0:T(8,128)(2,1)} %convolution_convert_fusion.2), channel_id=1, source_target_pairs={{0,4},{4,0},{8,12},{12,8},{1,5},{5,1},{9,13},{13,9},{2,6},{6,2},{1... | collective-permute-start | bytes 786440 | tf_op jit(solution)/shard_map/ppermute | solution.py:124
  63.1 106.8 %collective-permute-start.14 = (bf16[512,1024]{1,0:T(8,128)(2,1)}, bf16[512,1024]{1,0:T(8,128)(2,1)}, u32[]{:S(2)}, u32[]{:S(2)}) collective-permute-start(bf16[512,1024]{1,0:T(8,128)(2,1)} %pad_maximum_fusion.2), channel_id=1, source_target_pairs={{0,2},{2,0},{1,3},{3,1},{4,6},{6,4},{5,7},{7,5},{8,10},{10,8},{9,1... | collective-permute-start | bytes 3145736 | tf_op jit(solution)/shard_map/ppermute | solution.py:30
  71.4 9.7 %collective-permute-start.3 = (bf16[2,1,64,1024]{3,2,1,0:T(8,128)(2,1)S(1)}, bf16[2,1,64,1024]{3,2,1,0:T(8,128)(2,1)S(1)}, u32[]{:S(2)}, u32[]{:S(2)}) collective-permute-start(bf16[2,1,64,1024]{3,2,1,0:T(8,128)(2,1)S(1)} %fusion.23), channel_id=1, source_target_pairs={{0,8},{4,12},{8,0},{12,4},{1,9},{5,13},{9,1},{13,5},{2,10},{6,14},... | collective-permute-start | bytes 786440 | tf_op jit(solution)/shard_map/ppermute | solution.py:30
  72.8 13.5 %copy-start.14 = (bf16[16,8,8,128]{3,2,1,0:T(8,128)(2,1)}, bf16[16,8,8,128]{3,2,1,0:T(8,128)(2,1)S(1)}, u32[]{:S(2)}) copy-start(bf16[16,8,8,128]{3,2,1,0:T(8,128)(2,1)S(1)} %copy.264) | copy-start | bytes 786436
  73.6 8.4 %copy-start.23 = (bf16[2,64,8,128]{3,1,0,2:T(8,128)(2,1)S(1)}, bf16[2,64,8,128]{3,1,0,2:T(8,128)(2,1)}, u32[]{:S(2)}) copy-start(bf16[2,64,8,128]{3,1,0,2:T(8,128)(2,1)} %copy.208) | copy-start | bytes 786436
  82.2 7.7 %copy-start.2 = (f32[8,128,128]{1,2,0}, f32[8,128,128]{1,2,0:S(1)}, u32[]{:S(2)}) copy-start(f32[8,128,128]{1,2,0:S(1)} %fusion.50) | copy-start | bytes 1572868
  109.0 7.5 %copy-start.11 = (bf16[1,1,128,1024]{2,3,1,0:T(8,128)(2,1)S(1)}, bf16[1,1,128,1024]{2,3,1,0:T(8,128)(2,1)}, u32[]{:S(2)}) copy-start(bf16[1,1,128,1024]{2,3,1,0:T(8,128)(2,1)} %copy-done.10) | copy-start | bytes 786436
  109.0 7.5 %copy-start.17 = (f32[1,2,64,8,128]{4,2,3,1,0:T(8,128)S(1)}, f32[1,2,64,8,128]{4,2,3,1,0:T(8,128)}, u32[]{:S(2)}) copy-start(f32[1,2,64,8,128]{4,2,3,1,0:T(8,128)} %convolution_bitcast_fusion.1) | copy-start | bytes 1572868
  111.8 37.4 %collective-permute-start.15 = (bf16[128,1024]{1,0:T(8,128)(2,1)}, bf16[128,1024]{1,0:T(8,128)(2,1)}, u32[]{:S(2)}, u32[]{:S(2)}) collective-permute-start(bf16[128,1024]{1,0:T(8,128)(2,1)} %bitcast.216), channel_id=1, source_target_pairs={{0,4},{4,0},{8,12},{12,8},{1,5},{5,1},{9,13},{13,9},{2,6},{6,2},{1... | collective-permute-start | bytes 786440 | tf_op jit(solution)/shard_map/ppermute | solution.py:127
  111.8 42.8 %collective-permute-start.16 = (bf16[128,1024]{1,0:T(8,128)(2,1)}, bf16[128,1024]{1,0:T(8,128)(2,1)}, u32[]{:S(2)}, u32[]{:S(2)}) collective-permute-start(bf16[128,1024]{1,0:T(8,128)(2,1)} %bitcast.216), channel_id=1, source_target_pairs={{0,8},{4,12},{8,0},{12,4},{1,9},{5,13},{9,1},{13,5},{2,10},{6,14},... | collective-permute-start | bytes 786440 | tf_op jit(solution)/shard_map/ppermute | solution.py:127
  113.5 41.1 %collective-permute-start.17 = (bf16[128,1024]{1,0:T(8,128)(2,1)}, bf16[128,1024]{1,0:T(8,128)(2,1)}, u32[]{:S(2)}, u32[]{:S(2)}) collective-permute-start(bf16[128,1024]{1,0:T(8,128)(2,1)} %bitcast.216), channel_id=1, source_target_pairs={{0,12},{4,8},{8,4},{12,0},{1,13},{5,9},{9,5},{13,1},{2,14},{6,10},... | collective-permute-start | bytes 786440 | tf_op jit(solution)/shard_map/ppermute | solution.py:127
  118.9 27.4 %collective-permute-start.12 = (bf16[2,1,64,1024]{3,0,2,1:T(2,128)(2,1)S(1)}, bf16[2,1,64,1024]{3,0,2,1:T(2,128)(2,1)S(1)}, u32[]{:S(2)}, u32[]{:S(2)}) collective-permute-start(bf16[2,1,64,1024]{3,0,2,1:T(2,128)(2,1)S(1)} %fusion.34), channel_id=1, source_target_pairs={{0,8},{4,12},{8,0},{12,4},{1,9},{5,13},{9,1},{13,5},{2,10},{6,14},... | collective-permute-start | bytes 786440 | tf_op jit(solution)/shard_map/ppermute | solution.py:30
  146.4 25.8 %collective-permute-start.11 = (bf16[2,1,128,1024]{3,2,1,0:T(8,128)(2,1)}, bf16[2,1,128,1024]{3,2,1,0:T(8,128)(2,1)}, u32[]{:S(2)}, u32[]{:S(2)}) collective-permute-start(bf16[2,1,128,1024]{3,2,1,0:T(8,128)(2,1)} %get-tuple-element.14), channel_id=1, source_target_pairs={{4,0},{8,4},{12,8},{5,1},{9,5},{13,9},{6,2},{10,6},{14,10},{7,3},{... | collective-permute-start | bytes 1572872 | tf_op jit(solution)/shard_map/ppermute | solution.py:22
  149.2 23.0 %collective-permute-start.10 = (bf16[2,1,128,1024]{3,2,1,0:T(8,128)(2,1)}, bf16[2,1,128,1024]{3,2,1,0:T(8,128)(2,1)}, u32[]{:S(2)}, u32[]{:S(2)}) collective-permute-start(bf16[2,1,128,1024]{3,2,1,0:T(8,128)(2,1)} %get-tuple-element.13), channel_id=1, source_target_pairs={{0,4},{4,8},{8,12},{1,5},{5,9},{9,13},{2,6},{6,10},{10,14},{3,7},{... | collective-permute-start | bytes 1572872 | tf_op jit(solution)/shard_map/ppermute | solution.py:20
  154.5 12.5 %collective-permute-start.13 = (bf16[2,1,64,1024]{3,0,2,1:T(2,128)(2,1)S(1)}, bf16[2,1,64,1024]{3,0,2,1:T(2,128)(2,1)S(1)}, u32[]{:S(2)}, u32[]{:S(2)}) collective-permute-start(bf16[2,1,64,1024]{3,0,2,1:T(2,128)(2,1)S(1)} %fusion.24), channel_id=1, source_target_pairs={{0,4},{4,0},{8,12},{12,8},{1,5},{5,1},{9,13},{13,9},{2,6},{6,2},{1... | collective-permute-start | bytes 786440 | tf_op jit(solution)/shard_map/ppermute | solution.py:30
  156.8 22.0 %collective-permute-start.18 = (bf16[512,1024]{1,0:T(8,128)(2,1)}, bf16[512,1024]{1,0:T(8,128)(2,1)}, u32[]{:S(2)}, u32[]{:S(2)}) collective-permute-start(bf16[512,1024]{1,0:T(8,128)(2,1)} %pad_maximum_fusion.3), channel_id=1, source_target_pairs={{0,2},{2,0},{1,3},{3,1},{4,6},{6,4},{5,7},{7,5},{8,10},{10,8},{9,1... | collective-permute-start | bytes 3145736 | tf_op jit(solution)/shard_map/ppermute | solution.py:30
  172.3 6.5 %copy-start.28 = (bf16[1024,1024]{1,0:T(8,128)(2,1)S(1)}, bf16[1024,1024]{1,0:T(8,128)(2,1)}, u32[]{:S(2)}) copy-start(bf16[1024,1024]{1,0:T(8,128)(2,1)} %constant_dynamic-update-slice_fusion.6) | copy-start | bytes 6291460
  173.9 6.2 %copy-start.29 = (bf16[1024,1024]{1,0:T(8,128)(2,1)S(1)}, bf16[1024,1024]{1,0:T(8,128)(2,1)}, u32[]{:S(2)}) copy-start(bf16[1024,1024]{1,0:T(8,128)(2,1)} %constant_dynamic-update-slice_fusion) | copy-start | bytes 6291460
  (18 other events, 41.0 us)

commit v3 on v2

--- a/solution.py
+++ b/solution.py
@@ -62,21 +62,32 @@
     chosen = jnp.concatenate([local_ids, local_ids + pattern], axis=2) + 2
     near_pair = jax.vmap(pick_blocks, in_axes=(1, 0), out_axes=1)(blocks_six, chosen)
     near_pair = near_pair.reshape(2, doc_count, 2, near_width, head_cols)
-    pooled = pool_pairs(key_value.astype(jnp.float32))
-    siblings = []
-    own_level = pooled
+    pieces = []
+    level_rows = key_value.astype(jnp.float32)
     for level_no in range(levels):
-        other = swapped(own_level, "seq", level_no)
-        siblings.append(other)
-        if level_no + 1 < levels:
-            upper = position >> level_no & 1 == 1
-            joined = jnp.where(
-                upper,
-                jnp.concatenate([other, own_level], axis=2),
-                jnp.concatenate([own_level, other], axis=2),
-            )
-            own_level = pool_pairs(joined)
-    far_pair = jnp.concatenate(siblings, axis=2).astype(jnp.bfloat16)
+        level_rows = pool_pairs(level_rows)
+        pieces.append(level_rows.astype(jnp.bfloat16))
+    feat_count = cotangent.shape[2] // seq_count
+    cot_rows = cotangent.reshape(doc_count * tok_count, cotangent.shape[2])
+    cot_height = doc_count * tok_count
+    far_parts = []
+    got_list = []
+    for step in range(1, seq_count):
+        pairs = [(i, i ^ step) for i in range(seq_count)]
+        piece = pieces[step.bit_length() - 1]
+        sent = lax.dynamic_slice_in_dim(
+            cot_rows, (position ^ step) * feat_count, feat_count, axis=1
+        )
+        if feat_count == head_cols:
+            payload = jnp.concatenate([sent, piece.reshape(-1, head_cols)], axis=0)
+            arrived = lax.ppermute(payload, "seq", pairs)
+            got = arrived[:cot_height]
+            far_parts.append(arrived[cot_height:].reshape(piece.shape))
+        else:
+            got = lax.ppermute(sent, "seq", pairs)
+            far_parts.append(lax.ppermute(piece, "seq", pairs))
+        got_list.append(got)
+    far_pair = jnp.concatenate(far_parts, axis=2)
     query_heads = queries.reshape(doc_count, 2, block, heads, HEAD_DIM)
     near_k = near_pair[0].reshape(doc_count, 2, near_width, heads, HEAD_DIM)
     near_v = near_pair[1].reshape(doc_count, 2, near_width, heads, HEAD_DIM)
@@ -107,8 +118,6 @@
         "dbhqk,dkhe->dbqhe", rounded_far, far_v, preferred_element_type=jnp.float32
     )
     attention = output.reshape(doc_count, tok_count, head_cols).astype(jnp.bfloat16)
-    feat_count = cotangent.shape[2] // seq_count
-    cot_rows = cotangent.reshape(doc_count * tok_count, cotangent.shape[2])
     out_rows = attention.reshape(doc_count * tok_count, head_cols)
     own_cols = lax.dynamic_slice_in_dim(cot_rows, position * feat_count, feat_count, axis=1)
     grad_sum = jnp.dot(own_cols, out_weight, preferred_element_type=jnp.float32)
@@ -116,10 +125,7 @@
     out_list = [out_rows]
     for step in range(1, seq_count):
         pairs = [(i, i ^ step) for i in range(seq_count)]
-        sent = lax.dynamic_slice_in_dim(
-            cot_rows, (position ^ step) * feat_count, feat_count, axis=1
-        )
-        got = lax.ppermute(sent, "seq", pairs)
+        got = got_list[step - 1]
         part = jnp.dot(got, out_weight, preferred_element_type=jnp.float32)
         back = lax.ppermute(part.astype(jnp.bfloat16), "seq", pairs)
         grad_sum = grad_sum + back.astype(jnp.float32)
@@ -186,22 +192,25 @@
     token_grad = back_six[:, :, 2:4].reshape(2, doc_count, tok_count, head_cols)
     token_grad = token_grad + beside_all[:, :, :tok_count] + beside_all[:, :, 3 * tok_count :]
     far_rows = jnp.stack([far_key_rows, far_value_rows]).reshape(
-        2, doc_count, levels, block, head_cols
-    )
-    carried = jnp.zeros((2, doc_count, block, head_cols), jnp.float32)
-    for level_no in reversed(range(levels)):
-        message = far_rows[:, :, level_no]
-        mine = jnp.zeros_like(message)
-        if level_no + 1 < levels:
-            upper = position >> level_no & 1 == 1
-            spread = jnp.repeat(carried, 2, axis=2) * 0.5
-            lower_half = spread[:, :, :block]
-            upper_half = spread[:, :, block:]
-            mine = jnp.where(upper, upper_half, lower_half)
-            message = message + jnp.where(upper, lower_half, upper_half)
-        returned = swapped(message.astype(jnp.bfloat16), "seq", level_no).astype(jnp.float32)
-        carried = returned + mine
-    token_grad = token_grad + jnp.repeat(carried, 2, axis=2) * 0.5
+        2, doc_count, levels * block, head_cols
+    )
+    level_sums = [None] * levels
+    offset = 0
+    for step in range(1, seq_count):
+        level_no = step.bit_length() - 1
+        height = pieces[level_no].shape[2]
+        segment = lax.slice_in_dim(far_rows, offset, offset + height, axis=2)
+        offset += height
+        returned = lax.ppermute(
+            segment.astype(jnp.bfloat16), "seq", [(i, i ^ step) for i in range(seq_count)]
+        ).astype(jnp.float32)
+        if level_sums[level_no] is None:
+            level_sums[level_no] = returned
+        else:
+            level_sums[level_no] = level_sums[level_no] + returned
+    for level_no in range(levels):
+        spread = 2 ** (level_no + 1)
+        token_grad = token_grad + jnp.repeat(level_sums[level_no], spread, axis=2) / float(spread)
     key_grad = token_grad[0].astype(jnp.bfloat16)
     value_grad = token_grad[1].astype(jnp.bfloat16)
     return (attention, query_grad, key_grad, value_grad, weight_grad)

time: 185 us -> 253 us (1.37)
  waiting for transfers between devices: 59.8 us -> 95.3 us
  starting transfers between devices: 33.6 us -> 66.4 us
  other arithmetic: 31.8 us -> 26.7 us
  local copies, waits for them, and re-layouts: 38.8 us -> 42.5 us
    ppermute x3 -> x6, waiting for transfers between devices: 19.8 us -> 61.2 us  [the longest x3 32.5 us: shards(): lax.ppermute(segment.astype(jnp.bfloat16), 'seq', [(i, i ^ step) for i in...]
    ppermute x3 -> x6, starting transfers between devices: 3.27 us -> 34.6 us  [the longest x3 30.3 us: shards(): lax.ppermute(segment.astype(jnp.bfloat16), 'seq', [(i, i ^ step) for i in...]
    ppermute x6 -> x2, waiting for transfers between devices: 40.1 us -> 33.6 us  [swapped(): lax.ppermute(shard, axis, [(i, i ^ 1 << stride) for i in range(lax.axis_s...]
    ppermute x3, starting transfers between devices: 10.8 us -> 15.1 us  [shards(): back = lax.ppermute(part.astype(jnp.bfloat16), 'seq', pairs)]
    gather x5, local copies, waits for them, and re-layouts: 0.98 us -> 4.99 us  [pick_blocks(): return blocks_doc[:, chosen_doc]]
    slice x0 -> x8, local copies, waits for them, and re-layouts: none -> 3.74 us  [the longest x3 3.39 us: shards(): got = arrived[:cot_height]]
    unnamed x75 -> x82, local copies, waits for them, and re-layouts: 13.8 us -> 10.6 us
    ppermute x2, starting transfers between devices: 10.7 us -> 7.63 us  [extended(): lax.ppermute(tail, axis, [(i, (i + 1) % count) for i in range(ends)])]
  transfers between devices with their start and end apart: 19 -> 18, of which waited for: 7 -> 8; matrix products, arithmetic and copies ran while one was open for 44% -> 22% of each run, Pallas kernels for 0% -> 0%
where the time goes in v3:
time: 253 us; the launch traced here: 251 us
  waiting for transfers between devices  95.3 us (38%)
  starting transfers between devices  66.4 us (26%)
  local copies, waits for them, and re-layouts  42.5 us (17%)
  other arithmetic  26.7 us (11%)
  matrix products  19 us (8%)
    ppermute x2, waiting for transfers between devices, swapped(): lax.ppermute(shard, axis, [(i, i ^ 1 << stride) for i in range(lax.axis_s...  33.6 us
    ppermute x3, waiting for transfers between devices, shards(): lax.ppermute(segment.astype(jnp.bfloat16), 'seq', [(i, i ^ step) for i in...  32.5 us
    ppermute x3, starting transfers between devices, shards(): lax.ppermute(segment.astype(jnp.bfloat16), 'seq', [(i, i ^ step) for i in...  30.3 us
    ppermute x3, waiting for transfers between devices, shards(): arrived = lax.ppermute(payload, 'seq', pairs)  28.7 us
    ppermute x3, starting transfers between devices, shards(): back = lax.ppermute(part.astype(jnp.bfloat16), 'seq', pairs)  15.1 us
    unnamed x82, local copies, waits for them, and re-layouts  10.6 us
    ppermute x2, starting transfers between devices, extended(): lax.ppermute(tail, axis, [(i, (i + 1) % count) for i in range(ends)])  7.63 us
    scatter-add x1, other arithmetic, place_blocks(): return holder.at[:, chosen_doc].add(grad_doc)  5.59 us
  transfers between devices with their start and end apart: 18, of which 8 were waited for; matrix products, arithmetic and copies ran while one was open for 22% of the time, Pallas kernels for 0%

profile of v3, /device:TPU:6, one launch (start us, length us, event | category | flops | bytes accessed | tf_op | source)
XLA Modules:
  0.0 251.3 jit_solution(9818068307172606012)
XLA Ops:
  0.6 2.0 pad_maximum_fusion.6
  4.0 5.4 %collective-permute-start = (bf16[2,1,128,1024]{3,2,1,0:T(8,128)(2,1)}, bf16[2,1,128,1024]{3,2,1,0:T(8,128)(2,1)}, u32[]{:S(2)}, u32[]{:S(2)}) collective-permute-start(bf16[2,1,128,1024]{3,2,1,0:T(8,128)(2,1)} %pad_maximum_fusion.6), channel_id=1, source_target_pairs={{0,4},{4,8},{8,12},{1,5},{5,9},{9,13},{2,6},{6,10},{10,14},{3,7},{... | collective-permute-start | bytes 1572872 | tf_op jit(solution)/shard_map/ppermute | solution.py:20
  19.5 1.8 collective-permute-start.2
  21.4 1.7 constant_dynamic-update-slice_fusion.4
  26.1 4.2 %collective-permute-done.4 = bf16[192,1024]{1,0:T(8,128)(2,1)S(1)} collective-permute-done((bf16[192,1024]{1,0:T(8,128)(2,1)}, bf16[192,1024]{1,0:T(8,128)(2,1)S(1)}, u32[]{:S(2)}, u32[]{:S(2)}) %collective-permute-start.4) | collective-permute-done | bytes 393248 | tf_op jit(solution)/shard_map/ppermute | solution.py:83
  31.4 3.6 %collective-permute-start.7 = (bf16[128,1024]{1,0:T(8,128)(2,1)}, bf16[128,1024]{1,0:T(8,128)(2,1)}, u32[]{:S(2)}, u32[]{:S(2)}) collective-permute-start(bf16[128,1024]{1,0:T(8,128)(2,1)} %convolution_convert_fusion), channel_id=1, source_target_pairs={{0,12},{4,8},{8,4},{12,0},{1,13},{5,9},{9,5},{13,1},{2,14},{6,10},... | collective-permute-start | bytes 786440 | tf_op jit(solution)/shard_map/ppermute | solution.py:130
  35.0 24.5 %collective-permute-done.3 = bf16[192,1024]{1,0:T(8,128)(2,1)S(1)} collective-permute-done((bf16[192,1024]{1,0:T(8,128)(2,1)}, bf16[192,1024]{1,0:T(8,128)(2,1)S(1)}, u32[]{:S(2)}, u32[]{:S(2)}) %collective-permute-start.3) | collective-permute-done | bytes 393248 | tf_op jit(solution)/shard_map/ppermute | solution.py:83
  60.8 2.5 pad_maximum_fusion.1
  63.3 3.3 %gather_fusion = bf16[6,2,64,1024]{3,2,1,0:T(8,128)(2,1)} fusion(bf16[1,2,6,64,1024]{4,3,2,1,0:T(8,128)(2,1)} %bitcast.211, s32[6]{0:T(128)S(1)} %reshape.495), kind=kCustom, calls=%fused_computation | custom fusion | bytes 3145776 | tf_op jit(solution)/shard_map/vmap()/gather | solution.py:41
  69.6 1.6 fusion.49
  71.2 1.9 fusion.44
  74.0 1.8 copy.135
  77.3 1.6 fusion.12
  79.3 1.8 copy.142
  82.6 11.4 %collective-permute-start.5 = (bf16[128,1024]{1,0:T(8,128)(2,1)S(1)}, bf16[128,1024]{1,0:T(8,128)(2,1)S(1)}, u32[]{:S(2)}, u32[]{:S(2)}) collective-permute-start(bf16[128,1024]{1,0:T(8,128)(2,1)S(1)} %convolution_convert_fusion.2), channel_id=1, source_target_pairs={{0,4},{4,0},{8,12},{12,8},{1,5},{5,1},{9,13},{13,9},{2,6},{6,2},{1... | collective-permute-start | bytes 786440 | tf_op jit(solution)/shard_map/ppermute | solution.py:130
  107.1 3.1 %pad_maximum_fusion = f32[1,2,2,3,64,1024]{5,0,4,3,2,1:T(1,128)S(1)} fusion(f32[1,1,2,3,64,1024]{5,0,4,3,2,1:T(1,128)S(1)} %bitcast.213, f32[1,1,2,3,64,1024]{5,0,4,3,2,1:T(1,128)S(1)} %bitcast.214), kind=kLoop, calls=%fused_computation.2 | loop fusion | flops 786432 | bytes 6291456 | tf_op jit(solution)/shard_map/stack | solution.py:182
  110.2 2.4 copy.185
  113.0 5.6 %scatter_fusion = f32[2,6,64,1024]{3,2,1,0:T(8,128)S(1)} fusion(f32[2,6,64,1024]{3,2,1,0:T(8,128)S(1)} %broadcast.138, s32[6]{0:T(128)S(1)} %reshape.507, f32[6,2,64,1024]{3,2,1,0:T(8,128)} %bitcast.202), kind=kCustom, calls=%fused_computation.1 | custom fusion | flops 786432 | bytes 9437208 | tf_op jit(solution)/shard_map/vmap()/scatter-add | solution.py:46
  123.7 2.0 collective-permute-start.14
  125.7 2.4 collective-permute-start.16
  134.7 15.9 %collective-permute-done.12 = bf16[2,1,32,1024]{2,3,1,0:T(8,128)(2,1)S(1)} collective-permute-done((bf16[2,1,32,1024]{2,3,1,0:T(8,128)(2,1)S(1)}, bf16[2,1,32,1024]{2,3,1,0:T(8,128)(2,1)S(1)}, u32[]{:S(2)}, u32[]{:S(2)}) %collective-permute-start.12) | collective-permute-done | bytes 131104 | tf_op jit(solution)/shard_map/ppermute | solution.py:204
  150.5 27.6 %collective-permute-start.10 = (bf16[2,1,64,1024]{2,3,1,0:T(8,128)(2,1)S(1)}, bf16[2,1,64,1024]{2,3,1,0:T(8,128)(2,1)S(1)}, u32[]{:S(2)}, u32[]{:S(2)}) collective-permute-start(bf16[2,1,64,1024]{2,3,1,0:T(8,128)(2,1)S(1)} %bitcast.217), channel_id=1, source_target_pairs={{0,4},{4,0},{8,12},{12,8},{1,5},{5,1},{9,13},{13,9},{2,6},{6,2},{1... | collective-permute-start | bytes 786440 | tf_op jit(solution)/shard_map/ppermute | solution.py:204
  178.1 8.7 %collective-permute-done.11 = bf16[2,1,32,1024]{2,3,1,0:T(8,128)(2,1)S(1)} collective-permute-done((bf16[2,1,32,1024]{2,3,1,0:T(8,128)(2,1)S(1)}, bf16[2,1,32,1024]{2,3,1,0:T(8,128)(2,1)S(1)}, u32[]{:S(2)}, u32[]{:S(2)}) %collective-permute-start.11) | collective-permute-done | bytes 131104 | tf_op jit(solution)/shard_map/ppermute | solution.py:204
  190.3 7.9 %collective-permute-done.10 = bf16[2,1,64,1024]{2,3,1,0:T(8,128)(2,1)S(1)} collective-permute-done((bf16[2,1,64,1024]{2,3,1,0:T(8,128)(2,1)S(1)}, bf16[2,1,64,1024]{2,3,1,0:T(8,128)(2,1)S(1)}, u32[]{:S(2)}, u32[]{:S(2)}) %collective-permute-start.10) | collective-permute-done | bytes 262176 | tf_op jit(solution)/shard_map/ppermute | solution.py:204
  198.1 2.3 collective-permute-start.8
  205.4 1.7 constant_dynamic-update-slice_fusion.8
  207.0 1.7 constant_dynamic-update-slice_fusion.7
  208.7 1.7 constant_dynamic-update-slice_fusion.6
  210.4 1.8 fusion.10
  213.1 15.2 %collective-permute-done.13 = bf16[512,1024]{1,0:T(8,128)(2,1)S(1)} collective-permute-done((bf16[512,1024]{1,0:T(8,128)(2,1)}, bf16[512,1024]{1,0:T(8,128)(2,1)S(1)}, u32[]{:S(2)}, u32[]{:S(2)}) %collective-permute-start.13) | collective-permute-done | bytes 1048608 | tf_op jit(solution)/shard_map/ppermute | solution.py:30
  228.4 18.4 %collective-permute-done.17 = bf16[512,1024]{1,0:T(8,128)(2,1)S(1)} collective-permute-done((bf16[512,1024]{1,0:T(8,128)(2,1)S(1)}, bf16[512,1024]{1,0:T(8,128)(2,1)S(1)}, u32[]{:S(2)}, u32[]{:S(2)}) %collective-permute-start.17) | collective-permute-done | bytes 1048608 | tf_op jit(solution)/shard_map/ppermute | solution.py:30
  246.8 4.5 %fusion.51 = f32[1024,1024]{1,0:T(8,128)} fusion(bf16[1024,1024]{1,0:T(8,128)(2,1)S(1)} %constant_dynamic-update-slice_fusion, bf16[1024,1024]{1,0:T(8,128)(2,1)S(1)} %constant_dynamic-update-slice_fusion.5), kind=kOutput, calls=%fused_computation.116 | convolution fusion | flops 2147483648 | bytes 8388608 | tf_op jit(solution)/shard_map/tc,tw->cw/dot_general | solution.py:144
  (181 shorter events, 58.1 us)
Async XLA Ops:
  0.6 23.2 %copy-start = (bf16[1024,1024]{1,0:T(8,128)(2,1)S(1)}, bf16[1024,1024]{1,0:T(8,128)(2,1)}, u32[]{:S(2)}) copy-start(bf16[1024,1024]{1,0:T(8,128)(2,1)} %param.10) | copy-start | bytes 6291460
  2.7 58.1 %collective-permute-start.1 = (bf16[2,1,128,1024]{3,2,1,0:T(8,128)(2,1)}, bf16[2,1,128,1024]{3,2,1,0:T(8,128)(2,1)}, u32[]{:S(2)}, u32[]{:S(2)}) collective-permute-start(bf16[2,1,128,1024]{3,2,1,0:T(8,128)(2,1)} %pad_maximum_fusion.6), channel_id=1, source_target_pairs={{4,0},{8,4},{12,8},{5,1},{9,5},{13,9},{6,2},{10,6},{14,10},{7,3},{... | collective-permute-start | bytes 1572872 | tf_op jit(solution)/shard_map/ppermute | solution.py:22
  4.0 56.8 %collective-permute-start = (bf16[2,1,128,1024]{3,2,1,0:T(8,128)(2,1)}, bf16[2,1,128,1024]{3,2,1,0:T(8,128)(2,1)}, u32[]{:S(2)}, u32[]{:S(2)}) collective-permute-start(bf16[2,1,128,1024]{3,2,1,0:T(8,128)(2,1)} %pad_maximum_fusion.6), channel_id=1, source_target_pairs={{0,4},{4,8},{8,12},{1,5},{5,9},{9,13},{2,6},{6,10},{10,14},{3,7},{... | collective-permute-start | bytes 1572872 | tf_op jit(solution)/shard_map/ppermute | solution.py:20
  16.1 14.2 %collective-permute-start.4 = (bf16[192,1024]{1,0:T(8,128)(2,1)}, bf16[192,1024]{1,0:T(8,128)(2,1)S(1)}, u32[]{:S(2)}, u32[]{:S(2)}) collective-permute-start(bf16[192,1024]{1,0:T(8,128)(2,1)} %get-tuple-element.36), channel_id=1, source_target_pairs={{0,12},{4,8},{8,4},{12,0},{1,13},{5,9},{9,5},{13,1},{2,14},{6,10},... | collective-permute-start | bytes 1179656 | tf_op jit(solution)/shard_map/ppermute | solution.py:83
  17.5 42.1 %collective-permute-start.3 = (bf16[192,1024]{1,0:T(8,128)(2,1)}, bf16[192,1024]{1,0:T(8,128)(2,1)S(1)}, u32[]{:S(2)}, u32[]{:S(2)}) collective-permute-start(bf16[192,1024]{1,0:T(8,128)(2,1)} %get-tuple-element.35), channel_id=1, source_target_pairs={{0,8},{4,12},{8,0},{12,4},{1,9},{5,13},{9,1},{13,5},{2,10},{6,14},... | collective-permute-start | bytes 1179656 | tf_op jit(solution)/shard_map/ppermute | solution.py:83
  19.5 51.7 %collective-permute-start.2 = (bf16[256,1024]{1,0:T(8,128)(2,1)}, bf16[256,1024]{1,0:T(8,128)(2,1)}, u32[]{:S(2)}, u32[]{:S(2)}) collective-permute-start(bf16[256,1024]{1,0:T(8,128)(2,1)} %pad_maximum_fusion.7), channel_id=1, source_target_pairs={{0,4},{4,0},{8,12},{12,8},{1,5},{5,1},{9,13},{13,9},{2,6},{6,2},{1... | collective-permute-start | bytes 1572872 | tf_op jit(solution)/shard_map/ppermute | solution.py:83
  25.2 44.4 %copy-start.5 = (bf16[16,8,8,128]{3,2,1,0:T(8,128)(2,1)}, bf16[16,8,8,128]{3,2,1,0:T(8,128)(2,1)S(1)}, u32[]{:S(2)}) copy-start(bf16[16,8,8,128]{3,2,1,0:T(8,128)(2,1)S(1)} %copy.187) | copy-start | bytes 786436
  30.3 30.5 %copy-start.25 = (bf16[192,1024]{1,0:T(8,128)(2,1)}, bf16[192,1024]{1,0:T(8,128)(2,1)S(1)}, u32[]{:S(2)}) copy-start(bf16[192,1024]{1,0:T(8,128)(2,1)S(1)} %collective-permute-done.4) | copy-start | bytes 1179652
  31.4 29.4 %copy-start.14 = (bf16[1,128,1024]{2,1,0:T(8,128)(2,1)S(1)}, bf16[1,128,1024]{2,1,0:T(8,128)(2,1)}, u32[]{:S(2)}) copy-start(bf16[1,128,1024]{2,1,0:T(8,128)(2,1)} %param.8) | copy-start | bytes 786436
  31.4 29.4 %copy-start.15 = (bf16[1,128,1024]{2,1,0:T(8,128)(2,1)S(1)}, bf16[1,128,1024]{2,1,0:T(8,128)(2,1)}, u32[]{:S(2)}) copy-start(bf16[1,128,1024]{2,1,0:T(8,128)(2,1)} %param.7) | copy-start | bytes 786436
  31.4 66.5 %collective-permute-start.7 = (bf16[128,1024]{1,0:T(8,128)(2,1)}, bf16[128,1024]{1,0:T(8,128)(2,1)}, u32[]{:S(2)}, u32[]{:S(2)}) collective-permute-start(bf16[128,1024]{1,0:T(8,128)(2,1)} %convolution_convert_fusion), channel_id=1, source_target_pairs={{0,12},{4,8},{8,4},{12,0},{1,13},{5,9},{9,5},{13,1},{2,14},{6,10},... | collective-permute-start | bytes 786440 | tf_op jit(solution)/shard_map/ppermute | solution.py:130
  60.8 37.2 %collective-permute-start.6 = (bf16[128,1024]{1,0:T(8,128)(2,1)}, bf16[128,1024]{1,0:T(8,128)(2,1)}, u32[]{:S(2)}, u32[]{:S(2)}) collective-permute-start(bf16[128,1024]{1,0:T(8,128)(2,1)} %convolution_convert_fusion.1), channel_id=1, source_target_pairs={{0,8},{4,12},{8,0},{12,4},{1,9},{5,13},{9,1},{13,5},{2,10},{6,14},... | collective-permute-start | bytes 786440 | tf_op jit(solution)/shard_map/ppermute | solution.py:130
  77.0 25.3 %copy-start.2 = (f32[8,128,128]{1,2,0}, f32[8,128,128]{1,2,0:S(1)}, u32[]{:S(2)}) copy-start(f32[8,128,128]{1,2,0:S(1)} %fusion.52) | copy-start | bytes 1572868
  81.1 13.0 %copy-start.28 = (bf16[192,1024]{1,0:T(8,128)(2,1)S(1)}, bf16[192,1024]{1,0:T(8,128)(2,1)}, u32[]{:S(2)}) copy-start(bf16[192,1024]{1,0:T(8,128)(2,1)} %copy-done.27) | copy-start | bytes 1179652
  81.1 13.7 %copy-start.26 = (bf16[192,1024]{1,0:T(8,128)(2,1)S(1)}, bf16[192,1024]{1,0:T(8,128)(2,1)}, u32[]{:S(2)}) copy-start(bf16[192,1024]{1,0:T(8,128)(2,1)} %copy-done.25) | copy-start | bytes 1179652
  81.1 14.5 %copy-start.20 = (bf16[128,1024]{1,0:T(8,128)(2,1)S(1)}, bf16[128,1024]{1,0:T(8,128)(2,1)}, u32[]{:S(2)}) copy-start(bf16[128,1024]{1,0:T(8,128)(2,1)} %copy-done.19) | copy-start | bytes 786436
  81.1 14.5 %copy-start.29 = (bf16[128,1024]{1,0:T(8,128)(2,1)S(1)}, bf16[128,1024]{1,0:T(8,128)(2,1)}, u32[]{:S(2)}) copy-start(bf16[128,1024]{1,0:T(8,128)(2,1)} %get-tuple-element.20) | copy-start | bytes 786436
  82.6 14.1 %copy-start.4 = (f32[2,8,64,192]{3,2,1,0:T(8,128)S(1)}, f32[2,8,64,192]{3,2,1,0:T(8,128)}, u32[]{:S(2)}) copy-start(f32[2,8,64,192]{3,2,1,0:T(8,128)} %get-tuple-element.38) | copy-start | bytes 2359300
  82.6 14.0 %copy-start.30 = (bf16[48,8,8,128]{3,2,1,0:T(8,128)(2,1)S(1)}, bf16[48,8,8,128]{3,2,1,0:T(8,128)(2,1)}, u32[]{:S(2)}) copy-start(bf16[48,8,8,128]{3,2,1,0:T(8,128)(2,1)} %copy.188) | copy-start | bytes 2359300
  82.6 15.8 %collective-permute-start.5 = (bf16[128,1024]{1,0:T(8,128)(2,1)S(1)}, bf16[128,1024]{1,0:T(8,128)(2,1)S(1)}, u32[]{:S(2)}, u32[]{:S(2)}) collective-permute-start(bf16[128,1024]{1,0:T(8,128)(2,1)S(1)} %convolution_convert_fusion.2), channel_id=1, source_target_pairs={{0,4},{4,0},{8,12},{12,8},{1,5},{5,1},{9,13},{13,9},{2,6},{6,2},{1... | collective-permute-start | bytes 786440 | tf_op jit(solution)/shard_map/ppermute | solution.py:130
  123.7 78.2 %collective-permute-start.14 = (bf16[128,1024]{1,0:T(8,128)(2,1)}, bf16[128,1024]{1,0:T(8,128)(2,1)}, u32[]{:S(2)}, u32[]{:S(2)}) collective-permute-start(bf16[128,1024]{1,0:T(8,128)(2,1)} %bitcast.195), channel_id=1, source_target_pairs={{0,4},{4,0},{8,12},{12,8},{1,5},{5,1},{9,13},{13,9},{2,6},{6,2},{1... | collective-permute-start | bytes 786440 | tf_op jit(solution)/shard_map/ppermute | solution.py:133
  125.7 76.8 %collective-permute-start.15 = (bf16[128,1024]{1,0:T(8,128)(2,1)}, bf16[128,1024]{1,0:T(8,128)(2,1)}, u32[]{:S(2)}, u32[]{:S(2)}) collective-permute-start(bf16[128,1024]{1,0:T(8,128)(2,1)} %bitcast.195), channel_id=1, source_target_pairs={{0,8},{4,12},{8,0},{12,4},{1,9},{5,13},{9,1},{13,5},{2,10},{6,14},... | collective-permute-start | bytes 786440 | tf_op jit(solution)/shard_map/ppermute | solution.py:133
  125.7 76.8 %collective-permute-start.16 = (bf16[128,1024]{1,0:T(8,128)(2,1)}, bf16[128,1024]{1,0:T(8,128)(2,1)}, u32[]{:S(2)}, u32[]{:S(2)}) collective-permute-start(bf16[128,1024]{1,0:T(8,128)(2,1)} %bitcast.195), channel_id=1, source_target_pairs={{0,12},{4,8},{8,4},{12,0},{1,13},{5,9},{9,5},{13,1},{2,14},{6,10},... | collective-permute-start | bytes 786440 | tf_op jit(solution)/shard_map/ppermute | solution.py:133
  130.1 20.4 %collective-permute-start.12 = (bf16[2,1,32,1024]{2,3,1,0:T(8,128)(2,1)S(1)}, bf16[2,1,32,1024]{2,3,1,0:T(8,128)(2,1)S(1)}, u32[]{:S(2)}, u32[]{:S(2)}) collective-permute-start(bf16[2,1,32,1024]{2,3,1,0:T(8,128)(2,1)S(1)} %get-tuple-element.26), channel_id=1, source_target_pairs={{0,12},{4,8},{8,4},{12,0},{1,13},{5,9},{9,5},{13,1},{2,14},{6,10},... | collective-permute-start | bytes 393224 | tf_op jit(solution)/shard_map/ppermute | solution.py:204
  131.6 55.2 %collective-permute-start.11 = (bf16[2,1,32,1024]{2,3,1,0:T(8,128)(2,1)S(1)}, bf16[2,1,32,1024]{2,3,1,0:T(8,128)(2,1)S(1)}, u32[]{:S(2)}, u32[]{:S(2)}) collective-permute-start(bf16[2,1,32,1024]{2,3,1,0:T(8,128)(2,1)S(1)} %get-tuple-element.25), channel_id=1, source_target_pairs={{0,8},{4,12},{8,0},{12,4},{1,9},{5,13},{9,1},{13,5},{2,10},{6,14},... | collective-permute-start | bytes 393224 | tf_op jit(solution)/shard_map/ppermute | solution.py:204
  150.5 47.6 %collective-permute-start.10 = (bf16[2,1,64,1024]{2,3,1,0:T(8,128)(2,1)S(1)}, bf16[2,1,64,1024]{2,3,1,0:T(8,128)(2,1)S(1)}, u32[]{:S(2)}, u32[]{:S(2)}) collective-permute-start(bf16[2,1,64,1024]{2,3,1,0:T(8,128)(2,1)S(1)} %bitcast.217), channel_id=1, source_target_pairs={{0,4},{4,0},{8,12},{12,8},{1,5},{5,1},{9,13},{13,9},{2,6},{6,2},{1... | collective-permute-start | bytes 786440 | tf_op jit(solution)/shard_map/ppermute | solution.py:204
  186.8 23.5 %collective-permute-start.9 = (bf16[2,1,128,1024]{3,2,1,0:T(8,128)(2,1)}, bf16[2,1,128,1024]{3,2,1,0:T(8,128)(2,1)}, u32[]{:S(2)}, u32[]{:S(2)}) collective-permute-start(bf16[2,1,128,1024]{3,2,1,0:T(8,128)(2,1)} %get-tuple-element.14), channel_id=1, source_target_pairs={{4,0},{8,4},{12,8},{5,1},{9,5},{13,9},{6,2},{10,6},{14,10},{7,3},{... | collective-permute-start | bytes 1572872 | tf_op jit(solution)/shard_map/ppermute | solution.py:22
  198.1 12.2 %collective-permute-start.8 = (bf16[2,1,128,1024]{3,2,1,0:T(8,128)(2,1)}, bf16[2,1,128,1024]{3,2,1,0:T(8,128)(2,1)}, u32[]{:S(2)}, u32[]{:S(2)}) collective-permute-start(bf16[2,1,128,1024]{3,2,1,0:T(8,128)(2,1)} %get-tuple-element.13), channel_id=1, source_target_pairs={{0,4},{4,8},{8,12},{1,5},{5,9},{9,13},{2,6},{6,10},{10,14},{3,7},{... | collective-permute-start | bytes 1572872 | tf_op jit(solution)/shard_map/ppermute | solution.py:20
  201.9 26.4 %collective-permute-start.13 = (bf16[512,1024]{1,0:T(8,128)(2,1)}, bf16[512,1024]{1,0:T(8,128)(2,1)S(1)}, u32[]{:S(2)}, u32[]{:S(2)}) collective-permute-start(bf16[512,1024]{1,0:T(8,128)(2,1)} %pad_maximum_fusion.2), channel_id=1, source_target_pairs={{0,2},{2,0},{1,3},{3,1},{4,6},{6,4},{5,7},{7,5},{8,10},{10,8},{9,1... | collective-permute-start | bytes 3145736 | tf_op jit(solution)/shard_map/ppermute | solution.py:30
  203.8 42.9 %collective-permute-start.17 = (bf16[512,1024]{1,0:T(8,128)(2,1)S(1)}, bf16[512,1024]{1,0:T(8,128)(2,1)S(1)}, u32[]{:S(2)}, u32[]{:S(2)}) collective-permute-start(bf16[512,1024]{1,0:T(8,128)(2,1)S(1)} %pad_maximum_fusion.3), channel_id=1, source_target_pairs={{0,2},{2,0},{1,3},{3,1},{4,6},{6,4},{5,7},{7,5},{8,10},{10,8},{9,1... | collective-permute-start | bytes 3145736 | tf_op jit(solution)/shard_map/ppermute | solution.py:30
  210.4 17.9 %copy-start.34 = (bf16[1024,1024]{1,0:T(8,128)(2,1)S(1)}, bf16[1024,1024]{1,0:T(8,128)(2,1)}, u32[]{:S(2)}) copy-start(bf16[1024,1024]{1,0:T(8,128)(2,1)} %get-tuple-element.34) | copy-start | bytes 6291460
  212.2 34.5 %copy-start.33 = (bf16[1024,1024]{1,0:T(8,128)(2,1)S(1)}, bf16[1024,1024]{1,0:T(8,128)(2,1)}, u32[]{:S(2)}) copy-start(bf16[1024,1024]{1,0:T(8,128)(2,1)} %constant_dynamic-update-slice_fusion.6) | copy-start | bytes 6291460
  (24 other events, 91.8 us)

commit v4 on v3

--- a/solution.py
+++ b/solution.py
@@ -87,7 +87,16 @@
             got = lax.ppermute(sent, "seq", pairs)
             far_parts.append(lax.ppermute(piece, "seq", pairs))
         got_list.append(got)
-    far_pair = jnp.concatenate(far_parts, axis=2)
+    far_levels = []
+    for level_no in range(levels):
+        count = 1 << level_no
+        group = jnp.stack(far_parts[count - 1 : 2 * count - 1], axis=0)
+        order = jnp.arange(count, dtype=jnp.int32) ^ (position & (count - 1))
+        group = jnp.take(group, order, axis=0)
+        far_levels.append(
+            jnp.moveaxis(group, 0, 2).reshape(2, doc_count, count * group.shape[3], head_cols)
+        )
+    far_pair = jnp.concatenate(far_levels, axis=2)
     query_heads = queries.reshape(doc_count, 2, block, heads, HEAD_DIM)
     near_k = near_pair[0].reshape(doc_count, 2, near_width, heads, HEAD_DIM)
     near_v = near_pair[1].reshape(doc_count, 2, near_width, heads, HEAD_DIM)
@@ -194,23 +203,21 @@
     far_rows = jnp.stack([far_key_rows, far_value_rows]).reshape(
         2, doc_count, levels * block, head_cols
     )
-    level_sums = [None] * levels
-    offset = 0
-    for step in range(1, seq_count):
-        level_no = step.bit_length() - 1
-        height = pieces[level_no].shape[2]
-        segment = lax.slice_in_dim(far_rows, offset, offset + height, axis=2)
-        offset += height
-        returned = lax.ppermute(
-            segment.astype(jnp.bfloat16), "seq", [(i, i ^ step) for i in range(seq_count)]
-        ).astype(jnp.float32)
-        if level_sums[level_no] is None:
-            level_sums[level_no] = returned
-        else:
-            level_sums[level_no] = level_sums[level_no] + returned
-    for level_no in range(levels):
-        spread = 2 ** (level_no + 1)
-        token_grad = token_grad + jnp.repeat(level_sums[level_no], spread, axis=2) / float(spread)
+    far_rows = far_rows.reshape(2, doc_count, levels, block, head_cols)
+    carried = jnp.zeros((2, doc_count, block, head_cols), jnp.float32)
+    for level_no in reversed(range(levels)):
+        message = far_rows[:, :, level_no]
+        mine = jnp.zeros_like(message)
+        if level_no + 1 < levels:
+            upper = position >> level_no & 1 == 1
+            spread = jnp.repeat(carried, 2, axis=2) * 0.5
+            lower_half = spread[:, :, :block]
+            upper_half = spread[:, :, block:]
+            mine = jnp.where(upper, upper_half, lower_half)
+            message = message + jnp.where(upper, lower_half, upper_half)
+        returned = swapped(message.astype(jnp.bfloat16), "seq", level_no).astype(jnp.float32)
+        carried = returned + mine
+    token_grad = token_grad + jnp.repeat(carried, 2, axis=2) * 0.5
     key_grad = token_grad[0].astype(jnp.bfloat16)
     value_grad = token_grad[1].astype(jnp.bfloat16)
     return (attention, query_grad, key_grad, value_grad, weight_grad)

time: 253 us -> 195 us (0.77)
  starting transfers between devices: 66.4 us -> 30.6 us
  waiting for transfers between devices: 95.3 us -> 61.6 us
  other arithmetic: 26.7 us -> 33.9 us
  local copies, waits for them, and re-layouts: 42.5 us -> 45.4 us
    ppermute x3 -> x0, waiting for transfers between devices: 32.5 us -> none  [shards(): lax.ppermute(segment.astype(jnp.bfloat16), 'seq', [(i, i ^ step) for i in...]
    ppermute x3 -> x0, starting transfers between devices: 30.3 us -> none  [shards(): lax.ppermute(segment.astype(jnp.bfloat16), 'seq', [(i, i ^ step) for i in...]
    ppermute x3, starting transfers between devices: 15.1 us -> 4.9 us  [shards(): back = lax.ppermute(part.astype(jnp.bfloat16), 'seq', pairs)]
    ppermute x2, starting transfers between devices: 7.63 us -> 10.7 us  [extended(): lax.ppermute(tail, axis, [(i, (i + 1) % count) for i in range(ends)])]
    div x4 -> x0, local copies, waits for them, and re-layouts: 2.72 us -> none  [shards(): jnp.repeat(level_sums[level_no], spread, axis=2) / float(spread)]
    unnamed x82 -> x78, local copies, waits for them, and re-layouts: 10.6 us -> 9.96 us
    ppermute x2 -> x4, waiting for transfers between devices: 33.6 us -> 33.6 us  [swapped(): lax.ppermute(shard, axis, [(i, i ^ 1 << stride) for i in range(lax.axis_s...]
  transfers between devices with their start and end apart: 18 -> 17, of which waited for: 8 -> 6; matrix products, arithmetic and copies ran while one was open for 22% -> 47% of each run, Pallas kernels for 0% -> 0%
where the time goes in v4:
time: 195 us; the launch traced here: 192 us
  waiting for transfers between devices  61.6 us (32%)
  local copies, waits for them, and re-layouts  45.4 us (23%)
  other arithmetic  33.9 us (17%)
  starting transfers between devices  30.6 us (16%)
  matrix products  19 us (10%)
    ppermute x4, waiting for transfers between devices, swapped(): lax.ppermute(shard, axis, [(i, i ^ 1 << stride) for i in range(lax.axis_s...  33.6 us
    ppermute x3, waiting for transfers between devices, shards(): arrived = lax.ppermute(payload, 'seq', pairs)  26.3 us
    ppermute x2, starting transfers between devices, extended(): lax.ppermute(tail, axis, [(i, (i + 1) % count) for i in range(ends)])  10.7 us
    unnamed x78, local copies, waits for them, and re-layouts  9.96 us
    scatter-add x1, other arithmetic, place_blocks(): return holder.at[:, chosen_doc].add(grad_doc)  5.59 us
    gather x5, local copies, waits for them, and re-layouts, pick_blocks(): return blocks_doc[:, chosen_doc]  4.97 us
    ppermute x3, starting transfers between devices, shards(): back = lax.ppermute(part.astype(jnp.bfloat16), 'seq', pairs)  4.9 us
    dot_general x1, matrix products, shards(): jnp.einsum('tc,tw->cw', feat_docs, whole_output, preferred_element_type=j...  4.45 us
  transfers between devices with their start and end apart: 17, of which 6 were waited for; matrix products, arithmetic and copies ran while one was open for 47% of the time, Pallas kernels for 0%

profile of v4, /device:TPU:6, one launch (start us, length us, event | category | flops | bytes accessed | tf_op | source)
XLA Modules:
  0.0 191.8 jit_solution(5469002109974166411)
XLA Ops:
  0.6 2.0 %pad_maximum_fusion.7 = bf16[2,1,128,1024]{3,2,1,0:T(8,128)(2,1)} fusion(bf16[1,1,128,1024]{3,2,1,0:T(8,128)(2,1)} %bitcast.249, bf16[1,1,128,1024]{3,2,1,0:T(8,128)(2,1)} %bitcast.251), kind=kLoop, calls=%fused_computation.52 | loop fusion | flops 262144 | bytes 1048576 | tf_op jit(solution)/shard_map/stack | solution.py:58
  4.0 5.4 %collective-permute-start = (bf16[2,1,128,1024]{3,2,1,0:T(8,128)(2,1)}, bf16[2,1,128,1024]{3,2,1,0:T(8,128)(2,1)}, u32[]{:S(2)}, u32[]{:S(2)}) collective-permute-start(bf16[2,1,128,1024]{3,2,1,0:T(8,128)(2,1)} %pad_maximum_fusion.7), channel_id=1, source_target_pairs={{0,4},{4,8},{8,12},{1,5},{5,9},{9,13},{2,6},{6,10},{10,14},{3,7},{... | collective-permute-start | bytes 1572872 | tf_op jit(solution)/shard_map/ppermute | solution.py:20
  20.2 1.8 collective-permute-start.2
  24.1 1.7 constant_dynamic-update-slice_fusion.4
  27.1 3.8 %collective-permute-done.4 = bf16[192,1024]{1,0:T(8,128)(2,1)S(1)} collective-permute-done((bf16[192,1024]{1,0:T(8,128)(2,1)}, bf16[192,1024]{1,0:T(8,128)(2,1)S(1)}, u32[]{:S(2)}, u32[]{:S(2)}) %collective-permute-start.4) | collective-permute-done | bytes 393248 | tf_op jit(solution)/shard_map/ppermute | solution.py:83
  31.0 22.5 %collective-permute-done.3 = bf16[192,1024]{1,0:T(8,128)(2,1)S(1)} collective-permute-done((bf16[192,1024]{1,0:T(8,128)(2,1)}, bf16[192,1024]{1,0:T(8,128)(2,1)S(1)}, u32[]{:S(2)}, u32[]{:S(2)}) %collective-permute-start.3) | collective-permute-done | bytes 393248 | tf_op jit(solution)/shard_map/ppermute | solution.py:83
  54.3 2.2 %gather_fusion = bf16[2,2,32,1024]{3,2,1,0:T(8,128)(2,1)} fusion(bf16[2,2,32,1024]{3,2,1,0:T(8,128)(2,1)} %maximum_bitcast_fusion, s32[1024]{0:T(1024)S(1)} %pad_clamp_fusion), kind=kCustom, calls=%fused_computation | custom fusion | bytes 524296 | tf_op jit(solution)/shard_map/jit(_take)/gather | solution.py:95
  58.8 4.3 %collective-permute-start.7 = (bf16[128,1024]{1,0:T(8,128)(2,1)}, bf16[128,1024]{1,0:T(8,128)(2,1)}, u32[]{:S(2)}, u32[]{:S(2)}) collective-permute-start(bf16[128,1024]{1,0:T(8,128)(2,1)} %convolution_convert_fusion), channel_id=1, source_target_pairs={{0,12},{4,8},{8,4},{12,0},{1,13},{5,9},{9,5},{13,1},{2,14},{6,10},... | collective-permute-start | bytes 786440 | tf_op jit(solution)/shard_map/ppermute | solution.py:139
  64.2 2.5 %pad_maximum_fusion.1 = bf16[2,1,384,1024]{3,2,1,0:T(8,128)(2,1)} fusion(bf16[2,1,128,1024]{3,2,1,0:T(8,128)(2,1)} %collective-permute-done.1, bf16[1,1,128,1024]{3,2,1,0:T(8,128)(2,1)S(1)} %bitcast.250, bf16[1,1,128,1024]{3,2,1,0:T(8,128)(2,1)S(1)} %bitcast.252, bf16[2,1,128,1024]{3,2,1,0:T(8,128)(2,1)} %collective-permute-done), kind=kLoop, calls=%fused_computation.5 | loop fusion | flops 6291456 | bytes 3145728 | tf_op jit(solution)/shard_map/concatenate | solution.py:18
  66.7 3.2 %gather_fusion.1 = bf16[6,2,64,1024]{3,2,1,0:T(8,128)(2,1)} fusion(bf16[1,2,6,64,1024]{4,3,2,1,0:T(8,128)(2,1)} %bitcast.234, s32[6]{0:T(128)S(1)} %reshape.548), kind=kCustom, calls=%fused_computation.1 | custom fusion | bytes 3145776 | tf_op jit(solution)/shard_map/vmap()/gather | solution.py:41
  69.9 1.6 copy.145
  73.0 1.6 fusion.55
  74.6 1.9 fusion.52
  77.3 1.8 copy.149
  80.6 1.6 fusion.12
  82.7 1.8 copy.156
  91.0 1.6 collective-permute-done.5
  101.4 3.1 %pad_maximum_fusion = f32[1,2,2,3,64,1024]{5,0,4,3,2,1:T(1,128)S(1)} fusion(f32[1,1,2,3,64,1024]{5,0,4,3,2,1:T(1,128)S(1)} %bitcast.236, f32[1,1,2,3,64,1024]{5,0,4,3,2,1:T(1,128)S(1)} %bitcast.237), kind=kLoop, calls=%fused_computation.3 | loop fusion | flops 786432 | bytes 6291456 | tf_op jit(solution)/shard_map/stack | solution.py:191
  104.4 2.4 %copy.203 = f32[1,2,2,3,64,1024]{5,4,1,3,2,0:T(8,128)} copy(f32[1,2,2,3,64,1024]{5,0,4,3,2,1:T(1,128)S(1)} %pad_maximum_fusion) | data formatting | bytes 6291456 | tf_op jit(solution)/shard_map/stack | solution.py:191
  107.2 5.6 %scatter_fusion = f32[2,6,64,1024]{3,2,1,0:T(8,128)S(1)} fusion(f32[2,6,64,1024]{3,2,1,0:T(8,128)S(1)} %broadcast.205, s32[6]{0:T(128)S(1)} %reshape.560, f32[6,2,64,1024]{3,2,1,0:T(8,128)} %bitcast.223), kind=kCustom, calls=%fused_computation.2 | custom fusion | flops 786432 | bytes 9437208 | tf_op jit(solution)/shard_map/vmap()/scatter-add | solution.py:46
  119.3 2.4 %collective-permute-start.14 = (bf16[128,1024]{1,0:T(8,128)(2,1)}, bf16[128,1024]{1,0:T(8,128)(2,1)}, u32[]{:S(2)}, u32[]{:S(2)}) collective-permute-start(bf16[128,1024]{1,0:T(8,128)(2,1)} %bitcast.217), channel_id=1, source_target_pairs={{0,8},{4,12},{8,0},{12,4},{1,9},{5,13},{9,1},{13,5},{2,10},{6,14},... | collective-permute-start | bytes 786440 | tf_op jit(solution)/shard_map/ppermute | solution.py:142
  125.9 1.9 %collective-permute-start.10 = (bf16[2,1,64,1024]{3,0,2,1:T(2,128)(2,1)S(1)}, bf16[2,1,64,1024]{3,0,2,1:T(2,128)(2,1)S(1)}, u32[]{:S(2)}, u32[]{:S(2)}) collective-permute-start(bf16[2,1,64,1024]{3,0,2,1:T(2,128)(2,1)S(1)} %fusion.34), channel_id=1, source_target_pairs={{0,8},{4,12},{8,0},{12,4},{1,9},{5,13},{9,1},{13,5},{2,10},{6,14},... | collective-permute-start | bytes 786440 | tf_op jit(solution)/shard_map/ppermute | solution.py:30
  130.1 23.9 %collective-permute-done.10 = bf16[2,1,64,1024]{3,0,2,1:T(2,128)(2,1)S(1)} collective-permute-done((bf16[2,1,64,1024]{3,0,2,1:T(2,128)(2,1)S(1)}, bf16[2,1,64,1024]{3,0,2,1:T(2,128)(2,1)S(1)}, u32[]{:S(2)}, u32[]{:S(2)}) %collective-permute-start.10) | collective-permute-done | bytes 262176 | tf_op jit(solution)/shard_map/ppermute | solution.py:30
  156.5 5.4 %collective-permute-start.8 = (bf16[2,1,128,1024]{3,2,1,0:T(8,128)(2,1)}, bf16[2,1,128,1024]{3,2,1,0:T(8,128)(2,1)}, u32[]{:S(2)}, u32[]{:S(2)}) collective-permute-start(bf16[2,1,128,1024]{3,2,1,0:T(8,128)(2,1)} %get-tuple-element.13), channel_id=1, source_target_pairs={{0,4},{4,8},{8,12},{1,5},{5,9},{9,13},{2,6},{6,10},{10,14},{3,7},{... | collective-permute-start | bytes 1572872 | tf_op jit(solution)/shard_map/ppermute | solution.py:20
  161.9 2.2 %pad_maximum_fusion.3 = bf16[512,1024]{1,0:T(8,128)(2,1)} fusion(bf16[128,1024]{1,0:T(8,128)(2,1)} %collective-permute-done.15, bf16[128,1024]{1,0:T(8,128)(2,1)} %collective-permute-done.14, bf16[128,1024]{1,0:T(8,128)(2,1)S(1)} %collective-permute-done.13, bf16[128,1024]{1,0:T(8,128)(2,1)} %bitcast.217), kind=kLoop, calls=%fused_computation.33 | loop fusion | flops 4194304 | bytes 2097152 | tf_op jit(solution)/shard_map/concatenate | solution.py:145
  166.0 1.7 constant_dynamic-update-slice_fusion.7
  167.7 1.7 constant_dynamic-update-slice_fusion.6
  169.3 5.1 %collective-permute-done.11 = bf16[2,1,64,1024]{3,0,2,1:T(2,128)(2,1)S(1)} collective-permute-done((bf16[2,1,64,1024]{3,0,2,1:T(2,128)(2,1)S(1)}, bf16[2,1,64,1024]{3,0,2,1:T(2,128)(2,1)S(1)}, u32[]{:S(2)}, u32[]{:S(2)}) %collective-permute-start.11) | collective-permute-done | bytes 262176 | tf_op jit(solution)/shard_map/ppermute | solution.py:30
  175.4 1.8 mul.188
  177.2 2.0 %fusion.10 = bf16[2,1,128,1024]{3,2,1,0:T(8,128)(2,1)S(1)} fusion(f32[2,1,128,1024]{3,2,1,0:T(8,128)} %mul.188, f32[2,1,128,1024]{3,2,1,0:T(8,128)S(1)} %bitcast.246, bf16[2,1,128,1024]{3,2,1,0:T(8,128)(2,1)} %collective-permute-done.9, bf16[2,1,256,1024]{3,2,1,0:T(8,128)(2,1)S(1)} %bitcast.227, bf16[2,1,128,1024]{3,2,1,0:T(8,128)(2,1)} %collective-permute-done.8), kind=kLoop, calls=%fused_computation.29 | loop fusion | flops 4194304 | bytes 4718592 | tf_op jit(solution)/shard_map/convert.1
  181.4 4.7 %collective-permute-done.16 = bf16[512,1024]{1,0:T(8,128)(2,1)} collective-permute-done((bf16[512,1024]{1,0:T(8,128)(2,1)}, bf16[512,1024]{1,0:T(8,128)(2,1)}, u32[]{:S(2)}, u32[]{:S(2)}) %collective-permute-start.16) | collective-permute-done | bytes 1048608 | tf_op jit(solution)/shard_map/ppermute | solution.py:30
  187.4 4.5 %fusion.57 = f32[1024,1024]{1,0:T(8,128)} fusion(bf16[1024,1024]{1,0:T(8,128)(2,1)S(1)} %constant_dynamic-update-slice_fusion, bf16[1024,1024]{1,0:T(8,128)(2,1)S(1)} %constant_dynamic-update-slice_fusion.5), kind=kOutput, calls=%fused_computation.134 | convolution fusion | flops 2147483648 | bytes 8388608 | tf_op jit(solution)/shard_map/tc,tw->cw/dot_general | solution.py:153
  (179 shorter events, 61.2 us)
Async XLA Ops:
  0.6 25.2 %copy-start = (bf16[1024,1024]{1,0:T(8,128)(2,1)S(1)}, bf16[1024,1024]{1,0:T(8,128)(2,1)}, u32[]{:S(2)}) copy-start(bf16[1024,1024]{1,0:T(8,128)(2,1)} %param.10) | copy-start | bytes 6291460
  2.7 61.5 %collective-permute-start.1 = (bf16[2,1,128,1024]{3,2,1,0:T(8,128)(2,1)}, bf16[2,1,128,1024]{3,2,1,0:T(8,128)(2,1)}, u32[]{:S(2)}, u32[]{:S(2)}) collective-permute-start(bf16[2,1,128,1024]{3,2,1,0:T(8,128)(2,1)} %pad_maximum_fusion.7), channel_id=1, source_target_pairs={{4,0},{8,4},{12,8},{5,1},{9,5},{13,9},{6,2},{10,6},{14,10},{7,3},{... | collective-permute-start | bytes 1572872 | tf_op jit(solution)/shard_map/ppermute | solution.py:22
  4.0 60.3 %collective-permute-start = (bf16[2,1,128,1024]{3,2,1,0:T(8,128)(2,1)}, bf16[2,1,128,1024]{3,2,1,0:T(8,128)(2,1)}, u32[]{:S(2)}, u32[]{:S(2)}) collective-permute-start(bf16[2,1,128,1024]{3,2,1,0:T(8,128)(2,1)} %pad_maximum_fusion.7), channel_id=1, source_target_pairs={{0,4},{4,8},{8,12},{1,5},{5,9},{9,13},{2,6},{6,10},{10,14},{3,7},{... | collective-permute-start | bytes 1572872 | tf_op jit(solution)/shard_map/ppermute | solution.py:20
  14.0 5.4 %copy-start.27 = (bf16[2,64,1024]{2,1,0:T(8,128)(2,1)S(1)}, bf16[2,64,1024]{2,1,0:T(8,128)(2,1)}, u32[]{:S(2)}) copy-start(bf16[2,64,1024]{2,1,0:T(8,128)(2,1)} %get-tuple-element.28) | copy-start | bytes 786436
  14.6 7.4 %copy-start.33 = (s32[1,2,2]{2,1,0:T(2,128)S(1)}, s32[1,2,2]{2,1,0:T(2,128)}, u32[]{:S(2)}) copy-start(s32[1,2,2]{2,1,0:T(2,128)} %param.9) | copy-start | bytes 52
  16.8 14.2 %collective-permute-start.4 = (bf16[192,1024]{1,0:T(8,128)(2,1)}, bf16[192,1024]{1,0:T(8,128)(2,1)S(1)}, u32[]{:S(2)}, u32[]{:S(2)}) collective-permute-start(bf16[192,1024]{1,0:T(8,128)(2,1)} %get-tuple-element.34), channel_id=1, source_target_pairs={{0,12},{4,8},{8,4},{12,0},{1,13},{5,9},{9,5},{13,1},{2,14},{6,10},... | collective-permute-start | bytes 1179656 | tf_op jit(solution)/shard_map/ppermute | solution.py:83
  18.2 35.2 %collective-permute-start.3 = (bf16[192,1024]{1,0:T(8,128)(2,1)}, bf16[192,1024]{1,0:T(8,128)(2,1)S(1)}, u32[]{:S(2)}, u32[]{:S(2)}) collective-permute-start(bf16[192,1024]{1,0:T(8,128)(2,1)} %get-tuple-element.33), channel_id=1, source_target_pairs={{0,8},{4,12},{8,0},{12,4},{1,9},{5,13},{9,1},{13,5},{2,10},{6,14},... | collective-permute-start | bytes 1179656 | tf_op jit(solution)/shard_map/ppermute | solution.py:83
  20.2 54.3 %collective-permute-start.2 = (bf16[256,1024]{1,0:T(8,128)(2,1)}, bf16[256,1024]{1,0:T(8,128)(2,1)}, u32[]{:S(2)}, u32[]{:S(2)}) collective-permute-start(bf16[256,1024]{1,0:T(8,128)(2,1)} %pad_maximum_fusion.8), channel_id=1, source_target_pairs={{0,4},{4,0},{8,12},{12,8},{1,5},{5,1},{9,13},{13,9},{2,6},{6,2},{1... | collective-permute-start | bytes 1572872 | tf_op jit(solution)/shard_map/ppermute | solution.py:83
  23.2 49.7 %copy-start.5 = (bf16[16,8,8,128]{3,2,1,0:T(8,128)(2,1)}, bf16[16,8,8,128]{3,2,1,0:T(8,128)(2,1)S(1)}, u32[]{:S(2)}) copy-start(bf16[16,8,8,128]{3,2,1,0:T(8,128)(2,1)S(1)} %copy.205) | copy-start | bytes 786436
  25.8 30.7 %copy-start.18 = (bf16[128,1024]{1,0:T(8,128)(2,1)}, bf16[128,1024]{1,0:T(8,128)(2,1)S(1)}, u32[]{:S(2)}) copy-start(bf16[128,1024]{1,0:T(8,128)(2,1)S(1)} %get-tuple-element.8) | copy-start | bytes 786436
  31.0 27.8 %copy-start.23 = (bf16[192,1024]{1,0:T(8,128)(2,1)}, bf16[192,1024]{1,0:T(8,128)(2,1)S(1)}, u32[]{:S(2)}) copy-start(bf16[192,1024]{1,0:T(8,128)(2,1)S(1)} %collective-permute-done.4) | copy-start | bytes 1179652
  53.4 9.6 %copy-start.25 = (bf16[192,1024]{1,0:T(8,128)(2,1)}, bf16[192,1024]{1,0:T(8,128)(2,1)S(1)}, u32[]{:S(2)}) copy-start(bf16[192,1024]{1,0:T(8,128)(2,1)S(1)} %collective-permute-done.3) | copy-start | bytes 1179652
  57.6 6.7 %copy-start.11 = (bf16[1,128,1024]{2,1,0:T(8,128)(2,1)S(1)}, bf16[1,128,1024]{2,1,0:T(8,128)(2,1)}, u32[]{:S(2)}) copy-start(bf16[1,128,1024]{2,1,0:T(8,128)(2,1)} %param.8) | copy-start | bytes 786436
  57.6 6.7 %copy-start.12 = (bf16[1,128,1024]{2,1,0:T(8,128)(2,1)S(1)}, bf16[1,128,1024]{2,1,0:T(8,128)(2,1)}, u32[]{:S(2)}) copy-start(bf16[1,128,1024]{2,1,0:T(8,128)(2,1)} %param.7) | copy-start | bytes 786436
  58.8 32.2 %collective-permute-start.7 = (bf16[128,1024]{1,0:T(8,128)(2,1)}, bf16[128,1024]{1,0:T(8,128)(2,1)}, u32[]{:S(2)}, u32[]{:S(2)}) collective-permute-start(bf16[128,1024]{1,0:T(8,128)(2,1)} %convolution_convert_fusion), channel_id=1, source_target_pairs={{0,12},{4,8},{8,4},{12,0},{1,13},{5,9},{9,5},{13,1},{2,14},{6,10},... | collective-permute-start | bytes 786440 | tf_op jit(solution)/shard_map/ppermute | solution.py:139
  64.2 26.8 %collective-permute-start.6 = (bf16[128,1024]{1,0:T(8,128)(2,1)}, bf16[128,1024]{1,0:T(8,128)(2,1)}, u32[]{:S(2)}, u32[]{:S(2)}) collective-permute-start(bf16[128,1024]{1,0:T(8,128)(2,1)} %convolution_convert_fusion.1), channel_id=1, source_target_pairs={{0,8},{4,12},{8,0},{12,4},{1,9},{5,13},{9,1},{13,5},{2,10},{6,14},... | collective-permute-start | bytes 786440 | tf_op jit(solution)/shard_map/ppermute | solution.py:139
  80.4 16.2 %copy-start.2 = (f32[8,128,128]{1,2,0}, f32[8,128,128]{1,2,0:S(1)}, u32[]{:S(2)}) copy-start(f32[8,128,128]{1,2,0:S(1)} %fusion.58) | copy-start | bytes 1572868
  86.0 6.6 %collective-permute-start.5 = (bf16[128,1024]{1,0:T(8,128)(2,1)S(1)}, bf16[128,1024]{1,0:T(8,128)(2,1)S(1)}, u32[]{:S(2)}, u32[]{:S(2)}) collective-permute-start(bf16[128,1024]{1,0:T(8,128)(2,1)S(1)} %convolution_convert_fusion.2), channel_id=1, source_target_pairs={{0,4},{4,0},{8,12},{12,8},{1,5},{5,1},{9,13},{13,9},{2,6},{6,2},{1... | collective-permute-start | bytes 786440 | tf_op jit(solution)/shard_map/ppermute | solution.py:139
  89.2 90.9 %collective-permute-start.12 = (bf16[512,1024]{1,0:T(8,128)(2,1)}, bf16[512,1024]{1,0:T(8,128)(2,1)}, u32[]{:S(2)}, u32[]{:S(2)}) collective-permute-start(bf16[512,1024]{1,0:T(8,128)(2,1)} %pad_maximum_fusion.2), channel_id=1, source_target_pairs={{0,2},{2,0},{1,3},{3,1},{4,6},{6,4},{5,7},{7,5},{8,10},{10,8},{9,1... | collective-permute-start | bytes 3145736 | tf_op jit(solution)/shard_map/ppermute | solution.py:30
  115.6 7.5 %copy-start.7 = (bf16[16,8,8,128]{3,2,1,0:T(8,128)(2,1)S(1)}, bf16[16,8,8,128]{3,2,1,0:T(8,128)(2,1)}, u32[]{:S(2)}) copy-start(bf16[16,8,8,128]{3,2,1,0:T(8,128)(2,1)} %copy-done.5) | copy-start | bytes 786436
  115.9 7.5 %copy-start.13 = (bf16[1,1,128,1024]{2,3,1,0:T(8,128)(2,1)S(1)}, bf16[1,1,128,1024]{2,3,1,0:T(8,128)(2,1)}, u32[]{:S(2)}) copy-start(bf16[1,1,128,1024]{2,3,1,0:T(8,128)(2,1)} %copy.149) | copy-start | bytes 786436
  115.9 7.5 %copy-start.20 = (f32[1,2,64,8,128]{4,2,3,1,0:T(8,128)S(1)}, f32[1,2,64,8,128]{4,2,3,1,0:T(8,128)}, u32[]{:S(2)}) copy-start(f32[1,2,64,8,128]{4,2,3,1,0:T(8,128)} %convolution_bitcast_fusion.1) | copy-start | bytes 1572868
  118.8 37.8 %collective-permute-start.13 = (bf16[128,1024]{1,0:T(8,128)(2,1)}, bf16[128,1024]{1,0:T(8,128)(2,1)S(1)}, u32[]{:S(2)}, u32[]{:S(2)}) collective-permute-start(bf16[128,1024]{1,0:T(8,128)(2,1)} %bitcast.217), channel_id=1, source_target_pairs={{0,4},{4,0},{8,12},{12,8},{1,5},{5,1},{9,13},{13,9},{2,6},{6,2},{1... | collective-permute-start | bytes 786440 | tf_op jit(solution)/shard_map/ppermute | solution.py:142
  119.3 42.6 %collective-permute-start.14 = (bf16[128,1024]{1,0:T(8,128)(2,1)}, bf16[128,1024]{1,0:T(8,128)(2,1)}, u32[]{:S(2)}, u32[]{:S(2)}) collective-permute-start(bf16[128,1024]{1,0:T(8,128)(2,1)} %bitcast.217), channel_id=1, source_target_pairs={{0,8},{4,12},{8,0},{12,4},{1,9},{5,13},{9,1},{13,5},{2,10},{6,14},... | collective-permute-start | bytes 786440 | tf_op jit(solution)/shard_map/ppermute | solution.py:142
  121.7 40.2 %collective-permute-start.15 = (bf16[128,1024]{1,0:T(8,128)(2,1)}, bf16[128,1024]{1,0:T(8,128)(2,1)}, u32[]{:S(2)}, u32[]{:S(2)}) collective-permute-start(bf16[128,1024]{1,0:T(8,128)(2,1)} %bitcast.217), channel_id=1, source_target_pairs={{0,12},{4,8},{8,4},{12,0},{1,13},{5,9},{9,5},{13,1},{2,14},{6,10},... | collective-permute-start | bytes 786440 | tf_op jit(solution)/shard_map/ppermute | solution.py:142
  125.9 28.0 %collective-permute-start.10 = (bf16[2,1,64,1024]{3,0,2,1:T(2,128)(2,1)S(1)}, bf16[2,1,64,1024]{3,0,2,1:T(2,128)(2,1)S(1)}, u32[]{:S(2)}, u32[]{:S(2)}) collective-permute-start(bf16[2,1,64,1024]{3,0,2,1:T(2,128)(2,1)S(1)} %fusion.34), channel_id=1, source_target_pairs={{0,8},{4,12},{8,0},{12,4},{1,9},{5,13},{9,1},{13,5},{2,10},{6,14},... | collective-permute-start | bytes 786440 | tf_op jit(solution)/shard_map/ppermute | solution.py:30
  153.9 23.3 %collective-permute-start.9 = (bf16[2,1,128,1024]{3,2,1,0:T(8,128)(2,1)}, bf16[2,1,128,1024]{3,2,1,0:T(8,128)(2,1)}, u32[]{:S(2)}, u32[]{:S(2)}) collective-permute-start(bf16[2,1,128,1024]{3,2,1,0:T(8,128)(2,1)} %get-tuple-element.14), channel_id=1, source_target_pairs={{4,0},{8,4},{12,8},{5,1},{9,5},{13,9},{6,2},{10,6},{14,10},{7,3},{... | collective-permute-start | bytes 1572872 | tf_op jit(solution)/shard_map/ppermute | solution.py:22
  156.5 20.7 %collective-permute-start.8 = (bf16[2,1,128,1024]{3,2,1,0:T(8,128)(2,1)}, bf16[2,1,128,1024]{3,2,1,0:T(8,128)(2,1)}, u32[]{:S(2)}, u32[]{:S(2)}) collective-permute-start(bf16[2,1,128,1024]{3,2,1,0:T(8,128)(2,1)} %get-tuple-element.13), channel_id=1, source_target_pairs={{0,4},{4,8},{8,12},{1,5},{5,9},{9,13},{2,6},{6,10},{10,14},{3,7},{... | collective-permute-start | bytes 1572872 | tf_op jit(solution)/shard_map/ppermute | solution.py:20
  161.9 12.5 %collective-permute-start.11 = (bf16[2,1,64,1024]{3,0,2,1:T(2,128)(2,1)S(1)}, bf16[2,1,64,1024]{3,0,2,1:T(2,128)(2,1)S(1)}, u32[]{:S(2)}, u32[]{:S(2)}) collective-permute-start(bf16[2,1,64,1024]{3,0,2,1:T(2,128)(2,1)S(1)} %fusion.23), channel_id=1, source_target_pairs={{0,4},{4,0},{8,12},{12,8},{1,5},{5,1},{9,13},{13,9},{2,6},{6,2},{1... | collective-permute-start | bytes 786440 | tf_op jit(solution)/shard_map/ppermute | solution.py:30
  164.1 22.0 %collective-permute-start.16 = (bf16[512,1024]{1,0:T(8,128)(2,1)}, bf16[512,1024]{1,0:T(8,128)(2,1)}, u32[]{:S(2)}, u32[]{:S(2)}) collective-permute-start(bf16[512,1024]{1,0:T(8,128)(2,1)} %pad_maximum_fusion.3), channel_id=1, source_target_pairs={{0,2},{2,0},{1,3},{3,1},{4,6},{6,4},{5,7},{7,5},{8,10},{10,8},{9,1... | collective-permute-start | bytes 3145736 | tf_op jit(solution)/shard_map/ppermute | solution.py:30
  179.2 6.8 %copy-start.31 = (bf16[1024,1024]{1,0:T(8,128)(2,1)S(1)}, bf16[1024,1024]{1,0:T(8,128)(2,1)}, u32[]{:S(2)}) copy-start(bf16[1024,1024]{1,0:T(8,128)(2,1)} %constant_dynamic-update-slice_fusion.6) | copy-start | bytes 6291460
  187.4 4.5 %copy-start.1 = (bf16[1024,1024]{1,0:T(8,128)(2,1)S(1)}, bf16[1024,1024]{1,0:T(8,128)(2,1)}, u32[]{:S(2)}) copy-start(bf16[1024,1024]{1,0:T(8,128)(2,1)} %param.10) | copy-start | bytes 6291460
  (19 other events, 47.0 us)

commit v5 on v2

--- a/solution.py
+++ b/solution.py
@@ -77,6 +77,9 @@
             )
             own_level = pool_pairs(joined)
     far_pair = jnp.concatenate(siblings, axis=2).astype(jnp.bfloat16)
+    cot_rows, near_pair, far_pair = lax.optimization_barrier(
+        (cotangent.reshape(doc_count * tok_count, cotangent.shape[2]), near_pair, far_pair)
+    )
     query_heads = queries.reshape(doc_count, 2, block, heads, HEAD_DIM)
     near_k = near_pair[0].reshape(doc_count, 2, near_width, heads, HEAD_DIM)
     near_v = near_pair[1].reshape(doc_count, 2, near_width, heads, HEAD_DIM)
@@ -108,7 +111,6 @@
     )
     attention = output.reshape(doc_count, tok_count, head_cols).astype(jnp.bfloat16)
     feat_count = cotangent.shape[2] // seq_count
-    cot_rows = cotangent.reshape(doc_count * tok_count, cotangent.shape[2])
     out_rows = attention.reshape(doc_count * tok_count, head_cols)
     own_cols = lax.dynamic_slice_in_dim(cot_rows, position * feat_count, feat_count, axis=1)
     grad_sum = jnp.dot(own_cols, out_weight, preferred_element_type=jnp.float32)

time: 185 us -> 202 us (1.092); the launches traced: 185 us -> 199 us
  waiting for transfers between devices: 59.8 us -> 81 us
  matrix products: 19.2 us -> 15.8 us
  starting transfers between devices: 33.6 us -> 31.5 us
    ppermute x3, waiting for transfers between devices: 0.01 us -> 7.14 us  [shards(): back = lax.ppermute(part.astype(jnp.bfloat16), 'seq', pairs)]
    ppermute x3, starting transfers between devices: 10.8 us -> 4.02 us  [shards(): back = lax.ppermute(part.astype(jnp.bfloat16), 'seq', pairs)]
    ppermute x2, waiting for transfers between devices: 0.01 us -> 5.68 us  [extended(): lax.ppermute(head, axis, [((i + 1) % count, i) for i in range(ends)])]
    unnamed x75 -> x66, local copies, waits for them, and re-layouts: 13.8 us -> 8.27 us
    ppermute x3, waiting for transfers between devices: 19.8 us -> 25.2 us  [shards(): got = lax.ppermute(sent, 'seq', pairs)]
    gather x5, local copies, waits for them, and re-layouts: 0.98 us -> 4.98 us  [pick_blocks(): return blocks_doc[:, chosen_doc]]
    ppermute x6, starting transfers between devices: 1.46 us -> 5.38 us  [swapped(): lax.ppermute(shard, axis, [(i, i ^ 1 << stride) for i in range(lax.axis_s...]
    ppermute x6, waiting for transfers between devices: 40.1 us -> 43 us  [swapped(): lax.ppermute(shard, axis, [(i, i ^ 1 << stride) for i in range(lax.axis_s...]
  transfers between devices with their start and end apart: 19 -> 19, of which waited for: 7 -> 8; matrix products, arithmetic and copies ran while one was open for 44% -> 32% of each run, Pallas kernels for 0% -> 0%
where the time goes in v5:
time: 202 us; the launch traced here: 199 us
  waiting for transfers between devices  81 us (40%)
  local copies, waits for them, and re-layouts  38.5 us (19%)
  starting transfers between devices  31.5 us (16%)
  other arithmetic  30.9 us (15%)
  matrix products  15.8 us (8%)
    ppermute x6, waiting for transfers between devices, swapped(): lax.ppermute(shard, axis, [(i, i ^ 1 << stride) for i in range(lax.axis_s...  43 us
    ppermute x3, waiting for transfers between devices, shards(): got = lax.ppermute(sent, 'seq', pairs)  25.2 us
    ppermute x2, starting transfers between devices, extended(): lax.ppermute(tail, axis, [(i, (i + 1) % count) for i in range(ends)])  10.7 us
    unnamed x66, local copies, waits for them, and re-layouts  8.27 us
    ppermute x3, waiting for transfers between devices, shards(): back = lax.ppermute(part.astype(jnp.bfloat16), 'seq', pairs)  7.14 us
    ppermute x2, waiting for transfers between devices, extended(): lax.ppermute(head, axis, [((i + 1) % count, i) for i in range(ends)])  5.68 us
    scatter-add x1, other arithmetic, place_blocks(): return holder.at[:, chosen_doc].add(grad_doc)  5.59 us
    ppermute x6, starting transfers between devices, swapped(): lax.ppermute(shard, axis, [(i, i ^ 1 << stride) for i in range(lax.axis_s...  5.38 us
  transfers between devices with their start and end apart: 19, of which 8 were waited for; matrix products, arithmetic and copies ran while one was open for 32% of the time, Pallas kernels for 0%

profile of v5, /device:TPU:6, one launch (start us, length us, event | category | flops | bytes accessed | tf_op | source)
XLA Modules:
  0.0 199.2 jit_solution(484130686606477944)
XLA Ops:
  5.3 1.6 collective-permute-start.2
  9.0 5.4 %collective-permute-start = (bf16[2,1,128,1024]{3,2,1,0:T(8,128)(2,1)}, bf16[2,1,128,1024]{3,2,1,0:T(8,128)(2,1)}, u32[]{:S(2)}, u32[]{:S(2)}) collective-permute-start(bf16[2,1,128,1024]{3,2,1,0:T(8,128)(2,1)} %pad_maximum_fusion.7), channel_id=1, source_target_pairs={{0,4},{4,8},{8,12},{1,5},{5,9},{9,13},{2,6},{6,10},{10,14},{3,7},{... | collective-permute-start | bytes 1572872 | tf_op jit(solution)/shard_map/ppermute | solution.py:20
  14.5 5.9 %collective-permute-done.2 = f32[2,1,64,1024]{3,2,1,0:T(8,128)} collective-permute-done((f32[2,1,64,1024]{3,2,1,0:T(8,128)}, f32[2,1,64,1024]{3,2,1,0:T(8,128)}, u32[]{:S(2)}, u32[]{:S(2)}) %collective-permute-start.2) | collective-permute-done | bytes 524320 | tf_op jit(solution)/shard_map/ppermute | solution.py:30
  22.6 1.8 reduce_sum.55
  25.5 2.7 %collective-permute-start.3 = (bf16[2,1,64,1024]{3,2,1,0:T(8,128)(2,1)S(1)}, bf16[2,1,64,1024]{3,2,1,0:T(8,128)(2,1)S(1)}, u32[]{:S(2)}, u32[]{:S(2)}) collective-permute-start(bf16[2,1,64,1024]{3,2,1,0:T(8,128)(2,1)S(1)} %fusion.23), channel_id=1, source_target_pairs={{0,8},{4,12},{8,0},{12,4},{1,9},{5,13},{9,1},{13,5},{2,10},{6,14},... | collective-permute-start | bytes 786440 | tf_op jit(solution)/shard_map/ppermute | solution.py:30
  30.2 5.7 %collective-permute-done.1 = bf16[2,1,128,1024]{3,2,1,0:T(8,128)(2,1)} collective-permute-done((bf16[2,1,128,1024]{3,2,1,0:T(8,128)(2,1)}, bf16[2,1,128,1024]{3,2,1,0:T(8,128)(2,1)}, u32[]{:S(2)}, u32[]{:S(2)}) %collective-permute-start.1) | collective-permute-done | bytes 524320 | tf_op jit(solution)/shard_map/ppermute | solution.py:22
  35.8 2.6 %pad_maximum_fusion.1 = bf16[2,1,384,1024]{3,2,1,0:T(8,128)(2,1)} fusion(bf16[2,1,128,1024]{3,2,1,0:T(8,128)(2,1)} %collective-permute-done.1, bf16[1,1,128,1024]{3,2,1,0:T(8,128)(2,1)S(1)} %bitcast.244, bf16[1,1,128,1024]{3,2,1,0:T(8,128)(2,1)} %bitcast.245, bf16[2,1,128,1024]{3,2,1,0:T(8,128)(2,1)} %collective-permute-done), kind=kLoop, calls=%fused_computation.4 | loop fusion | flops 6291456 | bytes 3145728 | tf_op jit(solution)/shard_map/concatenate | solution.py:18
  38.4 3.2 %gather_fusion = bf16[6,2,64,1024]{3,2,1,0:T(8,128)(2,1)} fusion(bf16[1,2,6,64,1024]{4,3,2,1,0:T(8,128)(2,1)} %bitcast.227, s32[6]{0:T(128)S(1)} %reshape.542), kind=kCustom, calls=%fused_computation | custom fusion | bytes 3145776 | tf_op jit(solution)/shard_map/vmap()/gather | solution.py:41
  45.7 1.6 fusion.47
  51.4 1.8 copy.212
  54.6 1.7 collective-permute-start.8
  56.3 2.7 %collective-permute-start.4 = (bf16[128,1024]{1,0:T(8,128)(2,1)S(1)}, bf16[128,1024]{1,0:T(8,128)(2,1)S(1)}, u32[]{:S(2)}, u32[]{:S(2)}) collective-permute-start(bf16[128,1024]{1,0:T(8,128)(2,1)S(1)} %get-tuple-element.21), channel_id=1, source_target_pairs={{0,4},{4,0},{8,12},{12,8},{1,5},{5,1},{9,13},{13,9},{2,6},{6,2},{1... | collective-permute-start | bytes 786440 | tf_op jit(solution)/shard_map/ppermute | solution.py:124
  60.8 5.0 %collective-permute-done.8 = bf16[128,1024]{1,0:T(8,128)(2,1)S(1)} collective-permute-done((bf16[128,1024]{1,0:T(8,128)(2,1)S(1)}, bf16[128,1024]{1,0:T(8,128)(2,1)S(1)}, u32[]{:S(2)}, u32[]{:S(2)}) %collective-permute-start.8) | collective-permute-done | bytes 262176 | tf_op jit(solution)/shard_map/ppermute | solution.py:124
  66.2 1.7 collective-permute-start.9
  67.9 20.2 %collective-permute-done.6 = bf16[128,1024]{1,0:T(8,128)(2,1)S(1)} collective-permute-done((bf16[128,1024]{1,0:T(8,128)(2,1)S(1)}, bf16[128,1024]{1,0:T(8,128)(2,1)S(1)}, u32[]{:S(2)}, u32[]{:S(2)}) %collective-permute-start.6) | collective-permute-done | bytes 262176 | tf_op jit(solution)/shard_map/ppermute | solution.py:124
  89.2 2.2 %collective-permute-start.5 = (bf16[128,1024]{1,0:T(8,128)(2,1)S(1)}, bf16[128,1024]{1,0:T(8,128)(2,1)S(1)}, u32[]{:S(2)}, u32[]{:S(2)}) collective-permute-start(bf16[128,1024]{1,0:T(8,128)(2,1)S(1)} %convolution_convert_fusion.2), channel_id=1, source_target_pairs={{0,4},{4,0},{8,12},{12,8},{1,5},{5,1},{9,13},{13,9},{2,6},{6,2},{1... | collective-permute-start | bytes 786440 | tf_op jit(solution)/shard_map/ppermute | solution.py:126
  93.1 7.1 %collective-permute-done.7 = bf16[128,1024]{1,0:T(8,128)(2,1)S(1)} collective-permute-done((bf16[128,1024]{1,0:T(8,128)(2,1)S(1)}, bf16[128,1024]{1,0:T(8,128)(2,1)S(1)}, u32[]{:S(2)}, u32[]{:S(2)}) %collective-permute-start.7) | collective-permute-done | bytes 262176 | tf_op jit(solution)/shard_map/ppermute | solution.py:126
  107.9 3.1 %pad_maximum_fusion = f32[1,2,2,3,64,1024]{5,0,4,3,2,1:T(1,128)S(1)} fusion(f32[1,1,2,3,64,1024]{5,0,4,3,2,1:T(1,128)S(1)} %bitcast.229, f32[1,1,2,3,64,1024]{5,0,4,3,2,1:T(1,128)S(1)} %bitcast.230), kind=kLoop, calls=%fused_computation.2 | loop fusion | flops 786432 | bytes 6291456 | tf_op jit(solution)/shard_map/stack | solution.py:178
  111.0 2.4 %copy.259 = f32[1,2,2,3,64,1024]{5,4,1,3,2,0:T(8,128)} copy(f32[1,2,2,3,64,1024]{5,0,4,3,2,1:T(1,128)S(1)} %pad_maximum_fusion) | data formatting | bytes 6291456 | tf_op jit(solution)/shard_map/stack | solution.py:178
  113.8 5.6 %scatter_fusion = f32[2,6,64,1024]{3,2,1,0:T(8,128)S(1)} fusion(f32[2,6,64,1024]{3,2,1,0:T(8,128)S(1)} %broadcast.159, s32[6]{0:T(128)S(1)} %reshape.554, f32[6,2,64,1024]{3,2,1,0:T(8,128)} %bitcast.215), kind=kCustom, calls=%fused_computation.1 | custom fusion | flops 786432 | bytes 9437208 | tf_op jit(solution)/shard_map/vmap()/scatter-add | solution.py:46
  125.3 2.5 %collective-permute-start.16 = (bf16[128,1024]{1,0:T(8,128)(2,1)}, bf16[128,1024]{1,0:T(8,128)(2,1)}, u32[]{:S(2)}, u32[]{:S(2)}) collective-permute-start(bf16[128,1024]{1,0:T(8,128)(2,1)} %bitcast.209), channel_id=1, source_target_pairs={{0,8},{4,12},{8,0},{12,4},{1,9},{5,13},{9,1},{13,5},{2,10},{6,14},... | collective-permute-start | bytes 786440 | tf_op jit(solution)/shard_map/ppermute | solution.py:129
  127.7 1.9 collective-permute-start.17
  134.7 26.0 %collective-permute-done.12 = bf16[2,1,64,1024]{3,0,2,1:T(2,128)(2,1)S(1)} collective-permute-done((bf16[2,1,64,1024]{3,0,2,1:T(2,128)(2,1)S(1)}, bf16[2,1,64,1024]{3,0,2,1:T(2,128)(2,1)S(1)}, u32[]{:S(2)}, u32[]{:S(2)}) %collective-permute-start.12) | collective-permute-done | bytes 262176 | tf_op jit(solution)/shard_map/ppermute | solution.py:30
  163.3 5.4 %collective-permute-start.10 = (bf16[2,1,128,1024]{3,2,1,0:T(8,128)(2,1)}, bf16[2,1,128,1024]{3,2,1,0:T(8,128)(2,1)}, u32[]{:S(2)}, u32[]{:S(2)}) collective-permute-start(bf16[2,1,128,1024]{3,2,1,0:T(8,128)(2,1)} %get-tuple-element.19), channel_id=1, source_target_pairs={{0,4},{4,8},{8,12},{1,5},{5,9},{9,13},{2,6},{6,10},{10,14},{3,7},{... | collective-permute-start | bytes 1572872 | tf_op jit(solution)/shard_map/ppermute | solution.py:20
  168.6 2.2 %pad_maximum_fusion.3 = bf16[512,1024]{1,0:T(8,128)(2,1)} fusion(bf16[128,1024]{1,0:T(8,128)(2,1)} %collective-permute-done.17, bf16[128,1024]{1,0:T(8,128)(2,1)} %collective-permute-done.16, bf16[128,1024]{1,0:T(8,128)(2,1)S(1)} %collective-permute-done.15, bf16[128,1024]{1,0:T(8,128)(2,1)} %bitcast.209), kind=kLoop, calls=%fused_computation.33 | loop fusion | flops 4194304 | bytes 2097152 | tf_op jit(solution)/shard_map/concatenate | solution.py:132
  172.1 1.7 constant_dynamic-update-slice_fusion.7
  173.7 1.7 constant_dynamic-update-slice_fusion.6
  175.4 7.1 %collective-permute-done.13 = bf16[2,1,64,1024]{3,0,2,1:T(2,128)(2,1)S(1)} collective-permute-done((bf16[2,1,64,1024]{3,0,2,1:T(2,128)(2,1)S(1)}, bf16[2,1,64,1024]{3,0,2,1:T(2,128)(2,1)S(1)}, u32[]{:S(2)}, u32[]{:S(2)}) %collective-permute-start.13) | collective-permute-done | bytes 262176 | tf_op jit(solution)/shard_map/ppermute | solution.py:30
  183.5 1.8 mul.187
  185.3 2.0 fusion.10
  189.4 4.0 %collective-permute-done.18 = bf16[512,1024]{1,0:T(8,128)(2,1)} collective-permute-done((bf16[512,1024]{1,0:T(8,128)(2,1)}, bf16[512,1024]{1,0:T(8,128)(2,1)}, u32[]{:S(2)}, u32[]{:S(2)}) %collective-permute-start.18) | collective-permute-done | bytes 1048608 | tf_op jit(solution)/shard_map/ppermute | solution.py:30
  194.7 4.5 %fusion.49 = f32[1024,1024]{1,0:T(8,128)} fusion(bf16[1024,1024]{1,0:T(8,128)(2,1)S(1)} %constant_dynamic-update-slice_fusion, bf16[1024,1024]{1,0:T(8,128)(2,1)S(1)} %constant_dynamic-update-slice_fusion.5), kind=kOutput, calls=%fused_computation.116 | convolution fusion | flops 2147483648 | bytes 8388608 | tf_op jit(solution)/shard_map/tc,tw->cw/dot_general | solution.py:140
  (160 shorter events, 53.4 us)
Async XLA Ops:
  0.6 58.4 %copy-start = (bf16[1024,1024]{1,0:T(8,128)(2,1)S(1)}, bf16[1024,1024]{1,0:T(8,128)(2,1)}, u32[]{:S(2)}) copy-start(bf16[1024,1024]{1,0:T(8,128)(2,1)} %param.10) | copy-start | bytes 6291460
  0.6 6.2 %copy-start.12 = (bf16[1,128,1024]{2,1,0:T(8,128)(2,1)S(1)}, bf16[1,128,1024]{2,1,0:T(8,128)(2,1)}, u32[]{:S(2)}) copy-start(bf16[1,128,1024]{2,1,0:T(8,128)(2,1)} %param.8) | copy-start | bytes 786436
  0.7 6.2 %copy-start.13 = (bf16[1,128,1024]{2,1,0:T(8,128)(2,1)S(1)}, bf16[1,128,1024]{2,1,0:T(8,128)(2,1)}, u32[]{:S(2)}) copy-start(bf16[1,128,1024]{2,1,0:T(8,128)(2,1)} %param.7) | copy-start | bytes 786436
  1.9 12.5 %copy-start.26 = (s32[1,2,2]{2,1,0:T(2,128)S(1)}, s32[1,2,2]{2,1,0:T(2,128)}, u32[]{:S(2)}) copy-start(s32[1,2,2]{2,1,0:T(2,128)} %param.9) | copy-start | bytes 52
  5.3 15.1 %collective-permute-start.2 = (f32[2,1,64,1024]{3,2,1,0:T(8,128)}, f32[2,1,64,1024]{3,2,1,0:T(8,128)}, u32[]{:S(2)}, u32[]{:S(2)}) collective-permute-start(f32[2,1,64,1024]{3,2,1,0:T(8,128)} %get-tuple-element.32), channel_id=1, source_target_pairs={{0,4},{4,0},{8,12},{12,8},{1,5},{5,1},{9,13},{13,9},{2,6},{6,2},{1... | collective-permute-start | bytes 1572872 | tf_op jit(solution)/shard_map/ppermute | solution.py:30
  7.7 28.1 %collective-permute-start.1 = (bf16[2,1,128,1024]{3,2,1,0:T(8,128)(2,1)}, bf16[2,1,128,1024]{3,2,1,0:T(8,128)(2,1)}, u32[]{:S(2)}, u32[]{:S(2)}) collective-permute-start(bf16[2,1,128,1024]{3,2,1,0:T(8,128)(2,1)} %pad_maximum_fusion.7), channel_id=1, source_target_pairs={{4,0},{8,4},{12,8},{5,1},{9,5},{13,9},{6,2},{10,6},{14,10},{7,3},{... | collective-permute-start | bytes 1572872 | tf_op jit(solution)/shard_map/ppermute | solution.py:22
  9.0 26.8 %collective-permute-start = (bf16[2,1,128,1024]{3,2,1,0:T(8,128)(2,1)}, bf16[2,1,128,1024]{3,2,1,0:T(8,128)(2,1)}, u32[]{:S(2)}, u32[]{:S(2)}) collective-permute-start(bf16[2,1,128,1024]{3,2,1,0:T(8,128)(2,1)} %pad_maximum_fusion.7), channel_id=1, source_target_pairs={{0,4},{4,8},{8,12},{1,5},{5,9},{9,13},{2,6},{6,10},{10,14},{3,7},{... | collective-permute-start | bytes 1572872 | tf_op jit(solution)/shard_map/ppermute | solution.py:20
  25.5 18.8 %collective-permute-start.3 = (bf16[2,1,64,1024]{3,2,1,0:T(8,128)(2,1)S(1)}, bf16[2,1,64,1024]{3,2,1,0:T(8,128)(2,1)S(1)}, u32[]{:S(2)}, u32[]{:S(2)}) collective-permute-start(bf16[2,1,64,1024]{3,2,1,0:T(8,128)(2,1)S(1)} %fusion.23), channel_id=1, source_target_pairs={{0,8},{4,12},{8,0},{12,4},{1,9},{5,13},{9,1},{13,5},{2,10},{6,14},... | collective-permute-start | bytes 786440 | tf_op jit(solution)/shard_map/ppermute | solution.py:30
  29.3 16.5 %copy-start.6 = (bf16[16,8,8,128]{3,2,1,0:T(8,128)(2,1)}, bf16[16,8,8,128]{3,2,1,0:T(8,128)(2,1)S(1)}, u32[]{:S(2)}) copy-start(bf16[16,8,8,128]{3,2,1,0:T(8,128)(2,1)S(1)} %copy.261) | copy-start | bytes 786436
  50.3 52.8 %copy-start.2 = (f32[8,128,128]{1,2,0}, f32[8,128,128]{1,2,0:S(1)}, u32[]{:S(2)}) copy-start(f32[8,128,128]{1,2,0:S(1)} %fusion.50) | copy-start | bytes 1572868
  53.1 6.4 %copy-start.5 = (f32[2,8,64,192]{3,2,1,0:T(8,128)S(1)}, f32[2,8,64,192]{3,2,1,0:T(8,128)}, u32[]{:S(2)}) copy-start(f32[2,8,64,192]{3,2,1,0:T(8,128)} %get-tuple-element.35) | copy-start | bytes 2359300
  53.1 6.4 %copy-start.21 = (bf16[48,8,8,128]{3,2,1,0:T(8,128)(2,1)S(1)}, bf16[48,8,8,128]{3,2,1,0:T(8,128)(2,1)}, u32[]{:S(2)}) copy-start(bf16[48,8,8,128]{3,2,1,0:T(8,128)(2,1)} %copy.262) | copy-start | bytes 2359300
  54.6 11.2 %collective-permute-start.8 = (bf16[128,1024]{1,0:T(8,128)(2,1)S(1)}, bf16[128,1024]{1,0:T(8,128)(2,1)S(1)}, u32[]{:S(2)}, u32[]{:S(2)}) collective-permute-start(bf16[128,1024]{1,0:T(8,128)(2,1)S(1)} %get-tuple-element.22), channel_id=1, source_target_pairs={{0,12},{4,8},{8,4},{12,0},{1,13},{5,9},{9,5},{13,1},{2,14},{6,10},... | collective-permute-start | bytes 786440 | tf_op jit(solution)/shard_map/ppermute | solution.py:124
  56.3 31.9 %collective-permute-start.6 = (bf16[128,1024]{1,0:T(8,128)(2,1)S(1)}, bf16[128,1024]{1,0:T(8,128)(2,1)S(1)}, u32[]{:S(2)}, u32[]{:S(2)}) collective-permute-start(bf16[128,1024]{1,0:T(8,128)(2,1)S(1)} %get-tuple-element.23), channel_id=1, source_target_pairs={{0,8},{4,12},{8,0},{12,4},{1,9},{5,13},{9,1},{13,5},{2,10},{6,14},... | collective-permute-start | bytes 786440 | tf_op jit(solution)/shard_map/ppermute | solution.py:124
  56.3 32.4 %collective-permute-start.4 = (bf16[128,1024]{1,0:T(8,128)(2,1)S(1)}, bf16[128,1024]{1,0:T(8,128)(2,1)S(1)}, u32[]{:S(2)}, u32[]{:S(2)}) collective-permute-start(bf16[128,1024]{1,0:T(8,128)(2,1)S(1)} %get-tuple-element.21), channel_id=1, source_target_pairs={{0,4},{4,0},{8,12},{12,8},{1,5},{5,1},{9,13},{13,9},{2,6},{6,2},{1... | collective-permute-start | bytes 786440 | tf_op jit(solution)/shard_map/ppermute | solution.py:124
  66.2 26.8 %collective-permute-start.9 = (bf16[128,1024]{1,0:T(8,128)(2,1)S(1)}, bf16[128,1024]{1,0:T(8,128)(2,1)S(1)}, u32[]{:S(2)}, u32[]{:S(2)}) collective-permute-start(bf16[128,1024]{1,0:T(8,128)(2,1)S(1)} %convolution_convert_fusion), channel_id=1, source_target_pairs={{0,12},{4,8},{8,4},{12,0},{1,13},{5,9},{9,5},{13,1},{2,14},{6,10},... | collective-permute-start | bytes 786440 | tf_op jit(solution)/shard_map/ppermute | solution.py:126
  88.6 11.6 %collective-permute-start.7 = (bf16[128,1024]{1,0:T(8,128)(2,1)S(1)}, bf16[128,1024]{1,0:T(8,128)(2,1)S(1)}, u32[]{:S(2)}, u32[]{:S(2)}) collective-permute-start(bf16[128,1024]{1,0:T(8,128)(2,1)S(1)} %convolution_convert_fusion.1), channel_id=1, source_target_pairs={{0,8},{4,12},{8,0},{12,4},{1,9},{5,13},{9,1},{13,5},{2,10},{6,14},... | collective-permute-start | bytes 786440 | tf_op jit(solution)/shard_map/ppermute | solution.py:126
  89.2 11.0 %collective-permute-start.5 = (bf16[128,1024]{1,0:T(8,128)(2,1)S(1)}, bf16[128,1024]{1,0:T(8,128)(2,1)S(1)}, u32[]{:S(2)}, u32[]{:S(2)}) collective-permute-start(bf16[128,1024]{1,0:T(8,128)(2,1)S(1)} %convolution_convert_fusion.2), channel_id=1, source_target_pairs={{0,4},{4,0},{8,12},{12,8},{1,5},{5,1},{9,13},{13,9},{2,6},{6,2},{1... | collective-permute-start | bytes 786440 | tf_op jit(solution)/shard_map/ppermute | solution.py:126
  92.5 95.7 %collective-permute-start.14 = (bf16[512,1024]{1,0:T(8,128)(2,1)}, bf16[512,1024]{1,0:T(8,128)(2,1)}, u32[]{:S(2)}, u32[]{:S(2)}) collective-permute-start(bf16[512,1024]{1,0:T(8,128)(2,1)} %pad_maximum_fusion.2), channel_id=1, source_target_pairs={{0,2},{2,0},{1,3},{3,1},{4,6},{6,4},{5,7},{7,5},{8,10},{10,8},{9,1... | collective-permute-start | bytes 3145736 | tf_op jit(solution)/shard_map/ppermute | solution.py:30
  93.1 8.6 %copy-start.24 = (bf16[1024,1024]{1,0:T(8,128)(2,1)}, bf16[1024,1024]{1,0:T(8,128)(2,1)S(1)}, u32[]{:S(2)}) copy-start(bf16[1024,1024]{1,0:T(8,128)(2,1)S(1)} %constant_dynamic-update-slice_fusion.1) | copy-start | bytes 6291460
  122.1 7.5 %copy-start.8 = (bf16[16,8,8,128]{3,2,1,0:T(8,128)(2,1)S(1)}, bf16[16,8,8,128]{3,2,1,0:T(8,128)(2,1)}, u32[]{:S(2)}) copy-start(bf16[16,8,8,128]{3,2,1,0:T(8,128)(2,1)} %copy-done.6) | copy-start | bytes 786436
  122.4 7.5 %copy-start.14 = (bf16[1,1,128,1024]{2,3,1,0:T(8,128)(2,1)S(1)}, bf16[1,1,128,1024]{2,3,1,0:T(8,128)(2,1)}, u32[]{:S(2)}) copy-start(bf16[1,1,128,1024]{2,3,1,0:T(8,128)(2,1)} %copy.205) | copy-start | bytes 786436
  122.4 7.5 %copy-start.19 = (f32[1,2,64,8,128]{4,2,3,1,0:T(8,128)S(1)}, f32[1,2,64,8,128]{4,2,3,1,0:T(8,128)}, u32[]{:S(2)}) copy-start(f32[1,2,64,8,128]{4,2,3,1,0:T(8,128)} %convolution_bitcast_fusion.1) | copy-start | bytes 1572868
  125.2 38.0 %collective-permute-start.15 = (bf16[128,1024]{1,0:T(8,128)(2,1)}, bf16[128,1024]{1,0:T(8,128)(2,1)S(1)}, u32[]{:S(2)}, u32[]{:S(2)}) collective-permute-start(bf16[128,1024]{1,0:T(8,128)(2,1)} %bitcast.209), channel_id=1, source_target_pairs={{0,4},{4,0},{8,12},{12,8},{1,5},{5,1},{9,13},{13,9},{2,6},{6,2},{1... | collective-permute-start | bytes 786440 | tf_op jit(solution)/shard_map/ppermute | solution.py:129
  125.3 43.4 %collective-permute-start.16 = (bf16[128,1024]{1,0:T(8,128)(2,1)}, bf16[128,1024]{1,0:T(8,128)(2,1)}, u32[]{:S(2)}, u32[]{:S(2)}) collective-permute-start(bf16[128,1024]{1,0:T(8,128)(2,1)} %bitcast.209), channel_id=1, source_target_pairs={{0,8},{4,12},{8,0},{12,4},{1,9},{5,13},{9,1},{13,5},{2,10},{6,14},... | collective-permute-start | bytes 786440 | tf_op jit(solution)/shard_map/ppermute | solution.py:129
  127.7 40.9 %collective-permute-start.17 = (bf16[128,1024]{1,0:T(8,128)(2,1)}, bf16[128,1024]{1,0:T(8,128)(2,1)}, u32[]{:S(2)}, u32[]{:S(2)}) collective-permute-start(bf16[128,1024]{1,0:T(8,128)(2,1)} %bitcast.209), channel_id=1, source_target_pairs={{0,12},{4,8},{8,4},{12,0},{1,13},{5,9},{9,5},{13,1},{2,14},{6,10},... | collective-permute-start | bytes 786440 | tf_op jit(solution)/shard_map/ppermute | solution.py:129
  132.4 28.3 %collective-permute-start.12 = (bf16[2,1,64,1024]{3,0,2,1:T(2,128)(2,1)S(1)}, bf16[2,1,64,1024]{3,0,2,1:T(2,128)(2,1)S(1)}, u32[]{:S(2)}, u32[]{:S(2)}) collective-permute-start(bf16[2,1,64,1024]{3,0,2,1:T(2,128)(2,1)S(1)} %fusion.33), channel_id=1, source_target_pairs={{0,8},{4,12},{8,0},{12,4},{1,9},{5,13},{9,1},{13,5},{2,10},{6,14},... | collective-permute-start | bytes 786440 | tf_op jit(solution)/shard_map/ppermute | solution.py:30
  160.7 24.6 %collective-permute-start.11 = (bf16[2,1,128,1024]{3,2,1,0:T(8,128)(2,1)}, bf16[2,1,128,1024]{3,2,1,0:T(8,128)(2,1)}, u32[]{:S(2)}, u32[]{:S(2)}) collective-permute-start(bf16[2,1,128,1024]{3,2,1,0:T(8,128)(2,1)} %get-tuple-element.20), channel_id=1, source_target_pairs={{4,0},{8,4},{12,8},{5,1},{9,5},{13,9},{6,2},{10,6},{14,10},{7,3},{... | collective-permute-start | bytes 1572872 | tf_op jit(solution)/shard_map/ppermute | solution.py:22
  163.3 22.0 %collective-permute-start.10 = (bf16[2,1,128,1024]{3,2,1,0:T(8,128)(2,1)}, bf16[2,1,128,1024]{3,2,1,0:T(8,128)(2,1)}, u32[]{:S(2)}, u32[]{:S(2)}) collective-permute-start(bf16[2,1,128,1024]{3,2,1,0:T(8,128)(2,1)} %get-tuple-element.19), channel_id=1, source_target_pairs={{0,4},{4,8},{8,12},{1,5},{5,9},{9,13},{2,6},{6,10},{10,14},{3,7},{... | collective-permute-start | bytes 1572872 | tf_op jit(solution)/shard_map/ppermute | solution.py:20
  168.6 13.9 %collective-permute-start.13 = (bf16[2,1,64,1024]{3,0,2,1:T(2,128)(2,1)S(1)}, bf16[2,1,64,1024]{3,0,2,1:T(2,128)(2,1)S(1)}, u32[]{:S(2)}, u32[]{:S(2)}) collective-permute-start(bf16[2,1,64,1024]{3,0,2,1:T(2,128)(2,1)S(1)} %fusion.24), channel_id=1, source_target_pairs={{0,4},{4,0},{8,12},{12,8},{1,5},{5,1},{9,13},{13,9},{2,6},{6,2},{1... | collective-permute-start | bytes 786440 | tf_op jit(solution)/shard_map/ppermute | solution.py:30
  170.8 22.6 %collective-permute-start.18 = (bf16[512,1024]{1,0:T(8,128)(2,1)}, bf16[512,1024]{1,0:T(8,128)(2,1)}, u32[]{:S(2)}, u32[]{:S(2)}) collective-permute-start(bf16[512,1024]{1,0:T(8,128)(2,1)} %pad_maximum_fusion.3), channel_id=1, source_target_pairs={{0,2},{2,0},{1,3},{3,1},{4,6},{6,4},{5,7},{7,5},{8,10},{10,8},{9,1... | collective-permute-start | bytes 3145736 | tf_op jit(solution)/shard_map/ppermute | solution.py:30
  187.3 6.1 %copy-start.23 = (bf16[1024,1024]{1,0:T(8,128)(2,1)S(1)}, bf16[1024,1024]{1,0:T(8,128)(2,1)}, u32[]{:S(2)}) copy-start(bf16[1024,1024]{1,0:T(8,128)(2,1)} %constant_dynamic-update-slice_fusion.6) | copy-start | bytes 6291460
  (14 other events, 28.1 us)

commit v6 on v2

--- a/solution.py
+++ b/solution.py
@@ -119,7 +119,17 @@
         sent = lax.dynamic_slice_in_dim(
             cot_rows, (position ^ step) * feat_count, feat_count, axis=1
         )
-        got = lax.ppermute(sent, "seq", pairs)
+        half = sent.shape[0] // 2
+        core = lax.axis_index("head")
+        got_half = lax.ppermute(
+            lax.dynamic_slice_in_dim(sent, core * half, half, axis=0), "seq", pairs
+        )
+        other_half = swapped(got_half, "head", 0)
+        got = jnp.where(
+            core == 0,
+            jnp.concatenate([got_half, other_half], axis=0),
+            jnp.concatenate([other_half, got_half], axis=0),
+        )
         part = jnp.dot(got, out_weight, preferred_element_type=jnp.float32)
         back = lax.ppermute(part.astype(jnp.bfloat16), "seq", pairs)
         grad_sum = grad_sum + back.astype(jnp.float32)

time: 185 us -> 186 us (level)
  other arithmetic: 31.8 us -> 35.5 us
  local copies, waits for them, and re-layouts: 38.8 us -> 35.1 us
    ppermute x3, waiting for transfers between devices: 19.8 us -> 6.55 us  [shards(): lax.ppermute(lax.dynamic_slice_in_dim(sent, core * half, half, axis=0), '...]
    ppermute x3, waiting for transfers between devices: 0.01 us -> 13 us  [shards(): back = lax.ppermute(part.astype(jnp.bfloat16), 'seq', pairs)]
    ppermute x3, starting transfers between devices: 10.8 us -> 4.39 us  [shards(): back = lax.ppermute(part.astype(jnp.bfloat16), 'seq', pairs)]
    ppermute x6 -> x9, starting transfers between devices: 1.46 us -> 7.87 us  [swapped(): lax.ppermute(shard, axis, [(i, i ^ 1 << stride) for i in range(lax.axis_s...]
    unnamed x1 -> x4, other arithmetic: 1.25 us -> 5.65 us
    unnamed x75 -> x76, local copies, waits for them, and re-layouts: 13.8 us -> 10.7 us
    ppermute x6 -> x9, waiting for transfers between devices: 40.1 us -> 39 us  [swapped(): lax.ppermute(shard, axis, [(i, i ^ 1 << stride) for i in range(lax.axis_s...]
  transfers between devices with their start and end apart: 19 -> 22, of which waited for: 7 -> 7; matrix products, arithmetic and copies ran while one was open for 44% -> 44% of each run, Pallas kernels for 0% -> 0%
where the time goes in v6:
time: 186 us; the launch traced here: 184 us
  waiting for transfers between devices  58.5 us (31%)
  other arithmetic  35.5 us (19%)
  local copies, waits for them, and re-layouts  35.1 us (19%)
  starting transfers between devices  34.3 us (18%)
  matrix products  19.2 us (10%)
    ppermute x9, waiting for transfers between devices, swapped(): lax.ppermute(shard, axis, [(i, i ^ 1 << stride) for i in range(lax.axis_s...  39 us
    ppermute x3, waiting for transfers between devices, shards(): back = lax.ppermute(part.astype(jnp.bfloat16), 'seq', pairs)  13 us
    ppermute x2, starting transfers between devices, extended(): lax.ppermute(tail, axis, [(i, (i + 1) % count) for i in range(ends)])  10.7 us
    unnamed x76, local copies, waits for them, and re-layouts  10.7 us
    ppermute x9, starting transfers between devices, swapped(): lax.ppermute(shard, axis, [(i, i ^ 1 << stride) for i in range(lax.axis_s...  7.87 us
    ppermute x3, waiting for transfers between devices, shards(): lax.ppermute(lax.dynamic_slice_in_dim(sent, core * half, half, axis=0), '...  6.55 us
    unnamed x4, other arithmetic  5.65 us
    scatter-add x1, other arithmetic, place_blocks(): return holder.at[:, chosen_doc].add(grad_doc)  5.59 us
  transfers between devices with their start and end apart: 22, of which 7 were waited for; matrix products, arithmetic and copies ran while one was open for 44% of the time, Pallas kernels for 0%

profile of v6, /device:TPU:6, one launch (start us, length us, event | category | flops | bytes accessed | tf_op | source)
XLA Modules:
  0.0 183.9 jit_solution(5982389932930896146)
XLA Ops:
  0.7 2.0 %pad_maximum_fusion.7 = bf16[2,1,128,1024]{3,2,1,0:T(8,128)(2,1)} fusion(bf16[1,1,128,1024]{3,2,1,0:T(8,128)(2,1)} %bitcast.249, bf16[1,1,128,1024]{3,2,1,0:T(8,128)(2,1)} %bitcast.251), kind=kLoop, calls=%fused_computation.52 | loop fusion | flops 262144 | bytes 1048576 | tf_op jit(solution)/shard_map/stack | solution.py:58
  4.0 5.4 %collective-permute-start = (bf16[2,1,128,1024]{3,2,1,0:T(8,128)(2,1)}, bf16[2,1,128,1024]{3,2,1,0:T(8,128)(2,1)}, u32[]{:S(2)}, u32[]{:S(2)}) collective-permute-start(bf16[2,1,128,1024]{3,2,1,0:T(8,128)(2,1)} %pad_maximum_fusion.7), channel_id=1, source_target_pairs={{0,4},{4,8},{8,12},{1,5},{5,9},{9,13},{2,6},{6,10},{10,14},{3,7},{... | collective-permute-start | bytes 1572872 | tf_op jit(solution)/shard_map/ppermute | solution.py:20
  9.3 1.9 %dynamic-slice_bitcast_fusion.1 = (bf16[64,1024]{1,0:T(8,128)(2,1)}, bf16[64,1024]{1,0:T(8,128)(2,1)S(1)}, bf16[64,1024]{1,0:T(8,128)(2,1)S(1)}) fusion(bf16[1,128,4096]{2,1,0:T(8,128)(2,1)} %param.11, s32[]{:T(128)S(6)} %select_n.96, s32[]{:T(128)S(6)} %select_n.104, s32[]{:T(128)S(6)} %select_n.98, s32[]{:T(128)S(6)} %select_n.101), kind=kLoop, calls=%fused_computation.91 | loop fusion | bytes 786448 | tf_op jit(solution)/shard_map/dynamic_slice | solution.py:125
  12.1 1.8 collective-permute-start.7
  13.9 1.8 collective-permute-start.10
  16.8 1.4 convert_reduce_fusion
  19.4 1.7 constant_dynamic-update-slice_fusion.4
  23.9 5.1 %collective-permute-done.7 = bf16[64,1024]{1,0:T(8,128)(2,1)S(1)} collective-permute-done((bf16[64,1024]{1,0:T(8,128)(2,1)S(1)}, bf16[64,1024]{1,0:T(8,128)(2,1)S(1)}, u32[]{:S(2)}, u32[]{:S(2)}) %collective-permute-start.7) | collective-permute-done | bytes 131104 | tf_op jit(solution)/shard_map/ppermute | solution.py:124
  30.0 2.5 %collective-permute-start.2 = (f32[2,1,64,1024]{3,2,1,0:T(8,128)}, f32[2,1,64,1024]{3,2,1,0:T(8,128)}, u32[]{:S(2)}, u32[]{:S(2)}) collective-permute-start(f32[2,1,64,1024]{3,2,1,0:T(8,128)} %get-tuple-element.31), channel_id=1, source_target_pairs={{0,4},{4,0},{8,12},{12,8},{1,5},{5,1},{9,13},{13,9},{2,6},{6,2},{1... | collective-permute-start | bytes 1572872 | tf_op jit(solution)/shard_map/ppermute | solution.py:30
  32.6 1.8 constant_dynamic-update-slice_fusion.3
  34.3 1.9 %constant_dynamic-update-slice_fusion.2 = (bf16[1024,1024]{1,0:T(8,128)(2,1)}, bf16[128,1024]{1,0:T(8,128)(2,1)S(1)}) fusion(bf16[1024,1024]{1,0:T(8,128)(2,1)} %get-tuple-element.11, bf16[64,1024]{1,0:T(8,128)(2,1)} %copy-done.29, bf16[64,1024]{1,0:T(8,128)(2,1)} %collective-permute-done.8, pred[]{:T(512)S(6)} %eq.10), kind=kLoop, calls=%fused_computation.96 | loop fusion | flops 1179648 | bytes 786433
  38.1 3.3 %collective-permute-start.12 = (bf16[128,1024]{1,0:T(8,128)(2,1)}, bf16[128,1024]{1,0:T(8,128)(2,1)}, u32[]{:S(2)}, u32[]{:S(2)}) collective-permute-start(bf16[128,1024]{1,0:T(8,128)(2,1)} %convolution_convert_fusion), channel_id=1, source_target_pairs={{0,12},{4,8},{8,4},{12,0},{1,13},{5,9},{9,5},{13,1},{2,14},{6,10},... | collective-permute-start | bytes 786440 | tf_op jit(solution)/shard_map/ppermute | solution.py:134
  54.2 3.9 %collective-permute-start.3 = (bf16[2,1,64,1024]{3,2,1,0:T(8,128)(2,1)S(1)}, bf16[2,1,64,1024]{3,2,1,0:T(8,128)(2,1)S(1)}, u32[]{:S(2)}, u32[]{:S(2)}) collective-permute-start(bf16[2,1,64,1024]{3,2,1,0:T(8,128)(2,1)S(1)} %fusion.23), channel_id=1, source_target_pairs={{0,8},{4,12},{8,0},{12,4},{1,9},{5,13},{9,1},{13,5},{2,10},{6,14},... | collective-permute-start | bytes 786440 | tf_op jit(solution)/shard_map/ppermute | solution.py:30
  58.1 13.0 %collective-permute-done.9 = bf16[128,1024]{1,0:T(8,128)(2,1)} collective-permute-done((bf16[128,1024]{1,0:T(8,128)(2,1)}, bf16[128,1024]{1,0:T(8,128)(2,1)}, u32[]{:S(2)}, u32[]{:S(2)}) %collective-permute-start.9) | collective-permute-done | bytes 262176 | tf_op jit(solution)/shard_map/ppermute | solution.py:134
  79.9 1.7 multiply_reduce_fusion
  81.6 2.1 %convolution_bitcast_fusion = f32[1,2,192,8,128]{4,2,3,1,0:T(8,128)} fusion(bf16[2,64,8,128]{3,2,1,0:T(8,128)(2,1)S(1)} %bitcast.259, f32[2,8,64,192]{3,2,1,0:T(8,128)S(1)} %get-tuple-element.33, f32[2,8,64]{2,1,0:T(8,128)S(1)} %copy_add_fusion.1, f32[2,8,64]{2,1,0:T(8,128)S(1)} %copy_maximum_fusion), kind=kOutput, calls=%fused_computation.6 | convolution fusion | flops 50921472 | bytes 2629632 | tf_op jit(solution)/shard_map/dbhqk,dbqhe->dbkhe/dot_general | solution.py:176
  89.9 3.1 %pad_maximum_fusion = f32[1,2,2,3,64,1024]{5,0,4,3,2,1:T(1,128)S(1)} fusion(f32[1,1,2,3,64,1024]{5,0,4,3,2,1:T(1,128)S(1)} %bitcast.235, f32[1,1,2,3,64,1024]{5,0,4,3,2,1:T(1,128)S(1)} %bitcast.236), kind=kLoop, calls=%fused_computation.2 | loop fusion | flops 786432 | bytes 6291456 | tf_op jit(solution)/shard_map/stack | solution.py:186
  93.0 2.4 %copy.260 = f32[1,2,2,3,64,1024]{5,4,1,3,2,0:T(8,128)} copy(f32[1,2,2,3,64,1024]{5,0,4,3,2,1:T(1,128)S(1)} %pad_maximum_fusion) | data formatting | bytes 6291456 | tf_op jit(solution)/shard_map/stack | solution.py:186
  95.8 5.6 %scatter_fusion = f32[2,6,64,1024]{3,2,1,0:T(8,128)S(1)} fusion(f32[2,6,64,1024]{3,2,1,0:T(8,128)S(1)} %broadcast.159, s32[6]{0:T(128)S(1)} %reshape.562, f32[6,2,64,1024]{3,2,1,0:T(8,128)} %bitcast.222), kind=kCustom, calls=%fused_computation.1 | custom fusion | flops 786432 | bytes 9437208 | tf_op jit(solution)/shard_map/vmap()/scatter-add | solution.py:46
  107.2 3.2 %collective-permute-start.19 = (bf16[128,1024]{1,0:T(8,128)(2,1)}, bf16[128,1024]{1,0:T(8,128)(2,1)}, u32[]{:S(2)}, u32[]{:S(2)}) collective-permute-start(bf16[128,1024]{1,0:T(8,128)(2,1)} %bitcast.216), channel_id=1, source_target_pairs={{0,8},{4,12},{8,0},{12,4},{1,9},{5,13},{9,1},{13,5},{2,10},{6,14},... | collective-permute-start | bytes 786440 | tf_op jit(solution)/shard_map/ppermute | solution.py:137
  117.0 27.5 %collective-permute-done.15 = bf16[2,1,64,1024]{3,0,2,1:T(2,128)(2,1)S(1)} collective-permute-done((bf16[2,1,64,1024]{3,0,2,1:T(2,128)(2,1)S(1)}, bf16[2,1,64,1024]{3,0,2,1:T(2,128)(2,1)S(1)}, u32[]{:S(2)}, u32[]{:S(2)}) %collective-permute-start.15) | collective-permute-done | bytes 262176 | tf_op jit(solution)/shard_map/ppermute | solution.py:30
  147.1 5.3 %collective-permute-start.13 = (bf16[2,1,128,1024]{3,2,1,0:T(8,128)(2,1)}, bf16[2,1,128,1024]{3,2,1,0:T(8,128)(2,1)}, u32[]{:S(2)}, u32[]{:S(2)}) collective-permute-start(bf16[2,1,128,1024]{3,2,1,0:T(8,128)(2,1)} %get-tuple-element.19), channel_id=1, source_target_pairs={{0,4},{4,8},{8,12},{1,5},{5,9},{9,13},{2,6},{6,10},{10,14},{3,7},{... | collective-permute-start | bytes 1572872 | tf_op jit(solution)/shard_map/ppermute | solution.py:20
  152.5 2.3 %pad_maximum_fusion.3 = bf16[512,1024]{1,0:T(8,128)(2,1)} fusion(bf16[128,1024]{1,0:T(8,128)(2,1)} %collective-permute-done.20, bf16[128,1024]{1,0:T(8,128)(2,1)} %collective-permute-done.19, bf16[128,1024]{1,0:T(8,128)(2,1)} %collective-permute-done.18, bf16[128,1024]{1,0:T(8,128)(2,1)} %bitcast.216), kind=kLoop, calls=%fused_computation.33 | loop fusion | flops 4194304 | bytes 2097152 | tf_op jit(solution)/shard_map/concatenate | solution.py:140
  155.2 1.7 constant_dynamic-update-slice_fusion.8
  156.9 1.7 constant_dynamic-update-slice_fusion.7
  158.6 1.7 constant_dynamic-update-slice_fusion.6
  160.3 6.9 %collective-permute-done.16 = bf16[2,1,64,1024]{3,0,2,1:T(2,128)(2,1)S(1)} collective-permute-done((bf16[2,1,64,1024]{3,0,2,1:T(2,128)(2,1)S(1)}, bf16[2,1,64,1024]{3,0,2,1:T(2,128)(2,1)S(1)}, u32[]{:S(2)}, u32[]{:S(2)}) %collective-permute-start.16) | collective-permute-done | bytes 262176 | tf_op jit(solution)/shard_map/ppermute | solution.py:30
  168.1 1.8 mul.193
  169.9 2.3 %constant_dynamic-update-slice_fusion = bf16[1024,1024]{1,0:T(8,128)(2,1)} fusion(bf16[1024,1024]{1,0:T(8,128)(2,1)} %get-tuple-element.7, bf16[512,1024]{1,0:T(8,128)(2,1)} %collective-permute-done.17), kind=kLoop, calls=%fused_computation.94 | loop fusion | bytes 2097152 | tf_op jit(solution)/shard_map/concatenate | solution.py:143
  172.3 1.7 fusion.10
  174.8 3.3 %collective-permute-done.21 = bf16[512,1024]{1,0:T(8,128)(2,1)} collective-permute-done((bf16[512,1024]{1,0:T(8,128)(2,1)}, bf16[512,1024]{1,0:T(8,128)(2,1)}, u32[]{:S(2)}, u32[]{:S(2)}) %collective-permute-start.21) | collective-permute-done | bytes 1048608 | tf_op jit(solution)/shard_map/ppermute | solution.py:30
  179.5 4.5 %fusion.49 = f32[1024,1024]{1,0:T(8,128)} fusion(bf16[1024,1024]{1,0:T(8,128)(2,1)S(1)} %copy-done.31, bf16[1024,1024]{1,0:T(8,128)(2,1)S(1)} %constant_dynamic-update-slice_fusion.5), kind=kOutput, calls=%fused_computation.121 | convolution fusion | flops 2147483648 | bytes 8388608 | tf_op jit(solution)/shard_map/tc,tw->cw/dot_general | solution.py:148
  (178 shorter events, 56.5 us)
Async XLA Ops:
  0.6 20.5 %copy-start = (bf16[1024,1024]{1,0:T(8,128)(2,1)S(1)}, bf16[1024,1024]{1,0:T(8,128)(2,1)}, u32[]{:S(2)}) copy-start(bf16[1024,1024]{1,0:T(8,128)(2,1)} %param.10) | copy-start | bytes 6291460
  0.6 16.1 %copy-start.9 = (bf16[1,128,1024]{2,1,0:T(8,128)(2,1)S(1)}, bf16[1,128,1024]{2,1,0:T(8,128)(2,1)}, u32[]{:S(2)}) copy-start(bf16[1,128,1024]{2,1,0:T(8,128)(2,1)} %param.7) | copy-start | bytes 786436
  2.7 42.1 %collective-permute-start.1 = (bf16[2,1,128,1024]{3,2,1,0:T(8,128)(2,1)}, bf16[2,1,128,1024]{3,2,1,0:T(8,128)(2,1)}, u32[]{:S(2)}, u32[]{:S(2)}) collective-permute-start(bf16[2,1,128,1024]{3,2,1,0:T(8,128)(2,1)} %pad_maximum_fusion.7), channel_id=1, source_target_pairs={{4,0},{8,4},{12,8},{5,1},{9,5},{13,9},{6,2},{10,6},{14,10},{7,3},{... | collective-permute-start | bytes 1572872 | tf_op jit(solution)/shard_map/ppermute | solution.py:22
  4.0 41.9 %collective-permute-start = (bf16[2,1,128,1024]{3,2,1,0:T(8,128)(2,1)}, bf16[2,1,128,1024]{3,2,1,0:T(8,128)(2,1)}, u32[]{:S(2)}, u32[]{:S(2)}) collective-permute-start(bf16[2,1,128,1024]{3,2,1,0:T(8,128)(2,1)} %pad_maximum_fusion.7), channel_id=1, source_target_pairs={{0,4},{4,8},{8,12},{1,5},{5,9},{9,13},{2,6},{6,10},{10,14},{3,7},{... | collective-permute-start | bytes 1572872 | tf_op jit(solution)/shard_map/ppermute | solution.py:20
  11.3 12.6 %collective-permute-start.4 = (bf16[64,1024]{1,0:T(8,128)(2,1)S(1)}, bf16[64,1024]{1,0:T(8,128)(2,1)S(1)}, u32[]{:S(2)}, u32[]{:S(2)}) collective-permute-start(bf16[64,1024]{1,0:T(8,128)(2,1)S(1)} %get-tuple-element.22), channel_id=1, source_target_pairs={{0,4},{4,0},{8,12},{12,8},{1,5},{5,1},{9,13},{13,9},{2,6},{6,2},{1... | collective-permute-start | bytes 393224 | tf_op jit(solution)/shard_map/ppermute | solution.py:124
  12.1 16.9 %collective-permute-start.7 = (bf16[64,1024]{1,0:T(8,128)(2,1)S(1)}, bf16[64,1024]{1,0:T(8,128)(2,1)S(1)}, u32[]{:S(2)}, u32[]{:S(2)}) collective-permute-start(bf16[64,1024]{1,0:T(8,128)(2,1)S(1)} %get-tuple-element.23), channel_id=1, source_target_pairs={{0,8},{4,12},{8,0},{12,4},{1,9},{5,13},{9,1},{13,5},{2,10},{6,14},... | collective-permute-start | bytes 393224 | tf_op jit(solution)/shard_map/ppermute | solution.py:124
  13.9 16.2 %collective-permute-start.10 = (bf16[64,1024]{1,0:T(8,128)(2,1)}, bf16[64,1024]{1,0:T(8,128)(2,1)S(1)}, u32[]{:S(2)}, u32[]{:S(2)}) collective-permute-start(bf16[64,1024]{1,0:T(8,128)(2,1)} %get-tuple-element.21), channel_id=1, source_target_pairs={{0,12},{4,8},{8,4},{12,0},{1,13},{5,9},{9,5},{13,1},{2,14},{6,10},... | collective-permute-start | bytes 393224 | tf_op jit(solution)/shard_map/ppermute | solution.py:124
  19.4 9.7 %copy-start.28 = (bf16[1,128,1024]{2,1,0:T(8,128)(2,1)S(1)}, bf16[1,128,1024]{2,1,0:T(8,128)(2,1)}, u32[]{:S(2)}) copy-start(bf16[1,128,1024]{2,1,0:T(8,128)(2,1)} %param.6) | copy-start | bytes 786436
  21.2 13.2 %copy-start.16 = (bf16[128,1024]{1,0:T(8,128)(2,1)}, bf16[128,1024]{1,0:T(8,128)(2,1)S(1)}, u32[]{:S(2)}) copy-start(bf16[128,1024]{1,0:T(8,128)(2,1)S(1)} %get-tuple-element.14) | copy-start | bytes 786436
  23.9 8.6 %collective-permute-start.5 = (bf16[64,1024]{1,0:T(8,128)(2,1)S(1)}, bf16[64,1024]{1,0:T(8,128)(2,1)}, u32[]{:S(2)}, u32[]{:S(2)}) collective-permute-start(bf16[64,1024]{1,0:T(8,128)(2,1)S(1)} %collective-permute-done.4), channel_id=1, source_target_pairs={{0,1},{1,0},{2,3},{3,2},{4,5},{5,4},{6,7},{7,6},{8,9},{9,8},{10,11... | collective-permute-start | bytes 393224 | tf_op jit(solution)/shard_map/ppermute | solution.py:30
  29.0 5.3 %collective-permute-start.8 = (bf16[64,1024]{1,0:T(8,128)(2,1)S(1)}, bf16[64,1024]{1,0:T(8,128)(2,1)}, u32[]{:S(2)}, u32[]{:S(2)}) collective-permute-start(bf16[64,1024]{1,0:T(8,128)(2,1)S(1)} %collective-permute-done.7), channel_id=1, source_target_pairs={{0,1},{1,0},{2,3},{3,2},{4,5},{5,4},{6,7},{7,6},{8,9},{9,8},{10,11... | collective-permute-start | bytes 393224 | tf_op jit(solution)/shard_map/ppermute | solution.py:30
  30.0 18.7 %collective-permute-start.2 = (f32[2,1,64,1024]{3,2,1,0:T(8,128)}, f32[2,1,64,1024]{3,2,1,0:T(8,128)}, u32[]{:S(2)}, u32[]{:S(2)}) collective-permute-start(f32[2,1,64,1024]{3,2,1,0:T(8,128)} %get-tuple-element.31), channel_id=1, source_target_pairs={{0,4},{4,0},{8,12},{12,8},{1,5},{5,1},{9,13},{13,9},{2,6},{6,2},{1... | collective-permute-start | bytes 1572872 | tf_op jit(solution)/shard_map/ppermute | solution.py:30
  32.5 3.7 %collective-permute-start.11 = (bf16[64,1024]{1,0:T(8,128)(2,1)S(1)}, bf16[64,1024]{1,0:T(8,128)(2,1)S(1)}, u32[]{:S(2)}, u32[]{:S(2)}) collective-permute-start(bf16[64,1024]{1,0:T(8,128)(2,1)S(1)} %collective-permute-done.10), channel_id=1, source_target_pairs={{0,1},{1,0},{2,3},{3,2},{4,5},{5,4},{6,7},{7,6},{8,9},{9,8},{10,11... | collective-permute-start | bytes 393224 | tf_op jit(solution)/shard_map/ppermute | solution.py:30
  38.1 20.0 %collective-permute-start.12 = (bf16[128,1024]{1,0:T(8,128)(2,1)}, bf16[128,1024]{1,0:T(8,128)(2,1)}, u32[]{:S(2)}, u32[]{:S(2)}) collective-permute-start(bf16[128,1024]{1,0:T(8,128)(2,1)} %convolution_convert_fusion), channel_id=1, source_target_pairs={{0,12},{4,8},{8,4},{12,0},{1,13},{5,9},{9,5},{13,1},{2,14},{6,10},... | collective-permute-start | bytes 786440 | tf_op jit(solution)/shard_map/ppermute | solution.py:134
  42.6 28.5 %collective-permute-start.9 = (bf16[128,1024]{1,0:T(8,128)(2,1)}, bf16[128,1024]{1,0:T(8,128)(2,1)}, u32[]{:S(2)}, u32[]{:S(2)}) collective-permute-start(bf16[128,1024]{1,0:T(8,128)(2,1)} %convolution_convert_fusion.1), channel_id=1, source_target_pairs={{0,8},{4,12},{8,0},{12,4},{1,9},{5,13},{9,1},{13,5},{2,10},{6,14},... | collective-permute-start | bytes 786440 | tf_op jit(solution)/shard_map/ppermute | solution.py:134
  44.8 26.3 %collective-permute-start.6 = (bf16[128,1024]{1,0:T(8,128)(2,1)}, bf16[128,1024]{1,0:T(8,128)(2,1)}, u32[]{:S(2)}, u32[]{:S(2)}) collective-permute-start(bf16[128,1024]{1,0:T(8,128)(2,1)} %convolution_convert_fusion.2), channel_id=1, source_target_pairs={{0,4},{4,0},{8,12},{12,8},{1,5},{5,1},{9,13},{13,9},{2,6},{6,2},{1... | collective-permute-start | bytes 786440 | tf_op jit(solution)/shard_map/ppermute | solution.py:134
  45.9 124.1 %collective-permute-start.17 = (bf16[512,1024]{1,0:T(8,128)(2,1)}, bf16[512,1024]{1,0:T(8,128)(2,1)}, u32[]{:S(2)}, u32[]{:S(2)}) collective-permute-start(bf16[512,1024]{1,0:T(8,128)(2,1)} %pad_maximum_fusion.2), channel_id=1, source_target_pairs={{0,2},{2,0},{1,3},{3,1},{4,6},{6,4},{5,7},{7,5},{8,10},{10,8},{9,1... | collective-permute-start | bytes 3145736 | tf_op jit(solution)/shard_map/ppermute | solution.py:30
  52.2 18.9 %copy-start.20 = (f32[128,1024]{1,0:T(8,128)S(1)}, f32[128,1024]{1,0:T(8,128)}, u32[]{:S(2)}) copy-start(f32[128,1024]{1,0:T(8,128)} %fusion.48) | copy-start | bytes 1572868
  54.2 22.1 %collective-permute-start.3 = (bf16[2,1,64,1024]{3,2,1,0:T(8,128)(2,1)S(1)}, bf16[2,1,64,1024]{3,2,1,0:T(8,128)(2,1)S(1)}, u32[]{:S(2)}, u32[]{:S(2)}) collective-permute-start(bf16[2,1,64,1024]{3,2,1,0:T(8,128)(2,1)S(1)} %fusion.23), channel_id=1, source_target_pairs={{0,8},{4,12},{8,0},{12,4},{1,9},{5,13},{9,1},{13,5},{2,10},{6,14},... | collective-permute-start | bytes 786440 | tf_op jit(solution)/shard_map/ppermute | solution.py:30
  72.4 9.2 %copy-start.14 = (bf16[16,8,8,128]{3,2,1,0:T(8,128)(2,1)}, bf16[16,8,8,128]{3,2,1,0:T(8,128)(2,1)S(1)}, u32[]{:S(2)}) copy-start(bf16[16,8,8,128]{3,2,1,0:T(8,128)(2,1)S(1)} %copy.264) | copy-start | bytes 786436
  77.5 7.7 %copy-start.2 = (f32[8,128,128]{1,2,0}, f32[8,128,128]{1,2,0:S(1)}, u32[]{:S(2)}) copy-start(f32[8,128,128]{1,2,0:S(1)} %fusion.50) | copy-start | bytes 1572868
  104.4 7.5 %copy-start.11 = (bf16[1,1,128,1024]{2,3,1,0:T(8,128)(2,1)S(1)}, bf16[1,1,128,1024]{2,3,1,0:T(8,128)(2,1)}, u32[]{:S(2)}) copy-start(bf16[1,1,128,1024]{2,3,1,0:T(8,128)(2,1)} %copy-done.10) | copy-start | bytes 786436
  104.4 7.5 %copy-start.19 = (f32[1,2,64,8,128]{4,2,3,1,0:T(8,128)S(1)}, f32[1,2,64,8,128]{4,2,3,1,0:T(8,128)}, u32[]{:S(2)}) copy-start(f32[1,2,64,8,128]{4,2,3,1,0:T(8,128)} %convolution_bitcast_fusion.1) | copy-start | bytes 1572868
  107.2 39.9 %collective-permute-start.18 = (bf16[128,1024]{1,0:T(8,128)(2,1)}, bf16[128,1024]{1,0:T(8,128)(2,1)}, u32[]{:S(2)}, u32[]{:S(2)}) collective-permute-start(bf16[128,1024]{1,0:T(8,128)(2,1)} %bitcast.216), channel_id=1, source_target_pairs={{0,4},{4,0},{8,12},{12,8},{1,5},{5,1},{9,13},{13,9},{2,6},{6,2},{1... | collective-permute-start | bytes 786440 | tf_op jit(solution)/shard_map/ppermute | solution.py:137
  107.2 45.2 %collective-permute-start.19 = (bf16[128,1024]{1,0:T(8,128)(2,1)}, bf16[128,1024]{1,0:T(8,128)(2,1)}, u32[]{:S(2)}, u32[]{:S(2)}) collective-permute-start(bf16[128,1024]{1,0:T(8,128)(2,1)} %bitcast.216), channel_id=1, source_target_pairs={{0,8},{4,12},{8,0},{12,4},{1,9},{5,13},{9,1},{13,5},{2,10},{6,14},... | collective-permute-start | bytes 786440 | tf_op jit(solution)/shard_map/ppermute | solution.py:137
  110.5 42.0 %collective-permute-start.20 = (bf16[128,1024]{1,0:T(8,128)(2,1)}, bf16[128,1024]{1,0:T(8,128)(2,1)}, u32[]{:S(2)}, u32[]{:S(2)}) collective-permute-start(bf16[128,1024]{1,0:T(8,128)(2,1)} %bitcast.216), channel_id=1, source_target_pairs={{0,12},{4,8},{8,4},{12,0},{1,13},{5,9},{9,5},{13,1},{2,14},{6,10},... | collective-permute-start | bytes 786440 | tf_op jit(solution)/shard_map/ppermute | solution.py:137
  114.4 30.1 %collective-permute-start.15 = (bf16[2,1,64,1024]{3,0,2,1:T(2,128)(2,1)S(1)}, bf16[2,1,64,1024]{3,0,2,1:T(2,128)(2,1)S(1)}, u32[]{:S(2)}, u32[]{:S(2)}) collective-permute-start(bf16[2,1,64,1024]{3,0,2,1:T(2,128)(2,1)S(1)} %fusion.34), channel_id=1, source_target_pairs={{0,8},{4,12},{8,0},{12,4},{1,9},{5,13},{9,1},{13,5},{2,10},{6,14},... | collective-permute-start | bytes 786440 | tf_op jit(solution)/shard_map/ppermute | solution.py:30
  144.5 27.8 %collective-permute-start.14 = (bf16[2,1,128,1024]{3,2,1,0:T(8,128)(2,1)}, bf16[2,1,128,1024]{3,2,1,0:T(8,128)(2,1)}, u32[]{:S(2)}, u32[]{:S(2)}) collective-permute-start(bf16[2,1,128,1024]{3,2,1,0:T(8,128)(2,1)} %get-tuple-element.20), channel_id=1, source_target_pairs={{4,0},{8,4},{12,8},{5,1},{9,5},{13,9},{6,2},{10,6},{14,10},{7,3},{... | collective-permute-start | bytes 1572872 | tf_op jit(solution)/shard_map/ppermute | solution.py:22
  147.1 25.2 %collective-permute-start.13 = (bf16[2,1,128,1024]{3,2,1,0:T(8,128)(2,1)}, bf16[2,1,128,1024]{3,2,1,0:T(8,128)(2,1)}, u32[]{:S(2)}, u32[]{:S(2)}) collective-permute-start(bf16[2,1,128,1024]{3,2,1,0:T(8,128)(2,1)} %get-tuple-element.19), channel_id=1, source_target_pairs={{0,4},{4,8},{8,12},{1,5},{5,9},{9,13},{2,6},{6,10},{10,14},{3,7},{... | collective-permute-start | bytes 1572872 | tf_op jit(solution)/shard_map/ppermute | solution.py:20
  152.4 14.7 %collective-permute-start.16 = (bf16[2,1,64,1024]{3,0,2,1:T(2,128)(2,1)S(1)}, bf16[2,1,64,1024]{3,0,2,1:T(2,128)(2,1)S(1)}, u32[]{:S(2)}, u32[]{:S(2)}) collective-permute-start(bf16[2,1,64,1024]{3,0,2,1:T(2,128)(2,1)S(1)} %fusion.24), channel_id=1, source_target_pairs={{0,4},{4,0},{8,12},{12,8},{1,5},{5,1},{9,13},{13,9},{2,6},{6,2},{1... | collective-permute-start | bytes 786440 | tf_op jit(solution)/shard_map/ppermute | solution.py:30
  154.7 23.4 %collective-permute-start.21 = (bf16[512,1024]{1,0:T(8,128)(2,1)}, bf16[512,1024]{1,0:T(8,128)(2,1)}, u32[]{:S(2)}, u32[]{:S(2)}) collective-permute-start(bf16[512,1024]{1,0:T(8,128)(2,1)} %pad_maximum_fusion.3), channel_id=1, source_target_pairs={{0,2},{2,0},{1,3},{3,1},{4,6},{6,4},{5,7},{7,5},{8,10},{10,8},{9,1... | collective-permute-start | bytes 3145736 | tf_op jit(solution)/shard_map/ppermute | solution.py:30
  172.3 5.8 %copy-start.30 = (bf16[1024,1024]{1,0:T(8,128)(2,1)S(1)}, bf16[1024,1024]{1,0:T(8,128)(2,1)}, u32[]{:S(2)}) copy-start(bf16[1024,1024]{1,0:T(8,128)(2,1)} %constant_dynamic-update-slice_fusion.6) | copy-start | bytes 6291460
  (23 other events, 63.3 us)

commit v7 on v6

--- a/solution.py
+++ b/solution.py
@@ -113,7 +113,6 @@
     own_cols = lax.dynamic_slice_in_dim(cot_rows, position * feat_count, feat_count, axis=1)
     grad_sum = jnp.dot(own_cols, out_weight, preferred_element_type=jnp.float32)
     feat_list = [own_cols]
-    out_list = [out_rows]
     for step in range(1, seq_count):
         pairs = [(i, i ^ step) for i in range(seq_count)]
         sent = lax.dynamic_slice_in_dim(
@@ -134,10 +133,12 @@
         back = lax.ppermute(part.astype(jnp.bfloat16), "seq", pairs)
         grad_sum = grad_sum + back.astype(jnp.float32)
         feat_list.append(got)
-        out_list.append(lax.ppermute(out_rows, "seq", pairs))
     attn_grad = grad_sum.astype(jnp.bfloat16)
-    feat_docs = jnp.concatenate(feat_list, axis=0)
-    whole_output = jnp.concatenate(out_list, axis=0)
+    feat_order = jnp.arange(seq_count, dtype=jnp.int32) ^ position
+    feat_docs = jnp.take(jnp.stack(feat_list, axis=0), feat_order, axis=0).reshape(
+        seq_count * cot_rows.shape[0], feat_count
+    )
+    whole_output = lax.all_gather(out_rows, "seq", axis=0, tiled=True)
     dp_count = lax.axis_size("dp")
     if dp_count == 2:
         feat_docs = jnp.concatenate([feat_docs, swapped(feat_docs, "dp", 0)], axis=0)

time: 186 us -> 180 us (0.968)
  the two profiles are of different devices: /device:TPU:6 before, /device:TPU:18 now
where the time goes in v7:
time: 180 us; the launch traced here: 179 us
  waiting for transfers between devices  44.4 us (25%)
  other arithmetic  34.6 us (19%)
  local copies, waits for them, and re-layouts  32.2 us (18%)
  starting transfers between devices  26.9 us (15%)
  matrix products  26.4 us (15%)
  between operations  14.8 us (8%)
    ppermute x9, waiting for transfers between devices, swapped(): lax.ppermute(shard, axis, [(i, i ^ 1 << stride) for i in range(lax.axis_s...  21.1 us
    all_gather x1, waiting for transfers between devices, shards(): whole_output = lax.all_gather(out_rows, 'seq', axis=0, tiled=True)  12.1 us
    ppermute x3, waiting for transfers between devices, shards(): lax.ppermute(lax.dynamic_slice_in_dim(sent, core * half, half, axis=0), '...  9.64 us
    ppermute x2, starting transfers between devices, extended(): lax.ppermute(tail, axis, [(i, (i + 1) % count) for i in range(ends)])  7.14 us
    dot_general x3, matrix products, shards(): part = jnp.dot(got, out_weight, preferred_element_type=jnp.float32)  6.6 us
    dot_general x1, matrix products, shards(): jnp.einsum('tc,tw->cw', feat_docs, whole_output, preferred_element_type=j...  6.41 us
    ppermute x2, starting transfers between devices, extended(): lax.ppermute(head, axis, [((i + 1) % count, i) for i in range(ends)])  6.33 us
    ppermute x9, starting transfers between devices, swapped(): lax.ppermute(shard, axis, [(i, i ^ 1 << stride) for i in range(lax.axis_s...  5.65 us
  transfers between devices with their start and end apart: 20, of which 6 were waited for; matrix products, arithmetic and copies ran while one was open for 47% of the time, Pallas kernels for 0%

profile of v7, /device:TPU:18, one launch (start us, length us, event | category | flops | bytes accessed | tf_op | source)
XLA Modules:
  0.0 179.3 jit_solution(14284245836785975555)
XLA Ops:
  7.2 2.0 %pad_maximum_fusion.6 = bf16[2,1,128,1024]{3,2,1,0:T(8,128)(2,1)} fusion(bf16[1,1,128,1024]{3,2,1,0:T(8,128)(2,1)} %bitcast.251, bf16[1,1,128,1024]{3,2,1,0:T(8,128)(2,1)} %bitcast.253), kind=kLoop, calls=%fused_computation.60 | loop fusion | flops 262144 | bytes 1048576 | tf_op jit(solution)/shard_map/stack | solution.py:58
  9.3 2.3 %collective-permute-start.1 = (bf16[2,1,128,1024]{3,2,1,0:T(8,128)(2,1)}, bf16[2,1,128,1024]{3,2,1,0:T(8,128)(2,1)}, u32[]{:S(2)}, u32[]{:S(2)}) collective-permute-start(bf16[2,1,128,1024]{3,2,1,0:T(8,128)(2,1)} %pad_maximum_fusion.6), channel_id=1, source_target_pairs={{4,0},{8,4},{12,8},{5,1},{9,5},{13,9},{6,2},{10,6},{14,10},{7,3},{... | collective-permute-start | bytes 1572872 | tf_op jit(solution)/shard_map/ppermute | solution.py:22
  11.6 4.3 %collective-permute-start = (bf16[2,1,128,1024]{3,2,1,0:T(8,128)(2,1)}, bf16[2,1,128,1024]{3,2,1,0:T(8,128)(2,1)}, u32[]{:S(2)}, u32[]{:S(2)}) collective-permute-start(bf16[2,1,128,1024]{3,2,1,0:T(8,128)(2,1)} %pad_maximum_fusion.6), channel_id=1, source_target_pairs={{0,4},{4,8},{8,12},{1,5},{5,9},{9,13},{2,6},{6,10},{10,14},{3,7},{... | collective-permute-start | bytes 1572872 | tf_op jit(solution)/shard_map/ppermute | solution.py:20
  15.9 2.0 %dynamic-slice_bitcast_fusion.2 = (bf16[64,1024]{1,0:T(8,128)(2,1)}, bf16[64,1024]{1,0:T(8,128)(2,1)}, bf16[64,1024]{1,0:T(8,128)(2,1)}) fusion(bf16[1,128,4096]{2,1,0:T(8,128)(2,1)} %param.11, s32[]{:T(128)S(6)} %select_n.146, s32[]{:T(128)S(6)} %select_n.148, s32[]{:T(128)S(6)} %select_n.154, s32[]{:T(128)S(6)} %select_n.151), kind=kLoop, calls=%fused_computation.123 | loop fusion | bytes 786448 | tf_op jit(solution)/shard_map/dynamic_slice | solution.py:124
  18.0 1.8 collective-permute-start.7
  19.7 1.7 collective-permute-start.4
  27.4 9.6 %collective-permute-done.10 = bf16[64,1024]{1,0:T(8,128)(2,1)} collective-permute-done((bf16[64,1024]{1,0:T(8,128)(2,1)}, bf16[64,1024]{1,0:T(8,128)(2,1)}, u32[]{:S(2)}, u32[]{:S(2)}) %collective-permute-start.10) | collective-permute-done | bytes 131104 | tf_op jit(solution)/shard_map/ppermute | solution.py:123
  40.9 2.2 %convolution_convert_fusion = bf16[128,1024]{1,0:T(8,128)(2,1)} fusion(bf16[1024,1024]{1,0:T(8,128)(2,1)S(1)} %copy-done, bf16[64,1024]{1,0:T(8,128)(2,1)} %collective-permute-done.11, bf16[64,1024]{1,0:T(8,128)(2,1)} %collective-permute-done.10, pred[]{:T(512)S(6)} %eq.10), kind=kOutput, calls=%fused_computation.29 | convolution fusion | flops 269746176 | bytes 2621441 | tf_op jit(solution)/shard_map/dot_general | solution.py:132
  43.1 2.1 %convolution_convert_fusion.1 = bf16[128,1024]{1,0:T(8,128)(2,1)} fusion(bf16[1024,1024]{1,0:T(8,128)(2,1)S(1)} %copy-done, bf16[64,1024]{1,0:T(8,128)(2,1)S(1)} %collective-permute-done.8, bf16[64,1024]{1,0:T(8,128)(2,1)} %collective-permute-done.7, pred[]{:T(512)S(6)} %eq.10), kind=kOutput, calls=%fused_computation.30 | convolution fusion | flops 269746176 | bytes 2621441 | tf_op jit(solution)/shard_map/dot_general | solution.py:132
  47.5 4.3 %collective-permute-start.9 = (bf16[128,1024]{1,0:T(8,128)(2,1)}, bf16[128,1024]{1,0:T(8,128)(2,1)}, u32[]{:S(2)}, u32[]{:S(2)}) collective-permute-start(bf16[128,1024]{1,0:T(8,128)(2,1)} %convolution_convert_fusion.1), channel_id=1, source_target_pairs={{0,8},{4,12},{8,0},{12,4},{1,9},{5,13},{9,1},{13,5},{2,10},{6,14},... | collective-permute-start | bytes 786440 | tf_op jit(solution)/shard_map/ppermute | solution.py:133
  52.9 2.8 %gather_fusion = bf16[4,128,1024]{2,1,0:T(8,128)(2,1)} fusion(bf16[4,128,1024]{2,1,0:T(8,128)(2,1)} %pad_maximum_fusion.2, s32[1024]{0:T(1024)S(1)} %pad_clamp_fusion), kind=kCustom, calls=%fused_computation | custom fusion | bytes 2097168 | tf_op jit(solution)/shard_map/jit(_take)/gather | solution.py:138
  55.7 2.2 %convolution_convert_fusion.2 = bf16[128,1024]{1,0:T(8,128)(2,1)} fusion(bf16[1024,1024]{1,0:T(8,128)(2,1)S(1)} %copy-done, bf16[64,1024]{1,0:T(8,128)(2,1)} %copy-done.28, bf16[64,1024]{1,0:T(8,128)(2,1)S(1)} %collective-permute-done.4, pred[]{:T(512)S(6)} %eq.10), kind=kOutput, calls=%fused_computation.31 | convolution fusion | flops 269746176 | bytes 2621441 | tf_op jit(solution)/shard_map/dot_general | solution.py:132
  61.1 1.8 %gather_fusion.1 = bf16[6,2,64,1024]{3,2,1,0:T(8,128)(2,1)} fusion(bf16[1,2,6,64,1024]{4,3,2,1,0:T(8,128)(2,1)S(1)} %bitcast.237, s32[6]{0:T(128)S(1)} %reshape.748), kind=kCustom, calls=%fused_computation.1 | custom fusion | bytes 3145776 | tf_op jit(solution)/shard_map/vmap()/gather | solution.py:41
  62.9 1.6 copy.197
  70.2 1.5 collective-permute-done.6
  75.6 5.2 %collective-permute-done.3 = bf16[2,1,64,1024]{3,2,1,0:T(8,128)(2,1)S(1)} collective-permute-done((bf16[2,1,64,1024]{3,2,1,0:T(8,128)(2,1)S(1)}, bf16[2,1,64,1024]{3,2,1,0:T(8,128)(2,1)S(1)}, u32[]{:S(2)}, u32[]{:S(2)}) %collective-permute-start.3) | collective-permute-done | bytes 262176 | tf_op jit(solution)/shard_map/ppermute | solution.py:30
  82.4 2.5 %convolution_bitcast_fusion.2 = f32[1,2,64,8,128]{4,2,3,1,0:T(8,128)} fusion(bf16[2,192,8,128]{3,2,1,0:T(8,128)(2,1)} %bitcast.267, f32[2,8,64,192]{3,2,1,0:T(8,128)S(1)} %get-tuple-element.25, f32[2,8,64]{2,1,0:T(8,128)S(1)} %copy_add_fusion.1, f32[2,8,64]{2,1,0:T(8,128)S(1)} %copy_maximum_fusion), kind=kOutput, calls=%fused_computation.18 | convolution fusion | flops 50921472 | bytes 2105344 | tf_op jit(solution)/shard_map/dbhqk,dbkhe->dbqhe/dot_general | solution.py:103
  84.9 1.6 multiply_reduce_fusion
  86.5 2.1 %convolution_bitcast_fusion = f32[1,2,192,8,128]{4,2,3,1,0:T(8,128)} fusion(bf16[2,64,8,128]{3,2,1,0:T(8,128)(2,1)S(1)} %bitcast.262, f32[2,8,64,192]{3,2,1,0:T(8,128)S(1)} %get-tuple-element.25, f32[2,8,64]{2,1,0:T(8,128)S(1)} %copy_add_fusion.1, f32[2,8,64]{2,1,0:T(8,128)S(1)} %copy_maximum_fusion), kind=kOutput, calls=%fused_computation.14 | convolution fusion | flops 50921472 | bytes 2629632 | tf_op jit(solution)/shard_map/dbhqk,dbqhe->dbkhe/dot_general | solution.py:177
  95.1 3.4 %collective-permute-start.15 = (bf16[2,1,64,1024]{3,0,2,1:T(2,128)(2,1)}, bf16[2,1,64,1024]{3,0,2,1:T(2,128)(2,1)}, u32[]{:S(2)}, u32[]{:S(2)}) collective-permute-start(bf16[2,1,64,1024]{3,0,2,1:T(2,128)(2,1)} %fusion.58), channel_id=1, source_target_pairs={{0,8},{4,12},{8,0},{12,4},{1,9},{5,13},{9,1},{13,5},{2,10},{6,14},... | collective-permute-start | bytes 786440 | tf_op jit(solution)/shard_map/ppermute | solution.py:30
  101.6 3.1 %pad_maximum_fusion = f32[1,2,2,3,64,1024]{5,0,4,3,2,1:T(1,128)S(1)} fusion(f32[1,1,2,3,64,1024]{5,0,4,3,2,1:T(1,128)S(1)} %bitcast.239, f32[1,1,2,3,64,1024]{5,0,4,3,2,1:T(1,128)S(1)} %bitcast.240), kind=kLoop, calls=%fused_computation.3 | loop fusion | flops 786432 | bytes 6291456 | tf_op jit(solution)/shard_map/stack | solution.py:187
  104.6 2.4 %copy.260 = f32[1,2,2,3,64,1024]{5,4,1,3,2,0:T(8,128)} copy(f32[1,2,2,3,64,1024]{5,0,4,3,2,1:T(1,128)S(1)} %pad_maximum_fusion) | data formatting | bytes 6291456 | tf_op jit(solution)/shard_map/stack | solution.py:187
  107.4 5.4 %scatter_fusion = f32[2,6,64,1024]{3,2,1,0:T(8,128)S(1)} fusion(f32[2,6,64,1024]{3,2,1,0:T(8,128)S(1)} %broadcast.224, s32[6]{0:T(128)S(1)} %reshape.760, f32[6,2,64,1024]{3,2,1,0:T(8,128)} %bitcast.226), kind=kCustom, calls=%fused_computation.2 | custom fusion | flops 786432 | bytes 9437208 | tf_op jit(solution)/shard_map/vmap()/scatter-add | solution.py:46
  114.2 4.0 %collective-permute-start.14 = (bf16[2,1,128,1024]{3,2,1,0:T(8,128)(2,1)}, bf16[2,1,128,1024]{3,2,1,0:T(8,128)(2,1)}, u32[]{:S(2)}, u32[]{:S(2)}) collective-permute-start(bf16[2,1,128,1024]{3,2,1,0:T(8,128)(2,1)} %get-tuple-element.12), channel_id=1, source_target_pairs={{4,0},{8,4},{12,8},{5,1},{9,5},{13,9},{6,2},{10,6},{14,10},{7,3},{... | collective-permute-start | bytes 1572872 | tf_op jit(solution)/shard_map/ppermute | solution.py:22
  118.2 2.9 %collective-permute-start.13 = (bf16[2,1,128,1024]{3,2,1,0:T(8,128)(2,1)}, bf16[2,1,128,1024]{3,2,1,0:T(8,128)(2,1)}, u32[]{:S(2)}, u32[]{:S(2)}) collective-permute-start(bf16[2,1,128,1024]{3,2,1,0:T(8,128)(2,1)} %get-tuple-element.11), channel_id=1, source_target_pairs={{0,4},{4,8},{8,12},{1,5},{5,9},{9,13},{2,6},{6,10},{10,14},{3,7},{... | collective-permute-start | bytes 1572872 | tf_op jit(solution)/shard_map/ppermute | solution.py:20
  126.3 1.8 convert_element_type.170
  129.2 12.1 %all-gather.2.cloned.1.call-done = bf16[512,1024]{1,0:T(8,128)(2,1)} async-done(((bf16[128,1024]{1,0:T(8,128)(2,1)}), bf16[512,1024]{1,0:T(8,128)(2,1)}) %all-gather.2.cloned.1.call-update) | async-done | bytes 1048592 | tf_op jit(solution)/shard_map/all_gather | solution.py:141
  143.7 2.7 %collective-permute-done.16 = bf16[2,1,64,1024]{3,0,2,1:T(2,128)(2,1)} collective-permute-done((bf16[2,1,64,1024]{3,0,2,1:T(2,128)(2,1)}, bf16[2,1,64,1024]{3,0,2,1:T(2,128)(2,1)}, u32[]{:S(2)}, u32[]{:S(2)}) %collective-permute-start.16) | collective-permute-done | bytes 262176 | tf_op jit(solution)/shard_map/ppermute | solution.py:30
  148.4 1.7 mul.193
  150.1 1.9 %fusion.17 = bf16[2,1,128,1024]{3,2,1,0:T(8,128)(2,1)S(1)} fusion(f32[2,1,128,1024]{3,2,1,0:T(8,128)} %mul.193, f32[2,1,128,1024]{3,2,1,0:T(8,128)S(1)} %bitcast.248, bf16[2,1,128,1024]{3,2,1,0:T(8,128)(2,1)} %collective-permute-done.14, bf16[2,1,256,1024]{3,2,1,0:T(8,128)(2,1)S(1)} %bitcast.230, bf16[2,1,128,1024]{3,2,1,0:T(8,128)(2,1)} %collective-permute-done.13), kind=kLoop, calls=%fused_computation.36 | loop fusion | flops 4194304 | bytes 4718592 | tf_op jit(solution)/shard_map/convert.1
  152.9 13.2 %collective-permute-done.18 = bf16[512,1024]{1,0:T(8,128)(2,1)} collective-permute-done((bf16[512,1024]{1,0:T(8,128)(2,1)}, bf16[512,1024]{1,0:T(8,128)(2,1)}, u32[]{:S(2)}, u32[]{:S(2)}) %collective-permute-start.18) | collective-permute-done | bytes 1048608 | tf_op jit(solution)/shard_map/ppermute | solution.py:30
  166.1 6.4 %fusion = f32[1024,1024]{1,0:T(8,128)} fusion(bf16[512,1024]{1,0:T(8,128)(2,1)} %collective-permute-done.17, bf16[512,1024]{1,0:T(8,128)(2,1)} %bitcast_select_fusion, bf16[512,1024]{1,0:T(8,128)(2,1)} %collective-permute-done.18, bf16[512,1024]{1,0:T(8,128)(2,1)S(1)} %copy-done.30), kind=kOutput, calls=%fused_computation.5 | convolution fusion | flops 2155872256 | bytes 8388608 | tf_op jit(solution)/shard_map/tc,tw->cw/dot_general | solution.py:149
  (170 shorter events, 49.8 us)
Async XLA Ops:
  7.2 19.0 %copy-start = (bf16[1024,1024]{1,0:T(8,128)(2,1)S(1)}, bf16[1024,1024]{1,0:T(8,128)(2,1)}, u32[]{:S(2)}) copy-start(bf16[1024,1024]{1,0:T(8,128)(2,1)} %param.10) | copy-start | bytes 6291460
  7.2 15.3 %copy-start.17 = (bf16[1,128,1024]{2,1,0:T(8,128)(2,1)S(1)}, bf16[1,128,1024]{2,1,0:T(8,128)(2,1)}, u32[]{:S(2)}) copy-start(bf16[1,128,1024]{2,1,0:T(8,128)(2,1)} %param.7) | copy-start | bytes 786436
  7.2 15.5 %copy-start.29 = (s32[1,2,2]{2,1,0:T(2,128)S(1)}, s32[1,2,2]{2,1,0:T(2,128)}, u32[]{:S(2)}) copy-start(s32[1,2,2]{2,1,0:T(2,128)} %param.9) | copy-start | bytes 52
  7.2 134.1 %all-gather.2.cloned.1.call-start = ((), (), s32[]{:S(2)}) async-start(), calls=%async_computation | async-start | bytes 1310720 | tf_op jit(solution)/shard_map/all_gather | solution.py:141
  9.3 49.9 %collective-permute-start.1 = (bf16[2,1,128,1024]{3,2,1,0:T(8,128)(2,1)}, bf16[2,1,128,1024]{3,2,1,0:T(8,128)(2,1)}, u32[]{:S(2)}, u32[]{:S(2)}) collective-permute-start(bf16[2,1,128,1024]{3,2,1,0:T(8,128)(2,1)} %pad_maximum_fusion.6), channel_id=1, source_target_pairs={{4,0},{8,4},{12,8},{5,1},{9,5},{13,9},{6,2},{10,6},{14,10},{7,3},{... | collective-permute-start | bytes 1572872 | tf_op jit(solution)/shard_map/ppermute | solution.py:22
  11.6 47.5 %collective-permute-start = (bf16[2,1,128,1024]{3,2,1,0:T(8,128)(2,1)}, bf16[2,1,128,1024]{3,2,1,0:T(8,128)(2,1)}, u32[]{:S(2)}, u32[]{:S(2)}) collective-permute-start(bf16[2,1,128,1024]{3,2,1,0:T(8,128)(2,1)} %pad_maximum_fusion.6), channel_id=1, source_target_pairs={{0,4},{4,8},{8,12},{1,5},{5,9},{9,13},{2,6},{6,10},{10,14},{3,7},{... | collective-permute-start | bytes 1572872 | tf_op jit(solution)/shard_map/ppermute | solution.py:20
  18.0 19.1 %collective-permute-start.10 = (bf16[64,1024]{1,0:T(8,128)(2,1)}, bf16[64,1024]{1,0:T(8,128)(2,1)}, u32[]{:S(2)}, u32[]{:S(2)}) collective-permute-start(bf16[64,1024]{1,0:T(8,128)(2,1)} %get-tuple-element.14), channel_id=1, source_target_pairs={{0,12},{4,8},{8,4},{12,0},{1,13},{5,9},{9,5},{13,1},{2,14},{6,10},... | collective-permute-start | bytes 393224 | tf_op jit(solution)/shard_map/ppermute | solution.py:123
  18.0 22.2 %collective-permute-start.7 = (bf16[64,1024]{1,0:T(8,128)(2,1)}, bf16[64,1024]{1,0:T(8,128)(2,1)}, u32[]{:S(2)}, u32[]{:S(2)}) collective-permute-start(bf16[64,1024]{1,0:T(8,128)(2,1)} %get-tuple-element.15), channel_id=1, source_target_pairs={{0,8},{4,12},{8,0},{12,4},{1,9},{5,13},{9,1},{13,5},{2,10},{6,14},... | collective-permute-start | bytes 393224 | tf_op jit(solution)/shard_map/ppermute | solution.py:123
  19.7 20.5 %collective-permute-start.4 = (bf16[64,1024]{1,0:T(8,128)(2,1)}, bf16[64,1024]{1,0:T(8,128)(2,1)S(1)}, u32[]{:S(2)}, u32[]{:S(2)}) collective-permute-start(bf16[64,1024]{1,0:T(8,128)(2,1)} %get-tuple-element.13), channel_id=1, source_target_pairs={{0,4},{4,0},{8,12},{12,8},{1,5},{5,1},{9,13},{13,9},{2,6},{6,2},{1... | collective-permute-start | bytes 393224 | tf_op jit(solution)/shard_map/ppermute | solution.py:123
  37.1 3.7 %collective-permute-start.11 = (bf16[64,1024]{1,0:T(8,128)(2,1)}, bf16[64,1024]{1,0:T(8,128)(2,1)}, u32[]{:S(2)}, u32[]{:S(2)}) collective-permute-start(bf16[64,1024]{1,0:T(8,128)(2,1)} %collective-permute-done.10), channel_id=1, source_target_pairs={{0,1},{1,0},{2,3},{3,2},{4,5},{5,4},{6,7},{7,6},{8,9},{9,8},{10,11... | collective-permute-start | bytes 393224 | tf_op jit(solution)/shard_map/ppermute | solution.py:30
  40.2 24.5 %collective-permute-start.2 = (f32[2,1,64,1024]{3,2,1,0:T(8,128)}, f32[2,1,64,1024]{3,2,1,0:T(8,128)}, u32[]{:S(2)}, u32[]{:S(2)}) collective-permute-start(f32[2,1,64,1024]{3,2,1,0:T(8,128)} %get-tuple-element.23), channel_id=1, source_target_pairs={{0,4},{4,0},{8,12},{12,8},{1,5},{5,1},{9,13},{13,9},{2,6},{6,2},{1... | collective-permute-start | bytes 1572872 | tf_op jit(solution)/shard_map/ppermute | solution.py:30
  40.2 2.9 %collective-permute-start.8 = (bf16[64,1024]{1,0:T(8,128)(2,1)}, bf16[64,1024]{1,0:T(8,128)(2,1)S(1)}, u32[]{:S(2)}, u32[]{:S(2)}) collective-permute-start(bf16[64,1024]{1,0:T(8,128)(2,1)} %collective-permute-done.7), channel_id=1, source_target_pairs={{0,1},{1,0},{2,3},{3,2},{4,5},{5,4},{6,7},{7,6},{8,9},{9,8},{10,11... | collective-permute-start | bytes 393224 | tf_op jit(solution)/shard_map/ppermute | solution.py:30
  40.8 6.7 %collective-permute-start.5 = (bf16[64,1024]{1,0:T(8,128)(2,1)S(1)}, bf16[64,1024]{1,0:T(8,128)(2,1)S(1)}, u32[]{:S(2)}, u32[]{:S(2)}) collective-permute-start(bf16[64,1024]{1,0:T(8,128)(2,1)S(1)} %collective-permute-done.4), channel_id=1, source_target_pairs={{0,1},{1,0},{2,3},{3,2},{4,5},{5,4},{6,7},{7,6},{8,9},{9,8},{10,11... | collective-permute-start | bytes 393224 | tf_op jit(solution)/shard_map/ppermute | solution.py:30
  43.1 27.1 %collective-permute-start.12 = (bf16[128,1024]{1,0:T(8,128)(2,1)}, bf16[128,1024]{1,0:T(8,128)(2,1)}, u32[]{:S(2)}, u32[]{:S(2)}) collective-permute-start(bf16[128,1024]{1,0:T(8,128)(2,1)} %convolution_convert_fusion), channel_id=1, source_target_pairs={{0,12},{4,8},{8,4},{12,0},{1,13},{5,9},{9,5},{13,1},{2,14},{6,10},... | collective-permute-start | bytes 786440 | tf_op jit(solution)/shard_map/ppermute | solution.py:133
  47.5 22.7 %collective-permute-start.9 = (bf16[128,1024]{1,0:T(8,128)(2,1)}, bf16[128,1024]{1,0:T(8,128)(2,1)}, u32[]{:S(2)}, u32[]{:S(2)}) collective-permute-start(bf16[128,1024]{1,0:T(8,128)(2,1)} %convolution_convert_fusion.1), channel_id=1, source_target_pairs={{0,8},{4,12},{8,0},{12,4},{1,9},{5,13},{9,1},{13,5},{2,10},{6,14},... | collective-permute-start | bytes 786440 | tf_op jit(solution)/shard_map/ppermute | solution.py:133
  59.2 12.5 %collective-permute-start.6 = (bf16[128,1024]{1,0:T(8,128)(2,1)}, bf16[128,1024]{1,0:T(8,128)(2,1)}, u32[]{:S(2)}, u32[]{:S(2)}) collective-permute-start(bf16[128,1024]{1,0:T(8,128)(2,1)} %convolution_convert_fusion.2), channel_id=1, source_target_pairs={{0,4},{4,0},{8,12},{12,8},{1,5},{5,1},{9,13},{13,9},{2,6},{6,2},{1... | collective-permute-start | bytes 786440 | tf_op jit(solution)/shard_map/ppermute | solution.py:133
  59.2 93.7 %collective-permute-start.17 = (bf16[512,1024]{1,0:T(8,128)(2,1)}, bf16[512,1024]{1,0:T(8,128)(2,1)}, u32[]{:S(2)}, u32[]{:S(2)}) collective-permute-start(bf16[512,1024]{1,0:T(8,128)(2,1)} %bitcast_select_fusion), channel_id=1, source_target_pairs={{0,2},{2,0},{1,3},{3,1},{4,6},{6,4},{5,7},{7,5},{8,10},{10,8},{9,1... | collective-permute-start | bytes 3145736 | tf_op jit(solution)/shard_map/ppermute | solution.py:30
  67.2 7.7 %copy-start.6 = (bf16[48,8,8,128]{3,2,1,0:T(8,128)(2,1)}, bf16[48,8,8,128]{3,2,1,0:T(8,128)(2,1)S(1)}, u32[]{:S(2)}) copy-start(bf16[48,8,8,128]{3,2,1,0:T(8,128)(2,1)S(1)} %copy.261) | copy-start | bytes 2359300
  69.2 11.6 %collective-permute-start.3 = (bf16[2,1,64,1024]{3,2,1,0:T(8,128)(2,1)S(1)}, bf16[2,1,64,1024]{3,2,1,0:T(8,128)(2,1)S(1)}, u32[]{:S(2)}, u32[]{:S(2)}) collective-permute-start(bf16[2,1,64,1024]{3,2,1,0:T(8,128)(2,1)S(1)} %fusion.30), channel_id=1, source_target_pairs={{0,8},{4,12},{8,0},{12,4},{1,9},{5,13},{9,1},{13,5},{2,10},{6,14},... | collective-permute-start | bytes 786440 | tf_op jit(solution)/shard_map/ppermute | solution.py:30
  73.8 7.3 %copy-start.24 = (bf16[2,64,8,128]{3,1,0,2:T(8,128)(2,1)S(1)}, bf16[2,64,8,128]{3,1,0,2:T(8,128)(2,1)}, u32[]{:S(2)}) copy-start(bf16[2,64,8,128]{3,1,0,2:T(8,128)(2,1)} %copy.208) | copy-start | bytes 786436
  93.0 6.4 %copy-start.8 = (bf16[2,8,64,192]{3,2,1,0:T(8,128)(2,1)}, bf16[2,8,64,192]{3,2,1,0:T(8,128)(2,1)S(1)}, u32[]{:S(2)}) copy-start(bf16[2,8,64,192]{3,2,1,0:T(8,128)(2,1)S(1)} %multiply_convert_fusion) | copy-start | bytes 1179652
  95.1 26.0 %collective-permute-start.15 = (bf16[2,1,64,1024]{3,0,2,1:T(2,128)(2,1)}, bf16[2,1,64,1024]{3,0,2,1:T(2,128)(2,1)}, u32[]{:S(2)}, u32[]{:S(2)}) collective-permute-start(bf16[2,1,64,1024]{3,0,2,1:T(2,128)(2,1)} %fusion.58), channel_id=1, source_target_pairs={{0,8},{4,12},{8,0},{12,4},{1,9},{5,13},{9,1},{13,5},{2,10},{6,14},... | collective-permute-start | bytes 786440 | tf_op jit(solution)/shard_map/ppermute | solution.py:30
  113.1 8.0 %copy-start.4 = (bf16[2,1,4,64,1024]{4,3,2,0,1:T(8,128)(2,1)}, bf16[2,1,4,64,1024]{4,3,2,0,1:T(8,128)(2,1)S(1)}, u32[]{:S(2)}) copy-start(bf16[2,1,4,64,1024]{4,3,2,0,1:T(8,128)(2,1)S(1)} %maximum_convert_fusion) | copy-start | bytes 3145732
  113.1 10.5 %copy-start.11 = (f32[1,128,8,128]{3,2,0,1:T(8,128)S(1)}, f32[1,128,8,128]{3,2,0,1:T(8,128)}, u32[]{:S(2)}) copy-start(f32[1,128,8,128]{3,2,0,1:T(8,128)} %copy-done.10) | copy-start | bytes 1572868
  113.1 10.5 %copy-start.13 = (f32[1,128,8,128]{3,2,0,1:T(8,128)S(1)}, f32[1,128,8,128]{3,2,0,1:T(8,128)}, u32[]{:S(2)}) copy-start(f32[1,128,8,128]{3,2,0,1:T(8,128)} %copy-done.12) | copy-start | bytes 1572868
  114.2 35.9 %collective-permute-start.14 = (bf16[2,1,128,1024]{3,2,1,0:T(8,128)(2,1)}, bf16[2,1,128,1024]{3,2,1,0:T(8,128)(2,1)}, u32[]{:S(2)}, u32[]{:S(2)}) collective-permute-start(bf16[2,1,128,1024]{3,2,1,0:T(8,128)(2,1)} %get-tuple-element.12), channel_id=1, source_target_pairs={{4,0},{8,4},{12,8},{5,1},{9,5},{13,9},{6,2},{10,6},{14,10},{7,3},{... | collective-permute-start | bytes 1572872 | tf_op jit(solution)/shard_map/ppermute | solution.py:22
  118.2 31.9 %collective-permute-start.13 = (bf16[2,1,128,1024]{3,2,1,0:T(8,128)(2,1)}, bf16[2,1,128,1024]{3,2,1,0:T(8,128)(2,1)}, u32[]{:S(2)}, u32[]{:S(2)}) collective-permute-start(bf16[2,1,128,1024]{3,2,1,0:T(8,128)(2,1)} %get-tuple-element.11), channel_id=1, source_target_pairs={{0,4},{4,8},{8,12},{1,5},{5,9},{9,13},{2,6},{6,10},{10,14},{3,7},{... | collective-permute-start | bytes 1572872 | tf_op jit(solution)/shard_map/ppermute | solution.py:20
  125.0 21.4 %collective-permute-start.16 = (bf16[2,1,64,1024]{3,0,2,1:T(2,128)(2,1)}, bf16[2,1,64,1024]{3,0,2,1:T(2,128)(2,1)}, u32[]{:S(2)}, u32[]{:S(2)}) collective-permute-start(bf16[2,1,64,1024]{3,0,2,1:T(2,128)(2,1)} %fusion.31), channel_id=1, source_target_pairs={{0,4},{4,0},{8,12},{12,8},{1,5},{5,1},{9,13},{13,9},{2,6},{6,2},{1... | collective-permute-start | bytes 786440 | tf_op jit(solution)/shard_map/ppermute | solution.py:30
  129.2 17.3 %copy-start.3 = (f32[2,64,2,1024]{3,0,2,1:T(2,128)S(1)}, f32[2,64,2,1024]{3,0,2,1:T(2,128)}, u32[]{:S(2)}) copy-start(f32[2,64,2,1024]{3,0,2,1:T(2,128)} %copy-done.2) | copy-start | bytes 3145732
  141.3 24.8 %collective-permute-start.18 = (bf16[512,1024]{1,0:T(8,128)(2,1)}, bf16[512,1024]{1,0:T(8,128)(2,1)}, u32[]{:S(2)}, u32[]{:S(2)}) collective-permute-start(bf16[512,1024]{1,0:T(8,128)(2,1)} %all-gather.2.cloned.1.call-done), channel_id=1, source_target_pairs={{0,2},{2,0},{1,3},{3,1},{4,6},{6,4},{5,7},{7,5},{8,10},{10,8},{9,1... | collective-permute-start | bytes 3145736 | tf_op jit(solution)/shard_map/ppermute | solution.py:30
  150.1 16.0 %copy-start.30 = (bf16[512,1024]{1,0:T(8,128)(2,1)S(1)}, bf16[512,1024]{1,0:T(8,128)(2,1)}, u32[]{:S(2)}) copy-start(bf16[512,1024]{1,0:T(8,128)(2,1)} %all-gather.2.cloned.1.call-done) | copy-start | bytes 3145732
  166.1 6.4 %copy-start.1 = (bf16[1024,1024]{1,0:T(8,128)(2,1)S(1)}, bf16[1024,1024]{1,0:T(8,128)(2,1)}, u32[]{:S(2)}) copy-start(bf16[1024,1024]{1,0:T(8,128)(2,1)} %param.10) | copy-start | bytes 6291460
  (19 other events, 49.8 us)
Sparse Core Ops, SparseCore 0:
  101.7 39.5 all-gather.1

commit v8 on v4

--- a/solution.py
+++ b/solution.py
@@ -69,7 +69,8 @@
         pieces.append(level_rows.astype(jnp.bfloat16))
     feat_count = cotangent.shape[2] // seq_count
     cot_rows = cotangent.reshape(doc_count * tok_count, cotangent.shape[2])
-    cot_height = doc_count * tok_count
+    core = lax.axis_index("head")
+    half = cot_rows.shape[0] // 2
     far_parts = []
     got_list = []
     for step in range(1, seq_count):
@@ -78,15 +79,23 @@
         sent = lax.dynamic_slice_in_dim(
             cot_rows, (position ^ step) * feat_count, feat_count, axis=1
         )
+        sent_half = lax.dynamic_slice_in_dim(sent, core * half, half, axis=0)
         if feat_count == head_cols:
-            payload = jnp.concatenate([sent, piece.reshape(-1, head_cols)], axis=0)
+            payload = jnp.concatenate([sent_half, piece.reshape(-1, head_cols)], axis=0)
             arrived = lax.ppermute(payload, "seq", pairs)
-            got = arrived[:cot_height]
-            far_parts.append(arrived[cot_height:].reshape(piece.shape))
+            got_half = arrived[:half]
+            far_parts.append(arrived[half:].reshape(piece.shape))
         else:
-            got = lax.ppermute(sent, "seq", pairs)
+            got_half = lax.ppermute(sent_half, "seq", pairs)
             far_parts.append(lax.ppermute(piece, "seq", pairs))
-        got_list.append(got)
+        other_half = swapped(got_half, "head", 0)
+        got_list.append(
+            jnp.where(
+                core == 0,
+                jnp.concatenate([got_half, other_half], axis=0),
+                jnp.concatenate([other_half, got_half], axis=0),
+            )
+        )
     far_levels = []
     for level_no in range(levels):
         count = 1 << level_no
@@ -131,7 +140,6 @@
     own_cols = lax.dynamic_slice_in_dim(cot_rows, position * feat_count, feat_count, axis=1)
     grad_sum = jnp.dot(own_cols, out_weight, preferred_element_type=jnp.float32)
     feat_list = [own_cols]
-    out_list = [out_rows]
     for step in range(1, seq_count):
         pairs = [(i, i ^ step) for i in range(seq_count)]
         got = got_list[step - 1]
@@ -139,10 +147,12 @@
         back = lax.ppermute(part.astype(jnp.bfloat16), "seq", pairs)
         grad_sum = grad_sum + back.astype(jnp.float32)
         feat_list.append(got)
-        out_list.append(lax.ppermute(out_rows, "seq", pairs))
     attn_grad = grad_sum.astype(jnp.bfloat16)
-    feat_docs = jnp.concatenate(feat_list, axis=0)
-    whole_output = jnp.concatenate(out_list, axis=0)
+    feat_order = jnp.arange(seq_count, dtype=jnp.int32) ^ position
+    feat_docs = jnp.take(jnp.stack(feat_list, axis=0), feat_order, axis=0).reshape(
+        seq_count * cot_rows.shape[0], feat_count
+    )
+    whole_output = lax.all_gather(out_rows, "seq", axis=0, tiled=True)
     dp_count = lax.axis_size("dp")
     if dp_count == 2:
         feat_docs = jnp.concatenate([feat_docs, swapped(feat_docs, "dp", 0)], axis=0)
@@ -201,9 +211,8 @@
     token_grad = back_six[:, :, 2:4].reshape(2, doc_count, tok_count, head_cols)
     token_grad = token_grad + beside_all[:, :, :tok_count] + beside_all[:, :, 3 * tok_count :]
     far_rows = jnp.stack([far_key_rows, far_value_rows]).reshape(
-        2, doc_count, levels * block, head_cols
-    )
-    far_rows = far_rows.reshape(2, doc_count, levels, block, head_cols)
+        2, doc_count, levels, block, head_cols
+    )
     carried = jnp.zeros((2, doc_count, block, head_cols), jnp.float32)
     for level_no in reversed(range(levels)):
         message = far_rows[:, :, level_no]

time: 195 us -> 182 us (0.933)
  the two profiles are of different devices: /device:TPU:6 before, /device:TPU:16 now
where the time goes in v8:
time: 182 us; the launch traced here: 181 us
  local copies, waits for them, and re-layouts  40.8 us (22%)
  waiting for transfers between devices  39.6 us (22%)
  other arithmetic  36.6 us (20%)
  starting transfers between devices  26.1 us (14%)
  matrix products  23.1 us (13%)
  between operations  15 us (8%)
    ppermute x7, waiting for transfers between devices, swapped(): lax.ppermute(shard, axis, [(i, i ^ 1 << stride) for i in range(lax.axis_s...  14.5 us
    ppermute x3, waiting for transfers between devices, shards(): arrived = lax.ppermute(payload, 'seq', pairs)  13.4 us
    all_gather x1, waiting for transfers between devices, shards(): whole_output = lax.all_gather(out_rows, 'seq', axis=0, tiled=True)  10.5 us
    ppermute x2, starting transfers between devices, extended(): lax.ppermute(head, axis, [((i + 1) % count, i) for i in range(ends)])  6.77 us
    ppermute x2, starting transfers between devices, extended(): lax.ppermute(tail, axis, [(i, (i + 1) % count) for i in range(ends)])  6.45 us
    dot_general x1, matrix products, shards(): jnp.einsum('tc,tw->cw', feat_docs, whole_output, preferred_element_type=j...  6.41 us
    ppermute x3, starting transfers between devices, shards(): back = lax.ppermute(part.astype(jnp.bfloat16), 'seq', pairs)  5.83 us
    scatter-add x1, other arithmetic, place_blocks(): return holder.at[:, chosen_doc].add(grad_doc)  5.69 us
  transfers between devices with their start and end apart: 18, of which 5 were waited for; matrix products, arithmetic and copies ran while one was open for 50% of the time, Pallas kernels for 0%

profile of v8, /device:TPU:16, one launch (start us, length us, event | category | flops | bytes accessed | tf_op | source)
XLA Modules:
  0.0 181.1 jit_solution(8363724886264079672)
XLA Ops:
  7.2 2.0 %pad_maximum_fusion.6 = bf16[2,1,128,1024]{3,2,1,0:T(8,128)(2,1)} fusion(bf16[1,1,128,1024]{3,2,1,0:T(8,128)(2,1)} %bitcast.257, bf16[1,1,128,1024]{3,2,1,0:T(8,128)(2,1)} %bitcast.259), kind=kLoop, calls=%fused_computation.60 | loop fusion | flops 262144 | bytes 1048576 | tf_op jit(solution)/shard_map/stack | solution.py:58
  9.2 2.3 %collective-permute-start.1 = (bf16[2,1,128,1024]{3,2,1,0:T(8,128)(2,1)}, bf16[2,1,128,1024]{3,2,1,0:T(8,128)(2,1)}, u32[]{:S(2)}, u32[]{:S(2)}) collective-permute-start(bf16[2,1,128,1024]{3,2,1,0:T(8,128)(2,1)} %pad_maximum_fusion.6), channel_id=1, source_target_pairs={{4,0},{8,4},{12,8},{5,1},{9,5},{13,9},{6,2},{10,6},{14,10},{7,3},{... | collective-permute-start | bytes 1572872 | tf_op jit(solution)/shard_map/ppermute | solution.py:22
  11.6 4.3 %collective-permute-start = (bf16[2,1,128,1024]{3,2,1,0:T(8,128)(2,1)}, bf16[2,1,128,1024]{3,2,1,0:T(8,128)(2,1)}, u32[]{:S(2)}, u32[]{:S(2)}) collective-permute-start(bf16[2,1,128,1024]{3,2,1,0:T(8,128)(2,1)} %pad_maximum_fusion.6), channel_id=1, source_target_pairs={{0,4},{4,8},{8,12},{1,5},{5,9},{9,13},{2,6},{6,10},{10,14},{3,7},{... | collective-permute-start | bytes 1572872 | tf_op jit(solution)/shard_map/ppermute | solution.py:20
  22.6 1.7 collective-permute-start.3
  25.1 1.7 collective-permute-start.2
  32.1 13.4 %collective-permute-done.4 = bf16[128,1024]{1,0:T(8,128)(2,1)} collective-permute-done((bf16[128,1024]{1,0:T(8,128)(2,1)S(1)}, bf16[128,1024]{1,0:T(8,128)(2,1)}, u32[]{:S(2)}, u32[]{:S(2)}) %collective-permute-start.4) | collective-permute-done | bytes 262176 | tf_op jit(solution)/shard_map/ppermute | solution.py:85
  45.5 1.7 slice_bitcast_fusion.2
  47.2 1.7 slice_bitcast_fusion.3
  50.2 2.2 %convolution_convert_fusion = bf16[128,1024]{1,0:T(8,128)(2,1)} fusion(bf16[1024,1024]{1,0:T(8,128)(2,1)S(1)} %copy-done, bf16[64,1024]{1,0:T(8,128)(2,1)} %collective-permute-done.9, bf16[64,1024]{1,0:T(8,128)(2,1)} %get-tuple-element.30, pred[]{:T(512)S(6)} %eq.8), kind=kOutput, calls=%fused_computation.30 | convolution fusion | flops 269746176 | bytes 2621441 | tf_op jit(solution)/shard_map/dot_general | solution.py:146
  52.4 1.5 collective-permute-start.10
  55.1 4.3 %collective-permute-start.8 = (bf16[128,1024]{1,0:T(8,128)(2,1)}, bf16[128,1024]{1,0:T(8,128)(2,1)}, u32[]{:S(2)}, u32[]{:S(2)}) collective-permute-start(bf16[128,1024]{1,0:T(8,128)(2,1)} %convolution_convert_fusion.1), channel_id=1, source_target_pairs={{0,8},{4,12},{8,0},{12,4},{1,9},{5,13},{9,1},{13,5},{2,10},{6,14},... | collective-permute-start | bytes 786440 | tf_op jit(solution)/shard_map/ppermute | solution.py:147
  59.4 1.7 maximum_select_fusion.8
  63.4 1.8 copy.149
  66.1 1.6 slice_bitcast_fusion.4
  69.8 2.5 %pad_maximum_fusion.1 = bf16[2,1,384,1024]{3,2,1,0:T(8,128)(2,1)} fusion(bf16[2,1,128,1024]{3,2,1,0:T(8,128)(2,1)} %collective-permute-done.1, bf16[1,1,128,1024]{3,2,1,0:T(8,128)(2,1)S(1)} %bitcast.258, bf16[1,1,128,1024]{3,2,1,0:T(8,128)(2,1)S(1)} %bitcast.260, bf16[2,1,128,1024]{3,2,1,0:T(8,128)(2,1)} %collective-permute-done), kind=kLoop, calls=%fused_computation.13 | loop fusion | flops 6291456 | bytes 3145728 | tf_op jit(solution)/shard_map/concatenate | solution.py:18
  72.2 3.3 %gather_fusion.2 = bf16[6,2,64,1024]{3,2,1,0:T(8,128)(2,1)} fusion(bf16[1,2,6,64,1024]{4,3,2,1,0:T(8,128)(2,1)} %bitcast.244, s32[6]{0:T(128)S(1)} %reshape.750), kind=kCustom, calls=%fused_computation.2 | custom fusion | bytes 3145776 | tf_op jit(solution)/shard_map/vmap()/gather | solution.py:41
  75.5 1.6 copy.145
  80.1 2.2 %convolution_convert_fusion.2 = bf16[128,1024]{1,0:T(8,128)(2,1)} fusion(bf16[1024,1024]{1,0:T(8,128)(2,1)S(1)} %copy-done, bf16[64,1024]{1,0:T(8,128)(2,1)} %collective-permute-done.5, bf16[64,1024]{1,0:T(8,128)(2,1)} %get-tuple-element.25, pred[]{:T(512)S(6)} %eq.8), kind=kOutput, calls=%fused_computation.32 | convolution fusion | flops 269746176 | bytes 2621441 | tf_op jit(solution)/shard_map/dot_general | solution.py:146
  84.6 2.0 %gather_fusion.1 = bf16[4,128,1024]{2,1,0:T(8,128)(2,1)S(1)} fusion(bf16[4,128,1024]{2,1,0:T(8,128)(2,1)} %pad_maximum_fusion.2, s32[1024]{0:T(1024)} %pad_clamp_fusion), kind=kCustom, calls=%fused_computation.1 | custom fusion | bytes 2097168 | tf_op jit(solution)/shard_map/jit(_take)/gather | solution.py:152
  93.6 2.1 %convolution_bitcast_fusion = f32[1,2,192,8,128]{4,2,3,1,0:T(8,128)} fusion(bf16[2,64,8,128]{3,2,1,0:T(8,128)(2,1)S(1)} %bitcast.268, f32[2,8,64,192]{3,2,1,0:T(8,128)S(1)} %copy-done.5, f32[2,8,64]{2,1,0:T(8,128)S(1)} %copy_add_fusion.1, f32[2,8,64]{2,1,0:T(8,128)S(1)} %copy_maximum_fusion), kind=kOutput, calls=%fused_computation.15 | convolution fusion | flops 50921472 | bytes 2629632 | tf_op jit(solution)/shard_map/dbhqk,dbqhe->dbkhe/dot_general | solution.py:191
  104.8 3.1 %pad_maximum_fusion = f32[1,2,2,3,64,1024]{5,0,4,3,2,1:T(1,128)S(1)} fusion(f32[1,1,2,3,64,1024]{5,0,4,3,2,1:T(1,128)S(1)} %bitcast.246, f32[1,1,2,3,64,1024]{5,0,4,3,2,1:T(1,128)S(1)} %bitcast.247), kind=kLoop, calls=%fused_computation.4 | loop fusion | flops 786432 | bytes 6291456 | tf_op jit(solution)/shard_map/stack | solution.py:201
  107.8 2.4 %copy.203 = f32[1,2,2,3,64,1024]{5,4,1,3,2,0:T(8,128)} copy(f32[1,2,2,3,64,1024]{5,0,4,3,2,1:T(1,128)S(1)} %pad_maximum_fusion) | data formatting | bytes 6291456 | tf_op jit(solution)/shard_map/stack | solution.py:201
  110.9 5.7 %scatter_fusion = f32[2,6,64,1024]{3,2,1,0:T(8,128)S(1)} fusion(f32[2,6,64,1024]{3,2,1,0:T(8,128)S(1)} %broadcast.270, s32[6]{0:T(128)S(1)} %copy-done.35, f32[6,2,64,1024]{3,2,1,0:T(8,128)} %bitcast.233), kind=kCustom, calls=%fused_computation.3 | custom fusion | flops 786432 | bytes 9437208 | tf_op jit(solution)/shard_map/vmap()/scatter-add | solution.py:46
  117.9 4.4 %collective-permute-start.12 = (bf16[2,1,128,1024]{3,2,1,0:T(8,128)(2,1)}, bf16[2,1,128,1024]{3,2,1,0:T(8,128)(2,1)}, u32[]{:S(2)}, u32[]{:S(2)}) collective-permute-start(bf16[2,1,128,1024]{3,2,1,0:T(8,128)(2,1)} %get-tuple-element.12), channel_id=1, source_target_pairs={{4,0},{8,4},{12,8},{5,1},{9,5},{13,9},{6,2},{10,6},{14,10},{7,3},{... | collective-permute-start | bytes 1572872 | tf_op jit(solution)/shard_map/ppermute | solution.py:22
  122.4 2.2 %collective-permute-start.11 = (bf16[2,1,128,1024]{3,2,1,0:T(8,128)(2,1)}, bf16[2,1,128,1024]{3,2,1,0:T(8,128)(2,1)}, u32[]{:S(2)}, u32[]{:S(2)}) collective-permute-start(bf16[2,1,128,1024]{3,2,1,0:T(8,128)(2,1)} %get-tuple-element.11), channel_id=1, source_target_pairs={{0,4},{4,8},{8,12},{1,5},{5,9},{9,13},{2,6},{6,10},{10,14},{3,7},{... | collective-permute-start | bytes 1572872 | tf_op jit(solution)/shard_map/ppermute | solution.py:20
  129.8 1.8 convert_element_type.183
  132.6 10.5 %all-gather.2.cloned.1.call-done = bf16[512,1024]{1,0:T(8,128)(2,1)} async-done(((bf16[128,1024]{1,0:T(8,128)(2,1)}), bf16[512,1024]{1,0:T(8,128)(2,1)}) %all-gather.2.cloned.1.call-update) | async-done | bytes 1048592 | tf_op jit(solution)/shard_map/all_gather | solution.py:155
  146.9 2.6 %collective-permute-done.14 = bf16[2,1,64,1024]{3,0,2,1:T(2,128)(2,1)} collective-permute-done((bf16[2,1,64,1024]{3,0,2,1:T(2,128)(2,1)}, bf16[2,1,64,1024]{3,0,2,1:T(2,128)(2,1)}, u32[]{:S(2)}, u32[]{:S(2)}) %collective-permute-start.14) | collective-permute-done | bytes 262176 | tf_op jit(solution)/shard_map/ppermute | solution.py:30
  151.5 1.7 mul.194
  153.3 1.9 %fusion.17 = bf16[2,1,128,1024]{3,2,1,0:T(8,128)(2,1)S(1)} fusion(f32[2,1,128,1024]{3,2,1,0:T(8,128)} %mul.194, f32[2,1,128,1024]{3,2,1,0:T(8,128)S(1)} %bitcast.254, bf16[2,1,128,1024]{3,2,1,0:T(8,128)(2,1)} %collective-permute-done.12, bf16[2,1,256,1024]{3,2,1,0:T(8,128)(2,1)S(1)} %bitcast.237, bf16[2,1,128,1024]{3,2,1,0:T(8,128)(2,1)} %collective-permute-done.11), kind=kLoop, calls=%fused_computation.37 | loop fusion | flops 4194304 | bytes 4718592 | tf_op jit(solution)/shard_map/convert.1
  156.0 11.9 %collective-permute-done.16 = bf16[512,1024]{1,0:T(8,128)(2,1)} collective-permute-done((bf16[512,1024]{1,0:T(8,128)(2,1)}, bf16[512,1024]{1,0:T(8,128)(2,1)}, u32[]{:S(2)}, u32[]{:S(2)}) %collective-permute-start.16) | collective-permute-done | bytes 1048608 | tf_op jit(solution)/shard_map/ppermute | solution.py:30
  167.9 6.4 %fusion = f32[1024,1024]{1,0:T(8,128)} fusion(bf16[512,1024]{1,0:T(8,128)(2,1)} %collective-permute-done.15, bf16[512,1024]{1,0:T(8,128)(2,1)} %bitcast_select_fusion, bf16[512,1024]{1,0:T(8,128)(2,1)} %collective-permute-done.16, bf16[512,1024]{1,0:T(8,128)(2,1)S(1)} %copy-done.38), kind=kOutput, calls=%fused_computation.6 | convolution fusion | flops 2155872256 | bytes 8388608 | tf_op jit(solution)/shard_map/tc,tw->cw/dot_general | solution.py:163
  (193 shorter events, 56.0 us)
Async XLA Ops:
  7.2 22.1 %copy-start = (bf16[1024,1024]{1,0:T(8,128)(2,1)S(1)}, bf16[1024,1024]{1,0:T(8,128)(2,1)}, u32[]{:S(2)}) copy-start(bf16[1024,1024]{1,0:T(8,128)(2,1)} %param.10) | copy-start | bytes 6291460
  7.2 135.9 %all-gather.2.cloned.1.call-start = ((), (), s32[]{:S(2)}) async-start(), calls=%async_computation | async-start | bytes 1310720 | tf_op jit(solution)/shard_map/all_gather | solution.py:155
  9.2 60.5 %collective-permute-start.1 = (bf16[2,1,128,1024]{3,2,1,0:T(8,128)(2,1)}, bf16[2,1,128,1024]{3,2,1,0:T(8,128)(2,1)}, u32[]{:S(2)}, u32[]{:S(2)}) collective-permute-start(bf16[2,1,128,1024]{3,2,1,0:T(8,128)(2,1)} %pad_maximum_fusion.6), channel_id=1, source_target_pairs={{4,0},{8,4},{12,8},{5,1},{9,5},{13,9},{6,2},{10,6},{14,10},{7,3},{... | collective-permute-start | bytes 1572872 | tf_op jit(solution)/shard_map/ppermute | solution.py:22
  11.6 58.1 %collective-permute-start = (bf16[2,1,128,1024]{3,2,1,0:T(8,128)(2,1)}, bf16[2,1,128,1024]{3,2,1,0:T(8,128)(2,1)}, u32[]{:S(2)}, u32[]{:S(2)}) collective-permute-start(bf16[2,1,128,1024]{3,2,1,0:T(8,128)(2,1)} %pad_maximum_fusion.6), channel_id=1, source_target_pairs={{0,4},{4,8},{8,12},{1,5},{5,9},{9,13},{2,6},{6,10},{10,14},{3,7},{... | collective-permute-start | bytes 1572872 | tf_op jit(solution)/shard_map/ppermute | solution.py:20
  19.8 7.0 %copy-start.36 = (s32[1,2,2]{2,1,0:T(2,128)S(1)}, s32[1,2,2]{2,1,0:T(2,128)}, u32[]{:S(2)}) copy-start(s32[1,2,2]{2,1,0:T(2,128)} %param.9) | copy-start | bytes 52
  22.6 22.9 %collective-permute-start.4 = (bf16[128,1024]{1,0:T(8,128)(2,1)S(1)}, bf16[128,1024]{1,0:T(8,128)(2,1)}, u32[]{:S(2)}, u32[]{:S(2)}) collective-permute-start(bf16[128,1024]{1,0:T(8,128)(2,1)S(1)} %get-tuple-element.33), channel_id=1, source_target_pairs={{0,12},{4,8},{8,4},{12,0},{1,13},{5,9},{9,5},{13,1},{2,14},{6,10},... | collective-permute-start | bytes 786440 | tf_op jit(solution)/shard_map/ppermute | solution.py:85
  22.6 24.6 %collective-permute-start.3 = (bf16[128,1024]{1,0:T(8,128)(2,1)}, bf16[128,1024]{1,0:T(8,128)(2,1)}, u32[]{:S(2)}, u32[]{:S(2)}) collective-permute-start(bf16[128,1024]{1,0:T(8,128)(2,1)} %get-tuple-element.32), channel_id=1, source_target_pairs={{0,8},{4,12},{8,0},{12,4},{1,9},{5,13},{9,1},{13,5},{2,10},{6,14},... | collective-permute-start | bytes 786440 | tf_op jit(solution)/shard_map/ppermute | solution.py:85
  24.3 6.3 %copy-start.29 = (bf16[1,128,1024]{2,1,0:T(8,128)(2,1)S(1)}, bf16[1,128,1024]{2,1,0:T(8,128)(2,1)}, u32[]{:S(2)}) copy-start(bf16[1,128,1024]{2,1,0:T(8,128)(2,1)} %param.6) | copy-start | bytes 786436
  25.1 36.8 %collective-permute-start.2 = (bf16[192,1024]{1,0:T(8,128)(2,1)}, bf16[192,1024]{1,0:T(8,128)(2,1)S(1)}, u32[]{:S(2)}, u32[]{:S(2)}) collective-permute-start(bf16[192,1024]{1,0:T(8,128)(2,1)} %pad_maximum_fusion.7), channel_id=1, source_target_pairs={{0,4},{4,0},{8,12},{12,8},{1,5},{5,1},{9,13},{13,9},{2,6},{6,2},{1... | collective-permute-start | bytes 1179656 | tf_op jit(solution)/shard_map/ppermute | solution.py:85
  47.2 3.0 %collective-permute-start.9 = (bf16[64,1024]{1,0:T(8,128)(2,1)}, bf16[64,1024]{1,0:T(8,128)(2,1)}, u32[]{:S(2)}, u32[]{:S(2)}) collective-permute-start(bf16[64,1024]{1,0:T(8,128)(2,1)} %get-tuple-element.30), channel_id=1, source_target_pairs={{0,1},{1,0},{2,3},{3,2},{4,5},{5,4},{6,7},{7,6},{8,9},{9,8},{10,11... | collective-permute-start | bytes 393224 | tf_op jit(solution)/shard_map/ppermute | solution.py:30
  49.6 4.4 %collective-permute-start.7 = (bf16[64,1024]{1,0:T(8,128)(2,1)}, bf16[64,1024]{1,0:T(8,128)(2,1)S(1)}, u32[]{:S(2)}, u32[]{:S(2)}) collective-permute-start(bf16[64,1024]{1,0:T(8,128)(2,1)} %get-tuple-element.27), channel_id=1, source_target_pairs={{0,1},{1,0},{2,3},{3,2},{4,5},{5,4},{6,7},{7,6},{8,9},{9,8},{10,11... | collective-permute-start | bytes 393224 | tf_op jit(solution)/shard_map/ppermute | solution.py:30
  52.4 37.7 %collective-permute-start.10 = (bf16[128,1024]{1,0:T(8,128)(2,1)}, bf16[128,1024]{1,0:T(8,128)(2,1)}, u32[]{:S(2)}, u32[]{:S(2)}) collective-permute-start(bf16[128,1024]{1,0:T(8,128)(2,1)} %convolution_convert_fusion), channel_id=1, source_target_pairs={{0,12},{4,8},{8,4},{12,0},{1,13},{5,9},{9,5},{13,1},{2,14},{6,10},... | collective-permute-start | bytes 786440 | tf_op jit(solution)/shard_map/ppermute | solution.py:147
  55.1 35.0 %collective-permute-start.8 = (bf16[128,1024]{1,0:T(8,128)(2,1)}, bf16[128,1024]{1,0:T(8,128)(2,1)}, u32[]{:S(2)}, u32[]{:S(2)}) collective-permute-start(bf16[128,1024]{1,0:T(8,128)(2,1)} %convolution_convert_fusion.1), channel_id=1, source_target_pairs={{0,8},{4,12},{8,0},{12,4},{1,9},{5,13},{9,1},{13,5},{2,10},{6,14},... | collective-permute-start | bytes 786440 | tf_op jit(solution)/shard_map/ppermute | solution.py:147
  62.7 7.1 %copy-start.17 = (bf16[1,128,1024]{2,1,0:T(8,128)(2,1)S(1)}, bf16[1,128,1024]{2,1,0:T(8,128)(2,1)}, u32[]{:S(2)}) copy-start(bf16[1,128,1024]{2,1,0:T(8,128)(2,1)} %param.8) | copy-start | bytes 786436
  62.7 7.1 %copy-start.18 = (bf16[1,128,1024]{2,1,0:T(8,128)(2,1)S(1)}, bf16[1,128,1024]{2,1,0:T(8,128)(2,1)}, u32[]{:S(2)}) copy-start(bf16[1,128,1024]{2,1,0:T(8,128)(2,1)} %param.7) | copy-start | bytes 786436
  67.7 12.5 %collective-permute-start.5 = (bf16[64,1024]{1,0:T(8,128)(2,1)}, bf16[64,1024]{1,0:T(8,128)(2,1)}, u32[]{:S(2)}, u32[]{:S(2)}) collective-permute-start(bf16[64,1024]{1,0:T(8,128)(2,1)} %get-tuple-element.25), channel_id=1, source_target_pairs={{0,1},{1,0},{2,3},{3,2},{4,5},{5,4},{6,7},{7,6},{8,9},{9,8},{10,11... | collective-permute-start | bytes 393224 | tf_op jit(solution)/shard_map/ppermute | solution.py:30
  82.4 8.9 %collective-permute-start.6 = (bf16[128,1024]{1,0:T(8,128)(2,1)}, bf16[128,1024]{1,0:T(8,128)(2,1)S(1)}, u32[]{:S(2)}, u32[]{:S(2)}) collective-permute-start(bf16[128,1024]{1,0:T(8,128)(2,1)} %convolution_convert_fusion.2), channel_id=1, source_target_pairs={{0,4},{4,0},{8,12},{12,8},{1,5},{5,1},{9,13},{13,9},{2,6},{6,2},{1... | collective-permute-start | bytes 786440 | tf_op jit(solution)/shard_map/ppermute | solution.py:147
  82.4 11.2 %copy-start.32 = (f32[2,8,64]{2,1,0:T(8,128)}, f32[2,8,64]{2,1,0:T(8,128)S(1)}, u32[]{:S(2)}) copy-start(f32[2,8,64]{2,1,0:T(8,128)S(1)} %copy_add_fusion.1) | copy-start | bytes 12292
  82.4 13.4 %copy-start.31 = (f32[2,8,64]{2,0,1:T(2,128)}, f32[2,8,64]{2,0,1:T(2,128)S(1)}, u32[]{:S(2)}) copy-start(f32[2,8,64]{2,0,1:T(2,128)S(1)} %copy.157) | copy-start | bytes 12292
  84.6 4.8 %copy-start.5 = (f32[2,8,64,192]{3,2,1,0:T(8,128)S(1)}, f32[2,8,64,192]{3,2,1,0:T(8,128)}, u32[]{:S(2)}) copy-start(f32[2,8,64,192]{3,2,1,0:T(8,128)} %copy-done.4) | copy-start | bytes 2359300
  87.9 68.1 %collective-permute-start.15 = (bf16[512,1024]{1,0:T(8,128)(2,1)}, bf16[512,1024]{1,0:T(8,128)(2,1)}, u32[]{:S(2)}, u32[]{:S(2)}) collective-permute-start(bf16[512,1024]{1,0:T(8,128)(2,1)} %bitcast_select_fusion), channel_id=1, source_target_pairs={{0,2},{2,0},{1,3},{3,1},{4,6},{6,4},{5,7},{7,5},{8,10},{10,8},{9,1... | collective-permute-start | bytes 3145736 | tf_op jit(solution)/shard_map/ppermute | solution.py:30
  101.7 22.9 %collective-permute-start.13 = (bf16[2,1,64,1024]{3,0,2,1:T(2,128)(2,1)}, bf16[2,1,64,1024]{3,0,2,1:T(2,128)(2,1)}, u32[]{:S(2)}, u32[]{:S(2)}) collective-permute-start(bf16[2,1,64,1024]{3,0,2,1:T(2,128)(2,1)} %fusion.58), channel_id=1, source_target_pairs={{0,8},{4,12},{8,0},{12,4},{1,9},{5,13},{9,1},{13,5},{2,10},{6,14},... | collective-permute-start | bytes 786440 | tf_op jit(solution)/shard_map/ppermute | solution.py:30
  116.8 7.8 %copy-start.6 = (bf16[2,1,4,64,1024]{4,3,2,0,1:T(8,128)(2,1)}, bf16[2,1,4,64,1024]{4,3,2,0,1:T(8,128)(2,1)S(1)}, u32[]{:S(2)}) copy-start(bf16[2,1,4,64,1024]{4,3,2,0,1:T(8,128)(2,1)S(1)} %maximum_convert_fusion) | copy-start | bytes 3145732
  116.8 10.3 %copy-start.13 = (f32[1,128,8,128]{3,2,0,1:T(8,128)S(1)}, f32[1,128,8,128]{3,2,0,1:T(8,128)}, u32[]{:S(2)}) copy-start(f32[1,128,8,128]{3,2,0,1:T(8,128)} %copy-done.12) | copy-start | bytes 1572868
  116.8 10.3 %copy-start.15 = (f32[1,128,8,128]{3,2,0,1:T(8,128)S(1)}, f32[1,128,8,128]{3,2,0,1:T(8,128)}, u32[]{:S(2)}) copy-start(f32[1,128,8,128]{3,2,0,1:T(8,128)} %copy-done.14) | copy-start | bytes 1572868
  117.9 35.3 %collective-permute-start.12 = (bf16[2,1,128,1024]{3,2,1,0:T(8,128)(2,1)}, bf16[2,1,128,1024]{3,2,1,0:T(8,128)(2,1)}, u32[]{:S(2)}, u32[]{:S(2)}) collective-permute-start(bf16[2,1,128,1024]{3,2,1,0:T(8,128)(2,1)} %get-tuple-element.12), channel_id=1, source_target_pairs={{4,0},{8,4},{12,8},{5,1},{9,5},{13,9},{6,2},{10,6},{14,10},{7,3},{... | collective-permute-start | bytes 1572872 | tf_op jit(solution)/shard_map/ppermute | solution.py:22
  122.4 30.9 %collective-permute-start.11 = (bf16[2,1,128,1024]{3,2,1,0:T(8,128)(2,1)}, bf16[2,1,128,1024]{3,2,1,0:T(8,128)(2,1)}, u32[]{:S(2)}, u32[]{:S(2)}) collective-permute-start(bf16[2,1,128,1024]{3,2,1,0:T(8,128)(2,1)} %get-tuple-element.11), channel_id=1, source_target_pairs={{0,4},{4,8},{8,12},{1,5},{5,9},{9,13},{2,6},{6,10},{10,14},{3,7},{... | collective-permute-start | bytes 1572872 | tf_op jit(solution)/shard_map/ppermute | solution.py:20
  128.5 21.1 %collective-permute-start.14 = (bf16[2,1,64,1024]{3,0,2,1:T(2,128)(2,1)}, bf16[2,1,64,1024]{3,0,2,1:T(2,128)(2,1)}, u32[]{:S(2)}, u32[]{:S(2)}) collective-permute-start(bf16[2,1,64,1024]{3,0,2,1:T(2,128)(2,1)} %fusion.30), channel_id=1, source_target_pairs={{0,4},{4,0},{8,12},{12,8},{1,5},{5,1},{9,13},{13,9},{2,6},{6,2},{1... | collective-permute-start | bytes 786440 | tf_op jit(solution)/shard_map/ppermute | solution.py:30
  132.6 17.0 %copy-start.3 = (f32[2,64,2,1024]{3,0,2,1:T(2,128)S(1)}, f32[2,64,2,1024]{3,0,2,1:T(2,128)}, u32[]{:S(2)}) copy-start(f32[2,64,2,1024]{3,0,2,1:T(2,128)} %copy-done.2) | copy-start | bytes 3145732
  143.1 24.8 %collective-permute-start.16 = (bf16[512,1024]{1,0:T(8,128)(2,1)}, bf16[512,1024]{1,0:T(8,128)(2,1)}, u32[]{:S(2)}, u32[]{:S(2)}) collective-permute-start(bf16[512,1024]{1,0:T(8,128)(2,1)} %all-gather.2.cloned.1.call-done), channel_id=1, source_target_pairs={{0,2},{2,0},{1,3},{3,1},{4,6},{6,4},{5,7},{7,5},{8,10},{10,8},{9,1... | collective-permute-start | bytes 3145736 | tf_op jit(solution)/shard_map/ppermute | solution.py:30
  153.2 14.6 %copy-start.38 = (bf16[512,1024]{1,0:T(8,128)(2,1)S(1)}, bf16[512,1024]{1,0:T(8,128)(2,1)}, u32[]{:S(2)}) copy-start(bf16[512,1024]{1,0:T(8,128)(2,1)} %all-gather.2.cloned.1.call-done) | copy-start | bytes 3145732
  167.8 6.4 %copy-start.1 = (bf16[1024,1024]{1,0:T(8,128)(2,1)S(1)}, bf16[1024,1024]{1,0:T(8,128)(2,1)}, u32[]{:S(2)}) copy-start(bf16[1024,1024]{1,0:T(8,128)(2,1)} %param.10) | copy-start | bytes 6291460
  (25 other events, 59.5 us)
Sparse Core Ops, SparseCore 0:
  104.9 38.1 all-gather.1

commit v9 on v7

--- a/solution.py
+++ b/solution.py
@@ -138,14 +138,8 @@
     feat_docs = jnp.take(jnp.stack(feat_list, axis=0), feat_order, axis=0).reshape(
         seq_count * cot_rows.shape[0], feat_count
     )
-    whole_output = lax.all_gather(out_rows, "seq", axis=0, tiled=True)
-    dp_count = lax.axis_size("dp")
-    if dp_count == 2:
-        feat_docs = jnp.concatenate([feat_docs, swapped(feat_docs, "dp", 0)], axis=0)
-        whole_output = jnp.concatenate([whole_output, swapped(whole_output, "dp", 0)], axis=0)
-    else:
-        feat_docs = lax.all_gather(feat_docs, "dp", axis=0, tiled=True)
-        whole_output = lax.all_gather(whole_output, "dp", axis=0, tiled=True)
+    feat_docs = lax.all_gather(feat_docs, "dp", axis=0, tiled=True)
+    whole_output = lax.all_gather(out_rows, ("dp", "seq"), axis=0, tiled=True)
     weight_grad = jnp.einsum(
         "tc,tw->cw", feat_docs, whole_output, preferred_element_type=jnp.float32
     )

time: 180 us -> 174 us (0.967)
  the two profiles are of different devices: /device:TPU:18 before, /device:TPU:6 now
where the time goes in v9:
time: 174 us; the launch traced here: 172 us
  other arithmetic  35.7 us (21%)
  waiting for transfers between devices  35.2 us (20%)
  local copies, waits for them, and re-layouts  33.1 us (19%)
  starting transfers between devices  30.9 us (18%)
  matrix products  22.1 us (13%)
  between operations  14.8 us (9%)
    ppermute x7, waiting for transfers between devices, swapped(): lax.ppermute(shard, axis, [(i, i ^ 1 << stride) for i in range(lax.axis_s...  28.9 us
    ppermute x2, starting transfers between devices, extended(): lax.ppermute(tail, axis, [(i, (i + 1) % count) for i in range(ends)])  12.2 us
    ppermute x7, starting transfers between devices, swapped(): lax.ppermute(shard, axis, [(i, i ^ 1 << stride) for i in range(lax.axis_s...  7.46 us
    dot_general x1, matrix products, shards(): jnp.einsum('tc,tw->cw', feat_docs, whole_output, preferred_element_type=j...  6.77 us
    dot_general x3, matrix products, shards(): part = jnp.dot(got, out_weight, preferred_element_type=jnp.float32)  6.51 us
    ppermute x3, waiting for transfers between devices, shards(): lax.ppermute(lax.dynamic_slice_in_dim(sent, core * half, half, axis=0), '...  6.01 us
    unnamed x61, local copies, waits for them, and re-layouts  5.82 us
    scatter-add x1, other arithmetic, place_blocks(): return holder.at[:, chosen_doc].add(grad_doc)  5.37 us
  transfers between devices with their start and end apart: 19, of which 5 were waited for; matrix products, arithmetic and copies ran while one was open for 46% of the time, Pallas kernels for 0%

profile of v9, /device:TPU:6, one launch (start us, length us, event | category | flops | bytes accessed | tf_op | source)
XLA Modules:
  0.0 171.6 jit_solution(12876262757878156139)
XLA Ops:
  7.2 2.0 %pad_maximum_fusion.6 = bf16[2,1,128,1024]{3,2,1,0:T(8,128)(2,1)} fusion(bf16[1,1,128,1024]{3,2,1,0:T(8,128)(2,1)} %bitcast.253, bf16[1,1,128,1024]{3,2,1,0:T(8,128)(2,1)} %bitcast.255), kind=kLoop, calls=%fused_computation.53 | loop fusion | flops 262144 | bytes 1048576 | tf_op jit(solution)/shard_map/stack | solution.py:58
  10.6 5.4 %collective-permute-start = (bf16[2,1,128,1024]{3,2,1,0:T(8,128)(2,1)}, bf16[2,1,128,1024]{3,2,1,0:T(8,128)(2,1)}, u32[]{:S(2)}, u32[]{:S(2)}) collective-permute-start(bf16[2,1,128,1024]{3,2,1,0:T(8,128)(2,1)} %pad_maximum_fusion.6), channel_id=1, source_target_pairs={{0,4},{4,8},{8,12},{1,5},{5,9},{9,13},{2,6},{6,10},{10,14},{3,7},{... | collective-permute-start | bytes 1572872 | tf_op jit(solution)/shard_map/ppermute | solution.py:20
  15.9 2.0 %dynamic-slice_bitcast_fusion.2 = (bf16[64,1024]{1,0:T(8,128)(2,1)}, bf16[64,1024]{1,0:T(8,128)(2,1)}, bf16[64,1024]{1,0:T(8,128)(2,1)}) fusion(bf16[1,128,4096]{2,1,0:T(8,128)(2,1)} %param.11, s32[]{:T(128)S(6)} %select_n.146, s32[]{:T(128)S(6)} %select_n.148, s32[]{:T(128)S(6)} %select_n.154, s32[]{:T(128)S(6)} %select_n.151), kind=kLoop, calls=%fused_computation.116 | loop fusion | bytes 786448 | tf_op jit(solution)/shard_map/dynamic_slice | solution.py:124
  17.9 1.4 collective-permute-start.10
  20.6 1.8 %collective-permute-start.4 = (bf16[64,1024]{1,0:T(8,128)(2,1)}, bf16[64,1024]{1,0:T(8,128)(2,1)S(1)}, u32[]{:S(2)}, u32[]{:S(2)}) collective-permute-start(bf16[64,1024]{1,0:T(8,128)(2,1)} %get-tuple-element.13), channel_id=1, source_target_pairs={{0,4},{4,0},{8,12},{12,8},{1,5},{5,1},{9,13},{13,9},{2,6},{6,2},{1... | collective-permute-start | bytes 393224 | tf_op jit(solution)/shard_map/ppermute | solution.py:123
  23.5 1.4 convert_reduce_fusion
  28.3 2.9 %collective-permute-done.10 = bf16[64,1024]{1,0:T(8,128)(2,1)} collective-permute-done((bf16[64,1024]{1,0:T(8,128)(2,1)}, bf16[64,1024]{1,0:T(8,128)(2,1)}, u32[]{:S(2)}, u32[]{:S(2)}) %collective-permute-start.10) | collective-permute-done | bytes 131104 | tf_op jit(solution)/shard_map/ppermute | solution.py:123
  34.3 3.1 %collective-permute-done.7 = bf16[64,1024]{1,0:T(8,128)(2,1)} collective-permute-done((bf16[64,1024]{1,0:T(8,128)(2,1)}, bf16[64,1024]{1,0:T(8,128)(2,1)}, u32[]{:S(2)}, u32[]{:S(2)}) %collective-permute-start.7) | collective-permute-done | bytes 131104 | tf_op jit(solution)/shard_map/ppermute | solution.py:123
  37.4 3.4 %collective-permute-start.2 = (f32[2,1,64,1024]{3,2,1,0:T(8,128)}, f32[2,1,64,1024]{3,2,1,0:T(8,128)}, u32[]{:S(2)}, u32[]{:S(2)}) collective-permute-start(f32[2,1,64,1024]{3,2,1,0:T(8,128)} %get-tuple-element.23), channel_id=1, source_target_pairs={{0,4},{4,0},{8,12},{12,8},{1,5},{5,1},{9,13},{13,9},{2,6},{6,2},{1... | collective-permute-start | bytes 1572872 | tf_op jit(solution)/shard_map/ppermute | solution.py:30
  41.4 2.2 %convolution_convert_fusion = bf16[128,1024]{1,0:T(8,128)(2,1)} fusion(bf16[1024,1024]{1,0:T(8,128)(2,1)S(1)} %copy-done, bf16[64,1024]{1,0:T(8,128)(2,1)} %collective-permute-done.11, bf16[64,1024]{1,0:T(8,128)(2,1)} %collective-permute-done.10, pred[]{:T(512)S(6)} %eq.10), kind=kOutput, calls=%fused_computation.22 | convolution fusion | flops 269746176 | bytes 2621441 | tf_op jit(solution)/shard_map/dot_general | solution.py:132
  43.6 3.4 %collective-permute-start.12 = (bf16[128,1024]{1,0:T(8,128)(2,1)}, bf16[128,1024]{1,0:T(8,128)(2,1)}, u32[]{:S(2)}, u32[]{:S(2)}) collective-permute-start(bf16[128,1024]{1,0:T(8,128)(2,1)} %convolution_convert_fusion), channel_id=1, source_target_pairs={{0,12},{4,8},{8,4},{12,0},{1,13},{5,9},{9,5},{13,1},{2,14},{6,10},... | collective-permute-start | bytes 786440 | tf_op jit(solution)/shard_map/ppermute | solution.py:133
  47.0 2.1 %convolution_convert_fusion.1 = bf16[128,1024]{1,0:T(8,128)(2,1)} fusion(bf16[1024,1024]{1,0:T(8,128)(2,1)S(1)} %copy-done, bf16[64,1024]{1,0:T(8,128)(2,1)S(1)} %collective-permute-done.8, bf16[64,1024]{1,0:T(8,128)(2,1)} %collective-permute-done.7, pred[]{:T(512)S(6)} %eq.10), kind=kOutput, calls=%fused_computation.23 | convolution fusion | flops 269746176 | bytes 2621441 | tf_op jit(solution)/shard_map/dot_general | solution.py:132
  53.2 2.8 %gather_fusion = bf16[4,128,1024]{2,1,0:T(8,128)(2,1)} fusion(bf16[4,128,1024]{2,1,0:T(8,128)(2,1)} %pad_maximum_fusion.2, s32[1024]{0:T(1024)S(1)} %pad_clamp_fusion), kind=kCustom, calls=%fused_computation | custom fusion | bytes 2097168 | tf_op jit(solution)/shard_map/jit(_take)/gather | solution.py:138
  56.0 2.4 %bitcast_select_fusion = bf16[512,1024]{1,0:T(8,128)(2,1)} fusion(bf16[4,128,1024]{2,1,0:T(8,128)(2,1)} %gather_fusion, pred[512]{0:T(512)(128)(4,1)S(1)} %broadcast_bitcast_fusion), kind=kLoop, calls=%fused_computation.34 | loop fusion | flops 524288 | bytes 2097664 | tf_op jit(solution)/shard_map/jit(_take)/select_n | solution.py:138
  58.6 2.1 %convolution_convert_fusion.2 = bf16[128,1024]{1,0:T(8,128)(2,1)} fusion(bf16[1024,1024]{1,0:T(8,128)(2,1)S(1)} %copy-done, bf16[64,1024]{1,0:T(8,128)(2,1)} %copy-done.26, bf16[64,1024]{1,0:T(8,128)(2,1)S(1)} %collective-permute-done.4, pred[]{:T(512)S(6)} %eq.10), kind=kOutput, calls=%fused_computation.24 | convolution fusion | flops 269746176 | bytes 2621441 | tf_op jit(solution)/shard_map/dot_general | solution.py:132
  62.5 1.8 %gather_fusion.1 = bf16[6,2,64,1024]{3,2,1,0:T(8,128)(2,1)} fusion(bf16[1,2,6,64,1024]{4,3,2,1,0:T(8,128)(2,1)S(1)} %bitcast.239, s32[6]{0:T(128)S(1)} %reshape.748), kind=kCustom, calls=%fused_computation.1 | custom fusion | bytes 3145776 | tf_op jit(solution)/shard_map/vmap()/gather | solution.py:41
  64.4 1.7 copy.197
  70.8 2.1 %collective-permute-start.3 = (bf16[2,1,64,1024]{3,2,1,0:T(8,128)(2,1)S(1)}, bf16[2,1,64,1024]{3,2,1,0:T(8,128)(2,1)S(1)}, u32[]{:S(2)}, u32[]{:S(2)}) collective-permute-start(bf16[2,1,64,1024]{3,2,1,0:T(8,128)(2,1)S(1)} %fusion.23), channel_id=1, source_target_pairs={{0,8},{4,12},{8,0},{12,4},{1,9},{5,13},{9,1},{13,5},{2,10},{6,14},... | collective-permute-start | bytes 786440 | tf_op jit(solution)/shard_map/ppermute | solution.py:30
  77.0 8.2 %collective-permute-done.3 = bf16[2,1,64,1024]{3,2,1,0:T(8,128)(2,1)S(1)} collective-permute-done((bf16[2,1,64,1024]{3,2,1,0:T(8,128)(2,1)S(1)}, bf16[2,1,64,1024]{3,2,1,0:T(8,128)(2,1)S(1)}, u32[]{:S(2)}, u32[]{:S(2)}) %collective-permute-start.3) | collective-permute-done | bytes 262176 | tf_op jit(solution)/shard_map/ppermute | solution.py:30
  88.1 1.6 multiply_reduce_fusion
  99.1 3.1 %pad_maximum_fusion = f32[1,2,2,3,64,1024]{5,0,4,3,2,1:T(1,128)S(1)} fusion(f32[1,1,2,3,64,1024]{5,0,4,3,2,1:T(1,128)S(1)} %bitcast.241, f32[1,1,2,3,64,1024]{5,0,4,3,2,1:T(1,128)S(1)} %bitcast.242), kind=kLoop, calls=%fused_computation.3 | loop fusion | flops 786432 | bytes 6291456 | tf_op jit(solution)/shard_map/stack | solution.py:181
  102.1 2.4 %copy.260 = f32[1,2,2,3,64,1024]{5,4,1,3,2,0:T(8,128)} copy(f32[1,2,2,3,64,1024]{5,0,4,3,2,1:T(1,128)S(1)} %pad_maximum_fusion) | data formatting | bytes 6291456 | tf_op jit(solution)/shard_map/stack | solution.py:181
  104.9 5.4 %scatter_fusion = f32[2,6,64,1024]{3,2,1,0:T(8,128)S(1)} fusion(f32[2,6,64,1024]{3,2,1,0:T(8,128)S(1)} %broadcast.224, s32[6]{0:T(128)S(1)} %reshape.760, f32[6,2,64,1024]{3,2,1,0:T(8,128)} %bitcast.228), kind=kCustom, calls=%fused_computation.2 | custom fusion | flops 786432 | bytes 9437208 | tf_op jit(solution)/shard_map/vmap()/scatter-add | solution.py:46
  111.6 1.4 collective-permute-start.14
  113.0 6.8 %collective-permute-start.13 = (bf16[2,1,128,1024]{3,2,1,0:T(8,128)(2,1)}, bf16[2,1,128,1024]{3,2,1,0:T(8,128)(2,1)}, u32[]{:S(2)}, u32[]{:S(2)}) collective-permute-start(bf16[2,1,128,1024]{3,2,1,0:T(8,128)(2,1)} %get-tuple-element.11), channel_id=1, source_target_pairs={{0,4},{4,8},{8,12},{1,5},{5,9},{9,13},{2,6},{6,10},{10,14},{3,7},{... | collective-permute-start | bytes 1572872 | tf_op jit(solution)/shard_map/ppermute | solution.py:20
  123.8 1.4 collective-permute-start.16
  126.4 1.8 %convert_element_type.170 = bf16[1,128,1024]{2,1,0:T(8,128)(2,1)} reshape(bf16[1,2,64,8,128]{4,3,2,1,0:T(8,128)(2,1)} %copy-done.19) | data formatting | bytes 524288 | tf_op jit(solution)/shard_map/convert_element_type | solution.py:109
  131.0 20.7 %collective-permute-done.16 = bf16[2,1,64,1024]{3,0,2,1:T(2,128)(2,1)} collective-permute-done((bf16[2,1,64,1024]{3,0,2,1:T(2,128)(2,1)}, bf16[2,1,64,1024]{3,0,2,1:T(2,128)(2,1)}, u32[]{:S(2)}, u32[]{:S(2)}) %collective-permute-start.16) | collective-permute-done | bytes 262176 | tf_op jit(solution)/shard_map/ppermute | solution.py:30
  151.7 1.4 multiply_bitcast_fusion.1
  153.6 1.7 mul.193
  155.4 1.8 %fusion.10 = bf16[2,1,128,1024]{3,2,1,0:T(8,128)(2,1)S(1)} fusion(f32[2,1,128,1024]{3,2,1,0:T(8,128)} %mul.193, f32[2,1,128,1024]{3,2,1,0:T(8,128)S(1)} %bitcast.250, bf16[2,1,128,1024]{3,2,1,0:T(8,128)(2,1)} %collective-permute-done.14, bf16[2,1,256,1024]{3,2,1,0:T(8,128)(2,1)S(1)} %bitcast.232, bf16[2,1,128,1024]{3,2,1,0:T(8,128)(2,1)} %collective-permute-done.13), kind=kLoop, calls=%fused_computation.29 | loop fusion | flops 4194304 | bytes 4718592 | tf_op jit(solution)/shard_map/convert.1
  158.0 6.8 %fusion.72 = f32[1024,1024]{1,0:T(8,128)} fusion(bf16[1024,1024]{1,0:T(8,128)(2,1)} %all-gather.3.cloned.1.call-done, bf16[1024,1024]{1,0:T(8,128)(2,1)} %all-gather.5.cloned.1.call-done), kind=kOutput, calls=%fused_computation.143 | convolution fusion | flops 2147483648 | bytes 8388608 | tf_op jit(solution)/shard_map/tc,tw->cw/dot_general | solution.py:143
  (163 shorter events, 48.2 us)
Async XLA Ops:
  7.2 19.9 %copy-start = (bf16[1024,1024]{1,0:T(8,128)(2,1)S(1)}, bf16[1024,1024]{1,0:T(8,128)(2,1)}, u32[]{:S(2)}) copy-start(bf16[1024,1024]{1,0:T(8,128)(2,1)} %param.10) | copy-start | bytes 6291460
  7.2 16.2 %copy-start.16 = (bf16[1,128,1024]{2,1,0:T(8,128)(2,1)S(1)}, bf16[1,128,1024]{2,1,0:T(8,128)(2,1)}, u32[]{:S(2)}) copy-start(bf16[1,128,1024]{2,1,0:T(8,128)(2,1)} %param.7) | copy-start | bytes 786436
  7.2 16.3 %copy-start.27 = (s32[1,2,2]{2,1,0:T(2,128)S(1)}, s32[1,2,2]{2,1,0:T(2,128)}, u32[]{:S(2)}) copy-start(s32[1,2,2]{2,1,0:T(2,128)} %param.9) | copy-start | bytes 52
  7.2 150.8 %all-gather.3.cloned.1.call-start = ((), (), s32[]{:S(2)}) async-start(), calls=%async_computation | async-start | bytes 3145728 | tf_op jit(solution)/shard_map/all_gather | solution.py:141
  9.3 51.5 %collective-permute-start.1 = (bf16[2,1,128,1024]{3,2,1,0:T(8,128)(2,1)}, bf16[2,1,128,1024]{3,2,1,0:T(8,128)(2,1)}, u32[]{:S(2)}, u32[]{:S(2)}) collective-permute-start(bf16[2,1,128,1024]{3,2,1,0:T(8,128)(2,1)} %pad_maximum_fusion.6), channel_id=1, source_target_pairs={{4,0},{8,4},{12,8},{5,1},{9,5},{13,9},{6,2},{10,6},{14,10},{7,3},{... | collective-permute-start | bytes 1572872 | tf_op jit(solution)/shard_map/ppermute | solution.py:22
  10.6 50.6 %collective-permute-start = (bf16[2,1,128,1024]{3,2,1,0:T(8,128)(2,1)}, bf16[2,1,128,1024]{3,2,1,0:T(8,128)(2,1)}, u32[]{:S(2)}, u32[]{:S(2)}) collective-permute-start(bf16[2,1,128,1024]{3,2,1,0:T(8,128)(2,1)} %pad_maximum_fusion.6), channel_id=1, source_target_pairs={{0,4},{4,8},{8,12},{1,5},{5,9},{9,13},{2,6},{6,10},{10,14},{3,7},{... | collective-permute-start | bytes 1572872 | tf_op jit(solution)/shard_map/ppermute | solution.py:20
  17.9 13.3 %collective-permute-start.10 = (bf16[64,1024]{1,0:T(8,128)(2,1)}, bf16[64,1024]{1,0:T(8,128)(2,1)}, u32[]{:S(2)}, u32[]{:S(2)}) collective-permute-start(bf16[64,1024]{1,0:T(8,128)(2,1)} %get-tuple-element.14), channel_id=1, source_target_pairs={{0,12},{4,8},{8,4},{12,0},{1,13},{5,9},{9,5},{13,1},{2,14},{6,10},... | collective-permute-start | bytes 393224 | tf_op jit(solution)/shard_map/ppermute | solution.py:123
  19.4 18.0 %collective-permute-start.7 = (bf16[64,1024]{1,0:T(8,128)(2,1)}, bf16[64,1024]{1,0:T(8,128)(2,1)}, u32[]{:S(2)}, u32[]{:S(2)}) collective-permute-start(bf16[64,1024]{1,0:T(8,128)(2,1)} %get-tuple-element.15), channel_id=1, source_target_pairs={{0,8},{4,12},{8,0},{12,4},{1,9},{5,13},{9,1},{13,5},{2,10},{6,14},... | collective-permute-start | bytes 393224 | tf_op jit(solution)/shard_map/ppermute | solution.py:123
  20.6 20.3 %collective-permute-start.4 = (bf16[64,1024]{1,0:T(8,128)(2,1)}, bf16[64,1024]{1,0:T(8,128)(2,1)S(1)}, u32[]{:S(2)}, u32[]{:S(2)}) collective-permute-start(bf16[64,1024]{1,0:T(8,128)(2,1)} %get-tuple-element.13), channel_id=1, source_target_pairs={{0,4},{4,0},{8,12},{12,8},{1,5},{5,1},{9,13},{13,9},{2,6},{6,2},{1... | collective-permute-start | bytes 393224 | tf_op jit(solution)/shard_map/ppermute | solution.py:123
  31.2 9.8 %collective-permute-start.11 = (bf16[64,1024]{1,0:T(8,128)(2,1)}, bf16[64,1024]{1,0:T(8,128)(2,1)}, u32[]{:S(2)}, u32[]{:S(2)}) collective-permute-start(bf16[64,1024]{1,0:T(8,128)(2,1)} %collective-permute-done.10), channel_id=1, source_target_pairs={{0,1},{1,0},{2,3},{3,2},{4,5},{5,4},{6,7},{7,6},{8,9},{9,8},{10,11... | collective-permute-start | bytes 393224 | tf_op jit(solution)/shard_map/ppermute | solution.py:30
  37.4 28.8 %collective-permute-start.2 = (f32[2,1,64,1024]{3,2,1,0:T(8,128)}, f32[2,1,64,1024]{3,2,1,0:T(8,128)}, u32[]{:S(2)}, u32[]{:S(2)}) collective-permute-start(f32[2,1,64,1024]{3,2,1,0:T(8,128)} %get-tuple-element.23), channel_id=1, source_target_pairs={{0,4},{4,0},{8,12},{12,8},{1,5},{5,1},{9,13},{13,9},{2,6},{6,2},{1... | collective-permute-start | bytes 1572872 | tf_op jit(solution)/shard_map/ppermute | solution.py:30
  40.8 2.8 %collective-permute-start.8 = (bf16[64,1024]{1,0:T(8,128)(2,1)}, bf16[64,1024]{1,0:T(8,128)(2,1)S(1)}, u32[]{:S(2)}, u32[]{:S(2)}) collective-permute-start(bf16[64,1024]{1,0:T(8,128)(2,1)} %collective-permute-done.7), channel_id=1, source_target_pairs={{0,1},{1,0},{2,3},{3,2},{4,5},{5,4},{6,7},{7,6},{8,9},{9,8},{10,11... | collective-permute-start | bytes 393224 | tf_op jit(solution)/shard_map/ppermute | solution.py:30
  41.1 10.3 %collective-permute-start.5 = (bf16[64,1024]{1,0:T(8,128)(2,1)S(1)}, bf16[64,1024]{1,0:T(8,128)(2,1)S(1)}, u32[]{:S(2)}, u32[]{:S(2)}) collective-permute-start(bf16[64,1024]{1,0:T(8,128)(2,1)S(1)} %collective-permute-done.4), channel_id=1, source_target_pairs={{0,1},{1,0},{2,3},{3,2},{4,5},{5,4},{6,7},{7,6},{8,9},{9,8},{10,11... | collective-permute-start | bytes 393224 | tf_op jit(solution)/shard_map/ppermute | solution.py:30
  43.6 29.3 %collective-permute-start.12 = (bf16[128,1024]{1,0:T(8,128)(2,1)}, bf16[128,1024]{1,0:T(8,128)(2,1)}, u32[]{:S(2)}, u32[]{:S(2)}) collective-permute-start(bf16[128,1024]{1,0:T(8,128)(2,1)} %convolution_convert_fusion), channel_id=1, source_target_pairs={{0,12},{4,8},{8,4},{12,0},{1,13},{5,9},{9,5},{13,1},{2,14},{6,10},... | collective-permute-start | bytes 786440 | tf_op jit(solution)/shard_map/ppermute | solution.py:133
  51.4 21.5 %collective-permute-start.9 = (bf16[128,1024]{1,0:T(8,128)(2,1)}, bf16[128,1024]{1,0:T(8,128)(2,1)}, u32[]{:S(2)}, u32[]{:S(2)}) collective-permute-start(bf16[128,1024]{1,0:T(8,128)(2,1)} %convolution_convert_fusion.1), channel_id=1, source_target_pairs={{0,8},{4,12},{8,0},{12,4},{1,9},{5,13},{9,1},{13,5},{2,10},{6,14},... | collective-permute-start | bytes 786440 | tf_op jit(solution)/shard_map/ppermute | solution.py:133
  58.4 99.6 %all-gather.5.cloned.1.call-start = ((), (), s32[]{:S(2)}) async-start(), calls=%async_computation.1 | async-start | bytes 2359296 | tf_op jit(solution)/shard_map/all_gather | solution.py:142
  60.8 12.3 %collective-permute-start.6 = (bf16[128,1024]{1,0:T(8,128)(2,1)}, bf16[128,1024]{1,0:T(8,128)(2,1)}, u32[]{:S(2)}, u32[]{:S(2)}) collective-permute-start(bf16[128,1024]{1,0:T(8,128)(2,1)} %convolution_convert_fusion.2), channel_id=1, source_target_pairs={{0,4},{4,0},{8,12},{12,8},{1,5},{5,1},{9,13},{13,9},{2,6},{6,2},{1... | collective-permute-start | bytes 786440 | tf_op jit(solution)/shard_map/ppermute | solution.py:133
  68.8 7.4 %copy-start.6 = (bf16[48,8,8,128]{3,2,1,0:T(8,128)(2,1)}, bf16[48,8,8,128]{3,2,1,0:T(8,128)(2,1)S(1)}, u32[]{:S(2)}) copy-start(bf16[48,8,8,128]{3,2,1,0:T(8,128)(2,1)S(1)} %copy.261) | copy-start | bytes 2359300
  68.8 4.2 %copy-start.21 = (f32[128,1024]{1,0:T(8,128)S(1)}, f32[128,1024]{1,0:T(8,128)}, u32[]{:S(2)}) copy-start(f32[128,1024]{1,0:T(8,128)} %fusion.45) | copy-start | bytes 1572868
  70.8 14.4 %collective-permute-start.3 = (bf16[2,1,64,1024]{3,2,1,0:T(8,128)(2,1)S(1)}, bf16[2,1,64,1024]{3,2,1,0:T(8,128)(2,1)S(1)}, u32[]{:S(2)}, u32[]{:S(2)}) collective-permute-start(bf16[2,1,64,1024]{3,2,1,0:T(8,128)(2,1)S(1)} %fusion.23), channel_id=1, source_target_pairs={{0,8},{4,12},{8,0},{12,4},{1,9},{5,13},{9,1},{13,5},{2,10},{6,14},... | collective-permute-start | bytes 786440 | tf_op jit(solution)/shard_map/ppermute | solution.py:30
  75.2 10.3 %copy-start.23 = (bf16[2,64,8,128]{3,1,0,2:T(8,128)(2,1)S(1)}, bf16[2,64,8,128]{3,1,0,2:T(8,128)(2,1)}, u32[]{:S(2)}) copy-start(bf16[2,64,8,128]{3,1,0,2:T(8,128)(2,1)} %copy.208) | copy-start | bytes 786436
  94.8 25.1 %collective-permute-start.15 = (bf16[2,1,64,1024]{3,0,2,1:T(2,128)(2,1)}, bf16[2,1,64,1024]{3,0,2,1:T(2,128)(2,1)}, u32[]{:S(2)}, u32[]{:S(2)}) collective-permute-start(bf16[2,1,64,1024]{3,0,2,1:T(2,128)(2,1)} %fusion.51), channel_id=1, source_target_pairs={{0,8},{4,12},{8,0},{12,4},{1,9},{5,13},{9,1},{13,5},{2,10},{6,14},... | collective-permute-start | bytes 786440 | tf_op jit(solution)/shard_map/ppermute | solution.py:30
  110.5 9.3 %copy-start.4 = (bf16[2,1,4,64,1024]{4,3,2,0,1:T(8,128)(2,1)}, bf16[2,1,4,64,1024]{4,3,2,0,1:T(8,128)(2,1)S(1)}, u32[]{:S(2)}) copy-start(bf16[2,1,4,64,1024]{4,3,2,0,1:T(8,128)(2,1)S(1)} %maximum_convert_fusion) | copy-start | bytes 3145732
  110.6 11.8 %copy-start.9 = (f32[1,128,8,128]{3,2,0,1:T(8,128)S(1)}, f32[1,128,8,128]{3,2,0,1:T(8,128)}, u32[]{:S(2)}) copy-start(f32[1,128,8,128]{3,2,0,1:T(8,128)} %copy-done.8) | copy-start | bytes 1572868
  110.6 11.8 %copy-start.11 = (f32[1,128,8,128]{3,2,0,1:T(8,128)S(1)}, f32[1,128,8,128]{3,2,0,1:T(8,128)}, u32[]{:S(2)}) copy-start(f32[1,128,8,128]{3,2,0,1:T(8,128)} %copy-done.10) | copy-start | bytes 1572868
  111.6 43.7 %collective-permute-start.14 = (bf16[2,1,128,1024]{3,2,1,0:T(8,128)(2,1)}, bf16[2,1,128,1024]{3,2,1,0:T(8,128)(2,1)}, u32[]{:S(2)}, u32[]{:S(2)}) collective-permute-start(bf16[2,1,128,1024]{3,2,1,0:T(8,128)(2,1)} %get-tuple-element.12), channel_id=1, source_target_pairs={{4,0},{8,4},{12,8},{5,1},{9,5},{13,9},{6,2},{10,6},{14,10},{7,3},{... | collective-permute-start | bytes 1572872 | tf_op jit(solution)/shard_map/ppermute | solution.py:22
  113.0 42.3 %collective-permute-start.13 = (bf16[2,1,128,1024]{3,2,1,0:T(8,128)(2,1)}, bf16[2,1,128,1024]{3,2,1,0:T(8,128)(2,1)}, u32[]{:S(2)}, u32[]{:S(2)}) collective-permute-start(bf16[2,1,128,1024]{3,2,1,0:T(8,128)(2,1)} %get-tuple-element.11), channel_id=1, source_target_pairs={{0,4},{4,8},{8,12},{1,5},{5,9},{9,13},{2,6},{6,10},{10,14},{3,7},{... | collective-permute-start | bytes 1572872 | tf_op jit(solution)/shard_map/ppermute | solution.py:20
  121.0 4.2 %copy-start.7 = (bf16[48,8,8,128]{3,2,1,0:T(8,128)(2,1)S(1)}, bf16[48,8,8,128]{3,2,1,0:T(8,128)(2,1)}, u32[]{:S(2)}) copy-start(bf16[48,8,8,128]{3,2,1,0:T(8,128)(2,1)} %copy-done.6) | copy-start | bytes 2359300
  121.0 4.2 %copy-start.13 = (bf16[2,8,64,192]{3,2,1,0:T(8,128)(2,1)S(1)}, bf16[2,8,64,192]{3,2,1,0:T(8,128)(2,1)}, u32[]{:S(2)}) copy-start(bf16[2,8,64,192]{3,2,1,0:T(8,128)(2,1)} %copy-done.12) | copy-start | bytes 1179652
  123.8 27.9 %collective-permute-start.16 = (bf16[2,1,64,1024]{3,0,2,1:T(2,128)(2,1)}, bf16[2,1,64,1024]{3,0,2,1:T(2,128)(2,1)}, u32[]{:S(2)}, u32[]{:S(2)}) collective-permute-start(bf16[2,1,64,1024]{3,0,2,1:T(2,128)(2,1)} %fusion.24), channel_id=1, source_target_pairs={{0,4},{4,0},{8,12},{12,8},{1,5},{5,1},{9,13},{13,9},{2,6},{6,2},{1... | collective-permute-start | bytes 786440 | tf_op jit(solution)/shard_map/ppermute | solution.py:30
  129.2 22.5 %copy-start.3 = (f32[2,64,2,1024]{3,0,2,1:T(2,128)S(1)}, f32[2,64,2,1024]{3,0,2,1:T(2,128)}, u32[]{:S(2)}) copy-start(f32[2,64,2,1024]{3,0,2,1:T(2,128)} %copy-done.2) | copy-start | bytes 3145732
  158.0 6.8 %copy-start.1 = (bf16[1024,1024]{1,0:T(8,128)(2,1)S(1)}, bf16[1024,1024]{1,0:T(8,128)(2,1)}, u32[]{:S(2)}) copy-start(bf16[1024,1024]{1,0:T(8,128)(2,1)} %param.10) | copy-start | bytes 6291460
  (15 other events, 25.2 us)
Sparse Core Ops, SparseCore 0:
  58.5 32.1 all-gather.2
  93.7 59.1 all-gather.4

commit v10 on v9

--- a/solution.py
+++ b/solution.py
@@ -193,20 +193,19 @@
     far_rows = jnp.stack([far_key_rows, far_value_rows]).reshape(
         2, doc_count, levels, block, head_cols
     )
-    carried = jnp.zeros((2, doc_count, block, head_cols), jnp.float32)
-    for level_no in reversed(range(levels)):
-        message = far_rows[:, :, level_no]
-        mine = jnp.zeros_like(message)
-        if level_no + 1 < levels:
-            upper = position >> level_no & 1 == 1
-            spread = jnp.repeat(carried, 2, axis=2) * 0.5
-            lower_half = spread[:, :, :block]
-            upper_half = spread[:, :, block:]
-            mine = jnp.where(upper, upper_half, lower_half)
-            message = message + jnp.where(upper, lower_half, upper_half)
-        returned = swapped(message.astype(jnp.bfloat16), "seq", level_no).astype(jnp.float32)
-        carried = returned + mine
-    token_grad = token_grad + jnp.repeat(carried, 2, axis=2) * 0.5
+    for level_no in range(levels):
+        count = 1 << level_no
+        height = block // count
+        level_sum = None
+        for step in range(count, 2 * count):
+            slot = (position ^ step) & (count - 1)
+            segment = lax.dynamic_slice_in_dim(far_rows[:, :, level_no], slot * height, height, axis=2)
+            returned = lax.ppermute(
+                segment.astype(jnp.bfloat16), "seq", [(i, i ^ step) for i in range(seq_count)]
+            ).astype(jnp.float32)
+            level_sum = returned if level_sum is None else level_sum + returned
+        spread = 2 ** (level_no + 1)
+        token_grad = token_grad + jnp.repeat(level_sum, spread, axis=2) / float(spread)
     key_grad = token_grad[0].astype(jnp.bfloat16)
     value_grad = token_grad[1].astype(jnp.bfloat16)
     return (attention, query_grad, key_grad, value_grad, weight_grad)

time: 174 us -> 172 us (0.989)
  the two profiles are of different devices: /device:TPU:6 before, /device:TPU:30 now
where the time goes in v10:
time: 172 us; the launch traced here: 171 us
  waiting for transfers between devices  38.2 us (22%)
  local copies, waits for them, and re-layouts  36.5 us (21%)
  other arithmetic  33.7 us (20%)
  starting transfers between devices  25.1 us (15%)
  matrix products  22.8 us (13%)
  between operations  14.8 us (9%)
    ppermute x2, waiting for transfers between devices, extended(): lax.ppermute(tail, axis, [(i, (i + 1) % count) for i in range(ends)])  14.1 us
    ppermute x3, waiting for transfers between devices, shards(): lax.ppermute(lax.dynamic_slice_in_dim(sent, core * half, half, axis=0), '...  9.79 us
    ppermute x5, waiting for transfers between devices, swapped(): lax.ppermute(shard, axis, [(i, i ^ 1 << stride) for i in range(lax.axis_s...  9.23 us
    dot_general x1, matrix products, shards(): jnp.einsum('tc,tw->cw', feat_docs, whole_output, preferred_element_type=j...  6.77 us
    dot_general x3, matrix products, shards(): part = jnp.dot(got, out_weight, preferred_element_type=jnp.float32)  6.51 us
    ppermute x2, starting transfers between devices, extended(): lax.ppermute(head, axis, [((i + 1) % count, i) for i in range(ends)])  5.93 us
    unnamed x59, local copies, waits for them, and re-layouts  5.58 us
    scatter-add x1, other arithmetic, place_blocks(): return holder.at[:, chosen_doc].add(grad_doc)  5.38 us
  transfers between devices with their start and end apart: 20, of which 6 were waited for; matrix products, arithmetic and copies ran while one was open for 48% of the time, Pallas kernels for 0%

profile of v10, /device:TPU:30, one launch (start us, length us, event | category | flops | bytes accessed | tf_op | source)
XLA Modules:
  0.0 171.0 jit_solution(15193477399061602743)
XLA Ops:
  7.2 2.0 %pad_maximum_fusion.5 = bf16[2,1,128,1024]{3,2,1,0:T(8,128)(2,1)} fusion(bf16[1,1,128,1024]{3,2,1,0:T(8,128)(2,1)} %bitcast.249, bf16[1,1,128,1024]{3,2,1,0:T(8,128)(2,1)} %bitcast.251), kind=kLoop, calls=%fused_computation.50 | loop fusion | flops 262144 | bytes 1048576 | tf_op jit(solution)/shard_map/stack | solution.py:58
  9.3 3.1 %collective-permute-start.1 = (bf16[2,1,128,1024]{3,2,1,0:T(8,128)(2,1)}, bf16[2,1,128,1024]{3,2,1,0:T(8,128)(2,1)}, u32[]{:S(2)}, u32[]{:S(2)}) collective-permute-start(bf16[2,1,128,1024]{3,2,1,0:T(8,128)(2,1)} %pad_maximum_fusion.5), channel_id=1, source_target_pairs={{4,0},{8,4},{12,8},{5,1},{9,5},{13,9},{6,2},{10,6},{14,10},{7,3},{... | collective-permute-start | bytes 1572872 | tf_op jit(solution)/shard_map/ppermute | solution.py:22
  13.8 2.0 %dynamic-slice_bitcast_fusion.2 = (bf16[64,1024]{1,0:T(8,128)(2,1)}, bf16[64,1024]{1,0:T(8,128)(2,1)}, bf16[64,1024]{1,0:T(8,128)(2,1)}) fusion(bf16[1,128,4096]{2,1,0:T(8,128)(2,1)} %param.11, s32[]{:T(128)S(6)} %select_n.140, s32[]{:T(128)S(6)} %select_n.142, s32[]{:T(128)S(6)} %select_n.148, s32[]{:T(128)S(6)} %select_n.145), kind=kLoop, calls=%fused_computation.121 | loop fusion | bytes 786448 | tf_op jit(solution)/shard_map/dynamic_slice | solution.py:124
  15.8 2.4 %collective-permute-start.10 = (bf16[64,1024]{1,0:T(8,128)(2,1)}, bf16[64,1024]{1,0:T(8,128)(2,1)}, u32[]{:S(2)}, u32[]{:S(2)}) collective-permute-start(bf16[64,1024]{1,0:T(8,128)(2,1)} %get-tuple-element.16), channel_id=1, source_target_pairs={{0,12},{4,8},{8,4},{12,0},{1,13},{5,9},{9,5},{13,1},{2,14},{6,10},... | collective-permute-start | bytes 393224 | tf_op jit(solution)/shard_map/ppermute | solution.py:123
  18.2 1.7 collective-permute-start.7
  21.4 1.4 convert_reduce_fusion
  26.1 5.3 %collective-permute-done.10 = bf16[64,1024]{1,0:T(8,128)(2,1)} collective-permute-done((bf16[64,1024]{1,0:T(8,128)(2,1)}, bf16[64,1024]{1,0:T(8,128)(2,1)}, u32[]{:S(2)}, u32[]{:S(2)}) %collective-permute-start.10) | collective-permute-done | bytes 131104 | tf_op jit(solution)/shard_map/ppermute | solution.py:123
  33.9 4.5 %collective-permute-done.7 = bf16[64,1024]{1,0:T(8,128)(2,1)} collective-permute-done((bf16[64,1024]{1,0:T(8,128)(2,1)}, bf16[64,1024]{1,0:T(8,128)(2,1)}, u32[]{:S(2)}, u32[]{:S(2)}) %collective-permute-start.7) | collective-permute-done | bytes 131104 | tf_op jit(solution)/shard_map/ppermute | solution.py:123
  38.4 1.7 collective-permute-start.2
  40.5 2.2 %convolution_convert_fusion = bf16[128,1024]{1,0:T(8,128)(2,1)} fusion(bf16[1024,1024]{1,0:T(8,128)(2,1)S(1)} %copy-done, bf16[64,1024]{1,0:T(8,128)(2,1)} %collective-permute-done.11, bf16[64,1024]{1,0:T(8,128)(2,1)} %collective-permute-done.10, pred[]{:T(512)S(6)} %eq.9), kind=kOutput, calls=%fused_computation.22 | convolution fusion | flops 269746176 | bytes 2621441 | tf_op jit(solution)/shard_map/dot_general | solution.py:132
  43.2 2.1 %convolution_convert_fusion.1 = bf16[128,1024]{1,0:T(8,128)(2,1)} fusion(bf16[1024,1024]{1,0:T(8,128)(2,1)S(1)} %copy-done, bf16[64,1024]{1,0:T(8,128)(2,1)S(1)} %collective-permute-done.8, bf16[64,1024]{1,0:T(8,128)(2,1)} %collective-permute-done.7, pred[]{:T(512)S(6)} %eq.9), kind=kOutput, calls=%fused_computation.23 | convolution fusion | flops 269746176 | bytes 2621441 | tf_op jit(solution)/shard_map/dot_general | solution.py:132
  47.6 1.5 collective-permute-start.9
  50.2 2.8 %gather_fusion = bf16[4,128,1024]{2,1,0:T(8,128)(2,1)} fusion(bf16[4,128,1024]{2,1,0:T(8,128)(2,1)} %pad_maximum_fusion.2, s32[1024]{0:T(1024)S(1)} %pad_clamp_fusion), kind=kCustom, calls=%fused_computation | custom fusion | bytes 2097168 | tf_op jit(solution)/shard_map/jit(_take)/gather | solution.py:138
  53.0 2.4 %bitcast_select_fusion = bf16[512,1024]{1,0:T(8,128)(2,1)} fusion(bf16[4,128,1024]{2,1,0:T(8,128)(2,1)} %gather_fusion, pred[512]{0:T(512)(128)(4,1)S(1)} %broadcast_bitcast_fusion), kind=kLoop, calls=%fused_computation.35 | loop fusion | flops 524288 | bytes 2097664 | tf_op jit(solution)/shard_map/jit(_take)/select_n | solution.py:138
  55.7 2.1 %convolution_convert_fusion.2 = bf16[128,1024]{1,0:T(8,128)(2,1)} fusion(bf16[1024,1024]{1,0:T(8,128)(2,1)S(1)} %copy-done, bf16[64,1024]{1,0:T(8,128)(2,1)} %copy-done.20, bf16[64,1024]{1,0:T(8,128)(2,1)S(1)} %collective-permute-done.4, pred[]{:T(512)S(6)} %eq.9), kind=kOutput, calls=%fused_computation.24 | convolution fusion | flops 269746176 | bytes 2621441 | tf_op jit(solution)/shard_map/dot_general | solution.py:132
  57.8 2.6 %collective-permute-start.6 = (bf16[128,1024]{1,0:T(8,128)(2,1)}, bf16[128,1024]{1,0:T(8,128)(2,1)}, u32[]{:S(2)}, u32[]{:S(2)}) collective-permute-start(bf16[128,1024]{1,0:T(8,128)(2,1)} %convolution_convert_fusion.2), channel_id=1, source_target_pairs={{0,4},{4,0},{8,12},{12,8},{1,5},{5,1},{9,13},{13,9},{2,6},{6,2},{1... | collective-permute-start | bytes 786440 | tf_op jit(solution)/shard_map/ppermute | solution.py:133
  61.7 1.8 %gather_fusion.1 = bf16[6,2,64,1024]{3,2,1,0:T(8,128)(2,1)} fusion(bf16[1,2,6,64,1024]{4,3,2,1,0:T(8,128)(2,1)S(1)} %bitcast.235, s32[6]{0:T(128)S(1)} %reshape.776), kind=kCustom, calls=%fused_computation.1 | custom fusion | bytes 3145776 | tf_op jit(solution)/shard_map/vmap()/gather | solution.py:41
  63.5 1.7 copy.202
  74.6 9.2 %collective-permute-done.3 = bf16[2,1,64,1024]{3,2,1,0:T(8,128)(2,1)S(1)} collective-permute-done((bf16[2,1,64,1024]{3,2,1,0:T(8,128)(2,1)S(1)}, bf16[2,1,64,1024]{3,2,1,0:T(8,128)(2,1)S(1)}, u32[]{:S(2)}, u32[]{:S(2)}) %collective-permute-start.3) | collective-permute-done | bytes 262176 | tf_op jit(solution)/shard_map/ppermute | solution.py:30
  86.7 1.6 multiply_reduce_fusion
  98.0 3.4 %collective-permute-start.15 = (bf16[2,1,64,1024]{3,2,0,1:T(8,128)(2,1)}, bf16[2,1,64,1024]{3,2,0,1:T(8,128)(2,1)}, u32[]{:S(2)}, u32[]{:S(2)}) collective-permute-start(bf16[2,1,64,1024]{3,2,0,1:T(8,128)(2,1)} %bitcast.220), channel_id=1, source_target_pairs={{0,4},{4,0},{8,12},{12,8},{1,5},{5,1},{9,13},{13,9},{2,6},{6,2},{1... | collective-permute-start | bytes 786440 | tf_op jit(solution)/shard_map/ppermute | solution.py:203
  105.7 3.1 %pad_maximum_fusion = f32[1,2,2,3,64,1024]{5,0,4,3,2,1:T(1,128)S(1)} fusion(f32[1,1,2,3,64,1024]{5,0,4,3,2,1:T(1,128)S(1)} %bitcast.237, f32[1,1,2,3,64,1024]{5,0,4,3,2,1:T(1,128)S(1)} %bitcast.238), kind=kLoop, calls=%fused_computation.3 | loop fusion | flops 786432 | bytes 6291456 | tf_op jit(solution)/shard_map/stack | solution.py:181
  108.7 2.4 %copy.266 = f32[1,2,2,3,64,1024]{5,4,1,3,2,0:T(8,128)} copy(f32[1,2,2,3,64,1024]{5,0,4,3,2,1:T(1,128)S(1)} %pad_maximum_fusion) | data formatting | bytes 6291456 | tf_op jit(solution)/shard_map/stack | solution.py:181
  111.7 5.4 %scatter_fusion = f32[2,6,64,1024]{3,2,1,0:T(8,128)S(1)} fusion(f32[2,6,64,1024]{3,2,1,0:T(8,128)S(1)} %broadcast.223, s32[6]{0:T(128)S(1)} %copy-done.25, f32[6,2,64,1024]{3,2,1,0:T(8,128)} %bitcast.226), kind=kCustom, calls=%fused_computation.2 | custom fusion | flops 786432 | bytes 9437208 | tf_op jit(solution)/shard_map/vmap()/scatter-add | solution.py:46
  119.4 2.8 %collective-permute-start.14 = (bf16[2,1,128,1024]{3,2,1,0:T(8,128)(2,1)}, bf16[2,1,128,1024]{3,2,1,0:T(8,128)(2,1)}, u32[]{:S(2)}, u32[]{:S(2)}) collective-permute-start(bf16[2,1,128,1024]{3,2,1,0:T(8,128)(2,1)} %get-tuple-element.12), channel_id=1, source_target_pairs={{4,0},{8,4},{12,8},{5,1},{9,5},{13,9},{6,2},{10,6},{14,10},{7,3},{... | collective-permute-start | bytes 1572872 | tf_op jit(solution)/shard_map/ppermute | solution.py:22
  122.2 1.5 collective-permute-start.13
  125.2 1.8 %convert_element_type.198 = bf16[1,128,1024]{2,1,0:T(8,128)(2,1)} reshape(bf16[1,2,64,8,128]{4,3,2,1,0:T(8,128)(2,1)} %copy-done.13) | data formatting | bytes 524288 | tf_op jit(solution)/shard_map/convert_element_type | solution.py:109
  133.4 1.8 %div.44 = f32[2,1,128,1024]{3,2,1,0:T(8,128)} reshape(f32[2,64,2,1024]{3,2,1,0:T(2,128)S(1)} %broadcast_in_dim.33) | data formatting | bytes 2097152 | tf_op jit(solution)/shard_map/div | solution.py:208
  135.2 5.0 %collective-permute-done.14 = bf16[2,1,128,1024]{3,2,1,0:T(8,128)(2,1)} collective-permute-done((bf16[2,1,128,1024]{3,2,1,0:T(8,128)(2,1)}, bf16[2,1,128,1024]{3,2,1,0:T(8,128)(2,1)}, u32[]{:S(2)}, u32[]{:S(2)}) %collective-permute-start.14) | collective-permute-done | bytes 524320 | tf_op jit(solution)/shard_map/ppermute | solution.py:22
  140.2 14.1 %collective-permute-done.13 = bf16[2,1,128,1024]{3,2,1,0:T(8,128)(2,1)} collective-permute-done((bf16[2,1,128,1024]{3,2,1,0:T(8,128)(2,1)}, bf16[2,1,128,1024]{3,2,1,0:T(8,128)(2,1)}, u32[]{:S(2)}, u32[]{:S(2)}) %collective-permute-start.13) | collective-permute-done | bytes 524320 | tf_op jit(solution)/shard_map/ppermute | solution.py:20
  154.3 2.3 %fusion.11 = bf16[2,1,128,1024]{3,2,1,0:T(8,128)(2,1)S(1)} fusion(f32[2,1,128,1024]{3,2,1,0:T(8,128)} %div.48, f32[2,1,128,1024]{3,2,1,0:T(8,128)} %div.44, f32[2,1,128,1024]{3,2,1,0:T(8,128)S(1)} %bitcast.246, bf16[2,1,128,1024]{3,2,1,0:T(8,128)(2,1)} %collective-permute-done.14, bf16[2,1,256,1024]{3,2,1,0:T(8,128)(2,1)S(1)} %bitcast.228, ...), kind=kLoop, calls=%fused_computation.30 | loop fusion | flops 4456448 | bytes 5767168 | tf_op jit(solution)/shard_map/convert.1
  157.4 6.8 %fusion.75 = f32[1024,1024]{1,0:T(8,128)} fusion(bf16[1024,1024]{1,0:T(8,128)(2,1)} %all-gather.3.cloned.1.call-done, bf16[1024,1024]{1,0:T(8,128)(2,1)} %all-gather.5.cloned.1.call-done), kind=kOutput, calls=%fused_computation.150 | convolution fusion | flops 2147483648 | bytes 8388608 | tf_op jit(solution)/shard_map/tc,tw->cw/dot_general | solution.py:143
  (165 shorter events, 51.7 us)
Async XLA Ops:
  7.2 17.7 %copy-start = (bf16[1024,1024]{1,0:T(8,128)(2,1)S(1)}, bf16[1024,1024]{1,0:T(8,128)(2,1)}, u32[]{:S(2)}) copy-start(bf16[1024,1024]{1,0:T(8,128)(2,1)} %param.10) | copy-start | bytes 6291460
  7.2 14.1 %copy-start.10 = (bf16[1,128,1024]{2,1,0:T(8,128)(2,1)S(1)}, bf16[1,128,1024]{2,1,0:T(8,128)(2,1)}, u32[]{:S(2)}) copy-start(bf16[1,128,1024]{2,1,0:T(8,128)(2,1)} %param.7) | copy-start | bytes 786436
  7.2 14.2 %copy-start.26 = (s32[1,2,2]{2,1,0:T(2,128)S(1)}, s32[1,2,2]{2,1,0:T(2,128)}, u32[]{:S(2)}) copy-start(s32[1,2,2]{2,1,0:T(2,128)} %param.9) | copy-start | bytes 52
  7.2 150.2 %all-gather.3.cloned.1.call-start = ((), (), s32[]{:S(2)}) async-start(), calls=%async_computation | async-start | bytes 3145728 | tf_op jit(solution)/shard_map/all_gather | solution.py:141
  9.3 48.5 %collective-permute-start.1 = (bf16[2,1,128,1024]{3,2,1,0:T(8,128)(2,1)}, bf16[2,1,128,1024]{3,2,1,0:T(8,128)(2,1)}, u32[]{:S(2)}, u32[]{:S(2)}) collective-permute-start(bf16[2,1,128,1024]{3,2,1,0:T(8,128)(2,1)} %pad_maximum_fusion.5), channel_id=1, source_target_pairs={{4,0},{8,4},{12,8},{5,1},{9,5},{13,9},{6,2},{10,6},{14,10},{7,3},{... | collective-permute-start | bytes 1572872 | tf_op jit(solution)/shard_map/ppermute | solution.py:22
  12.4 47.9 %collective-permute-start = (bf16[2,1,128,1024]{3,2,1,0:T(8,128)(2,1)}, bf16[2,1,128,1024]{3,2,1,0:T(8,128)(2,1)}, u32[]{:S(2)}, u32[]{:S(2)}) collective-permute-start(bf16[2,1,128,1024]{3,2,1,0:T(8,128)(2,1)} %pad_maximum_fusion.5), channel_id=1, source_target_pairs={{0,4},{4,8},{8,12},{1,5},{5,9},{9,13},{2,6},{6,10},{10,14},{3,7},{... | collective-permute-start | bytes 1572872 | tf_op jit(solution)/shard_map/ppermute | solution.py:20
  15.8 15.6 %collective-permute-start.10 = (bf16[64,1024]{1,0:T(8,128)(2,1)}, bf16[64,1024]{1,0:T(8,128)(2,1)}, u32[]{:S(2)}, u32[]{:S(2)}) collective-permute-start(bf16[64,1024]{1,0:T(8,128)(2,1)} %get-tuple-element.16), channel_id=1, source_target_pairs={{0,12},{4,8},{8,4},{12,0},{1,13},{5,9},{9,5},{13,1},{2,14},{6,10},... | collective-permute-start | bytes 393224 | tf_op jit(solution)/shard_map/ppermute | solution.py:123
  18.2 20.2 %collective-permute-start.7 = (bf16[64,1024]{1,0:T(8,128)(2,1)}, bf16[64,1024]{1,0:T(8,128)(2,1)}, u32[]{:S(2)}, u32[]{:S(2)}) collective-permute-start(bf16[64,1024]{1,0:T(8,128)(2,1)} %get-tuple-element.17), channel_id=1, source_target_pairs={{0,8},{4,12},{8,0},{12,4},{1,9},{5,13},{9,1},{13,5},{2,10},{6,14},... | collective-permute-start | bytes 393224 | tf_op jit(solution)/shard_map/ppermute | solution.py:123
  19.9 20.1 %collective-permute-start.4 = (bf16[64,1024]{1,0:T(8,128)(2,1)}, bf16[64,1024]{1,0:T(8,128)(2,1)S(1)}, u32[]{:S(2)}, u32[]{:S(2)}) collective-permute-start(bf16[64,1024]{1,0:T(8,128)(2,1)} %get-tuple-element.15), channel_id=1, source_target_pairs={{0,4},{4,0},{8,12},{12,8},{1,5},{5,1},{9,13},{13,9},{2,6},{6,2},{1... | collective-permute-start | bytes 393224 | tf_op jit(solution)/shard_map/ppermute | solution.py:123
  31.4 8.8 %collective-permute-start.11 = (bf16[64,1024]{1,0:T(8,128)(2,1)}, bf16[64,1024]{1,0:T(8,128)(2,1)}, u32[]{:S(2)}, u32[]{:S(2)}) collective-permute-start(bf16[64,1024]{1,0:T(8,128)(2,1)} %collective-permute-done.10), channel_id=1, source_target_pairs={{0,1},{1,0},{2,3},{3,2},{4,5},{5,4},{6,7},{7,6},{8,9},{9,8},{10,11... | collective-permute-start | bytes 393224 | tf_op jit(solution)/shard_map/ppermute | solution.py:30
  38.4 27.0 %collective-permute-start.2 = (f32[2,1,64,1024]{3,2,1,0:T(8,128)}, f32[2,1,64,1024]{3,2,1,0:T(8,128)}, u32[]{:S(2)}, u32[]{:S(2)}) collective-permute-start(f32[2,1,64,1024]{3,2,1,0:T(8,128)} %get-tuple-element.25), channel_id=1, source_target_pairs={{0,4},{4,0},{8,12},{12,8},{1,5},{5,1},{9,13},{13,9},{2,6},{6,2},{1... | collective-permute-start | bytes 1572872 | tf_op jit(solution)/shard_map/ppermute | solution.py:30
  40.0 2.8 %collective-permute-start.8 = (bf16[64,1024]{1,0:T(8,128)(2,1)}, bf16[64,1024]{1,0:T(8,128)(2,1)S(1)}, u32[]{:S(2)}, u32[]{:S(2)}) collective-permute-start(bf16[64,1024]{1,0:T(8,128)(2,1)} %collective-permute-done.7), channel_id=1, source_target_pairs={{0,1},{1,0},{2,3},{3,2},{4,5},{5,4},{6,7},{7,6},{8,9},{9,8},{10,11... | collective-permute-start | bytes 393224 | tf_op jit(solution)/shard_map/ppermute | solution.py:30
  40.2 7.3 %collective-permute-start.5 = (bf16[64,1024]{1,0:T(8,128)(2,1)S(1)}, bf16[64,1024]{1,0:T(8,128)(2,1)S(1)}, u32[]{:S(2)}, u32[]{:S(2)}) collective-permute-start(bf16[64,1024]{1,0:T(8,128)(2,1)S(1)} %collective-permute-done.4), channel_id=1, source_target_pairs={{0,1},{1,0},{2,3},{3,2},{4,5},{5,4},{6,7},{7,6},{8,9},{9,8},{10,11... | collective-permute-start | bytes 393224 | tf_op jit(solution)/shard_map/ppermute | solution.py:30
  42.8 27.9 %collective-permute-start.12 = (bf16[128,1024]{1,0:T(8,128)(2,1)}, bf16[128,1024]{1,0:T(8,128)(2,1)}, u32[]{:S(2)}, u32[]{:S(2)}) collective-permute-start(bf16[128,1024]{1,0:T(8,128)(2,1)} %convolution_convert_fusion), channel_id=1, source_target_pairs={{0,12},{4,8},{8,4},{12,0},{1,13},{5,9},{9,5},{13,1},{2,14},{6,10},... | collective-permute-start | bytes 786440 | tf_op jit(solution)/shard_map/ppermute | solution.py:133
  47.6 23.1 %collective-permute-start.9 = (bf16[128,1024]{1,0:T(8,128)(2,1)}, bf16[128,1024]{1,0:T(8,128)(2,1)}, u32[]{:S(2)}, u32[]{:S(2)}) collective-permute-start(bf16[128,1024]{1,0:T(8,128)(2,1)} %convolution_convert_fusion.1), channel_id=1, source_target_pairs={{0,8},{4,12},{8,0},{12,4},{1,9},{5,13},{9,1},{13,5},{2,10},{6,14},... | collective-permute-start | bytes 786440 | tf_op jit(solution)/shard_map/ppermute | solution.py:133
  55.5 101.9 %all-gather.5.cloned.1.call-start = ((), (), s32[]{:S(2)}) async-start(), calls=%async_computation.1 | async-start | bytes 2359296 | tf_op jit(solution)/shard_map/all_gather | solution.py:142
  57.8 12.9 %collective-permute-start.6 = (bf16[128,1024]{1,0:T(8,128)(2,1)}, bf16[128,1024]{1,0:T(8,128)(2,1)}, u32[]{:S(2)}, u32[]{:S(2)}) collective-permute-start(bf16[128,1024]{1,0:T(8,128)(2,1)} %convolution_convert_fusion.2), channel_id=1, source_target_pairs={{0,4},{4,0},{8,12},{12,8},{1,5},{5,1},{9,13},{13,9},{2,6},{6,2},{1... | collective-permute-start | bytes 786440 | tf_op jit(solution)/shard_map/ppermute | solution.py:133
  68.0 5.9 %copy-start.4 = (bf16[48,8,8,128]{3,2,1,0:T(8,128)(2,1)}, bf16[48,8,8,128]{3,2,1,0:T(8,128)(2,1)S(1)}, u32[]{:S(2)}) copy-start(bf16[48,8,8,128]{3,2,1,0:T(8,128)(2,1)S(1)} %copy.267) | copy-start | bytes 2359300
  70.0 13.8 %collective-permute-start.3 = (bf16[2,1,64,1024]{3,2,1,0:T(8,128)(2,1)S(1)}, bf16[2,1,64,1024]{3,2,1,0:T(8,128)(2,1)S(1)}, u32[]{:S(2)}, u32[]{:S(2)}) collective-permute-start(bf16[2,1,64,1024]{3,2,1,0:T(8,128)(2,1)S(1)} %fusion.21), channel_id=1, source_target_pairs={{0,8},{4,12},{8,0},{12,4},{1,9},{5,13},{9,1},{13,5},{2,10},{6,14},... | collective-permute-start | bytes 786440 | tf_op jit(solution)/shard_map/ppermute | solution.py:30
  72.8 11.3 %copy-start.17 = (bf16[2,64,8,128]{3,1,0,2:T(8,128)(2,1)S(1)}, bf16[2,64,8,128]{3,1,0,2:T(8,128)(2,1)}, u32[]{:S(2)}) copy-start(bf16[2,64,8,128]{3,1,0,2:T(8,128)(2,1)} %copy.213) | copy-start | bytes 786436
  94.3 7.1 %copy-start.22 = (f32[2,8,64]{2,1,0:T(8,128)S(1)}, f32[2,8,64]{2,1,0:T(8,128)}, u32[]{:S(2)}) copy-start(f32[2,8,64]{2,1,0:T(8,128)} %copy-done.21) | copy-start | bytes 12292
  95.7 33.3 %collective-permute-start.17 = (bf16[2,1,32,1024]{3,0,2,1:T(2,128)(2,1)}, bf16[2,1,32,1024]{3,0,2,1:T(2,128)(2,1)}, u32[]{:S(2)}, u32[]{:S(2)}) collective-permute-start(bf16[2,1,32,1024]{3,0,2,1:T(2,128)(2,1)} %get-tuple-element.14), channel_id=1, source_target_pairs={{0,12},{4,8},{8,4},{12,0},{1,13},{5,9},{9,5},{13,1},{2,14},{6,10},... | collective-permute-start | bytes 393224 | tf_op jit(solution)/shard_map/ppermute | solution.py:203
  96.7 32.3 %collective-permute-start.16 = (bf16[2,1,32,1024]{3,0,2,1:T(2,128)(2,1)S(1)}, bf16[2,1,32,1024]{3,0,2,1:T(2,128)(2,1)}, u32[]{:S(2)}, u32[]{:S(2)}) collective-permute-start(bf16[2,1,32,1024]{3,0,2,1:T(2,128)(2,1)S(1)} %get-tuple-element.13), channel_id=1, source_target_pairs={{0,8},{4,12},{8,0},{12,4},{1,9},{5,13},{9,1},{13,5},{2,10},{6,14},... | collective-permute-start | bytes 393224 | tf_op jit(solution)/shard_map/ppermute | solution.py:203
  98.0 33.9 %collective-permute-start.15 = (bf16[2,1,64,1024]{3,2,0,1:T(8,128)(2,1)}, bf16[2,1,64,1024]{3,2,0,1:T(8,128)(2,1)}, u32[]{:S(2)}, u32[]{:S(2)}) collective-permute-start(bf16[2,1,64,1024]{3,2,0,1:T(8,128)(2,1)} %bitcast.220), channel_id=1, source_target_pairs={{0,4},{4,0},{8,12},{12,8},{1,5},{5,1},{9,13},{13,9},{2,6},{6,2},{1... | collective-permute-start | bytes 786440 | tf_op jit(solution)/shard_map/ppermute | solution.py:203
  117.3 6.5 %copy-start.5 = (bf16[48,8,8,128]{3,2,1,0:T(8,128)(2,1)S(1)}, bf16[48,8,8,128]{3,2,1,0:T(8,128)(2,1)}, u32[]{:S(2)}) copy-start(bf16[48,8,8,128]{3,2,1,0:T(8,128)(2,1)} %copy-done.4) | copy-start | bytes 2359300
  117.3 6.5 %copy-start.7 = (bf16[2,8,64,192]{3,2,1,0:T(8,128)(2,1)S(1)}, bf16[2,8,64,192]{3,2,1,0:T(8,128)(2,1)}, u32[]{:S(2)}) copy-start(bf16[2,8,64,192]{3,2,1,0:T(8,128)(2,1)} %copy-done.6) | copy-start | bytes 1179652
  117.4 6.8 %copy-start.12 = (bf16[1,1,128,1024]{2,3,1,0:T(8,128)(2,1)S(1)}, bf16[1,1,128,1024]{2,3,1,0:T(8,128)(2,1)}, u32[]{:S(2)}) copy-start(bf16[1,1,128,1024]{2,3,1,0:T(8,128)(2,1)} %copy-done.11) | copy-start | bytes 786436
  119.4 20.7 %collective-permute-start.14 = (bf16[2,1,128,1024]{3,2,1,0:T(8,128)(2,1)}, bf16[2,1,128,1024]{3,2,1,0:T(8,128)(2,1)}, u32[]{:S(2)}, u32[]{:S(2)}) collective-permute-start(bf16[2,1,128,1024]{3,2,1,0:T(8,128)(2,1)} %get-tuple-element.12), channel_id=1, source_target_pairs={{4,0},{8,4},{12,8},{5,1},{9,5},{13,9},{6,2},{10,6},{14,10},{7,3},{... | collective-permute-start | bytes 1572872 | tf_op jit(solution)/shard_map/ppermute | solution.py:22
  122.2 32.0 %collective-permute-start.13 = (bf16[2,1,128,1024]{3,2,1,0:T(8,128)(2,1)}, bf16[2,1,128,1024]{3,2,1,0:T(8,128)(2,1)}, u32[]{:S(2)}, u32[]{:S(2)}) collective-permute-start(bf16[2,1,128,1024]{3,2,1,0:T(8,128)(2,1)} %get-tuple-element.11), channel_id=1, source_target_pairs={{0,4},{4,8},{8,12},{1,5},{5,9},{9,13},{2,6},{6,10},{10,14},{3,7},{... | collective-permute-start | bytes 1572872 | tf_op jit(solution)/shard_map/ppermute | solution.py:20
  131.9 22.4 %copy-start.3 = (bf16[2,1,4,64,1024]{4,3,2,0,1:T(8,128)(2,1)S(1)}, bf16[2,1,4,64,1024]{4,3,2,0,1:T(8,128)(2,1)}, u32[]{:S(2)}) copy-start(bf16[2,1,4,64,1024]{4,3,2,0,1:T(8,128)(2,1)} %copy-done.2) | copy-start | bytes 3145732
  131.9 22.4 %copy-start.8 = (f32[2,1,2,64,1024]{4,3,2,0,1:T(8,128)S(1)}, f32[2,1,2,64,1024]{4,3,2,0,1:T(8,128)}, u32[]{:S(2)}) copy-start(f32[2,1,2,64,1024]{4,3,2,0,1:T(8,128)} %slice.78) | copy-start | bytes 3145732
  157.4 6.8 %copy-start.1 = (bf16[1024,1024]{1,0:T(8,128)(2,1)S(1)}, bf16[1024,1024]{1,0:T(8,128)(2,1)}, u32[]{:S(2)}) copy-start(bf16[1024,1024]{1,0:T(8,128)(2,1)} %param.10) | copy-start | bytes 6291460
  (15 other events, 29.6 us)
Sparse Core Ops, SparseCore 0:
  55.6 34.1 all-gather.2
  94.1 58.6 all-gather.4

commit v11 on v10

--- a/solution.py
+++ b/solution.py
@@ -67,6 +67,8 @@
     own_level = pooled
     for level_no in range(levels):
         other = swapped(own_level, "seq", level_no)
+        if level_no == 0:
+            cotangent, other = lax.optimization_barrier((cotangent, other))
         siblings.append(other)
         if level_no + 1 < levels:
             upper = position >> level_no & 1 == 1

time: 172 us -> 200 us (1.16)
  the two profiles are of different devices: /device:TPU:30 before, /device:TPU:6 now
where the time goes in v11:
time: 200 us; the launch traced here: 197 us
  waiting for transfers between devices  49 us (24%)
  other arithmetic  40.1 us (20%)
  local copies, waits for them, and re-layouts  35.5 us (18%)
  starting transfers between devices  31.7 us (16%)
  matrix products  25.6 us (13%)
  between operations  14.7 us (7%)
    all_gather x1, waiting for transfers between devices, shards(): whole_output = lax.all_gather(out_rows, ('dp', 'seq'), axis=0, tiled=True)  21.2 us
    ppermute x2, starting transfers between devices, extended(): lax.ppermute(tail, axis, [(i, (i + 1) % count) for i in range(ends)])  10.7 us
    ppermute x3, waiting for transfers between devices, shards(): lax.ppermute(lax.dynamic_slice_in_dim(sent, core * half, half, axis=0), '...  10.3 us
    ppermute x3, waiting for transfers between devices, shards(): back = lax.ppermute(part.astype(jnp.bfloat16), 'seq', pairs)  8.05 us
    dot_general x1, matrix products, shards(): jnp.einsum('tc,tw->cw', feat_docs, whole_output, preferred_element_type=j...  6.77 us
    ppermute x2, waiting for transfers between devices, extended(): lax.ppermute(head, axis, [((i + 1) % count, i) for i in range(ends)])  6.67 us
    dot_general x3, matrix products, shards(): part = jnp.dot(got, out_weight, preferred_element_type=jnp.float32)  6.63 us
    gather x5, local copies, waits for them, and re-layouts, pick_blocks(): return blocks_doc[:, chosen_doc]  5.49 us
  transfers between devices with their start and end apart: 20, of which 8 were waited for; matrix products, arithmetic and copies ran while one was open for 42% of the time, Pallas kernels for 0%

profile of v11, /device:TPU:6, one launch (start us, length us, event | category | flops | bytes accessed | tf_op | source)
XLA Modules:
  0.0 196.5 jit_solution(859610135531328627)
XLA Ops:
  7.2 2.0 %pad_maximum_fusion.5 = bf16[2,1,128,1024]{3,2,1,0:T(8,128)(2,1)} fusion(bf16[1,1,128,1024]{3,2,1,0:T(8,128)(2,1)} %bitcast.249, bf16[1,1,128,1024]{3,2,1,0:T(8,128)(2,1)} %bitcast.251), kind=kLoop, calls=%fused_computation.50 | loop fusion | flops 262144 | bytes 1048576 | tf_op jit(solution)/shard_map/stack | solution.py:58
  10.7 5.4 %collective-permute-start = (bf16[2,1,128,1024]{3,2,1,0:T(8,128)(2,1)}, bf16[2,1,128,1024]{3,2,1,0:T(8,128)(2,1)}, u32[]{:S(2)}, u32[]{:S(2)}) collective-permute-start(bf16[2,1,128,1024]{3,2,1,0:T(8,128)(2,1)} %pad_maximum_fusion.5), channel_id=1, source_target_pairs={{0,4},{4,8},{8,12},{1,5},{5,9},{9,13},{2,6},{6,10},{10,14},{3,7},{... | collective-permute-start | bytes 1572872 | tf_op jit(solution)/shard_map/ppermute | solution.py:20
  24.4 1.9 collective-permute-done.1
  27.9 2.5 %pad_maximum_fusion.1 = bf16[2,1,384,1024]{3,2,1,0:T(8,128)(2,1)} fusion(bf16[2,1,128,1024]{3,2,1,0:T(8,128)(2,1)} %collective-permute-done.1, bf16[1,1,128,1024]{3,2,1,0:T(8,128)(2,1)S(1)} %bitcast.250, bf16[1,1,128,1024]{3,2,1,0:T(8,128)(2,1)S(1)} %bitcast.252, bf16[2,1,128,1024]{3,2,1,0:T(8,128)(2,1)} %collective-permute-done), kind=kLoop, calls=%fused_computation.5 | loop fusion | flops 6291456 | bytes 3145728 | tf_op jit(solution)/shard_map/concatenate | solution.py:18
  30.4 3.3 %gather_fusion.1 = bf16[6,2,64,1024]{3,2,1,0:T(8,128)(2,1)} fusion(bf16[1,2,6,64,1024]{4,3,2,1,0:T(8,128)(2,1)} %bitcast.235, s32[6]{0:T(128)S(1)} %reshape.776), kind=kCustom, calls=%fused_computation.1 | custom fusion | bytes 3145776 | tf_op jit(solution)/shard_map/vmap()/gather | solution.py:41
  33.6 1.6 copy.202
  39.0 1.8 copy.208
  40.8 2.9 %reduce_sum.55 = f32[2,64,1024]{2,0,1:T(2,128)} reduce(f32[2,64,2,1024]{3,0,2,1:T(2,128)} %bitcast.245, f32[]{:T(128)} %constant.103.clone.1), dimensions={2}, to_apply=%region_2.3 | reduce | flops 131072 | bytes 1572868 | tf_op jit(solution)/shard_map/reduce_sum | solution.py:37
  44.8 3.4 %collective-permute-start.3 = (bf16[2,1,64,1024]{3,2,1,0:T(8,128)(2,1)S(1)}, bf16[2,1,64,1024]{3,2,1,0:T(8,128)(2,1)S(1)}, u32[]{:S(2)}, u32[]{:S(2)}) collective-permute-start(bf16[2,1,64,1024]{3,2,1,0:T(8,128)(2,1)S(1)} %fusion.21), channel_id=1, source_target_pairs={{0,8},{4,12},{8,0},{12,4},{1,9},{5,13},{9,1},{13,5},{2,10},{6,14},... | collective-permute-start | bytes 786440 | tf_op jit(solution)/shard_map/ppermute | solution.py:30
  49.6 2.0 %collective-permute-start.10 = (bf16[64,1024]{1,0:T(8,128)(2,1)S(1)}, bf16[64,1024]{1,0:T(8,128)(2,1)S(1)}, u32[]{:S(2)}, u32[]{:S(2)}) collective-permute-start(bf16[64,1024]{1,0:T(8,128)(2,1)S(1)} %get-tuple-element.20), channel_id=1, source_target_pairs={{0,12},{4,8},{8,4},{12,0},{1,13},{5,9},{9,5},{13,1},{2,14},{6,10},... | collective-permute-start | bytes 393224 | tf_op jit(solution)/shard_map/ppermute | solution.py:125
  51.6 2.0 %collective-permute-start.7 = (bf16[64,1024]{1,0:T(8,128)(2,1)S(1)}, bf16[64,1024]{1,0:T(8,128)(2,1)}, u32[]{:S(2)}, u32[]{:S(2)}) collective-permute-start(bf16[64,1024]{1,0:T(8,128)(2,1)S(1)} %get-tuple-element.21), channel_id=1, source_target_pairs={{0,8},{4,12},{8,0},{12,4},{1,9},{5,13},{9,1},{13,5},{2,10},{6,14},... | collective-permute-start | bytes 393224 | tf_op jit(solution)/shard_map/ppermute | solution.py:125
  56.3 1.6 fusion.74
  60.3 10.1 %collective-permute-done.7 = bf16[64,1024]{1,0:T(8,128)(2,1)} collective-permute-done((bf16[64,1024]{1,0:T(8,128)(2,1)S(1)}, bf16[64,1024]{1,0:T(8,128)(2,1)}, u32[]{:S(2)}, u32[]{:S(2)}) %collective-permute-start.7) | collective-permute-done | bytes 131104 | tf_op jit(solution)/shard_map/ppermute | solution.py:125
  73.4 1.6 fusion.13
  76.0 2.1 %convolution_convert_fusion = bf16[128,1024]{1,0:T(8,128)(2,1)} fusion(bf16[1024,1024]{1,0:T(8,128)(2,1)S(1)} %copy-done, bf16[64,1024]{1,0:T(8,128)(2,1)} %collective-permute-done.11, bf16[64,1024]{1,0:T(8,128)(2,1)S(1)} %collective-permute-done.10, pred[]{:T(512)S(6)} %eq.9), kind=kOutput, calls=%fused_computation.22 | convolution fusion | flops 269746176 | bytes 2621441 | tf_op jit(solution)/shard_map/dot_general | solution.py:134
  78.1 3.5 %collective-permute-start.12 = (bf16[128,1024]{1,0:T(8,128)(2,1)}, bf16[128,1024]{1,0:T(8,128)(2,1)}, u32[]{:S(2)}, u32[]{:S(2)}) collective-permute-start(bf16[128,1024]{1,0:T(8,128)(2,1)} %convolution_convert_fusion), channel_id=1, source_target_pairs={{0,12},{4,8},{8,4},{12,0},{1,13},{5,9},{9,5},{13,1},{2,14},{6,10},... | collective-permute-start | bytes 786440 | tf_op jit(solution)/shard_map/ppermute | solution.py:135
  81.7 2.2 %convolution_convert_fusion.1 = bf16[128,1024]{1,0:T(8,128)(2,1)} fusion(bf16[1024,1024]{1,0:T(8,128)(2,1)S(1)} %copy-done, bf16[64,1024]{1,0:T(8,128)(2,1)} %collective-permute-done.8, bf16[64,1024]{1,0:T(8,128)(2,1)} %collective-permute-done.7, pred[]{:T(512)S(6)} %eq.9), kind=kOutput, calls=%fused_computation.23 | convolution fusion | flops 269746176 | bytes 2621441 | tf_op jit(solution)/shard_map/dot_general | solution.py:134
  83.9 2.2 %convolution_convert_fusion.2 = bf16[128,1024]{1,0:T(8,128)(2,1)} fusion(bf16[1024,1024]{1,0:T(8,128)(2,1)S(1)} %copy-done, bf16[64,1024]{1,0:T(8,128)(2,1)} %collective-permute-done.5, bf16[64,1024]{1,0:T(8,128)(2,1)} %collective-permute-done.4, pred[]{:T(512)S(6)} %eq.9), kind=kOutput, calls=%fused_computation.24 | convolution fusion | flops 269746176 | bytes 2621441 | tf_op jit(solution)/shard_map/dot_general | solution.py:134
  92.9 2.5 %convolution_bitcast_fusion.2 = f32[1,2,64,8,128]{4,2,3,1,0:T(8,128)} fusion(bf16[2,192,8,128]{3,2,1,0:T(8,128)(2,1)} %bitcast.265, f32[2,8,64,192]{3,2,1,0:T(8,128)S(1)} %copy-done.2, f32[2,8,64]{2,1,0:T(8,128)S(1)} %copy-done.26, f32[2,8,64]{2,1,0:T(8,128)S(1)} %copy_maximum_fusion), kind=kOutput, calls=%fused_computation.11 | convolution fusion | flops 50921472 | bytes 2105344 | tf_op jit(solution)/shard_map/dbhqk,dbkhe->dbqhe/dot_general | solution.py:105
  95.5 8.0 %collective-permute-done.9 = bf16[128,1024]{1,0:T(8,128)(2,1)} collective-permute-done((bf16[128,1024]{1,0:T(8,128)(2,1)}, bf16[128,1024]{1,0:T(8,128)(2,1)}, u32[]{:S(2)}, u32[]{:S(2)}) %collective-permute-start.9) | collective-permute-done | bytes 262176 | tf_op jit(solution)/shard_map/ppermute | solution.py:135
  105.8 1.6 multiply_reduce_fusion
  114.5 3.2 %collective-permute-start.15 = (bf16[2,1,64,1024]{3,2,0,1:T(8,128)(2,1)}, bf16[2,1,64,1024]{3,2,0,1:T(8,128)(2,1)}, u32[]{:S(2)}, u32[]{:S(2)}) collective-permute-start(bf16[2,1,64,1024]{3,2,0,1:T(8,128)(2,1)} %bitcast.220), channel_id=1, source_target_pairs={{0,4},{4,0},{8,12},{12,8},{1,5},{5,1},{9,13},{13,9},{2,6},{6,2},{1... | collective-permute-start | bytes 786440 | tf_op jit(solution)/shard_map/ppermute | solution.py:205
  122.0 3.1 %pad_maximum_fusion = f32[1,2,2,3,64,1024]{5,0,4,3,2,1:T(1,128)S(1)} fusion(f32[1,1,2,3,64,1024]{5,0,4,3,2,1:T(1,128)S(1)} %bitcast.237, f32[1,1,2,3,64,1024]{5,0,4,3,2,1:T(1,128)S(1)} %bitcast.238), kind=kLoop, calls=%fused_computation.3 | loop fusion | flops 786432 | bytes 6291456 | tf_op jit(solution)/shard_map/stack | solution.py:183
  125.1 2.4 %copy.266 = f32[1,2,2,3,64,1024]{5,4,1,3,2,0:T(8,128)} copy(f32[1,2,2,3,64,1024]{5,0,4,3,2,1:T(1,128)S(1)} %pad_maximum_fusion) | data formatting | bytes 6291456 | tf_op jit(solution)/shard_map/stack | solution.py:183
  128.1 5.4 %scatter_fusion = f32[2,6,64,1024]{3,2,1,0:T(8,128)S(1)} fusion(f32[2,6,64,1024]{3,2,1,0:T(8,128)S(1)} %broadcast.223, s32[6]{0:T(128)S(1)} %copy-done.30, f32[6,2,64,1024]{3,2,1,0:T(8,128)} %bitcast.226), kind=kCustom, calls=%fused_computation.2 | custom fusion | flops 786432 | bytes 9437208 | tf_op jit(solution)/shard_map/vmap()/scatter-add | solution.py:46
  137.1 5.3 %collective-permute-start.13 = (bf16[2,1,128,1024]{3,2,1,0:T(8,128)(2,1)}, bf16[2,1,128,1024]{3,2,1,0:T(8,128)(2,1)}, u32[]{:S(2)}, u32[]{:S(2)}) collective-permute-start(bf16[2,1,128,1024]{3,2,1,0:T(8,128)(2,1)} %get-tuple-element.15), channel_id=1, source_target_pairs={{0,4},{4,8},{8,12},{1,5},{5,9},{9,13},{2,6},{6,10},{10,14},{3,7},{... | collective-permute-start | bytes 1572872 | tf_op jit(solution)/shard_map/ppermute | solution.py:20
  143.9 1.8 convert_element_type.198
  152.1 1.8 div.44
  153.9 4.7 %collective-permute-done.14 = bf16[2,1,128,1024]{3,2,1,0:T(8,128)(2,1)} collective-permute-done((bf16[2,1,128,1024]{3,2,1,0:T(8,128)(2,1)}, bf16[2,1,128,1024]{3,2,1,0:T(8,128)(2,1)}, u32[]{:S(2)}, u32[]{:S(2)}) %collective-permute-start.14) | collective-permute-done | bytes 524320 | tf_op jit(solution)/shard_map/ppermute | solution.py:22
  158.6 2.3 %fusion.11 = bf16[2,1,128,1024]{3,2,1,0:T(8,128)(2,1)S(1)} fusion(f32[2,1,128,1024]{3,2,1,0:T(8,128)} %div.48, f32[2,1,128,1024]{3,2,1,0:T(8,128)} %div.44, f32[2,1,128,1024]{3,2,1,0:T(8,128)S(1)} %bitcast.246, bf16[2,1,128,1024]{3,2,1,0:T(8,128)(2,1)} %collective-permute-done.14, bf16[2,1,256,1024]{3,2,1,0:T(8,128)(2,1)S(1)} %bitcast.228, ...), kind=kLoop, calls=%fused_computation.30 | loop fusion | flops 4456448 | bytes 5767168 | tf_op jit(solution)/shard_map/convert.1
  161.7 21.2 %all-gather.5.cloned.1.call-done = bf16[1024,1024]{1,0:T(8,128)(2,1)} async-done(((bf16[128,1024]{1,0:T(8,128)(2,1)}), bf16[1024,1024]{1,0:T(8,128)(2,1)}) %all-gather.5.cloned.1.call-update) | async-done | bytes 2097168 | tf_op jit(solution)/shard_map/all_gather | solution.py:144
  182.9 6.8 %fusion.75 = f32[1024,1024]{1,0:T(8,128)} fusion(bf16[1024,1024]{1,0:T(8,128)(2,1)} %all-gather.3.cloned.1.call-done, bf16[1024,1024]{1,0:T(8,128)(2,1)} %all-gather.5.cloned.1.call-done), kind=kOutput, calls=%fused_computation.150 | convolution fusion | flops 2147483648 | bytes 8388608 | tf_op jit(solution)/shard_map/tc,tw->cw/dot_general | solution.py:145
  (177 shorter events, 59.6 us)
Async XLA Ops:
  7.2 47.9 %copy-start = (bf16[1024,1024]{1,0:T(8,128)(2,1)S(1)}, bf16[1024,1024]{1,0:T(8,128)(2,1)}, u32[]{:S(2)}) copy-start(bf16[1024,1024]{1,0:T(8,128)(2,1)} %param.10) | copy-start | bytes 6291460
  7.2 154.6 %all-gather.3.cloned.1.call-start = ((), (), s32[]{:S(2)}) async-start(), calls=%async_computation | async-start | bytes 3145728 | tf_op jit(solution)/shard_map/all_gather | solution.py:143
  9.2 12.3 %copy-start.31 = (s32[1,2,2]{2,1,0:T(2,128)S(1)}, s32[1,2,2]{2,1,0:T(2,128)}, u32[]{:S(2)}) copy-start(s32[1,2,2]{2,1,0:T(2,128)} %param.9) | copy-start | bytes 52
  9.2 12.5 %copy-start.25 = (bf16[1,128,1024]{2,1,0:T(8,128)(2,1)S(1)}, bf16[1,128,1024]{2,1,0:T(8,128)(2,1)}, u32[]{:S(2)}) copy-start(bf16[1,128,1024]{2,1,0:T(8,128)(2,1)} %param.6) | copy-start | bytes 786436
  9.2 17.1 %collective-permute-start.1 = (bf16[2,1,128,1024]{3,2,1,0:T(8,128)(2,1)}, bf16[2,1,128,1024]{3,2,1,0:T(8,128)(2,1)}, u32[]{:S(2)}, u32[]{:S(2)}) collective-permute-start(bf16[2,1,128,1024]{3,2,1,0:T(8,128)(2,1)} %pad_maximum_fusion.5), channel_id=1, source_target_pairs={{4,0},{8,4},{12,8},{5,1},{9,5},{13,9},{6,2},{10,6},{14,10},{7,3},{... | collective-permute-start | bytes 1572872 | tf_op jit(solution)/shard_map/ppermute | solution.py:22
  10.7 17.2 %collective-permute-start = (bf16[2,1,128,1024]{3,2,1,0:T(8,128)(2,1)}, bf16[2,1,128,1024]{3,2,1,0:T(8,128)(2,1)}, u32[]{:S(2)}, u32[]{:S(2)}) collective-permute-start(bf16[2,1,128,1024]{3,2,1,0:T(8,128)(2,1)} %pad_maximum_fusion.5), channel_id=1, source_target_pairs={{0,4},{4,8},{8,12},{1,5},{5,9},{9,13},{2,6},{6,10},{10,14},{3,7},{... | collective-permute-start | bytes 1572872 | tf_op jit(solution)/shard_map/ppermute | solution.py:20
  17.1 10.8 %copy-start.11 = (bf16[1,128,1024]{2,1,0:T(8,128)(2,1)S(1)}, bf16[1,128,1024]{2,1,0:T(8,128)(2,1)}, u32[]{:S(2)}) copy-start(bf16[1,128,1024]{2,1,0:T(8,128)(2,1)} %param.8) | copy-start | bytes 786436
  17.1 10.8 %copy-start.12 = (bf16[1,128,1024]{2,1,0:T(8,128)(2,1)S(1)}, bf16[1,128,1024]{2,1,0:T(8,128)(2,1)}, u32[]{:S(2)}) copy-start(bf16[1,128,1024]{2,1,0:T(8,128)(2,1)} %param.7) | copy-start | bytes 786436
  20.8 16.9 %collective-permute-start.2 = (f32[2,1,64,1024]{3,2,1,0:T(8,128)}, f32[2,1,64,1024]{3,2,1,0:T(8,128)}, u32[]{:S(2)}, u32[]{:S(2)}) collective-permute-start(f32[2,1,64,1024]{3,2,1,0:T(8,128)} %get-tuple-element.29), channel_id=1, source_target_pairs={{0,4},{4,0},{8,12},{12,8},{1,5},{5,1},{9,13},{13,9},{2,6},{6,2},{1... | collective-permute-start | bytes 1572872 | tf_op jit(solution)/shard_map/ppermute | solution.py:30
  36.4 19.9 %copy-start.5 = (bf16[48,8,8,128]{3,2,1,0:T(8,128)(2,1)}, bf16[48,8,8,128]{3,2,1,0:T(8,128)(2,1)S(1)}, u32[]{:S(2)}) copy-start(bf16[48,8,8,128]{3,2,1,0:T(8,128)(2,1)S(1)} %copy.267) | copy-start | bytes 2359300
  44.8 26.1 %collective-permute-start.3 = (bf16[2,1,64,1024]{3,2,1,0:T(8,128)(2,1)S(1)}, bf16[2,1,64,1024]{3,2,1,0:T(8,128)(2,1)S(1)}, u32[]{:S(2)}, u32[]{:S(2)}) collective-permute-start(bf16[2,1,64,1024]{3,2,1,0:T(8,128)(2,1)S(1)} %fusion.21), channel_id=1, source_target_pairs={{0,8},{4,12},{8,0},{12,4},{1,9},{5,13},{9,1},{13,5},{2,10},{6,14},... | collective-permute-start | bytes 786440 | tf_op jit(solution)/shard_map/ppermute | solution.py:30
  49.6 10.7 %collective-permute-start.10 = (bf16[64,1024]{1,0:T(8,128)(2,1)S(1)}, bf16[64,1024]{1,0:T(8,128)(2,1)S(1)}, u32[]{:S(2)}, u32[]{:S(2)}) collective-permute-start(bf16[64,1024]{1,0:T(8,128)(2,1)S(1)} %get-tuple-element.20), channel_id=1, source_target_pairs={{0,12},{4,8},{8,4},{12,0},{1,13},{5,9},{9,5},{13,1},{2,14},{6,10},... | collective-permute-start | bytes 393224 | tf_op jit(solution)/shard_map/ppermute | solution.py:125
  51.6 18.8 %collective-permute-start.7 = (bf16[64,1024]{1,0:T(8,128)(2,1)S(1)}, bf16[64,1024]{1,0:T(8,128)(2,1)}, u32[]{:S(2)}, u32[]{:S(2)}) collective-permute-start(bf16[64,1024]{1,0:T(8,128)(2,1)S(1)} %get-tuple-element.21), channel_id=1, source_target_pairs={{0,8},{4,12},{8,0},{12,4},{1,9},{5,13},{9,1},{13,5},{2,10},{6,14},... | collective-permute-start | bytes 393224 | tf_op jit(solution)/shard_map/ppermute | solution.py:125
  54.5 15.9 %collective-permute-start.4 = (bf16[64,1024]{1,0:T(8,128)(2,1)S(1)}, bf16[64,1024]{1,0:T(8,128)(2,1)}, u32[]{:S(2)}, u32[]{:S(2)}) collective-permute-start(bf16[64,1024]{1,0:T(8,128)(2,1)S(1)} %get-tuple-element.19), channel_id=1, source_target_pairs={{0,4},{4,0},{8,12},{12,8},{1,5},{5,1},{9,13},{13,9},{2,6},{6,2},{1... | collective-permute-start | bytes 393224 | tf_op jit(solution)/shard_map/ppermute | solution.py:125
  60.3 15.7 %collective-permute-start.11 = (bf16[64,1024]{1,0:T(8,128)(2,1)S(1)}, bf16[64,1024]{1,0:T(8,128)(2,1)}, u32[]{:S(2)}, u32[]{:S(2)}) collective-permute-start(bf16[64,1024]{1,0:T(8,128)(2,1)S(1)} %collective-permute-done.10), channel_id=1, source_target_pairs={{0,1},{1,0},{2,3},{3,2},{4,5},{5,4},{6,7},{7,6},{8,9},{9,8},{10,11... | collective-permute-start | bytes 393224 | tf_op jit(solution)/shard_map/ppermute | solution.py:30
  70.4 11.3 %collective-permute-start.8 = (bf16[64,1024]{1,0:T(8,128)(2,1)}, bf16[64,1024]{1,0:T(8,128)(2,1)}, u32[]{:S(2)}, u32[]{:S(2)}) collective-permute-start(bf16[64,1024]{1,0:T(8,128)(2,1)} %collective-permute-done.7), channel_id=1, source_target_pairs={{0,1},{1,0},{2,3},{3,2},{4,5},{5,4},{6,7},{7,6},{8,9},{9,8},{10,11... | collective-permute-start | bytes 393224 | tf_op jit(solution)/shard_map/ppermute | solution.py:30
  70.4 13.5 %collective-permute-start.5 = (bf16[64,1024]{1,0:T(8,128)(2,1)}, bf16[64,1024]{1,0:T(8,128)(2,1)}, u32[]{:S(2)}, u32[]{:S(2)}) collective-permute-start(bf16[64,1024]{1,0:T(8,128)(2,1)} %collective-permute-done.4), channel_id=1, source_target_pairs={{0,1},{1,0},{2,3},{3,2},{4,5},{5,4},{6,7},{7,6},{8,9},{9,8},{10,11... | collective-permute-start | bytes 393224 | tf_op jit(solution)/shard_map/ppermute | solution.py:30
  78.1 17.4 %collective-permute-start.12 = (bf16[128,1024]{1,0:T(8,128)(2,1)}, bf16[128,1024]{1,0:T(8,128)(2,1)}, u32[]{:S(2)}, u32[]{:S(2)}) collective-permute-start(bf16[128,1024]{1,0:T(8,128)(2,1)} %convolution_convert_fusion), channel_id=1, source_target_pairs={{0,12},{4,8},{8,4},{12,0},{1,13},{5,9},{9,5},{13,1},{2,14},{6,10},... | collective-permute-start | bytes 786440 | tf_op jit(solution)/shard_map/ppermute | solution.py:135
  83.9 19.7 %collective-permute-start.9 = (bf16[128,1024]{1,0:T(8,128)(2,1)}, bf16[128,1024]{1,0:T(8,128)(2,1)}, u32[]{:S(2)}, u32[]{:S(2)}) collective-permute-start(bf16[128,1024]{1,0:T(8,128)(2,1)} %convolution_convert_fusion.1), channel_id=1, source_target_pairs={{0,8},{4,12},{8,0},{12,4},{1,9},{5,13},{9,1},{13,5},{2,10},{6,14},... | collective-permute-start | bytes 786440 | tf_op jit(solution)/shard_map/ppermute | solution.py:135
  86.2 17.4 %collective-permute-start.6 = (bf16[128,1024]{1,0:T(8,128)(2,1)}, bf16[128,1024]{1,0:T(8,128)(2,1)}, u32[]{:S(2)}, u32[]{:S(2)}) collective-permute-start(bf16[128,1024]{1,0:T(8,128)(2,1)} %convolution_convert_fusion.2), channel_id=1, source_target_pairs={{0,4},{4,0},{8,12},{12,8},{1,5},{5,1},{9,13},{13,9},{2,6},{6,2},{1... | collective-permute-start | bytes 786440 | tf_op jit(solution)/shard_map/ppermute | solution.py:135
  92.6 90.3 %all-gather.5.cloned.1.call-start = ((), (), s32[]{:S(2)}) async-start(), calls=%async_computation.1 | async-start | bytes 2359296 | tf_op jit(solution)/shard_map/all_gather | solution.py:144
  92.9 10.7 %copy-start.19 = (f32[128,1024]{1,0:T(8,128)S(1)}, f32[128,1024]{1,0:T(8,128)}, u32[]{:S(2)}) copy-start(f32[128,1024]{1,0:T(8,128)} %fusion.45) | copy-start | bytes 1572868
  95.5 10.3 %copy-start.23 = (bf16[48,8,8,128]{3,2,1,0:T(8,128)(2,1)S(1)}, bf16[48,8,8,128]{3,2,1,0:T(8,128)(2,1)}, u32[]{:S(2)}) copy-start(bf16[48,8,8,128]{3,2,1,0:T(8,128)(2,1)} %copy.269) | copy-start | bytes 2359300
  112.1 35.6 %collective-permute-start.17 = (bf16[2,1,32,1024]{3,0,2,1:T(2,128)(2,1)}, bf16[2,1,32,1024]{3,0,2,1:T(2,128)(2,1)}, u32[]{:S(2)}, u32[]{:S(2)}) collective-permute-start(bf16[2,1,32,1024]{3,0,2,1:T(2,128)(2,1)} %get-tuple-element.18), channel_id=1, source_target_pairs={{0,12},{4,8},{8,4},{12,0},{1,13},{5,9},{9,5},{13,1},{2,14},{6,10},... | collective-permute-start | bytes 393224 | tf_op jit(solution)/shard_map/ppermute | solution.py:205
  113.3 34.4 %collective-permute-start.16 = (bf16[2,1,32,1024]{3,0,2,1:T(2,128)(2,1)S(1)}, bf16[2,1,32,1024]{3,0,2,1:T(2,128)(2,1)}, u32[]{:S(2)}, u32[]{:S(2)}) collective-permute-start(bf16[2,1,32,1024]{3,0,2,1:T(2,128)(2,1)S(1)} %get-tuple-element.17), channel_id=1, source_target_pairs={{0,8},{4,12},{8,0},{12,4},{1,9},{5,13},{9,1},{13,5},{2,10},{6,14},... | collective-permute-start | bytes 393224 | tf_op jit(solution)/shard_map/ppermute | solution.py:205
  114.5 36.0 %collective-permute-start.15 = (bf16[2,1,64,1024]{3,2,0,1:T(8,128)(2,1)}, bf16[2,1,64,1024]{3,2,0,1:T(8,128)(2,1)}, u32[]{:S(2)}, u32[]{:S(2)}) collective-permute-start(bf16[2,1,64,1024]{3,2,0,1:T(8,128)(2,1)} %bitcast.220), channel_id=1, source_target_pairs={{0,4},{4,0},{8,12},{12,8},{1,5},{5,1},{9,13},{13,9},{2,6},{6,2},{1... | collective-permute-start | bytes 786440 | tf_op jit(solution)/shard_map/ppermute | solution.py:205
  133.6 8.8 %copy-start.6 = (bf16[48,8,8,128]{3,2,1,0:T(8,128)(2,1)S(1)}, bf16[48,8,8,128]{3,2,1,0:T(8,128)(2,1)}, u32[]{:S(2)}) copy-start(bf16[48,8,8,128]{3,2,1,0:T(8,128)(2,1)} %copy-done.5) | copy-start | bytes 2359300
  133.6 8.8 %copy-start.8 = (bf16[2,8,64,192]{3,2,1,0:T(8,128)(2,1)S(1)}, bf16[2,8,64,192]{3,2,1,0:T(8,128)(2,1)}, u32[]{:S(2)}) copy-start(bf16[2,8,64,192]{3,2,1,0:T(8,128)(2,1)} %copy-done.7) | copy-start | bytes 1179652
  133.7 9.1 %copy-start.14 = (bf16[1,1,128,1024]{2,3,1,0:T(8,128)(2,1)S(1)}, bf16[1,1,128,1024]{2,3,1,0:T(8,128)(2,1)}, u32[]{:S(2)}) copy-start(bf16[1,1,128,1024]{2,3,1,0:T(8,128)(2,1)} %copy-done.13) | copy-start | bytes 786436
  135.8 22.8 %collective-permute-start.14 = (bf16[2,1,128,1024]{3,2,1,0:T(8,128)(2,1)}, bf16[2,1,128,1024]{3,2,1,0:T(8,128)(2,1)}, u32[]{:S(2)}, u32[]{:S(2)}) collective-permute-start(bf16[2,1,128,1024]{3,2,1,0:T(8,128)(2,1)} %get-tuple-element.16), channel_id=1, source_target_pairs={{4,0},{8,4},{12,8},{5,1},{9,5},{13,9},{6,2},{10,6},{14,10},{7,3},{... | collective-permute-start | bytes 1572872 | tf_op jit(solution)/shard_map/ppermute | solution.py:22
  137.1 21.5 %collective-permute-start.13 = (bf16[2,1,128,1024]{3,2,1,0:T(8,128)(2,1)}, bf16[2,1,128,1024]{3,2,1,0:T(8,128)(2,1)}, u32[]{:S(2)}, u32[]{:S(2)}) collective-permute-start(bf16[2,1,128,1024]{3,2,1,0:T(8,128)(2,1)} %get-tuple-element.15), channel_id=1, source_target_pairs={{0,4},{4,8},{8,12},{1,5},{5,9},{9,13},{2,6},{6,10},{10,14},{3,7},{... | collective-permute-start | bytes 1572872 | tf_op jit(solution)/shard_map/ppermute | solution.py:20
  150.6 8.1 %copy-start.9 = (f32[2,1,2,64,1024]{4,3,2,0,1:T(8,128)S(1)}, f32[2,1,2,64,1024]{4,3,2,0,1:T(8,128)}, u32[]{:S(2)}) copy-start(f32[2,1,2,64,1024]{4,3,2,0,1:T(8,128)} %slice.78) | copy-start | bytes 3145732
  (21 other events, 63.9 us)
Sparse Core Ops, SparseCore 0:
  92.7 33.3 all-gather.2
  128.2 54.6 all-gather.4

commit v12 on v10

--- a/solution.py
+++ b/solution.py
@@ -118,17 +118,7 @@
         sent = lax.dynamic_slice_in_dim(
             cot_rows, (position ^ step) * feat_count, feat_count, axis=1
         )
-        half = sent.shape[0] // 2
-        core = lax.axis_index("head")
-        got_half = lax.ppermute(
-            lax.dynamic_slice_in_dim(sent, core * half, half, axis=0), "seq", pairs
-        )
-        other_half = swapped(got_half, "head", 0)
-        got = jnp.where(
-            core == 0,
-            jnp.concatenate([got_half, other_half], axis=0),
-            jnp.concatenate([other_half, got_half], axis=0),
-        )
+        got = lax.ppermute(sent, "seq", pairs)
         part = jnp.dot(got, out_weight, preferred_element_type=jnp.float32)
         back = lax.ppermute(part.astype(jnp.bfloat16), "seq", pairs)
         grad_sum = grad_sum + back.astype(jnp.float32)

time: 172 us -> 176 us (1.023)
  the two profiles are of different devices: /device:TPU:30 before, /device:TPU:6 now
where the time goes in v12:
time: 176 us; the launch traced here: 174 us
  local copies, waits for them, and re-layouts  36.6 us (21%)
  waiting for transfers between devices  34.8 us (20%)
  starting transfers between devices  33.5 us (19%)
  other arithmetic  32.4 us (18%)
  matrix products  21.7 us (12%)
  between operations  14.7 us (8%)
    ppermute x3, waiting for transfers between devices, shards(): got = lax.ppermute(sent, 'seq', pairs)  20.5 us
    ppermute x3, starting transfers between devices, shards(): back = lax.ppermute(part.astype(jnp.bfloat16), 'seq', pairs)  10.9 us
    ppermute x2, starting transfers between devices, extended(): lax.ppermute(tail, axis, [(i, (i + 1) % count) for i in range(ends)])  10.7 us
    ppermute x2, waiting for transfers between devices, extended(): lax.ppermute(head, axis, [((i + 1) % count, i) for i in range(ends)])  9.37 us
    dot_general x1, matrix products, shards(): jnp.einsum('tc,tw->cw', feat_docs, whole_output, preferred_element_type=j...  6.77 us
    unnamed x61, local copies, waits for them, and re-layouts  5.62 us
    dot_general x3, matrix products, shards(): part = jnp.dot(got, out_weight, preferred_element_type=jnp.float32)  5.42 us
    scatter-add x1, other arithmetic, place_blocks(): return holder.at[:, chosen_doc].add(grad_doc)  5.37 us
  transfers between devices with their start and end apart: 17, of which 5 were waited for; matrix products, arithmetic and copies ran while one was open for 46% of the time, Pallas kernels for 0%

profile of v12, /device:TPU:6, one launch (start us, length us, event | category | flops | bytes accessed | tf_op | source)
XLA Modules:
  0.0 173.8 jit_solution(12851073284739154507)
XLA Ops:
  7.2 2.0 %pad_maximum_fusion.5 = bf16[2,1,128,1024]{3,2,1,0:T(8,128)(2,1)} fusion(bf16[1,1,128,1024]{3,2,1,0:T(8,128)(2,1)} %bitcast.249, bf16[1,1,128,1024]{3,2,1,0:T(8,128)(2,1)} %bitcast.251), kind=kLoop, calls=%fused_computation.50 | loop fusion | flops 262144 | bytes 1048576 | tf_op jit(solution)/shard_map/stack | solution.py:58
  10.5 5.4 %collective-permute-start = (bf16[2,1,128,1024]{3,2,1,0:T(8,128)(2,1)}, bf16[2,1,128,1024]{3,2,1,0:T(8,128)(2,1)}, u32[]{:S(2)}, u32[]{:S(2)}) collective-permute-start(bf16[2,1,128,1024]{3,2,1,0:T(8,128)(2,1)} %pad_maximum_fusion.5), channel_id=1, source_target_pairs={{0,4},{4,8},{8,12},{1,5},{5,9},{9,13},{2,6},{6,10},{10,14},{3,7},{... | collective-permute-start | bytes 1572872 | tf_op jit(solution)/shard_map/ppermute | solution.py:20
  18.0 1.4 convert_reduce_fusion
  21.1 2.1 %dynamic-slice_bitcast_fusion.2 = (bf16[128,1024]{1,0:T(8,128)(2,1)}, bf16[1,128,1024]{2,1,0:T(8,128)(2,1)S(1)}, bf16[128,1024]{1,0:T(8,128)(2,1)}, bf16[128,1024]{1,0:T(8,128)(2,1)}) fusion(bf16[1,128,4096]{2,1,0:T(8,128)(2,1)} %param.11, s32[]{:T(128)S(6)} %select_n.80, s32[]{:T(128)S(6)} %select_n.79, s32[]{:T(128)S(6)} %select_n.82, s32[]{:T(128)S(6)} %select_n.81), kind=kLoop, calls=%fused_computation.88 | loop fusion | bytes 2097168 | tf_op jit(solution)/shard_map/dynamic_slice | solution.py:118
  23.2 3.3 %collective-permute-start.8 = (bf16[128,1024]{1,0:T(8,128)(2,1)}, bf16[128,1024]{1,0:T(8,128)(2,1)S(1)}, u32[]{:S(2)}, u32[]{:S(2)}) collective-permute-start(bf16[128,1024]{1,0:T(8,128)(2,1)} %get-tuple-element.17), channel_id=1, source_target_pairs={{0,12},{4,8},{8,4},{12,0},{1,13},{5,9},{9,5},{13,1},{2,14},{6,10},... | collective-permute-start | bytes 786440 | tf_op jit(solution)/shard_map/ppermute | solution.py:121
  30.5 14.6 %collective-permute-done.8 = bf16[128,1024]{1,0:T(8,128)(2,1)S(1)} collective-permute-done((bf16[128,1024]{1,0:T(8,128)(2,1)}, bf16[128,1024]{1,0:T(8,128)(2,1)S(1)}, u32[]{:S(2)}, u32[]{:S(2)}) %collective-permute-start.8) | collective-permute-done | bytes 262176 | tf_op jit(solution)/shard_map/ppermute | solution.py:121
  46.2 4.1 %collective-permute-done.6 = bf16[128,1024]{1,0:T(8,128)(2,1)} collective-permute-done((bf16[128,1024]{1,0:T(8,128)(2,1)}, bf16[128,1024]{1,0:T(8,128)(2,1)}, u32[]{:S(2)}, u32[]{:S(2)}) %collective-permute-start.6) | collective-permute-done | bytes 262176 | tf_op jit(solution)/shard_map/ppermute | solution.py:121
  50.3 1.6 collective-permute-start.9
  51.8 2.1 %convolution_convert_fusion.1 = bf16[128,1024]{1,0:T(8,128)(2,1)} fusion(bf16[128,1024]{1,0:T(8,128)(2,1)} %collective-permute-done.6, bf16[1024,1024]{1,0:T(8,128)(2,1)S(1)} %copy-done), kind=kOutput, calls=%fused_computation.23 | convolution fusion | flops 268566528 | bytes 2621440 | tf_op jit(solution)/shard_map/dot_general | solution.py:122
  53.9 1.8 %collective-permute-done.4 = bf16[128,1024]{1,0:T(8,128)(2,1)S(1)} collective-permute-done((bf16[128,1024]{1,0:T(8,128)(2,1)S(1)}, bf16[128,1024]{1,0:T(8,128)(2,1)S(1)}, u32[]{:S(2)}, u32[]{:S(2)}) %collective-permute-start.4) | collective-permute-done | bytes 262176 | tf_op jit(solution)/shard_map/ppermute | solution.py:121
  55.8 6.7 %collective-permute-start.7 = (bf16[128,1024]{1,0:T(8,128)(2,1)}, bf16[128,1024]{1,0:T(8,128)(2,1)}, u32[]{:S(2)}, u32[]{:S(2)}) collective-permute-start(bf16[128,1024]{1,0:T(8,128)(2,1)} %convolution_convert_fusion.1), channel_id=1, source_target_pairs={{0,8},{4,12},{8,0},{12,4},{1,9},{5,13},{9,1},{13,5},{2,10},{6,14},... | collective-permute-start | bytes 786440 | tf_op jit(solution)/shard_map/ppermute | solution.py:123
  62.5 2.1 %pad_maximum_fusion.2 = bf16[4,128,1024]{2,1,0:T(8,128)(2,1)} fusion(bf16[1,128,1024]{2,1,0:T(8,128)(2,1)S(1)} %bitcast.265, bf16[1,128,1024]{2,1,0:T(8,128)(2,1)} %bitcast.85, bf16[1,128,1024]{2,1,0:T(8,128)(2,1)S(1)} %bitcast.266, bf16[1,128,1024]{2,1,0:T(8,128)(2,1)S(1)} %get-tuple-element.16), kind=kLoop, calls=%fused_computation.34 | loop fusion | flops 1572864 | bytes 2097152 | tf_op jit(solution)/shard_map/stack | solution.py:128
  64.6 2.8 %gather_fusion = bf16[4,128,1024]{2,1,0:T(8,128)(2,1)} fusion(bf16[4,128,1024]{2,1,0:T(8,128)(2,1)} %pad_maximum_fusion.2, s32[1024]{0:T(1024)S(1)} %pad_clamp_fusion), kind=kCustom, calls=%fused_computation | custom fusion | bytes 2097168 | tf_op jit(solution)/shard_map/jit(_take)/gather | solution.py:128
  67.4 2.4 %bitcast_select_fusion = bf16[512,1024]{1,0:T(8,128)(2,1)} fusion(bf16[4,128,1024]{2,1,0:T(8,128)(2,1)} %gather_fusion, pred[512]{0:T(512)(128)(4,1)S(1)} %broadcast_bitcast_fusion), kind=kLoop, calls=%fused_computation.35 | loop fusion | flops 524288 | bytes 2097664 | tf_op jit(solution)/shard_map/jit(_take)/select_n | solution.py:128
  69.9 2.2 %convolution_convert_fusion.2 = bf16[128,1024]{1,0:T(8,128)(2,1)} fusion(bf16[128,1024]{1,0:T(8,128)(2,1)} %copy-done.19, bf16[1024,1024]{1,0:T(8,128)(2,1)S(1)} %copy-done), kind=kOutput, calls=%fused_computation.24 | convolution fusion | flops 268566528 | bytes 2621440 | tf_op jit(solution)/shard_map/dot_general | solution.py:122
  72.1 2.6 %collective-permute-start.5 = (bf16[128,1024]{1,0:T(8,128)(2,1)}, bf16[128,1024]{1,0:T(8,128)(2,1)}, u32[]{:S(2)}, u32[]{:S(2)}) collective-permute-start(bf16[128,1024]{1,0:T(8,128)(2,1)} %convolution_convert_fusion.2), channel_id=1, source_target_pairs={{0,4},{4,0},{8,12},{12,8},{1,5},{5,1},{9,13},{13,9},{2,6},{6,2},{1... | collective-permute-start | bytes 786440 | tf_op jit(solution)/shard_map/ppermute | solution.py:123
  76.1 1.8 %gather_fusion.1 = bf16[6,2,64,1024]{3,2,1,0:T(8,128)(2,1)} fusion(bf16[1,2,6,64,1024]{4,3,2,1,0:T(8,128)(2,1)S(1)} %bitcast.235, s32[6]{0:T(128)S(1)} %reshape.608), kind=kCustom, calls=%fused_computation.1 | custom fusion | bytes 3145776 | tf_op jit(solution)/shard_map/vmap()/gather | solution.py:41
  77.9 1.7 copy.202
  79.7 1.4 maximum_select_fusion
  89.0 4.9 %collective-permute-done.3 = bf16[2,1,64,1024]{3,2,1,0:T(8,128)(2,1)S(1)} collective-permute-done((bf16[2,1,64,1024]{3,2,1,0:T(8,128)(2,1)S(1)}, bf16[2,1,64,1024]{3,2,1,0:T(8,128)(2,1)S(1)}, u32[]{:S(2)}, u32[]{:S(2)}) %collective-permute-start.3) | collective-permute-done | bytes 262176 | tf_op jit(solution)/shard_map/ppermute | solution.py:30
  96.8 1.6 multiply_reduce_fusion
  107.7 3.8 %collective-permute-start.12 = (bf16[2,1,64,1024]{3,2,0,1:T(8,128)(2,1)}, bf16[2,1,64,1024]{3,2,0,1:T(8,128)(2,1)}, u32[]{:S(2)}, u32[]{:S(2)}) collective-permute-start(bf16[2,1,64,1024]{3,2,0,1:T(8,128)(2,1)} %bitcast.220), channel_id=1, source_target_pairs={{0,4},{4,0},{8,12},{12,8},{1,5},{5,1},{9,13},{13,9},{2,6},{6,2},{1... | collective-permute-start | bytes 786440 | tf_op jit(solution)/shard_map/ppermute | solution.py:193
  115.8 3.1 %pad_maximum_fusion = f32[1,2,2,3,64,1024]{5,0,4,3,2,1:T(1,128)S(1)} fusion(f32[1,1,2,3,64,1024]{5,0,4,3,2,1:T(1,128)S(1)} %bitcast.237, f32[1,1,2,3,64,1024]{5,0,4,3,2,1:T(1,128)S(1)} %bitcast.238), kind=kLoop, calls=%fused_computation.3 | loop fusion | flops 786432 | bytes 6291456 | tf_op jit(solution)/shard_map/stack | solution.py:171
  118.8 2.4 %copy.266 = f32[1,2,2,3,64,1024]{5,4,1,3,2,0:T(8,128)} copy(f32[1,2,2,3,64,1024]{5,0,4,3,2,1:T(1,128)S(1)} %pad_maximum_fusion) | data formatting | bytes 6291456 | tf_op jit(solution)/shard_map/stack | solution.py:171
  121.8 5.4 %scatter_fusion = f32[2,6,64,1024]{3,2,1,0:T(8,128)S(1)} fusion(f32[2,6,64,1024]{3,2,1,0:T(8,128)S(1)} %broadcast.202, s32[6]{0:T(128)S(1)} %copy-done.26, f32[6,2,64,1024]{3,2,1,0:T(8,128)} %bitcast.226), kind=kCustom, calls=%fused_computation.2 | custom fusion | flops 786432 | bytes 9437208 | tf_op jit(solution)/shard_map/vmap()/scatter-add | solution.py:46
  130.9 5.4 %collective-permute-start.10 = (bf16[2,1,128,1024]{3,2,1,0:T(8,128)(2,1)}, bf16[2,1,128,1024]{3,2,1,0:T(8,128)(2,1)}, u32[]{:S(2)}, u32[]{:S(2)}) collective-permute-start(bf16[2,1,128,1024]{3,2,1,0:T(8,128)(2,1)} %get-tuple-element.11), channel_id=1, source_target_pairs={{0,4},{4,8},{8,12},{1,5},{5,9},{9,13},{2,6},{6,10},{10,14},{3,7},{... | collective-permute-start | bytes 1572872 | tf_op jit(solution)/shard_map/ppermute | solution.py:20
  137.6 1.8 %convert_element_type.198 = bf16[1,128,1024]{2,1,0:T(8,128)(2,1)} reshape(bf16[1,2,64,8,128]{4,3,2,1,0:T(8,128)(2,1)} %copy-done.13) | data formatting | bytes 524288 | tf_op jit(solution)/shard_map/convert_element_type | solution.py:109
  143.0 1.3 div.48
  145.9 1.8 %div.44 = f32[2,1,128,1024]{3,2,1,0:T(8,128)} reshape(f32[2,64,2,1024]{3,2,1,0:T(2,128)S(1)} %broadcast_in_dim.33) | data formatting | bytes 2097152 | tf_op jit(solution)/shard_map/div | solution.py:198
  147.7 9.4 %collective-permute-done.11 = bf16[2,1,128,1024]{3,2,1,0:T(8,128)(2,1)} collective-permute-done((bf16[2,1,128,1024]{3,2,1,0:T(8,128)(2,1)}, bf16[2,1,128,1024]{3,2,1,0:T(8,128)(2,1)}, u32[]{:S(2)}, u32[]{:S(2)}) %collective-permute-start.11) | collective-permute-done | bytes 524320 | tf_op jit(solution)/shard_map/ppermute | solution.py:22
  157.0 2.3 %fusion.11 = bf16[2,1,128,1024]{3,2,1,0:T(8,128)(2,1)S(1)} fusion(f32[2,1,128,1024]{3,2,1,0:T(8,128)} %div.48, f32[2,1,128,1024]{3,2,1,0:T(8,128)} %div.44, f32[2,1,128,1024]{3,2,1,0:T(8,128)S(1)} %bitcast.246, bf16[2,1,128,1024]{3,2,1,0:T(8,128)(2,1)} %collective-permute-done.11, bf16[2,1,256,1024]{3,2,1,0:T(8,128)(2,1)S(1)} %bitcast.228, ...), kind=kLoop, calls=%fused_computation.30 | loop fusion | flops 4456448 | bytes 5767168 | tf_op jit(solution)/shard_map/convert.1
  160.2 6.8 %fusion.54 = f32[1024,1024]{1,0:T(8,128)} fusion(bf16[1024,1024]{1,0:T(8,128)(2,1)} %all-gather.3.cloned.1.call-done, bf16[1024,1024]{1,0:T(8,128)(2,1)} %all-gather.5.cloned.1.call-done), kind=kOutput, calls=%fused_computation.123 | convolution fusion | flops 2147483648 | bytes 8388608 | tf_op jit(solution)/shard_map/tc,tw->cw/dot_general | solution.py:133
  (157 shorter events, 47.2 us)
Async XLA Ops:
  7.2 22.0 %copy-start = (bf16[1024,1024]{1,0:T(8,128)(2,1)S(1)}, bf16[1024,1024]{1,0:T(8,128)(2,1)}, u32[]{:S(2)}) copy-start(bf16[1024,1024]{1,0:T(8,128)(2,1)} %param.10) | copy-start | bytes 6291460
  7.2 153.0 %all-gather.3.cloned.1.call-start = ((), (), s32[]{:S(2)}) async-start(), calls=%async_computation | async-start | bytes 3145728 | tf_op jit(solution)/shard_map/all_gather | solution.py:131
  9.3 62.8 %collective-permute-start.1 = (bf16[2,1,128,1024]{3,2,1,0:T(8,128)(2,1)}, bf16[2,1,128,1024]{3,2,1,0:T(8,128)(2,1)}, u32[]{:S(2)}, u32[]{:S(2)}) collective-permute-start(bf16[2,1,128,1024]{3,2,1,0:T(8,128)(2,1)} %pad_maximum_fusion.5), channel_id=1, source_target_pairs={{4,0},{8,4},{12,8},{5,1},{9,5},{13,9},{6,2},{10,6},{14,10},{7,3},{... | collective-permute-start | bytes 1572872 | tf_op jit(solution)/shard_map/ppermute | solution.py:22
  10.5 64.2 %collective-permute-start = (bf16[2,1,128,1024]{3,2,1,0:T(8,128)(2,1)}, bf16[2,1,128,1024]{3,2,1,0:T(8,128)(2,1)}, u32[]{:S(2)}, u32[]{:S(2)}) collective-permute-start(bf16[2,1,128,1024]{3,2,1,0:T(8,128)(2,1)} %pad_maximum_fusion.5), channel_id=1, source_target_pairs={{0,4},{4,8},{8,12},{1,5},{5,9},{9,13},{2,6},{6,10},{10,14},{3,7},{... | collective-permute-start | bytes 1572872 | tf_op jit(solution)/shard_map/ppermute | solution.py:20
  19.4 7.1 %copy-start.27 = (s32[1,2,2]{2,1,0:T(2,128)S(1)}, s32[1,2,2]{2,1,0:T(2,128)}, u32[]{:S(2)}) copy-start(s32[1,2,2]{2,1,0:T(2,128)} %param.9) | copy-start | bytes 52
  20.4 59.3 %collective-permute-start.2 = (f32[2,1,64,1024]{3,2,1,0:T(8,128)}, f32[2,1,64,1024]{3,2,1,0:T(8,128)}, u32[]{:S(2)}, u32[]{:S(2)}) collective-permute-start(f32[2,1,64,1024]{3,2,1,0:T(8,128)} %get-tuple-element.26), channel_id=1, source_target_pairs={{0,4},{4,0},{8,12},{12,8},{1,5},{5,1},{9,13},{13,9},{2,6},{6,2},{1... | collective-permute-start | bytes 1572872 | tf_op jit(solution)/shard_map/ppermute | solution.py:30
  23.2 21.8 %collective-permute-start.8 = (bf16[128,1024]{1,0:T(8,128)(2,1)}, bf16[128,1024]{1,0:T(8,128)(2,1)S(1)}, u32[]{:S(2)}, u32[]{:S(2)}) collective-permute-start(bf16[128,1024]{1,0:T(8,128)(2,1)} %get-tuple-element.17), channel_id=1, source_target_pairs={{0,12},{4,8},{8,4},{12,0},{1,13},{5,9},{9,5},{13,1},{2,14},{6,10},... | collective-permute-start | bytes 786440 | tf_op jit(solution)/shard_map/ppermute | solution.py:121
  26.5 23.8 %collective-permute-start.6 = (bf16[128,1024]{1,0:T(8,128)(2,1)}, bf16[128,1024]{1,0:T(8,128)(2,1)}, u32[]{:S(2)}, u32[]{:S(2)}) collective-permute-start(bf16[128,1024]{1,0:T(8,128)(2,1)} %get-tuple-element.18), channel_id=1, source_target_pairs={{0,8},{4,12},{8,0},{12,4},{1,9},{5,13},{9,1},{13,5},{2,10},{6,14},... | collective-permute-start | bytes 786440 | tf_op jit(solution)/shard_map/ppermute | solution.py:121
  29.2 15.9 %copy-start.21 = (bf16[128,1024]{1,0:T(8,128)(2,1)S(1)}, bf16[128,1024]{1,0:T(8,128)(2,1)}, u32[]{:S(2)}) copy-start(bf16[128,1024]{1,0:T(8,128)(2,1)} %get-tuple-element.15) | copy-start | bytes 786436
  45.0 10.8 %collective-permute-start.4 = (bf16[128,1024]{1,0:T(8,128)(2,1)S(1)}, bf16[128,1024]{1,0:T(8,128)(2,1)S(1)}, u32[]{:S(2)}, u32[]{:S(2)}) collective-permute-start(bf16[128,1024]{1,0:T(8,128)(2,1)S(1)} %copy-done.21), channel_id=1, source_target_pairs={{0,4},{4,0},{8,12},{12,8},{1,5},{5,1},{9,13},{13,9},{2,6},{6,2},{1... | collective-permute-start | bytes 786440 | tf_op jit(solution)/shard_map/ppermute | solution.py:121
  50.3 34.8 %collective-permute-start.9 = (bf16[128,1024]{1,0:T(8,128)(2,1)}, bf16[128,1024]{1,0:T(8,128)(2,1)}, u32[]{:S(2)}, u32[]{:S(2)}) collective-permute-start(bf16[128,1024]{1,0:T(8,128)(2,1)} %convolution_convert_fusion), channel_id=1, source_target_pairs={{0,12},{4,8},{8,4},{12,0},{1,13},{5,9},{9,5},{13,1},{2,14},{6,10},... | collective-permute-start | bytes 786440 | tf_op jit(solution)/shard_map/ppermute | solution.py:123
  55.8 6.8 %copy-start.19 = (bf16[128,1024]{1,0:T(8,128)(2,1)}, bf16[128,1024]{1,0:T(8,128)(2,1)S(1)}, u32[]{:S(2)}) copy-start(bf16[128,1024]{1,0:T(8,128)(2,1)S(1)} %collective-permute-done.4) | copy-start | bytes 786436
  55.8 29.3 %collective-permute-start.7 = (bf16[128,1024]{1,0:T(8,128)(2,1)}, bf16[128,1024]{1,0:T(8,128)(2,1)}, u32[]{:S(2)}, u32[]{:S(2)}) collective-permute-start(bf16[128,1024]{1,0:T(8,128)(2,1)} %convolution_convert_fusion.1), channel_id=1, source_target_pairs={{0,8},{4,12},{8,0},{12,4},{1,9},{5,13},{9,1},{13,5},{2,10},{6,14},... | collective-permute-start | bytes 786440 | tf_op jit(solution)/shard_map/ppermute | solution.py:123
  69.8 4.9 %copy-start.9 = (bf16[1,128,1024]{2,1,0:T(8,128)(2,1)S(1)}, bf16[1,128,1024]{2,1,0:T(8,128)(2,1)}, u32[]{:S(2)}) copy-start(bf16[1,128,1024]{2,1,0:T(8,128)(2,1)} %param.8) | copy-start | bytes 786436
  69.8 4.9 %copy-start.10 = (bf16[1,128,1024]{2,1,0:T(8,128)(2,1)S(1)}, bf16[1,128,1024]{2,1,0:T(8,128)(2,1)}, u32[]{:S(2)}) copy-start(bf16[1,128,1024]{2,1,0:T(8,128)(2,1)} %param.7) | copy-start | bytes 786436
  69.9 90.3 %all-gather.5.cloned.1.call-start = ((), (), s32[]{:S(2)}) async-start(), calls=%async_computation.1 | async-start | bytes 2359296 | tf_op jit(solution)/shard_map/all_gather | solution.py:132
  72.1 13.0 %collective-permute-start.5 = (bf16[128,1024]{1,0:T(8,128)(2,1)}, bf16[128,1024]{1,0:T(8,128)(2,1)}, u32[]{:S(2)}, u32[]{:S(2)}) collective-permute-start(bf16[128,1024]{1,0:T(8,128)(2,1)} %convolution_convert_fusion.2), channel_id=1, source_target_pairs={{0,4},{4,0},{8,12},{12,8},{1,5},{5,1},{9,13},{13,9},{2,6},{6,2},{1... | collective-permute-start | bytes 786440 | tf_op jit(solution)/shard_map/ppermute | solution.py:123
  82.4 6.0 %copy-start.4 = (bf16[48,8,8,128]{3,2,1,0:T(8,128)(2,1)}, bf16[48,8,8,128]{3,2,1,0:T(8,128)(2,1)S(1)}, u32[]{:S(2)}) copy-start(bf16[48,8,8,128]{3,2,1,0:T(8,128)(2,1)S(1)} %copy.267) | copy-start | bytes 2359300
  84.3 9.6 %collective-permute-start.3 = (bf16[2,1,64,1024]{3,2,1,0:T(8,128)(2,1)S(1)}, bf16[2,1,64,1024]{3,2,1,0:T(8,128)(2,1)S(1)}, u32[]{:S(2)}, u32[]{:S(2)}) collective-permute-start(bf16[2,1,64,1024]{3,2,1,0:T(8,128)(2,1)S(1)} %fusion.21), channel_id=1, source_target_pairs={{0,8},{4,12},{8,0},{12,4},{1,9},{5,13},{9,1},{13,5},{2,10},{6,14},... | collective-permute-start | bytes 786440 | tf_op jit(solution)/shard_map/ppermute | solution.py:30
  87.2 7.0 %copy-start.17 = (bf16[2,64,8,128]{3,1,0,2:T(8,128)(2,1)S(1)}, bf16[2,64,8,128]{3,1,0,2:T(8,128)(2,1)}, u32[]{:S(2)}) copy-start(bf16[2,64,8,128]{3,1,0,2:T(8,128)(2,1)} %copy.213) | copy-start | bytes 786436
  104.3 7.1 %copy-start.23 = (f32[2,8,64]{2,1,0:T(8,128)S(1)}, f32[2,8,64]{2,1,0:T(8,128)}, u32[]{:S(2)}) copy-start(f32[2,8,64]{2,1,0:T(8,128)} %copy-done.22) | copy-start | bytes 12292
  105.8 35.7 %collective-permute-start.14 = (bf16[2,1,32,1024]{3,0,2,1:T(2,128)(2,1)}, bf16[2,1,32,1024]{3,0,2,1:T(2,128)(2,1)}, u32[]{:S(2)}, u32[]{:S(2)}) collective-permute-start(bf16[2,1,32,1024]{3,0,2,1:T(2,128)(2,1)} %get-tuple-element.14), channel_id=1, source_target_pairs={{0,12},{4,8},{8,4},{12,0},{1,13},{5,9},{9,5},{13,1},{2,14},{6,10},... | collective-permute-start | bytes 393224 | tf_op jit(solution)/shard_map/ppermute | solution.py:193
  106.4 35.1 %collective-permute-start.13 = (bf16[2,1,32,1024]{3,0,2,1:T(2,128)(2,1)S(1)}, bf16[2,1,32,1024]{3,0,2,1:T(2,128)(2,1)}, u32[]{:S(2)}, u32[]{:S(2)}) collective-permute-start(bf16[2,1,32,1024]{3,0,2,1:T(2,128)(2,1)S(1)} %get-tuple-element.13), channel_id=1, source_target_pairs={{0,8},{4,12},{8,0},{12,4},{1,9},{5,13},{9,1},{13,5},{2,10},{6,14},... | collective-permute-start | bytes 393224 | tf_op jit(solution)/shard_map/ppermute | solution.py:193
  107.7 36.7 %collective-permute-start.12 = (bf16[2,1,64,1024]{3,2,0,1:T(8,128)(2,1)}, bf16[2,1,64,1024]{3,2,0,1:T(8,128)(2,1)}, u32[]{:S(2)}, u32[]{:S(2)}) collective-permute-start(bf16[2,1,64,1024]{3,2,0,1:T(8,128)(2,1)} %bitcast.220), channel_id=1, source_target_pairs={{0,4},{4,0},{8,12},{12,8},{1,5},{5,1},{9,13},{13,9},{2,6},{6,2},{1... | collective-permute-start | bytes 786440 | tf_op jit(solution)/shard_map/ppermute | solution.py:193
  127.4 8.8 %copy-start.5 = (bf16[48,8,8,128]{3,2,1,0:T(8,128)(2,1)S(1)}, bf16[48,8,8,128]{3,2,1,0:T(8,128)(2,1)}, u32[]{:S(2)}) copy-start(bf16[48,8,8,128]{3,2,1,0:T(8,128)(2,1)} %copy-done.4) | copy-start | bytes 2359300
  127.4 8.8 %copy-start.7 = (bf16[2,8,64,192]{3,2,1,0:T(8,128)(2,1)S(1)}, bf16[2,8,64,192]{3,2,1,0:T(8,128)(2,1)}, u32[]{:S(2)}) copy-start(bf16[2,8,64,192]{3,2,1,0:T(8,128)(2,1)} %copy-done.6) | copy-start | bytes 1179652
  127.5 9.1 %copy-start.12 = (bf16[1,1,128,1024]{2,3,1,0:T(8,128)(2,1)S(1)}, bf16[1,1,128,1024]{2,3,1,0:T(8,128)(2,1)}, u32[]{:S(2)}) copy-start(bf16[1,1,128,1024]{2,3,1,0:T(8,128)(2,1)} %copy-done.11) | copy-start | bytes 786436
  129.6 27.5 %collective-permute-start.11 = (bf16[2,1,128,1024]{3,2,1,0:T(8,128)(2,1)}, bf16[2,1,128,1024]{3,2,1,0:T(8,128)(2,1)}, u32[]{:S(2)}, u32[]{:S(2)}) collective-permute-start(bf16[2,1,128,1024]{3,2,1,0:T(8,128)(2,1)} %get-tuple-element.12), channel_id=1, source_target_pairs={{4,0},{8,4},{12,8},{5,1},{9,5},{13,9},{6,2},{10,6},{14,10},{7,3},{... | collective-permute-start | bytes 1572872 | tf_op jit(solution)/shard_map/ppermute | solution.py:22
  130.9 26.2 %collective-permute-start.10 = (bf16[2,1,128,1024]{3,2,1,0:T(8,128)(2,1)}, bf16[2,1,128,1024]{3,2,1,0:T(8,128)(2,1)}, u32[]{:S(2)}, u32[]{:S(2)}) collective-permute-start(bf16[2,1,128,1024]{3,2,1,0:T(8,128)(2,1)} %get-tuple-element.11), channel_id=1, source_target_pairs={{0,4},{4,8},{8,12},{1,5},{5,9},{9,13},{2,6},{6,10},{10,14},{3,7},{... | collective-permute-start | bytes 1572872 | tf_op jit(solution)/shard_map/ppermute | solution.py:20
  144.3 12.7 %copy-start.3 = (bf16[2,1,4,64,1024]{4,3,2,0,1:T(8,128)(2,1)S(1)}, bf16[2,1,4,64,1024]{4,3,2,0,1:T(8,128)(2,1)}, u32[]{:S(2)}) copy-start(bf16[2,1,4,64,1024]{4,3,2,0,1:T(8,128)(2,1)} %copy-done.2) | copy-start | bytes 3145732
  144.3 12.7 %copy-start.8 = (f32[2,1,2,64,1024]{4,3,2,0,1:T(8,128)S(1)}, f32[2,1,2,64,1024]{4,3,2,0,1:T(8,128)}, u32[]{:S(2)}) copy-start(f32[2,1,2,64,1024]{4,3,2,0,1:T(8,128)} %slice.78) | copy-start | bytes 3145732
  160.2 6.8 %copy-start.1 = (bf16[1024,1024]{1,0:T(8,128)(2,1)S(1)}, bf16[1024,1024]{1,0:T(8,128)(2,1)}, u32[]{:S(2)}) copy-start(bf16[1024,1024]{1,0:T(8,128)(2,1)} %param.10) | copy-start | bytes 6291460
  (13 other events, 23.3 us)
Sparse Core Ops, SparseCore 0:
  70.0 32.5 all-gather.2
  104.7 52.9 all-gather.4

commit v13 on v10

--- a/solution.py
+++ b/solution.py
@@ -62,21 +62,27 @@
     chosen = jnp.concatenate([local_ids, local_ids + pattern], axis=2) + 2
     near_pair = jax.vmap(pick_blocks, in_axes=(1, 0), out_axes=1)(blocks_six, chosen)
     near_pair = near_pair.reshape(2, doc_count, 2, near_width, head_cols)
-    pooled = pool_pairs(key_value.astype(jnp.float32))
-    siblings = []
-    own_level = pooled
+    pieces = []
+    level_rows = key_value.astype(jnp.float32)
     for level_no in range(levels):
-        other = swapped(own_level, "seq", level_no)
-        siblings.append(other)
-        if level_no + 1 < levels:
-            upper = position >> level_no & 1 == 1
-            joined = jnp.where(
-                upper,
-                jnp.concatenate([other, own_level], axis=2),
-                jnp.concatenate([own_level, other], axis=2),
-            )
-            own_level = pool_pairs(joined)
-    far_pair = jnp.concatenate(siblings, axis=2).astype(jnp.bfloat16)
+        level_rows = pool_pairs(level_rows)
+        pieces.append(level_rows.astype(jnp.bfloat16))
+    far_levels = []
+    for level_no in range(levels):
+        count = 1 << level_no
+        group = jnp.stack(
+            [
+                lax.ppermute(pieces[level_no], "seq", [(i, i ^ step) for i in range(seq_count)])
+                for step in range(count, 2 * count)
+            ],
+            axis=0,
+        )
+        order = jnp.arange(count, dtype=jnp.int32) ^ (position & (count - 1))
+        group = jnp.take(group, order, axis=0)
+        far_levels.append(
+            jnp.moveaxis(group, 0, 2).reshape(2, doc_count, count * group.shape[3], head_cols)
+        )
+    far_pair = jnp.concatenate(far_levels, axis=2)
     query_heads = queries.reshape(doc_count, 2, block, heads, HEAD_DIM)
     near_k = near_pair[0].reshape(doc_count, 2, near_width, heads, HEAD_DIM)
     near_v = near_pair[1].reshape(doc_count, 2, near_width, heads, HEAD_DIM)

time: 172 us -> 176 us (1.023)
  the two profiles are of different devices: /device:TPU:30 before, /device:TPU:6 now
where the time goes in v13:
time: 176 us; the launch traced here: 172 us
  starting transfers between devices  40.7 us (23%)
  local copies, waits for them, and re-layouts  32.1 us (18%)
  waiting for transfers between devices  32.1 us (18%)
  other arithmetic  30.8 us (18%)
  matrix products  21.9 us (12%)
  between operations  14.8 us (8%)
    all_gather x1, waiting for transfers between devices, shards(): whole_output = lax.all_gather(out_rows, ('dp', 'seq'), axis=0, tiled=True)  17.2 us
    ppermute x3, starting transfers between devices, shards(): lax.ppermute(lax.dynamic_slice_in_dim(sent, core * half, half, axis=0), '...  13.5 us
    ppermute x2, starting transfers between devices, extended(): lax.ppermute(tail, axis, [(i, (i + 1) % count) for i in range(ends)])  10.7 us
    dot_general x1, matrix products, shards(): jnp.einsum('tc,tw->cw', feat_docs, whole_output, preferred_element_type=j...  6.77 us
    dot_general x3, matrix products, shards(): part = jnp.dot(got, out_weight, preferred_element_type=jnp.float32)  5.65 us
    ppermute x3, waiting for transfers between devices, shards(): back = lax.ppermute(part.astype(jnp.bfloat16), 'seq', pairs)  5.59 us
    scatter-add x1, other arithmetic, place_blocks(): return holder.at[:, chosen_doc].add(grad_doc)  5.4 us
    ppermute x3, waiting for transfers between devices, shards(): lax.ppermute(pieces[level_no], 'seq', [(i, i ^ step) for i in range(seq_c...  5.06 us
  transfers between devices with their start and end apart: 21, of which 6 were waited for; matrix products, arithmetic and copies ran while one was open for 43% of the time, Pallas kernels for 0%

profile of v13, /device:TPU:6, one launch (start us, length us, event | category | flops | bytes accessed | tf_op | source)
XLA Modules:
  0.0 172.3 jit_solution(9023271583600860704)
XLA Ops:
  7.2 2.0 %pad_maximum_fusion.5 = bf16[2,1,128,1024]{3,2,1,0:T(8,128)(2,1)} fusion(bf16[1,1,128,1024]{3,2,1,0:T(8,128)(2,1)} %bitcast.257, bf16[1,1,128,1024]{3,2,1,0:T(8,128)(2,1)} %bitcast.259), kind=kLoop, calls=%fused_computation.50 | loop fusion | flops 262144 | bytes 1048576 | tf_op jit(solution)/shard_map/stack | solution.py:58
  10.5 5.3 %collective-permute-start = (bf16[2,1,128,1024]{3,2,1,0:T(8,128)(2,1)}, bf16[2,1,128,1024]{3,2,1,0:T(8,128)(2,1)}, u32[]{:S(2)}, u32[]{:S(2)}) collective-permute-start(bf16[2,1,128,1024]{3,2,1,0:T(8,128)(2,1)} %pad_maximum_fusion.5), channel_id=1, source_target_pairs={{0,4},{4,8},{8,12},{1,5},{5,9},{9,13},{2,6},{6,10},{10,14},{3,7},{... | collective-permute-start | bytes 1572872 | tf_op jit(solution)/shard_map/ppermute | solution.py:20
  18.0 1.4 convert_reduce_fusion
  20.2 1.5 collective-permute-start.4
  22.9 2.1 %dynamic-slice_bitcast_fusion.2 = (bf16[64,1024]{1,0:T(8,128)(2,1)}, bf16[64,1024]{1,0:T(8,128)(2,1)}, bf16[64,1024]{1,0:T(8,128)(2,1)}) fusion(bf16[1,128,4096]{2,1,0:T(8,128)(2,1)} %param.11, s32[]{:T(128)S(6)} %select_n.153, s32[]{:T(128)S(6)} %select_n.155, s32[]{:T(128)S(6)} %select_n.161, s32[]{:T(128)S(6)} %select_n.158), kind=kLoop, calls=%fused_computation.126 | loop fusion | bytes 786448 | tf_op jit(solution)/shard_map/dynamic_slice | solution.py:130
  25.0 2.9 %collective-permute-start.11 = (bf16[64,1024]{1,0:T(8,128)(2,1)}, bf16[64,1024]{1,0:T(8,128)(2,1)S(1)}, u32[]{:S(2)}, u32[]{:S(2)}) collective-permute-start(bf16[64,1024]{1,0:T(8,128)(2,1)} %get-tuple-element.16), channel_id=1, source_target_pairs={{0,12},{4,8},{8,4},{12,0},{1,13},{5,9},{9,5},{13,1},{2,14},{6,10},... | collective-permute-start | bytes 393224 | tf_op jit(solution)/shard_map/ppermute | solution.py:129
  33.7 8.7 %collective-permute-start.8 = (bf16[64,1024]{1,0:T(8,128)(2,1)}, bf16[64,1024]{1,0:T(8,128)(2,1)}, u32[]{:S(2)}, u32[]{:S(2)}) collective-permute-start(bf16[64,1024]{1,0:T(8,128)(2,1)} %get-tuple-element.17), channel_id=1, source_target_pairs={{0,8},{4,12},{8,0},{12,4},{1,9},{5,13},{9,1},{13,5},{2,10},{6,14},... | collective-permute-start | bytes 393224 | tf_op jit(solution)/shard_map/ppermute | solution.py:129
  42.7 2.0 %collective-permute-start.5 = (bf16[64,1024]{1,0:T(8,128)(2,1)}, bf16[64,1024]{1,0:T(8,128)(2,1)}, u32[]{:S(2)}, u32[]{:S(2)}) collective-permute-start(bf16[64,1024]{1,0:T(8,128)(2,1)} %get-tuple-element.15), channel_id=1, source_target_pairs={{0,4},{4,0},{8,12},{12,8},{1,5},{5,1},{9,13},{13,9},{2,6},{6,2},{1... | collective-permute-start | bytes 393224 | tf_op jit(solution)/shard_map/ppermute | solution.py:129
  47.1 1.6 collective-permute-done.8
  48.7 1.7 collective-permute-start.2
  52.1 4.7 %collective-permute-done.2 = bf16[2,1,64,1024]{3,2,0,1:T(8,128)(2,1)S(1)} collective-permute-done((bf16[2,1,64,1024]{3,2,0,1:T(8,128)(2,1)S(1)}, bf16[2,1,64,1024]{3,2,0,1:T(8,128)(2,1)S(1)}, u32[]{:S(2)}, u32[]{:S(2)}) %collective-permute-start.2) | collective-permute-done | bytes 262176 | tf_op jit(solution)/shard_map/ppermute | solution.py:75
  57.2 3.3 %collective-permute-start.13 = (bf16[128,1024]{1,0:T(8,128)(2,1)}, bf16[128,1024]{1,0:T(8,128)(2,1)}, u32[]{:S(2)}, u32[]{:S(2)}) collective-permute-start(bf16[128,1024]{1,0:T(8,128)(2,1)} %convolution_convert_fusion), channel_id=1, source_target_pairs={{0,12},{4,8},{8,4},{12,0},{1,13},{5,9},{9,5},{13,1},{2,14},{6,10},... | collective-permute-start | bytes 786440 | tf_op jit(solution)/shard_map/ppermute | solution.py:139
  60.5 2.2 %convolution_convert_fusion.1 = bf16[128,1024]{1,0:T(8,128)(2,1)} fusion(bf16[1024,1024]{1,0:T(8,128)(2,1)S(1)} %copy-done, bf16[64,1024]{1,0:T(8,128)(2,1)} %collective-permute-done.9, bf16[64,1024]{1,0:T(8,128)(2,1)} %collective-permute-done.8, pred[]{:T(512)S(6)} %eq.2), kind=kOutput, calls=%fused_computation.24 | convolution fusion | flops 269746176 | bytes 2621441 | tf_op jit(solution)/shard_map/dot_general | solution.py:138
  63.1 2.2 %convolution_convert_fusion.2 = bf16[128,1024]{1,0:T(8,128)(2,1)} fusion(bf16[1024,1024]{1,0:T(8,128)(2,1)S(1)} %copy-done, bf16[64,1024]{1,0:T(8,128)(2,1)} %collective-permute-done.6, bf16[64,1024]{1,0:T(8,128)(2,1)} %collective-permute-done.5, pred[]{:T(512)S(6)} %eq.2), kind=kOutput, calls=%fused_computation.25 | convolution fusion | flops 269746176 | bytes 2621441 | tf_op jit(solution)/shard_map/dot_general | solution.py:138
  71.2 1.3 pad_maximum_fusion.1
  72.5 1.8 %gather_fusion.2 = bf16[6,2,64,1024]{3,2,1,0:T(8,128)(2,1)} fusion(bf16[1,2,6,64,1024]{4,3,2,1,0:T(8,128)(2,1)S(1)} %bitcast.244, s32[6]{0:T(128)S(1)} %reshape.789), kind=kCustom, calls=%fused_computation.2 | custom fusion | bytes 3145776 | tf_op jit(solution)/shard_map/vmap()/gather | solution.py:41
  74.3 1.6 copy.153
  77.9 5.6 %collective-permute-done.10 = bf16[128,1024]{1,0:T(8,128)(2,1)} collective-permute-done((bf16[128,1024]{1,0:T(8,128)(2,1)}, bf16[128,1024]{1,0:T(8,128)(2,1)}, u32[]{:S(2)}, u32[]{:S(2)}) %collective-permute-start.10) | collective-permute-done | bytes 262176 | tf_op jit(solution)/shard_map/ppermute | solution.py:139
  85.8 1.6 multiply_reduce_fusion
  94.3 3.0 %collective-permute-start.18 = (bf16[2,1,32,1024]{3,0,2,1:T(2,128)(2,1)}, bf16[2,1,32,1024]{3,0,2,1:T(2,128)(2,1)}, u32[]{:S(2)}, u32[]{:S(2)}) collective-permute-start(bf16[2,1,32,1024]{3,0,2,1:T(2,128)(2,1)} %get-tuple-element.14), channel_id=1, source_target_pairs={{0,12},{4,8},{8,4},{12,0},{1,13},{5,9},{9,5},{13,1},{2,14},{6,10},... | collective-permute-start | bytes 393224 | tf_op jit(solution)/shard_map/ppermute | solution.py:209
  98.6 1.4 collective-permute-start.16
  104.2 3.1 %pad_maximum_fusion = f32[1,2,2,3,64,1024]{5,0,4,3,2,1:T(1,128)S(1)} fusion(f32[1,1,2,3,64,1024]{5,0,4,3,2,1:T(1,128)S(1)} %bitcast.246, f32[1,1,2,3,64,1024]{5,0,4,3,2,1:T(1,128)S(1)} %bitcast.247), kind=kLoop, calls=%fused_computation.4 | loop fusion | flops 786432 | bytes 6291456 | tf_op jit(solution)/shard_map/stack | solution.py:187
  107.2 2.4 %copy.215 = f32[1,2,2,3,64,1024]{5,4,1,3,2,0:T(8,128)} copy(f32[1,2,2,3,64,1024]{5,0,4,3,2,1:T(1,128)S(1)} %pad_maximum_fusion) | data formatting | bytes 6291456 | tf_op jit(solution)/shard_map/stack | solution.py:187
  110.0 5.4 %scatter_fusion = f32[2,6,64,1024]{3,2,1,0:T(8,128)S(1)} fusion(f32[2,6,64,1024]{3,2,1,0:T(8,128)S(1)} %broadcast.279, s32[6]{0:T(128)S(1)} %reshape.801, f32[6,2,64,1024]{3,2,1,0:T(8,128)} %bitcast.235), kind=kCustom, calls=%fused_computation.3 | custom fusion | flops 786432 | bytes 9437208 | tf_op jit(solution)/shard_map/vmap()/scatter-add | solution.py:46
  119.0 5.4 %collective-permute-start.14 = (bf16[2,1,128,1024]{3,2,1,0:T(8,128)(2,1)}, bf16[2,1,128,1024]{3,2,1,0:T(8,128)(2,1)}, u32[]{:S(2)}, u32[]{:S(2)}) collective-permute-start(bf16[2,1,128,1024]{3,2,1,0:T(8,128)(2,1)} %get-tuple-element.11), channel_id=1, source_target_pairs={{0,4},{4,8},{8,12},{1,5},{5,9},{9,13},{2,6},{6,10},{10,14},{3,7},{... | collective-permute-start | bytes 1572872 | tf_op jit(solution)/shard_map/ppermute | solution.py:20
  125.8 1.8 %convert_element_type.221 = bf16[1,128,1024]{2,1,0:T(8,128)(2,1)} reshape(bf16[1,2,64,8,128]{4,3,2,1,0:T(8,128)(2,1)} %copy-done.15) | data formatting | bytes 524288 | tf_op jit(solution)/shard_map/convert_element_type | solution.py:115
  131.2 1.3 div.48
  134.0 1.8 %div.44 = f32[2,1,128,1024]{3,2,1,0:T(8,128)} reshape(f32[2,64,2,1024]{3,2,1,0:T(2,128)S(1)} %broadcast_in_dim.51) | data formatting | bytes 2097152 | tf_op jit(solution)/shard_map/div | solution.py:214
  135.8 2.5 %collective-permute-done.15 = bf16[2,1,128,1024]{3,2,1,0:T(8,128)(2,1)} collective-permute-done((bf16[2,1,128,1024]{3,2,1,0:T(8,128)(2,1)}, bf16[2,1,128,1024]{3,2,1,0:T(8,128)(2,1)}, u32[]{:S(2)}, u32[]{:S(2)}) %collective-permute-start.15) | collective-permute-done | bytes 524320 | tf_op jit(solution)/shard_map/ppermute | solution.py:22
  138.4 2.3 %fusion.11 = bf16[2,1,128,1024]{3,2,1,0:T(8,128)(2,1)S(1)} fusion(f32[2,1,128,1024]{3,2,1,0:T(8,128)} %div.48, f32[2,1,128,1024]{3,2,1,0:T(8,128)} %div.44, f32[2,1,128,1024]{3,2,1,0:T(8,128)S(1)} %bitcast.254, bf16[2,1,128,1024]{3,2,1,0:T(8,128)(2,1)} %collective-permute-done.15, bf16[2,1,256,1024]{3,2,1,0:T(8,128)(2,1)S(1)} %bitcast.237, ...), kind=kLoop, calls=%fused_computation.31 | loop fusion | flops 4456448 | bytes 5767168 | tf_op jit(solution)/shard_map/convert.1
  141.5 17.2 %all-gather.5.cloned.1.call-done = bf16[1024,1024]{1,0:T(8,128)(2,1)} async-done(((bf16[128,1024]{1,0:T(8,128)(2,1)}), bf16[1024,1024]{1,0:T(8,128)(2,1)}) %all-gather.5.cloned.1.call-update) | async-done | bytes 2097168 | tf_op jit(solution)/shard_map/all_gather | solution.py:148
  158.7 6.8 %fusion.78 = f32[1024,1024]{1,0:T(8,128)} fusion(bf16[1024,1024]{1,0:T(8,128)(2,1)} %all-gather.3.cloned.1.call-done, bf16[1024,1024]{1,0:T(8,128)(2,1)} %all-gather.5.cloned.1.call-done), kind=kOutput, calls=%fused_computation.160 | convolution fusion | flops 2147483648 | bytes 8388608 | tf_op jit(solution)/shard_map/tc,tw->cw/dot_general | solution.py:149
  (169 shorter events, 49.6 us)
Async XLA Ops:
  7.2 23.0 %copy-start = (bf16[1024,1024]{1,0:T(8,128)(2,1)S(1)}, bf16[1024,1024]{1,0:T(8,128)(2,1)}, u32[]{:S(2)}) copy-start(bf16[1024,1024]{1,0:T(8,128)(2,1)} %param.10) | copy-start | bytes 6291460
  7.2 134.3 %all-gather.3.cloned.1.call-start = ((), (), s32[]{:S(2)}) async-start(), calls=%async_computation | async-start | bytes 3145728 | tf_op jit(solution)/shard_map/all_gather | solution.py:147
  9.2 61.9 %collective-permute-start.1 = (bf16[2,1,128,1024]{3,2,1,0:T(8,128)(2,1)}, bf16[2,1,128,1024]{3,2,1,0:T(8,128)(2,1)}, u32[]{:S(2)}, u32[]{:S(2)}) collective-permute-start(bf16[2,1,128,1024]{3,2,1,0:T(8,128)(2,1)} %pad_maximum_fusion.5), channel_id=1, source_target_pairs={{4,0},{8,4},{12,8},{5,1},{9,5},{13,9},{6,2},{10,6},{14,10},{7,3},{... | collective-permute-start | bytes 1572872 | tf_op jit(solution)/shard_map/ppermute | solution.py:22
  10.5 60.6 %collective-permute-start = (bf16[2,1,128,1024]{3,2,1,0:T(8,128)(2,1)}, bf16[2,1,128,1024]{3,2,1,0:T(8,128)(2,1)}, u32[]{:S(2)}, u32[]{:S(2)}) collective-permute-start(bf16[2,1,128,1024]{3,2,1,0:T(8,128)(2,1)} %pad_maximum_fusion.5), channel_id=1, source_target_pairs={{0,4},{4,8},{8,12},{1,5},{5,9},{9,13},{2,6},{6,10},{10,14},{3,7},{... | collective-permute-start | bytes 1572872 | tf_op jit(solution)/shard_map/ppermute | solution.py:20
  18.0 9.9 %copy-start.24 = (s32[1,2,2]{2,1,0:T(2,128)S(1)}, s32[1,2,2]{2,1,0:T(2,128)}, u32[]{:S(2)}) copy-start(s32[1,2,2]{2,1,0:T(2,128)} %param.9) | copy-start | bytes 52
  20.2 13.5 %collective-permute-start.4 = (bf16[2,1,32,1024]{3,2,0,1:T(8,128)(2,1)S(1)}, bf16[2,1,32,1024]{3,2,0,1:T(8,128)(2,1)S(1)}, u32[]{:S(2)}, u32[]{:S(2)}) collective-permute-start(bf16[2,1,32,1024]{3,2,0,1:T(8,128)(2,1)S(1)} %fusion.61), channel_id=1, source_target_pairs={{0,12},{4,8},{8,4},{12,0},{1,13},{5,9},{9,5},{13,1},{2,14},{6,10},... | collective-permute-start | bytes 393224 | tf_op jit(solution)/shard_map/ppermute | solution.py:75
  21.6 21.1 %collective-permute-start.3 = (bf16[2,1,32,1024]{3,2,0,1:T(8,128)(2,1)S(1)}, bf16[2,1,32,1024]{3,2,0,1:T(8,128)(2,1)}, u32[]{:S(2)}, u32[]{:S(2)}) collective-permute-start(bf16[2,1,32,1024]{3,2,0,1:T(8,128)(2,1)S(1)} %fusion.61), channel_id=1, source_target_pairs={{0,8},{4,12},{8,0},{12,4},{1,9},{5,13},{9,1},{13,5},{2,10},{6,14},... | collective-permute-start | bytes 393224 | tf_op jit(solution)/shard_map/ppermute | solution.py:75
  22.9 9.2 %copy-start.20 = (bf16[1,128,1024]{2,1,0:T(8,128)(2,1)S(1)}, bf16[1,128,1024]{2,1,0:T(8,128)(2,1)}, u32[]{:S(2)}) copy-start(bf16[1,128,1024]{2,1,0:T(8,128)(2,1)} %param.6) | copy-start | bytes 786436
  25.0 21.3 %collective-permute-start.11 = (bf16[64,1024]{1,0:T(8,128)(2,1)}, bf16[64,1024]{1,0:T(8,128)(2,1)S(1)}, u32[]{:S(2)}, u32[]{:S(2)}) collective-permute-start(bf16[64,1024]{1,0:T(8,128)(2,1)} %get-tuple-element.16), channel_id=1, source_target_pairs={{0,12},{4,8},{8,4},{12,0},{1,13},{5,9},{9,5},{13,1},{2,14},{6,10},... | collective-permute-start | bytes 393224 | tf_op jit(solution)/shard_map/ppermute | solution.py:129
  33.7 11.0 %copy-start.23 = (bf16[2,1,32,1024]{3,2,0,1:T(8,128)(2,1)}, bf16[2,1,32,1024]{3,2,0,1:T(8,128)(2,1)S(1)}, u32[]{:S(2)}) copy-start(bf16[2,1,32,1024]{3,2,0,1:T(8,128)(2,1)S(1)} %collective-permute-done.4) | copy-start | bytes 393220
  33.7 15.0 %collective-permute-start.8 = (bf16[64,1024]{1,0:T(8,128)(2,1)}, bf16[64,1024]{1,0:T(8,128)(2,1)}, u32[]{:S(2)}, u32[]{:S(2)}) collective-permute-start(bf16[64,1024]{1,0:T(8,128)(2,1)} %get-tuple-element.17), channel_id=1, source_target_pairs={{0,8},{4,12},{8,0},{12,4},{1,9},{5,13},{9,1},{13,5},{2,10},{6,14},... | collective-permute-start | bytes 393224 | tf_op jit(solution)/shard_map/ppermute | solution.py:129
  42.7 7.7 %collective-permute-start.5 = (bf16[64,1024]{1,0:T(8,128)(2,1)}, bf16[64,1024]{1,0:T(8,128)(2,1)}, u32[]{:S(2)}, u32[]{:S(2)}) collective-permute-start(bf16[64,1024]{1,0:T(8,128)(2,1)} %get-tuple-element.15), channel_id=1, source_target_pairs={{0,4},{4,0},{8,12},{12,8},{1,5},{5,1},{9,13},{13,9},{2,6},{6,2},{1... | collective-permute-start | bytes 393224 | tf_op jit(solution)/shard_map/ppermute | solution.py:129
  46.3 4.1 %collective-permute-start.12 = (bf16[64,1024]{1,0:T(8,128)(2,1)S(1)}, bf16[64,1024]{1,0:T(8,128)(2,1)S(1)}, u32[]{:S(2)}, u32[]{:S(2)}) collective-permute-start(bf16[64,1024]{1,0:T(8,128)(2,1)S(1)} %collective-permute-done.11), channel_id=1, source_target_pairs={{0,1},{1,0},{2,3},{3,2},{4,5},{5,4},{6,7},{7,6},{8,9},{9,8},{10,11... | collective-permute-start | bytes 393224 | tf_op jit(solution)/shard_map/ppermute | solution.py:30
  48.7 8.1 %collective-permute-start.2 = (bf16[2,1,64,1024]{3,2,0,1:T(8,128)(2,1)S(1)}, bf16[2,1,64,1024]{3,2,0,1:T(8,128)(2,1)S(1)}, u32[]{:S(2)}, u32[]{:S(2)}) collective-permute-start(bf16[2,1,64,1024]{3,2,0,1:T(8,128)(2,1)S(1)} %get-tuple-element.25), channel_id=1, source_target_pairs={{0,4},{4,0},{8,12},{12,8},{1,5},{5,1},{9,13},{13,9},{2,6},{6,2},{1... | collective-permute-start | bytes 786440 | tf_op jit(solution)/shard_map/ppermute | solution.py:75
  50.4 10.2 %collective-permute-start.9 = (bf16[64,1024]{1,0:T(8,128)(2,1)}, bf16[64,1024]{1,0:T(8,128)(2,1)}, u32[]{:S(2)}, u32[]{:S(2)}) collective-permute-start(bf16[64,1024]{1,0:T(8,128)(2,1)} %collective-permute-done.8), channel_id=1, source_target_pairs={{0,1},{1,0},{2,3},{3,2},{4,5},{5,4},{6,7},{7,6},{8,9},{9,8},{10,11... | collective-permute-start | bytes 393224 | tf_op jit(solution)/shard_map/ppermute | solution.py:30
  50.4 12.7 %collective-permute-start.6 = (bf16[64,1024]{1,0:T(8,128)(2,1)}, bf16[64,1024]{1,0:T(8,128)(2,1)}, u32[]{:S(2)}, u32[]{:S(2)}) collective-permute-start(bf16[64,1024]{1,0:T(8,128)(2,1)} %collective-permute-done.5), channel_id=1, source_target_pairs={{0,1},{1,0},{2,3},{3,2},{4,5},{5,4},{6,7},{7,6},{8,9},{9,8},{10,11... | collective-permute-start | bytes 393224 | tf_op jit(solution)/shard_map/ppermute | solution.py:30
  57.0 13.7 %copy-start.11 = (bf16[1,1,128,1024]{2,3,1,0:T(8,128)(2,1)}, bf16[1,1,128,1024]{2,3,1,0:T(8,128)(2,1)S(1)}, u32[]{:S(2)}) copy-start(bf16[1,1,128,1024]{2,3,1,0:T(8,128)(2,1)S(1)} %copy.160) | copy-start | bytes 786436
  57.2 27.9 %copy-start.13 = (bf16[1,1,128,1024]{2,3,1,0:T(8,128)(2,1)}, bf16[1,1,128,1024]{2,3,1,0:T(8,128)(2,1)S(1)}, u32[]{:S(2)}) copy-start(bf16[1,1,128,1024]{2,3,1,0:T(8,128)(2,1)S(1)} %copy.167) | copy-start | bytes 786436
  57.2 20.7 %collective-permute-start.13 = (bf16[128,1024]{1,0:T(8,128)(2,1)}, bf16[128,1024]{1,0:T(8,128)(2,1)}, u32[]{:S(2)}, u32[]{:S(2)}) collective-permute-start(bf16[128,1024]{1,0:T(8,128)(2,1)} %convolution_convert_fusion), channel_id=1, source_target_pairs={{0,12},{4,8},{8,4},{12,0},{1,13},{5,9},{9,5},{13,1},{2,14},{6,10},... | collective-permute-start | bytes 786440 | tf_op jit(solution)/shard_map/ppermute | solution.py:139
  62.8 20.7 %collective-permute-start.10 = (bf16[128,1024]{1,0:T(8,128)(2,1)}, bf16[128,1024]{1,0:T(8,128)(2,1)}, u32[]{:S(2)}, u32[]{:S(2)}) collective-permute-start(bf16[128,1024]{1,0:T(8,128)(2,1)} %convolution_convert_fusion.1), channel_id=1, source_target_pairs={{0,8},{4,12},{8,0},{12,4},{1,9},{5,13},{9,1},{13,5},{2,10},{6,14},... | collective-permute-start | bytes 786440 | tf_op jit(solution)/shard_map/ppermute | solution.py:139
  65.4 18.1 %collective-permute-start.7 = (bf16[128,1024]{1,0:T(8,128)(2,1)}, bf16[128,1024]{1,0:T(8,128)(2,1)}, u32[]{:S(2)}, u32[]{:S(2)}) collective-permute-start(bf16[128,1024]{1,0:T(8,128)(2,1)} %convolution_convert_fusion.2), channel_id=1, source_target_pairs={{0,4},{4,0},{8,12},{12,8},{1,5},{5,1},{9,13},{13,9},{2,6},{6,2},{1... | collective-permute-start | bytes 786440 | tf_op jit(solution)/shard_map/ppermute | solution.py:139
  70.6 88.1 %all-gather.5.cloned.1.call-start = ((), (), s32[]{:S(2)}) async-start(), calls=%async_computation.1 | async-start | bytes 2359296 | tf_op jit(solution)/shard_map/all_gather | solution.py:148
  76.3 8.4 %copy-start.4 = (bf16[48,8,8,128]{3,2,1,0:T(8,128)(2,1)}, bf16[48,8,8,128]{3,2,1,0:T(8,128)(2,1)S(1)}, u32[]{:S(2)}) copy-start(bf16[48,8,8,128]{3,2,1,0:T(8,128)(2,1)S(1)} %copy.216) | copy-start | bytes 2359300
  76.3 7.2 %copy-start.16 = (f32[128,1024]{1,0:T(8,128)S(1)}, f32[128,1024]{1,0:T(8,128)}, u32[]{:S(2)}) copy-start(f32[128,1024]{1,0:T(8,128)} %fusion.44) | copy-start | bytes 1572868
  94.3 35.4 %collective-permute-start.18 = (bf16[2,1,32,1024]{3,0,2,1:T(2,128)(2,1)}, bf16[2,1,32,1024]{3,0,2,1:T(2,128)(2,1)}, u32[]{:S(2)}, u32[]{:S(2)}) collective-permute-start(bf16[2,1,32,1024]{3,0,2,1:T(2,128)(2,1)} %get-tuple-element.14), channel_id=1, source_target_pairs={{0,12},{4,8},{8,4},{12,0},{1,13},{5,9},{9,5},{13,1},{2,14},{6,10},... | collective-permute-start | bytes 393224 | tf_op jit(solution)/shard_map/ppermute | solution.py:209
  97.3 32.4 %collective-permute-start.17 = (bf16[2,1,32,1024]{3,0,2,1:T(2,128)(2,1)S(1)}, bf16[2,1,32,1024]{3,0,2,1:T(2,128)(2,1)}, u32[]{:S(2)}, u32[]{:S(2)}) collective-permute-start(bf16[2,1,32,1024]{3,0,2,1:T(2,128)(2,1)S(1)} %get-tuple-element.13), channel_id=1, source_target_pairs={{0,8},{4,12},{8,0},{12,4},{1,9},{5,13},{9,1},{13,5},{2,10},{6,14},... | collective-permute-start | bytes 393224 | tf_op jit(solution)/shard_map/ppermute | solution.py:209
  98.6 34.0 %collective-permute-start.16 = (bf16[2,1,64,1024]{3,2,0,1:T(8,128)(2,1)}, bf16[2,1,64,1024]{3,2,0,1:T(8,128)(2,1)}, u32[]{:S(2)}, u32[]{:S(2)}) collective-permute-start(bf16[2,1,64,1024]{3,2,0,1:T(8,128)(2,1)} %bitcast.229), channel_id=1, source_target_pairs={{0,4},{4,0},{8,12},{12,8},{1,5},{5,1},{9,13},{13,9},{2,6},{6,2},{1... | collective-permute-start | bytes 786440 | tf_op jit(solution)/shard_map/ppermute | solution.py:209
  115.6 8.8 %copy-start.5 = (bf16[48,8,8,128]{3,2,1,0:T(8,128)(2,1)S(1)}, bf16[48,8,8,128]{3,2,1,0:T(8,128)(2,1)}, u32[]{:S(2)}) copy-start(bf16[48,8,8,128]{3,2,1,0:T(8,128)(2,1)} %copy-done.4) | copy-start | bytes 2359300
  115.6 8.8 %copy-start.7 = (bf16[2,8,64,192]{3,2,1,0:T(8,128)(2,1)S(1)}, bf16[2,8,64,192]{3,2,1,0:T(8,128)(2,1)}, u32[]{:S(2)}) copy-start(bf16[2,8,64,192]{3,2,1,0:T(8,128)(2,1)} %copy-done.6) | copy-start | bytes 1179652
  115.7 9.1 %copy-start.12 = (bf16[1,1,128,1024]{2,3,1,0:T(8,128)(2,1)S(1)}, bf16[1,1,128,1024]{2,3,1,0:T(8,128)(2,1)}, u32[]{:S(2)}) copy-start(bf16[1,1,128,1024]{2,3,1,0:T(8,128)(2,1)} %copy-done.11) | copy-start | bytes 786436
  117.8 20.6 %collective-permute-start.15 = (bf16[2,1,128,1024]{3,2,1,0:T(8,128)(2,1)}, bf16[2,1,128,1024]{3,2,1,0:T(8,128)(2,1)}, u32[]{:S(2)}, u32[]{:S(2)}) collective-permute-start(bf16[2,1,128,1024]{3,2,1,0:T(8,128)(2,1)} %get-tuple-element.12), channel_id=1, source_target_pairs={{4,0},{8,4},{12,8},{5,1},{9,5},{13,9},{6,2},{10,6},{14,10},{7,3},{... | collective-permute-start | bytes 1572872 | tf_op jit(solution)/shard_map/ppermute | solution.py:22
  119.0 19.3 %collective-permute-start.14 = (bf16[2,1,128,1024]{3,2,1,0:T(8,128)(2,1)}, bf16[2,1,128,1024]{3,2,1,0:T(8,128)(2,1)}, u32[]{:S(2)}, u32[]{:S(2)}) collective-permute-start(bf16[2,1,128,1024]{3,2,1,0:T(8,128)(2,1)} %get-tuple-element.11), channel_id=1, source_target_pairs={{0,4},{4,8},{8,12},{1,5},{5,9},{9,13},{2,6},{6,10},{10,14},{3,7},{... | collective-permute-start | bytes 1572872 | tf_op jit(solution)/shard_map/ppermute | solution.py:20
  (15 other events, 44.6 us)
Sparse Core Ops, SparseCore 0:
  70.7 33.0 all-gather.2
  105.9 52.7 all-gather.4

commit v14 on v13

--- a/solution.py
+++ b/solution.py
@@ -144,7 +144,14 @@
     feat_docs = jnp.take(jnp.stack(feat_list, axis=0), feat_order, axis=0).reshape(
         seq_count * cot_rows.shape[0], feat_count
     )
-    feat_docs = lax.all_gather(feat_docs, "dp", axis=0, tiled=True)
+    if lax.axis_size("dp") == 2:
+        feat_docs = jnp.take(
+            jnp.stack([feat_docs, swapped(feat_docs, "dp", 0)], axis=0),
+            jnp.arange(2, dtype=jnp.int32) ^ lax.axis_index("dp"),
+            axis=0,
+        ).reshape(2 * feat_docs.shape[0], feat_count)
+    else:
+        feat_docs = lax.all_gather(feat_docs, "dp", axis=0, tiled=True)
     whole_output = lax.all_gather(out_rows, ("dp", "seq"), axis=0, tiled=True)
     weight_grad = jnp.einsum(
         "tc,tw->cw", feat_docs, whole_output, preferred_element_type=jnp.float32

time: 176 us -> 176 us (level)
  the two profiles are of different devices: /device:TPU:6 before, /device:TPU:26 now
where the time goes in v14:
time: 176 us; the launch traced here: 175 us
  other arithmetic  40.5 us (23%)
  waiting for transfers between devices  35.2 us (20%)
  local copies, waits for them, and re-layouts  33.3 us (19%)
  starting transfers between devices  28.3 us (16%)
  matrix products  23.1 us (13%)
  between operations  14.8 us (8%)
    ppermute x2, waiting for transfers between devices, extended(): lax.ppermute(tail, axis, [(i, (i + 1) % count) for i in range(ends)])  17.1 us
    ppermute x3, waiting for transfers between devices, shards(): lax.ppermute(pieces[level_no], 'seq', [(i, i ^ step) for i in range(seq_c...  8.72 us
    dot_general x1, matrix products, shards(): jnp.einsum('tc,tw->cw', feat_docs, whole_output, preferred_element_type=j...  6.77 us
    ppermute x2, starting transfers between devices, extended(): lax.ppermute(head, axis, [((i + 1) % count, i) for i in range(ends)])  6.04 us
    dot_general x3, matrix products, shards(): part = jnp.dot(got, out_weight, preferred_element_type=jnp.float32)  5.69 us
    ppermute x3, starting transfers between devices, shards(): lax.ppermute(lax.dynamic_slice_in_dim(sent, core * half, half, axis=0), '...  5.61 us
    scatter-add x1, other arithmetic, place_blocks(): return holder.at[:, chosen_doc].add(grad_doc)  5.6 us
    ppermute x3, starting transfers between devices, shards(): back = lax.ppermute(part.astype(jnp.bfloat16), 'seq', pairs)  4.45 us
  transfers between devices with their start and end apart: 21, of which 7 were waited for; matrix products, arithmetic and copies ran while one was open for 50% of the time, Pallas kernels for 0%

profile of v14, /device:TPU:26, one launch (start us, length us, event | category | flops | bytes accessed | tf_op | source)
XLA Modules:
  0.0 175.2 jit_solution(8783089150458003683)
XLA Ops:
  7.2 2.0 %pad_maximum_fusion.6 = bf16[2,1,128,1024]{3,2,1,0:T(8,128)(2,1)} fusion(bf16[1,1,128,1024]{3,2,1,0:T(8,128)(2,1)} %bitcast.266, bf16[1,1,128,1024]{3,2,1,0:T(8,128)(2,1)} %bitcast.268), kind=kLoop, calls=%fused_computation.54 | loop fusion | flops 262144 | bytes 1048576 | tf_op jit(solution)/shard_map/stack | solution.py:58
  9.2 3.1 %collective-permute-start.1 = (bf16[2,1,128,1024]{3,2,1,0:T(8,128)(2,1)}, bf16[2,1,128,1024]{3,2,1,0:T(8,128)(2,1)}, u32[]{:S(2)}, u32[]{:S(2)}) collective-permute-start(bf16[2,1,128,1024]{3,2,1,0:T(8,128)(2,1)} %pad_maximum_fusion.6), channel_id=1, source_target_pairs={{4,0},{8,4},{12,8},{5,1},{9,5},{13,9},{6,2},{10,6},{14,10},{7,3},{... | collective-permute-start | bytes 1572872 | tf_op jit(solution)/shard_map/ppermute | solution.py:22
  15.8 1.4 convert_reduce_fusion
  19.3 2.4 %collective-permute-start.4 = (bf16[2,1,32,1024]{3,2,0,1:T(8,128)(2,1)}, bf16[2,1,32,1024]{3,2,0,1:T(8,128)(2,1)}, u32[]{:S(2)}, u32[]{:S(2)}) collective-permute-start(bf16[2,1,32,1024]{3,2,0,1:T(8,128)(2,1)} %fusion.61), channel_id=1, source_target_pairs={{0,12},{4,8},{8,4},{12,0},{1,13},{5,9},{9,5},{13,1},{2,14},{6,10},... | collective-permute-start | bytes 393224 | tf_op jit(solution)/shard_map/ppermute | solution.py:75
  21.8 1.7 collective-permute-start.3
  34.6 4.7 %collective-permute-start.8 = (bf16[64,1024]{1,0:T(8,128)(2,1)}, bf16[64,1024]{1,0:T(8,128)(2,1)}, u32[]{:S(2)}, u32[]{:S(2)}) collective-permute-start(bf16[64,1024]{1,0:T(8,128)(2,1)} %get-tuple-element.17), channel_id=1, source_target_pairs={{0,8},{4,12},{8,0},{12,4},{1,9},{5,13},{9,1},{13,5},{2,10},{6,14},... | collective-permute-start | bytes 393224 | tf_op jit(solution)/shard_map/ppermute | solution.py:129
  39.3 4.8 %collective-permute-done.3 = bf16[2,1,32,1024]{3,2,0,1:T(8,128)(2,1)} collective-permute-done((bf16[2,1,32,1024]{3,2,0,1:T(8,128)(2,1)}, bf16[2,1,32,1024]{3,2,0,1:T(8,128)(2,1)}, u32[]{:S(2)}, u32[]{:S(2)}) %collective-permute-start.3) | collective-permute-done | bytes 131104 | tf_op jit(solution)/shard_map/ppermute | solution.py:75
  46.5 3.1 %collective-permute-done.8 = bf16[64,1024]{1,0:T(8,128)(2,1)} collective-permute-done((bf16[64,1024]{1,0:T(8,128)(2,1)}, bf16[64,1024]{1,0:T(8,128)(2,1)}, u32[]{:S(2)}, u32[]{:S(2)}) %collective-permute-start.8) | collective-permute-done | bytes 131104 | tf_op jit(solution)/shard_map/ppermute | solution.py:129
  52.5 3.9 %collective-permute-done.2 = bf16[2,1,64,1024]{3,2,0,1:T(8,128)(2,1)S(1)} collective-permute-done((bf16[2,1,64,1024]{3,2,0,1:T(8,128)(2,1)S(1)}, bf16[2,1,64,1024]{3,2,0,1:T(8,128)(2,1)S(1)}, u32[]{:S(2)}, u32[]{:S(2)}) %collective-permute-start.2) | collective-permute-done | bytes 262176 | tf_op jit(solution)/shard_map/ppermute | solution.py:75
  57.5 2.2 %convolution_convert_fusion.1 = bf16[128,1024]{1,0:T(8,128)(2,1)} fusion(bf16[1024,1024]{1,0:T(8,128)(2,1)S(1)} %copy-done, bf16[64,1024]{1,0:T(8,128)(2,1)} %collective-permute-done.9, bf16[64,1024]{1,0:T(8,128)(2,1)} %collective-permute-done.8, pred[]{:T(512)S(6)} %eq.2), kind=kOutput, calls=%fused_computation.27 | convolution fusion | flops 269746176 | bytes 2621441 | tf_op jit(solution)/shard_map/dot_general | solution.py:138
  59.7 2.7 %collective-permute-start.10 = (bf16[128,1024]{1,0:T(8,128)(2,1)}, bf16[128,1024]{1,0:T(8,128)(2,1)}, u32[]{:S(2)}, u32[]{:S(2)}) collective-permute-start(bf16[128,1024]{1,0:T(8,128)(2,1)} %convolution_convert_fusion.1), channel_id=1, source_target_pairs={{0,8},{4,12},{8,0},{12,4},{1,9},{5,13},{9,1},{13,5},{2,10},{6,14},... | collective-permute-start | bytes 786440 | tf_op jit(solution)/shard_map/ppermute | solution.py:139
  63.8 2.3 %convolution_convert_fusion.2 = bf16[128,1024]{1,0:T(8,128)(2,1)} fusion(bf16[1024,1024]{1,0:T(8,128)(2,1)S(1)} %copy-done, bf16[64,1024]{1,0:T(8,128)(2,1)} %collective-permute-done.6, bf16[64,1024]{1,0:T(8,128)(2,1)} %collective-permute-done.5, pred[]{:T(512)S(6)} %eq.2), kind=kOutput, calls=%fused_computation.28 | convolution fusion | flops 269746176 | bytes 2621441 | tf_op jit(solution)/shard_map/dot_general | solution.py:138
  74.8 1.8 %gather_fusion.3 = bf16[6,2,64,1024]{3,2,1,0:T(8,128)(2,1)} fusion(bf16[1,2,6,64,1024]{4,3,2,1,0:T(8,128)(2,1)S(1)} %bitcast.253, s32[6]{0:T(128)S(1)} %reshape.853), kind=kCustom, calls=%fused_computation.3 | custom fusion | bytes 3145776 | tf_op jit(solution)/shard_map/vmap()/gather | solution.py:41
  76.6 1.6 copy.153
  80.4 2.5 %collective-permute-done.10 = bf16[128,1024]{1,0:T(8,128)(2,1)} collective-permute-done((bf16[128,1024]{1,0:T(8,128)(2,1)}, bf16[128,1024]{1,0:T(8,128)(2,1)}, u32[]{:S(2)}, u32[]{:S(2)}) %collective-permute-start.10) | collective-permute-done | bytes 262176 | tf_op jit(solution)/shard_map/ppermute | solution.py:139
  85.1 1.6 multiply_reduce_fusion
  86.8 2.0 %convolution_bitcast_fusion = f32[1,2,192,8,128]{4,2,3,1,0:T(8,128)} fusion(bf16[2,64,8,128]{3,2,1,0:T(8,128)(2,1)S(1)} %bitcast.277, f32[2,8,64,192]{3,2,1,0:T(8,128)S(1)} %get-tuple-element.27, f32[2,8,64]{2,1,0:T(8,128)S(1)} %copy_add_fusion.1, f32[2,8,64]{2,1,0:T(8,128)S(1)} %copy_maximum_fusion), kind=kOutput, calls=%fused_computation.11 | convolution fusion | flops 50921472 | bytes 2629632 | tf_op jit(solution)/shard_map/dbhqk,dbqhe->dbkhe/dot_general | solution.py:184
  95.8 3.6 %collective-permute-start.16 = (bf16[2,1,64,1024]{3,2,0,1:T(8,128)(2,1)}, bf16[2,1,64,1024]{3,2,0,1:T(8,128)(2,1)}, u32[]{:S(2)}, u32[]{:S(2)}) collective-permute-start(bf16[2,1,64,1024]{3,2,0,1:T(8,128)(2,1)} %bitcast.236), channel_id=1, source_target_pairs={{0,4},{4,0},{8,12},{12,8},{1,5},{5,1},{9,13},{13,9},{2,6},{6,2},{1... | collective-permute-start | bytes 786440 | tf_op jit(solution)/shard_map/ppermute | solution.py:216
  102.2 3.1 %pad_maximum_fusion = f32[1,2,2,3,64,1024]{5,0,4,3,2,1:T(1,128)S(1)} fusion(f32[1,1,2,3,64,1024]{5,0,4,3,2,1:T(1,128)S(1)} %bitcast.255, f32[1,1,2,3,64,1024]{5,0,4,3,2,1:T(1,128)S(1)} %bitcast.256), kind=kLoop, calls=%fused_computation.5 | loop fusion | flops 786432 | bytes 6291456 | tf_op jit(solution)/shard_map/stack | solution.py:194
  105.3 2.4 %copy.215 = f32[1,2,2,3,64,1024]{5,4,1,3,2,0:T(8,128)} copy(f32[1,2,2,3,64,1024]{5,0,4,3,2,1:T(1,128)S(1)} %pad_maximum_fusion) | data formatting | bytes 6291456 | tf_op jit(solution)/shard_map/stack | solution.py:194
  108.3 5.6 %scatter_fusion = f32[2,6,64,1024]{3,2,1,0:T(8,128)S(1)} fusion(f32[2,6,64,1024]{3,2,1,0:T(8,128)S(1)} %broadcast.344, s32[6]{0:T(128)S(1)} %copy-done.30, f32[6,2,64,1024]{3,2,1,0:T(8,128)} %bitcast.243), kind=kCustom, calls=%fused_computation.4 | custom fusion | flops 786432 | bytes 9437208 | tf_op jit(solution)/shard_map/vmap()/scatter-add | solution.py:46
  116.2 2.9 %collective-permute-start.15 = (bf16[2,1,128,1024]{3,2,1,0:T(8,128)(2,1)}, bf16[2,1,128,1024]{3,2,1,0:T(8,128)(2,1)}, u32[]{:S(2)}, u32[]{:S(2)}) collective-permute-start(bf16[2,1,128,1024]{3,2,1,0:T(8,128)(2,1)} %get-tuple-element.12), channel_id=1, source_target_pairs={{4,0},{8,4},{12,8},{5,1},{9,5},{13,9},{6,2},{10,6},{14,10},{7,3},{... | collective-permute-start | bytes 1572872 | tf_op jit(solution)/shard_map/ppermute | solution.py:22
  121.8 1.8 %convert_element_type.221 = bf16[1,128,1024]{2,1,0:T(8,128)(2,1)} reshape(bf16[1,2,64,8,128]{4,3,2,1,0:T(8,128)(2,1)} %copy-done.16) | data formatting | bytes 524288 | tf_op jit(solution)/shard_map/convert_element_type | solution.py:115
  127.2 1.3 div.48
  130.1 1.8 %div.44 = f32[2,1,128,1024]{3,2,1,0:T(8,128)} reshape(f32[2,64,2,1024]{3,2,1,0:T(2,128)S(1)} %broadcast_in_dim.69) | data formatting | bytes 2097152 | tf_op jit(solution)/shard_map/div | solution.py:221
  131.9 2.6 %collective-permute-done.15 = bf16[2,1,128,1024]{3,2,1,0:T(8,128)(2,1)} collective-permute-done((bf16[2,1,128,1024]{3,2,1,0:T(8,128)(2,1)}, bf16[2,1,128,1024]{3,2,1,0:T(8,128)(2,1)}, u32[]{:S(2)}, u32[]{:S(2)}) %collective-permute-start.15) | collective-permute-done | bytes 524320 | tf_op jit(solution)/shard_map/ppermute | solution.py:22
  134.5 17.1 %collective-permute-done.14 = bf16[2,1,128,1024]{3,2,1,0:T(8,128)(2,1)} collective-permute-done((bf16[2,1,128,1024]{3,2,1,0:T(8,128)(2,1)}, bf16[2,1,128,1024]{3,2,1,0:T(8,128)(2,1)}, u32[]{:S(2)}, u32[]{:S(2)}) %collective-permute-start.14) | collective-permute-done | bytes 524320 | tf_op jit(solution)/shard_map/ppermute | solution.py:20
  151.6 2.4 %fusion.11 = bf16[2,1,128,1024]{3,2,1,0:T(8,128)(2,1)S(1)} fusion(f32[2,1,128,1024]{3,2,1,0:T(8,128)} %div.48, f32[2,1,128,1024]{3,2,1,0:T(8,128)} %div.44, f32[2,1,128,1024]{3,2,1,0:T(8,128)S(1)} %bitcast.263, bf16[2,1,128,1024]{3,2,1,0:T(8,128)(2,1)} %collective-permute-done.15, bf16[2,1,256,1024]{3,2,1,0:T(8,128)(2,1)S(1)} %bitcast.246, ...), kind=kLoop, calls=%fused_computation.34 | loop fusion | flops 4456448 | bytes 5767168 | tf_op jit(solution)/shard_map/convert.1
  154.7 2.7 %pad_maximum_fusion.1 = bf16[2,512,1024]{2,1,0:T(8,128)(2,1)} fusion(bf16[1,512,1024]{2,1,0:T(8,128)(2,1)} %bitcast.97, bf16[1,512,1024]{2,1,0:T(8,128)(2,1)S(1)} %copy-done.8), kind=kLoop, calls=%fused_computation.7 | loop fusion | flops 1048576 | bytes 4194304 | tf_op jit(solution)/shard_map/stack | solution.py:149
  157.5 2.4 %gather_fusion.2 = bf16[2,512,1024]{2,1,0:T(8,128)(2,1)S(1)} fusion(bf16[2,512,1024]{2,1,0:T(8,128)(2,1)} %pad_maximum_fusion.1, s32[1024]{0:T(1024)} %pad_clamp_fusion), kind=kCustom, calls=%fused_computation.2 | custom fusion | bytes 4194312 | tf_op jit(solution)/shard_map/jit(_take)/gather | solution.py:148
  159.9 1.7 bitcast_select_fusion
  161.6 6.8 %fusion.79 = f32[1024,1024]{1,0:T(8,128)} fusion(bf16[1024,1024]{1,0:T(8,128)(2,1)} %bitcast_select_fusion, bf16[1024,1024]{1,0:T(8,128)(2,1)} %all-gather.2.cloned.1.call-done), kind=kOutput, calls=%fused_computation.169 | convolution fusion | flops 2147483648 | bytes 8388608 | tf_op jit(solution)/shard_map/tc,tw->cw/dot_general | solution.py:156
  (193 shorter events, 58.3 us)
Async XLA Ops:
  7.2 22.6 %copy-start = (bf16[1024,1024]{1,0:T(8,128)(2,1)S(1)}, bf16[1024,1024]{1,0:T(8,128)(2,1)}, u32[]{:S(2)}) copy-start(bf16[1024,1024]{1,0:T(8,128)(2,1)} %param.10) | copy-start | bytes 6291460
  7.2 154.4 %all-gather.2.cloned.1.call-start = ((), (), s32[]{:S(2)}) async-start(), calls=%async_computation | async-start | bytes 2359296 | tf_op jit(solution)/shard_map/all_gather | solution.py:155
  9.2 63.7 %collective-permute-start.1 = (bf16[2,1,128,1024]{3,2,1,0:T(8,128)(2,1)}, bf16[2,1,128,1024]{3,2,1,0:T(8,128)(2,1)}, u32[]{:S(2)}, u32[]{:S(2)}) collective-permute-start(bf16[2,1,128,1024]{3,2,1,0:T(8,128)(2,1)} %pad_maximum_fusion.6), channel_id=1, source_target_pairs={{4,0},{8,4},{12,8},{5,1},{9,5},{13,9},{6,2},{10,6},{14,10},{7,3},{... | collective-permute-start | bytes 1572872 | tf_op jit(solution)/shard_map/ppermute | solution.py:22
  12.4 61.1 %collective-permute-start = (bf16[2,1,128,1024]{3,2,1,0:T(8,128)(2,1)}, bf16[2,1,128,1024]{3,2,1,0:T(8,128)(2,1)}, u32[]{:S(2)}, u32[]{:S(2)}) collective-permute-start(bf16[2,1,128,1024]{3,2,1,0:T(8,128)(2,1)} %pad_maximum_fusion.6), channel_id=1, source_target_pairs={{0,4},{4,8},{8,12},{1,5},{5,9},{9,13},{2,6},{6,10},{10,14},{3,7},{... | collective-permute-start | bytes 1572872 | tf_op jit(solution)/shard_map/ppermute | solution.py:20
  15.8 10.6 %copy-start.32 = (s32[1,2,2]{2,1,0:T(2,128)S(1)}, s32[1,2,2]{2,1,0:T(2,128)}, u32[]{:S(2)}) copy-start(s32[1,2,2]{2,1,0:T(2,128)} %param.9) | copy-start | bytes 52
  17.2 6.2 %copy-start.23 = (bf16[1,128,4096]{2,1,0:T(8,128)(2,1)S(1)}, bf16[1,128,4096]{2,1,0:T(8,128)(2,1)}, u32[]{:S(2)}) copy-start(bf16[1,128,4096]{2,1,0:T(8,128)(2,1)} %param.11) | copy-start | bytes 3145732
  19.3 15.3 %collective-permute-start.4 = (bf16[2,1,32,1024]{3,2,0,1:T(8,128)(2,1)}, bf16[2,1,32,1024]{3,2,0,1:T(8,128)(2,1)}, u32[]{:S(2)}, u32[]{:S(2)}) collective-permute-start(bf16[2,1,32,1024]{3,2,0,1:T(8,128)(2,1)} %fusion.61), channel_id=1, source_target_pairs={{0,12},{4,8},{8,4},{12,0},{1,13},{5,9},{9,5},{13,1},{2,14},{6,10},... | collective-permute-start | bytes 393224 | tf_op jit(solution)/shard_map/ppermute | solution.py:75
  21.8 22.3 %collective-permute-start.3 = (bf16[2,1,32,1024]{3,2,0,1:T(8,128)(2,1)}, bf16[2,1,32,1024]{3,2,0,1:T(8,128)(2,1)}, u32[]{:S(2)}, u32[]{:S(2)}) collective-permute-start(bf16[2,1,32,1024]{3,2,0,1:T(8,128)(2,1)} %fusion.61), channel_id=1, source_target_pairs={{0,8},{4,12},{8,0},{12,4},{1,9},{5,13},{9,1},{13,5},{2,10},{6,14},... | collective-permute-start | bytes 393224 | tf_op jit(solution)/shard_map/ppermute | solution.py:75
  24.4 21.3 %collective-permute-start.11 = (bf16[64,1024]{1,0:T(8,128)(2,1)}, bf16[64,1024]{1,0:T(8,128)(2,1)S(1)}, u32[]{:S(2)}, u32[]{:S(2)}) collective-permute-start(bf16[64,1024]{1,0:T(8,128)(2,1)} %get-tuple-element.16), channel_id=1, source_target_pairs={{0,12},{4,8},{8,4},{12,0},{1,13},{5,9},{9,5},{13,1},{2,14},{6,10},... | collective-permute-start | bytes 393224 | tf_op jit(solution)/shard_map/ppermute | solution.py:129
  27.2 17.9 %copy-start.17 = (bf16[1,128,1024]{2,1,0:T(8,128)(2,1)}, bf16[1,128,1024]{2,1,0:T(8,128)(2,1)S(1)}, u32[]{:S(2)}) copy-start(bf16[1,128,1024]{2,1,0:T(8,128)(2,1)S(1)} %constant_dynamic-slice_fusion) | copy-start | bytes 786436
  31.0 18.7 %copy-start.24 = (bf16[2,1,64,1024]{3,2,0,1:T(8,128)(2,1)S(1)}, bf16[2,1,64,1024]{3,2,0,1:T(8,128)(2,1)}, u32[]{:S(2)}) copy-start(bf16[2,1,64,1024]{3,2,0,1:T(8,128)(2,1)} %get-tuple-element.25) | copy-start | bytes 786436
  34.6 15.0 %collective-permute-start.8 = (bf16[64,1024]{1,0:T(8,128)(2,1)}, bf16[64,1024]{1,0:T(8,128)(2,1)}, u32[]{:S(2)}, u32[]{:S(2)}) collective-permute-start(bf16[64,1024]{1,0:T(8,128)(2,1)} %get-tuple-element.17), channel_id=1, source_target_pairs={{0,8},{4,12},{8,0},{12,4},{1,9},{5,13},{9,1},{13,5},{2,10},{6,14},... | collective-permute-start | bytes 393224 | tf_op jit(solution)/shard_map/ppermute | solution.py:129
  44.1 6.7 %collective-permute-start.5 = (bf16[64,1024]{1,0:T(8,128)(2,1)}, bf16[64,1024]{1,0:T(8,128)(2,1)}, u32[]{:S(2)}, u32[]{:S(2)}) collective-permute-start(bf16[64,1024]{1,0:T(8,128)(2,1)} %get-tuple-element.15), channel_id=1, source_target_pairs={{0,4},{4,0},{8,12},{12,8},{1,5},{5,1},{9,13},{13,9},{2,6},{6,2},{1... | collective-permute-start | bytes 393224 | tf_op jit(solution)/shard_map/ppermute | solution.py:129
  45.7 5.2 %collective-permute-start.12 = (bf16[64,1024]{1,0:T(8,128)(2,1)S(1)}, bf16[64,1024]{1,0:T(8,128)(2,1)S(1)}, u32[]{:S(2)}, u32[]{:S(2)}) collective-permute-start(bf16[64,1024]{1,0:T(8,128)(2,1)S(1)} %collective-permute-done.11), channel_id=1, source_target_pairs={{0,1},{1,0},{2,3},{3,2},{4,5},{5,4},{6,7},{7,6},{8,9},{9,8},{10,11... | collective-permute-start | bytes 393224 | tf_op jit(solution)/shard_map/ppermute | solution.py:30
  49.7 6.8 %collective-permute-start.2 = (bf16[2,1,64,1024]{3,2,0,1:T(8,128)(2,1)S(1)}, bf16[2,1,64,1024]{3,2,0,1:T(8,128)(2,1)S(1)}, u32[]{:S(2)}, u32[]{:S(2)}) collective-permute-start(bf16[2,1,64,1024]{3,2,0,1:T(8,128)(2,1)S(1)} %copy-done.24), channel_id=1, source_target_pairs={{0,4},{4,0},{8,12},{12,8},{1,5},{5,1},{9,13},{13,9},{2,6},{6,2},{1... | collective-permute-start | bytes 786440 | tf_op jit(solution)/shard_map/ppermute | solution.py:75
  50.8 6.7 %collective-permute-start.9 = (bf16[64,1024]{1,0:T(8,128)(2,1)}, bf16[64,1024]{1,0:T(8,128)(2,1)}, u32[]{:S(2)}, u32[]{:S(2)}) collective-permute-start(bf16[64,1024]{1,0:T(8,128)(2,1)} %collective-permute-done.8), channel_id=1, source_target_pairs={{0,1},{1,0},{2,3},{3,2},{4,5},{5,4},{6,7},{7,6},{8,9},{9,8},{10,11... | collective-permute-start | bytes 393224 | tf_op jit(solution)/shard_map/ppermute | solution.py:30
  50.8 13.0 %collective-permute-start.6 = (bf16[64,1024]{1,0:T(8,128)(2,1)}, bf16[64,1024]{1,0:T(8,128)(2,1)}, u32[]{:S(2)}, u32[]{:S(2)}) collective-permute-start(bf16[64,1024]{1,0:T(8,128)(2,1)} %collective-permute-done.5), channel_id=1, source_target_pairs={{0,1},{1,0},{2,3},{3,2},{4,5},{5,4},{6,7},{7,6},{8,9},{9,8},{10,11... | collective-permute-start | bytes 393224 | tf_op jit(solution)/shard_map/ppermute | solution.py:30
  56.7 6.9 %copy-start.12 = (bf16[1,1,128,1024]{2,3,1,0:T(8,128)(2,1)}, bf16[1,1,128,1024]{2,3,1,0:T(8,128)(2,1)S(1)}, u32[]{:S(2)}) copy-start(bf16[1,1,128,1024]{2,3,1,0:T(8,128)(2,1)S(1)} %copy.160) | copy-start | bytes 786436
  56.9 32.0 %copy-start.14 = (bf16[1,1,128,1024]{2,3,1,0:T(8,128)(2,1)}, bf16[1,1,128,1024]{2,3,1,0:T(8,128)(2,1)S(1)}, u32[]{:S(2)}) copy-start(bf16[1,1,128,1024]{2,3,1,0:T(8,128)(2,1)S(1)} %copy.167) | copy-start | bytes 786436
  56.9 23.5 %collective-permute-start.13 = (bf16[128,1024]{1,0:T(8,128)(2,1)}, bf16[128,1024]{1,0:T(8,128)(2,1)}, u32[]{:S(2)}, u32[]{:S(2)}) collective-permute-start(bf16[128,1024]{1,0:T(8,128)(2,1)} %convolution_convert_fusion), channel_id=1, source_target_pairs={{0,12},{4,8},{8,4},{12,0},{1,13},{5,9},{9,5},{13,1},{2,14},{6,10},... | collective-permute-start | bytes 786440 | tf_op jit(solution)/shard_map/ppermute | solution.py:139
  59.7 23.1 %collective-permute-start.10 = (bf16[128,1024]{1,0:T(8,128)(2,1)}, bf16[128,1024]{1,0:T(8,128)(2,1)}, u32[]{:S(2)}, u32[]{:S(2)}) collective-permute-start(bf16[128,1024]{1,0:T(8,128)(2,1)} %convolution_convert_fusion.1), channel_id=1, source_target_pairs={{0,8},{4,12},{8,0},{12,4},{1,9},{5,13},{9,1},{13,5},{2,10},{6,14},... | collective-permute-start | bytes 786440 | tf_op jit(solution)/shard_map/ppermute | solution.py:139
  66.1 16.7 %collective-permute-start.7 = (bf16[128,1024]{1,0:T(8,128)(2,1)}, bf16[128,1024]{1,0:T(8,128)(2,1)}, u32[]{:S(2)}, u32[]{:S(2)}) collective-permute-start(bf16[128,1024]{1,0:T(8,128)(2,1)} %convolution_convert_fusion.2), channel_id=1, source_target_pairs={{0,4},{4,0},{8,12},{12,8},{1,5},{5,1},{9,13},{13,9},{2,6},{6,2},{1... | collective-permute-start | bytes 786440 | tf_op jit(solution)/shard_map/ppermute | solution.py:139
  72.9 81.8 %collective-permute-start.19 = (bf16[512,1024]{1,0:T(8,128)(2,1)}, bf16[512,1024]{1,0:T(8,128)(2,1)}, u32[]{:S(2)}, u32[]{:S(2)}) collective-permute-start(bf16[512,1024]{1,0:T(8,128)(2,1)} %bitcast_select_fusion.1), channel_id=1, source_target_pairs={{0,2},{2,0},{1,3},{3,1},{4,6},{6,4},{5,7},{7,5},{8,10},{10,8},{9,1... | collective-permute-start | bytes 3145736 | tf_op jit(solution)/shard_map/ppermute | solution.py:30
  92.9 26.6 %collective-permute-start.18 = (bf16[2,1,32,1024]{3,0,2,1:T(2,128)(2,1)}, bf16[2,1,32,1024]{3,0,2,1:T(2,128)(2,1)}, u32[]{:S(2)}, u32[]{:S(2)}) collective-permute-start(bf16[2,1,32,1024]{3,0,2,1:T(2,128)(2,1)} %get-tuple-element.14), channel_id=1, source_target_pairs={{0,12},{4,8},{8,4},{12,0},{1,13},{5,9},{9,5},{13,1},{2,14},{6,10},... | collective-permute-start | bytes 393224 | tf_op jit(solution)/shard_map/ppermute | solution.py:216
  93.7 32.0 %collective-permute-start.17 = (bf16[2,1,32,1024]{3,0,2,1:T(2,128)(2,1)S(1)}, bf16[2,1,32,1024]{3,0,2,1:T(2,128)(2,1)}, u32[]{:S(2)}, u32[]{:S(2)}) collective-permute-start(bf16[2,1,32,1024]{3,0,2,1:T(2,128)(2,1)S(1)} %get-tuple-element.13), channel_id=1, source_target_pairs={{0,8},{4,12},{8,0},{12,4},{1,9},{5,13},{9,1},{13,5},{2,10},{6,14},... | collective-permute-start | bytes 393224 | tf_op jit(solution)/shard_map/ppermute | solution.py:216
  95.8 32.8 %collective-permute-start.16 = (bf16[2,1,64,1024]{3,2,0,1:T(8,128)(2,1)}, bf16[2,1,64,1024]{3,2,0,1:T(8,128)(2,1)}, u32[]{:S(2)}, u32[]{:S(2)}) collective-permute-start(bf16[2,1,64,1024]{3,2,0,1:T(8,128)(2,1)} %bitcast.236), channel_id=1, source_target_pairs={{0,4},{4,0},{8,12},{12,8},{1,5},{5,1},{9,13},{13,9},{2,6},{6,2},{1... | collective-permute-start | bytes 786440 | tf_op jit(solution)/shard_map/ppermute | solution.py:216
  114.2 6.6 %copy-start.13 = (bf16[1,1,128,1024]{2,3,1,0:T(8,128)(2,1)S(1)}, bf16[1,1,128,1024]{2,3,1,0:T(8,128)(2,1)}, u32[]{:S(2)}) copy-start(bf16[1,1,128,1024]{2,3,1,0:T(8,128)(2,1)} %copy-done.12) | copy-start | bytes 786436
  116.2 18.3 %collective-permute-start.15 = (bf16[2,1,128,1024]{3,2,1,0:T(8,128)(2,1)}, bf16[2,1,128,1024]{3,2,1,0:T(8,128)(2,1)}, u32[]{:S(2)}, u32[]{:S(2)}) collective-permute-start(bf16[2,1,128,1024]{3,2,1,0:T(8,128)(2,1)} %get-tuple-element.12), channel_id=1, source_target_pairs={{4,0},{8,4},{12,8},{5,1},{9,5},{13,9},{6,2},{10,6},{14,10},{7,3},{... | collective-permute-start | bytes 1572872 | tf_op jit(solution)/shard_map/ppermute | solution.py:22
  119.5 32.1 %collective-permute-start.14 = (bf16[2,1,128,1024]{3,2,1,0:T(8,128)(2,1)}, bf16[2,1,128,1024]{3,2,1,0:T(8,128)(2,1)}, u32[]{:S(2)}, u32[]{:S(2)}) collective-permute-start(bf16[2,1,128,1024]{3,2,1,0:T(8,128)(2,1)} %get-tuple-element.11), channel_id=1, source_target_pairs={{0,4},{4,8},{8,12},{1,5},{5,9},{9,13},{2,6},{6,10},{10,14},{3,7},{... | collective-permute-start | bytes 1572872 | tf_op jit(solution)/shard_map/ppermute | solution.py:20
  128.5 23.0 %copy-start.3 = (bf16[2,1,4,64,1024]{4,3,2,0,1:T(8,128)(2,1)S(1)}, bf16[2,1,4,64,1024]{4,3,2,0,1:T(8,128)(2,1)}, u32[]{:S(2)}) copy-start(bf16[2,1,4,64,1024]{4,3,2,0,1:T(8,128)(2,1)} %copy-done.2) | copy-start | bytes 3145732
  128.5 23.0 %copy-start.9 = (f32[2,1,2,64,1024]{4,3,2,0,1:T(8,128)S(1)}, f32[2,1,2,64,1024]{4,3,2,0,1:T(8,128)}, u32[]{:S(2)}) copy-start(f32[2,1,2,64,1024]{4,3,2,0,1:T(8,128)} %slice.82) | copy-start | bytes 3145732
  161.6 6.8 %copy-start.1 = (bf16[1024,1024]{1,0:T(8,128)(2,1)S(1)}, bf16[1024,1024]{1,0:T(8,128)(2,1)}, u32[]{:S(2)}) copy-start(bf16[1024,1024]{1,0:T(8,128)(2,1)} %param.10) | copy-start | bytes 6291460
  (23 other events, 79.5 us)
Sparse Core Ops, SparseCore 0:
  94.6 56.6 all-gather.1

commit v15 on v14

--- a/solution.py
+++ b/solution.py
@@ -135,10 +135,14 @@
             jnp.concatenate([got_half, other_half], axis=0),
             jnp.concatenate([other_half, got_half], axis=0),
         )
-        part = jnp.dot(got, out_weight, preferred_element_type=jnp.float32)
+        feat_list.append(got)
+    feat_list, attention = lax.optimization_barrier((feat_list, attention))
+    out_rows = attention.reshape(doc_count * tok_count, head_cols)
+    for step in range(1, seq_count):
+        pairs = [(i, i ^ step) for i in range(seq_count)]
+        part = jnp.dot(feat_list[step], out_weight, preferred_element_type=jnp.float32)
         back = lax.ppermute(part.astype(jnp.bfloat16), "seq", pairs)
         grad_sum = grad_sum + back.astype(jnp.float32)
-        feat_list.append(got)
     attn_grad = grad_sum.astype(jnp.bfloat16)
     feat_order = jnp.arange(seq_count, dtype=jnp.int32) ^ position
     feat_docs = jnp.take(jnp.stack(feat_list, axis=0), feat_order, axis=0).reshape(

time: 176 us -> 185 us (1.051)
  the two profiles are of different devices: /device:TPU:26 before, /device:TPU:6 now
where the time goes in v15:
time: 185 us; the launch traced here: 182 us
  other arithmetic  43.6 us (24%)
  local copies, waits for them, and re-layouts  41.2 us (22%)
  waiting for transfers between devices  31.9 us (17%)
  starting transfers between devices  29.8 us (16%)
  matrix products  21.2 us (11%)
  between operations  14.8 us (8%)
    ppermute x3, waiting for transfers between devices, shards(): lax.ppermute(pieces[level_no], 'seq', [(i, i ^ step) for i in range(seq_c...  14.4 us
    ppermute x3, waiting for transfers between devices, shards(): back = lax.ppermute(part.astype(jnp.bfloat16), 'seq', pairs)  11.7 us
    ppermute x2, starting transfers between devices, extended(): lax.ppermute(tail, axis, [(i, (i + 1) % count) for i in range(ends)])  8.62 us
    dot_general x1, matrix products, shards(): jnp.einsum('tc,tw->cw', feat_docs, whole_output, preferred_element_type=j...  6.77 us
    gather x5, local copies, waits for them, and re-layouts, pick_blocks(): return blocks_doc[:, chosen_doc]  6.23 us
    scatter-add x1, other arithmetic, place_blocks(): return holder.at[:, chosen_doc].add(grad_doc)  5.59 us
    select_n x3, other arithmetic, shards(): jnp.where(core == 0, jnp.concatenate([got_half, other_half], axis=0), jnp...  5.25 us
    ppermute x2, waiting for transfers between devices, extended(): lax.ppermute(head, axis, [((i + 1) % count, i) for i in range(ends)])  5.07 us
  transfers between devices with their start and end apart: 21, of which 5 were waited for; matrix products, arithmetic and copies ran while one was open for 43% of the time, Pallas kernels for 0%

profile of v15, /device:TPU:6, one launch (start us, length us, event | category | flops | bytes accessed | tf_op | source)
XLA Modules:
  0.0 182.5 jit_solution(1396449301608755822)
XLA Ops:
  12.4 3.7 %collective-permute-start.10 = (bf16[2,1,32,1024]{3,2,0,1:T(8,128)(2,1)S(1)}, bf16[2,1,32,1024]{3,2,0,1:T(8,128)(2,1)S(1)}, u32[]{:S(2)}, u32[]{:S(2)}) collective-permute-start(bf16[2,1,32,1024]{3,2,0,1:T(8,128)(2,1)S(1)} %fusion.43), channel_id=1, source_target_pairs={{0,12},{4,8},{8,4},{12,0},{1,13},{5,9},{9,5},{13,1},{2,14},{6,10},... | collective-permute-start | bytes 393224 | tf_op jit(solution)/shard_map/ppermute | solution.py:75
  16.0 2.0 %dynamic-slice_bitcast_fusion.1 = (bf16[64,1024]{1,0:T(8,128)(2,1)}, bf16[64,1024]{1,0:T(8,128)(2,1)}, bf16[64,1024]{1,0:T(8,128)(2,1)}) fusion(bf16[1,128,4096]{2,1,0:T(8,128)(2,1)} %param.11, s32[]{:T(128)S(6)} %select_n.149, s32[]{:T(128)S(6)} %select_n.157, s32[]{:T(128)S(6)} %select_n.151, s32[]{:T(128)S(6)} %select_n.154), kind=kLoop, calls=%fused_computation.107 | loop fusion | bytes 786448 | tf_op jit(solution)/shard_map/dynamic_slice | solution.py:130
  18.8 2.1 %collective-permute-start.2 = (bf16[64,1024]{1,0:T(8,128)(2,1)}, bf16[64,1024]{1,0:T(8,128)(2,1)}, u32[]{:S(2)}, u32[]{:S(2)}) collective-permute-start(bf16[64,1024]{1,0:T(8,128)(2,1)} %get-tuple-element.27), channel_id=1, source_target_pairs={{0,8},{4,12},{8,0},{12,4},{1,9},{5,13},{9,1},{13,5},{2,10},{6,14},... | collective-permute-start | bytes 393224 | tf_op jit(solution)/shard_map/ppermute | solution.py:129
  31.7 2.0 %collective-permute-done.9 = bf16[2,1,32,1024]{3,2,0,1:T(8,128)(2,1)S(1)} collective-permute-done((bf16[2,1,32,1024]{3,2,0,1:T(8,128)(2,1)S(1)}, bf16[2,1,32,1024]{3,2,0,1:T(8,128)(2,1)S(1)}, u32[]{:S(2)}, u32[]{:S(2)}) %collective-permute-start.9) | collective-permute-done | bytes 131104 | tf_op jit(solution)/shard_map/ppermute | solution.py:75
  36.6 3.3 %collective-permute-start.6 = (bf16[2,1,128,1024]{3,2,1,0:T(8,128)(2,1)}, bf16[2,1,128,1024]{3,2,1,0:T(8,128)(2,1)}, u32[]{:S(2)}, u32[]{:S(2)}) collective-permute-start(bf16[2,1,128,1024]{3,2,1,0:T(8,128)(2,1)} %pad_maximum_fusion.6), channel_id=1, source_target_pairs={{0,4},{4,8},{8,12},{1,5},{5,9},{9,13},{2,6},{6,10},{10,14},{3,7},{... | collective-permute-start | bytes 1572872 | tf_op jit(solution)/shard_map/ppermute | solution.py:20
  40.1 12.4 %collective-permute-done.8 = bf16[2,1,64,1024]{3,2,0,1:T(8,128)(2,1)} collective-permute-done((bf16[2,1,64,1024]{3,2,0,1:T(8,128)(2,1)}, bf16[2,1,64,1024]{3,2,0,1:T(8,128)(2,1)}, u32[]{:S(2)}, u32[]{:S(2)}) %collective-permute-start.8) | collective-permute-done | bytes 262176 | tf_op jit(solution)/shard_map/ppermute | solution.py:75
  54.2 1.8 maximum_select_fusion
  56.0 1.8 maximum_select_fusion.1
  57.7 1.8 copy.157
  60.4 1.7 maximum_select_fusion.2
  63.6 2.5 %pad_maximum_fusion.2 = bf16[2,1,384,1024]{3,2,1,0:T(8,128)(2,1)} fusion(bf16[2,1,128,1024]{3,2,1,0:T(8,128)(2,1)} %collective-permute-done.7, bf16[1,1,128,1024]{3,2,1,0:T(8,128)(2,1)S(1)} %bitcast.280, bf16[1,1,128,1024]{3,2,1,0:T(8,128)(2,1)S(1)} %bitcast.282, bf16[2,1,128,1024]{3,2,1,0:T(8,128)(2,1)} %collective-permute-done.6), kind=kLoop, calls=%fused_computation.11 | loop fusion | flops 6291456 | bytes 3145728 | tf_op jit(solution)/shard_map/concatenate | solution.py:18
  66.1 3.3 %gather_fusion.3 = bf16[6,2,64,1024]{3,2,1,0:T(8,128)(2,1)} fusion(bf16[1,2,6,64,1024]{4,3,2,1,0:T(8,128)(2,1)} %bitcast.266, s32[6]{0:T(128)S(1)} %reshape.688), kind=kCustom, calls=%fused_computation.3 | custom fusion | bytes 3145776 | tf_op jit(solution)/shard_map/vmap()/gather | solution.py:41
  75.3 1.8 convert_element_type.217
  81.6 3.4 %collective-permute-start.11 = (bf16[128,1024]{1,0:T(8,128)(2,1)}, bf16[128,1024]{1,0:T(8,128)(2,1)}, u32[]{:S(2)}, u32[]{:S(2)}) collective-permute-start(bf16[128,1024]{1,0:T(8,128)(2,1)} %convolution_convert_fusion.2), channel_id=1, source_target_pairs={{0,4},{4,0},{8,12},{12,8},{1,5},{5,1},{9,13},{13,9},{2,6},{6,2},{1... | collective-permute-start | bytes 786440 | tf_op jit(solution)/shard_map/ppermute | solution.py:144
  86.1 2.8 %gather_fusion.1 = bf16[4,128,1024]{2,1,0:T(8,128)(2,1)} fusion(bf16[4,128,1024]{2,1,0:T(8,128)(2,1)} %pad_maximum_fusion.3, s32[1024]{0:T(1024)S(1)} %pad_clamp_fusion.1), kind=kCustom, calls=%fused_computation.1 | custom fusion | bytes 2097168 | tf_op jit(solution)/shard_map/jit(_take)/gather | solution.py:148
  88.9 2.4 %bitcast_select_fusion.1 = bf16[512,1024]{1,0:T(8,128)(2,1)} fusion(bf16[4,128,1024]{2,1,0:T(8,128)(2,1)} %gather_fusion.1, pred[512]{0:T(512)(128)(4,1)S(1)} %broadcast_bitcast_fusion), kind=kLoop, calls=%fused_computation.40 | loop fusion | flops 524288 | bytes 2097664 | tf_op jit(solution)/shard_map/jit(_take)/select_n | solution.py:148
  91.8 2.4 %bitcast_select_fusion.2 = bf16[1,512,1024]{2,1,0:T(8,128)(2,1)} fusion(pred[512]{0:T(512)(128)(4,1)S(1)} %broadcast_bitcast_fusion, bf16[1,512,1024]{2,1,0:T(8,128)(2,1)} %bitcast.257), kind=kLoop, calls=%fused_computation.41 | loop fusion | flops 524288 | bytes 2097664 | tf_op jit(solution)/shard_map/jit(_take)/select_n | solution.py:148
  94.3 11.7 %collective-permute-done.12 = bf16[128,1024]{1,0:T(8,128)(2,1)} collective-permute-done((bf16[128,1024]{1,0:T(8,128)(2,1)}, bf16[128,1024]{1,0:T(8,128)(2,1)}, u32[]{:S(2)}, u32[]{:S(2)}) %collective-permute-start.12) | collective-permute-done | bytes 262176 | tf_op jit(solution)/shard_map/ppermute | solution.py:144
  110.3 2.1 %convolution_bitcast_fusion = f32[1,2,192,8,128]{4,2,3,1,0:T(8,128)} fusion(bf16[2,64,8,128]{3,2,1,0:T(8,128)(2,1)S(1)} %bitcast.292, f32[2,8,64,192]{3,2,1,0:T(8,128)S(1)} %copy-done.3, f32[2,8,64]{2,1,0:T(8,128)S(1)} %copy_add_fusion.1, f32[2,8,64]{2,1,0:T(8,128)S(1)} %copy_maximum_fusion), kind=kOutput, calls=%fused_computation.13 | convolution fusion | flops 50921472 | bytes 2629632 | tf_op jit(solution)/shard_map/dbhqk,dbqhe->dbkhe/dot_general | solution.py:188
  115.6 2.2 %collective-permute-start.18 = (bf16[2,1,32,1024]{3,0,2,1:T(2,128)(2,1)}, bf16[2,1,32,1024]{3,0,2,1:T(2,128)(2,1)}, u32[]{:S(2)}, u32[]{:S(2)}) collective-permute-start(bf16[2,1,32,1024]{3,0,2,1:T(2,128)(2,1)} %get-tuple-element.24), channel_id=1, source_target_pairs={{0,12},{4,8},{8,4},{12,0},{1,13},{5,9},{9,5},{13,1},{2,14},{6,10},... | collective-permute-start | bytes 393224 | tf_op jit(solution)/shard_map/ppermute | solution.py:220
  119.1 2.2 %collective-permute-start.16 = (bf16[2,1,64,1024]{3,2,0,1:T(8,128)(2,1)}, bf16[2,1,64,1024]{3,2,0,1:T(8,128)(2,1)}, u32[]{:S(2)}, u32[]{:S(2)}) collective-permute-start(bf16[2,1,64,1024]{3,2,0,1:T(8,128)(2,1)} %bitcast.249), channel_id=1, source_target_pairs={{0,4},{4,0},{8,12},{12,8},{1,5},{5,1},{9,13},{13,9},{2,6},{6,2},{1... | collective-permute-start | bytes 786440 | tf_op jit(solution)/shard_map/ppermute | solution.py:220
  124.9 3.1 %pad_maximum_fusion = f32[1,2,2,3,64,1024]{5,0,4,3,2,1:T(1,128)S(1)} fusion(f32[1,1,2,3,64,1024]{5,0,4,3,2,1:T(1,128)S(1)} %bitcast.268, f32[1,1,2,3,64,1024]{5,0,4,3,2,1:T(1,128)S(1)} %bitcast.269), kind=kLoop, calls=%fused_computation.5 | loop fusion | flops 786432 | bytes 6291456 | tf_op jit(solution)/shard_map/stack | solution.py:198
  128.0 2.4 %copy.211 = f32[1,2,2,3,64,1024]{5,4,1,3,2,0:T(8,128)} copy(f32[1,2,2,3,64,1024]{5,0,4,3,2,1:T(1,128)S(1)} %pad_maximum_fusion) | data formatting | bytes 6291456 | tf_op jit(solution)/shard_map/stack | solution.py:198
  131.0 5.6 %scatter_fusion = f32[2,6,64,1024]{3,2,1,0:T(8,128)S(1)} fusion(f32[2,6,64,1024]{3,2,1,0:T(8,128)S(1)} %broadcast.323, s32[6]{0:T(128)S(1)} %copy-done.31, f32[6,2,64,1024]{3,2,1,0:T(8,128)} %bitcast.256), kind=kCustom, calls=%fused_computation.4 | custom fusion | flops 786432 | bytes 9437208 | tf_op jit(solution)/shard_map/vmap()/scatter-add | solution.py:46
  139.8 5.4 %collective-permute-start.14 = (bf16[2,1,128,1024]{3,2,1,0:T(8,128)(2,1)}, bf16[2,1,128,1024]{3,2,1,0:T(8,128)(2,1)}, u32[]{:S(2)}, u32[]{:S(2)}) collective-permute-start(bf16[2,1,128,1024]{3,2,1,0:T(8,128)(2,1)} %get-tuple-element.21), channel_id=1, source_target_pairs={{0,4},{4,8},{8,12},{1,5},{5,9},{9,13},{2,6},{6,10},{10,14},{3,7},{... | collective-permute-start | bytes 1572872 | tf_op jit(solution)/shard_map/ppermute | solution.py:20
  151.9 1.8 div.44
  153.7 5.1 %collective-permute-done.15 = bf16[2,1,128,1024]{3,2,1,0:T(8,128)(2,1)} collective-permute-done((bf16[2,1,128,1024]{3,2,1,0:T(8,128)(2,1)}, bf16[2,1,128,1024]{3,2,1,0:T(8,128)(2,1)}, u32[]{:S(2)}, u32[]{:S(2)}) %collective-permute-start.15) | collective-permute-done | bytes 524320 | tf_op jit(solution)/shard_map/ppermute | solution.py:22
  158.8 2.4 %fusion.13 = bf16[2,1,128,1024]{3,2,1,0:T(8,128)(2,1)S(1)} fusion(f32[2,1,128,1024]{3,2,1,0:T(8,128)} %div.48, f32[2,1,128,1024]{3,2,1,0:T(8,128)} %div.44, f32[2,1,128,1024]{3,2,1,0:T(8,128)S(1)} %bitcast.276, bf16[2,1,128,1024]{3,2,1,0:T(8,128)(2,1)} %collective-permute-done.15, bf16[2,1,256,1024]{3,2,1,0:T(8,128)(2,1)S(1)} %bitcast.259, ...), kind=kLoop, calls=%fused_computation.36 | loop fusion | flops 4456448 | bytes 5767168 | tf_op jit(solution)/shard_map/convert.1
  162.0 2.7 %pad_maximum_fusion.1 = bf16[2,512,1024]{2,1,0:T(8,128)(2,1)} fusion(bf16[1,512,1024]{2,1,0:T(8,128)(2,1)} %bitcast.95, bf16[1,512,1024]{2,1,0:T(8,128)(2,1)S(1)} %copy-done.11), kind=kLoop, calls=%fused_computation.7 | loop fusion | flops 1048576 | bytes 4194304 | tf_op jit(solution)/shard_map/stack | solution.py:153
  164.7 2.4 %gather_fusion.2 = bf16[2,512,1024]{2,1,0:T(8,128)(2,1)S(1)} fusion(bf16[2,512,1024]{2,1,0:T(8,128)(2,1)} %pad_maximum_fusion.1, s32[1024]{0:T(1024)} %pad_clamp_fusion), kind=kCustom, calls=%fused_computation.2 | custom fusion | bytes 4194312 | tf_op jit(solution)/shard_map/jit(_take)/gather | solution.py:152
  167.1 1.7 bitcast_select_fusion
  168.9 6.8 %fusion = f32[1024,1024]{1,0:T(8,128)} fusion(bf16[1024,1024]{1,0:T(8,128)(2,1)} %bitcast_select_fusion, bf16[1,1024,1024]{2,1,0:T(8,128)(2,1)} %all-gather.3.cloned.1.call-done), kind=kOutput, calls=%fused_computation.8 | convolution fusion | flops 2147483648 | bytes 8388608 | tf_op jit(solution)/shard_map/tc,tw->cw/dot_general | solution.py:160
  (188 shorter events, 59.4 us)
Async XLA Ops:
  7.2 69.9 %copy-start = (bf16[1024,1024]{1,0:T(8,128)(2,1)S(1)}, bf16[1024,1024]{1,0:T(8,128)(2,1)}, u32[]{:S(2)}) copy-start(bf16[1024,1024]{1,0:T(8,128)(2,1)} %param.10) | copy-start | bytes 6291460
  7.2 161.7 %all-gather.3.cloned.1.call-start = ((), (), s32[]{:S(2)}) async-start(), calls=%async_computation | async-start | bytes 2359296 | tf_op jit(solution)/shard_map/all_gather | solution.py:159
  10.9 13.2 %copy-start.32 = (s32[1,2,2]{2,1,0:T(2,128)S(1)}, s32[1,2,2]{2,1,0:T(2,128)}, u32[]{:S(2)}) copy-start(s32[1,2,2]{2,1,0:T(2,128)} %param.9) | copy-start | bytes 52
  10.9 14.0 %copy-start.13 = (bf16[1,128,1024]{2,1,0:T(8,128)(2,1)S(1)}, bf16[1,128,1024]{2,1,0:T(8,128)(2,1)}, u32[]{:S(2)}) copy-start(bf16[1,128,1024]{2,1,0:T(8,128)(2,1)} %param.8) | copy-start | bytes 786436
  10.9 14.0 %copy-start.14 = (bf16[1,128,1024]{2,1,0:T(8,128)(2,1)S(1)}, bf16[1,128,1024]{2,1,0:T(8,128)(2,1)}, u32[]{:S(2)}) copy-start(bf16[1,128,1024]{2,1,0:T(8,128)(2,1)} %param.7) | copy-start | bytes 786436
  11.7 15.3 %copy-start.27 = (bf16[1,128,1024]{2,1,0:T(8,128)(2,1)S(1)}, bf16[1,128,1024]{2,1,0:T(8,128)(2,1)}, u32[]{:S(2)}) copy-start(bf16[1,128,1024]{2,1,0:T(8,128)(2,1)} %param.6) | copy-start | bytes 786436
  12.4 18.1 %collective-permute-start.10 = (bf16[2,1,32,1024]{3,2,0,1:T(8,128)(2,1)S(1)}, bf16[2,1,32,1024]{3,2,0,1:T(8,128)(2,1)S(1)}, u32[]{:S(2)}, u32[]{:S(2)}) collective-permute-start(bf16[2,1,32,1024]{3,2,0,1:T(8,128)(2,1)S(1)} %fusion.43), channel_id=1, source_target_pairs={{0,12},{4,8},{8,4},{12,0},{1,13},{5,9},{9,5},{13,1},{2,14},{6,10},... | collective-permute-start | bytes 393224 | tf_op jit(solution)/shard_map/ppermute | solution.py:75
  16.0 17.7 %collective-permute-start.9 = (bf16[2,1,32,1024]{3,2,0,1:T(8,128)(2,1)S(1)}, bf16[2,1,32,1024]{3,2,0,1:T(8,128)(2,1)S(1)}, u32[]{:S(2)}, u32[]{:S(2)}) collective-permute-start(bf16[2,1,32,1024]{3,2,0,1:T(8,128)(2,1)S(1)} %fusion.43), channel_id=1, source_target_pairs={{0,8},{4,12},{8,0},{12,4},{1,9},{5,13},{9,1},{13,5},{2,10},{6,14},... | collective-permute-start | bytes 393224 | tf_op jit(solution)/shard_map/ppermute | solution.py:75
  18.0 17.0 %collective-permute-start = (bf16[64,1024]{1,0:T(8,128)(2,1)}, bf16[64,1024]{1,0:T(8,128)(2,1)}, u32[]{:S(2)}, u32[]{:S(2)}) collective-permute-start(bf16[64,1024]{1,0:T(8,128)(2,1)} %get-tuple-element.26), channel_id=1, source_target_pairs={{0,4},{4,0},{8,12},{12,8},{1,5},{5,1},{9,13},{13,9},{2,6},{6,2},{1... | collective-permute-start | bytes 393224 | tf_op jit(solution)/shard_map/ppermute | solution.py:129
  18.8 17.8 %collective-permute-start.2 = (bf16[64,1024]{1,0:T(8,128)(2,1)}, bf16[64,1024]{1,0:T(8,128)(2,1)}, u32[]{:S(2)}, u32[]{:S(2)}) collective-permute-start(bf16[64,1024]{1,0:T(8,128)(2,1)} %get-tuple-element.27), channel_id=1, source_target_pairs={{0,8},{4,12},{8,0},{12,4},{1,9},{5,13},{9,1},{13,5},{2,10},{6,14},... | collective-permute-start | bytes 393224 | tf_op jit(solution)/shard_map/ppermute | solution.py:129
  21.0 18.9 %collective-permute-start.4 = (bf16[64,1024]{1,0:T(8,128)(2,1)}, bf16[64,1024]{1,0:T(8,128)(2,1)}, u32[]{:S(2)}, u32[]{:S(2)}) collective-permute-start(bf16[64,1024]{1,0:T(8,128)(2,1)} %get-tuple-element.25), channel_id=1, source_target_pairs={{0,12},{4,8},{8,4},{12,0},{1,13},{5,9},{9,5},{13,1},{2,14},{6,10},... | collective-permute-start | bytes 393224 | tf_op jit(solution)/shard_map/ppermute | solution.py:129
  30.4 33.1 %collective-permute-start.7 = (bf16[2,1,128,1024]{3,2,1,0:T(8,128)(2,1)}, bf16[2,1,128,1024]{3,2,1,0:T(8,128)(2,1)}, u32[]{:S(2)}, u32[]{:S(2)}) collective-permute-start(bf16[2,1,128,1024]{3,2,1,0:T(8,128)(2,1)} %pad_maximum_fusion.6), channel_id=1, source_target_pairs={{4,0},{8,4},{12,8},{5,1},{9,5},{13,9},{6,2},{10,6},{14,10},{7,3},{... | collective-permute-start | bytes 1572872 | tf_op jit(solution)/shard_map/ppermute | solution.py:22
  33.7 18.8 %collective-permute-start.8 = (bf16[2,1,64,1024]{3,2,0,1:T(8,128)(2,1)}, bf16[2,1,64,1024]{3,2,0,1:T(8,128)(2,1)}, u32[]{:S(2)}, u32[]{:S(2)}) collective-permute-start(bf16[2,1,64,1024]{3,2,0,1:T(8,128)(2,1)} %get-tuple-element.33), channel_id=1, source_target_pairs={{0,4},{4,0},{8,12},{12,8},{1,5},{5,1},{9,13},{13,9},{2,6},{6,2},{1... | collective-permute-start | bytes 786440 | tf_op jit(solution)/shard_map/ppermute | solution.py:75
  35.0 19.1 %collective-permute-start.1 = (bf16[64,1024]{1,0:T(8,128)(2,1)}, bf16[64,1024]{1,0:T(8,128)(2,1)S(1)}, u32[]{:S(2)}, u32[]{:S(2)}) collective-permute-start(bf16[64,1024]{1,0:T(8,128)(2,1)} %collective-permute-done), channel_id=1, source_target_pairs={{0,1},{1,0},{2,3},{3,2},{4,5},{5,4},{6,7},{7,6},{8,9},{9,8},{10,11... | collective-permute-start | bytes 393224 | tf_op jit(solution)/shard_map/ppermute | solution.py:30
  36.6 27.0 %collective-permute-start.6 = (bf16[2,1,128,1024]{3,2,1,0:T(8,128)(2,1)}, bf16[2,1,128,1024]{3,2,1,0:T(8,128)(2,1)}, u32[]{:S(2)}, u32[]{:S(2)}) collective-permute-start(bf16[2,1,128,1024]{3,2,1,0:T(8,128)(2,1)} %pad_maximum_fusion.6), channel_id=1, source_target_pairs={{0,4},{4,8},{8,12},{1,5},{5,9},{9,13},{2,6},{6,10},{10,14},{3,7},{... | collective-permute-start | bytes 1572872 | tf_op jit(solution)/shard_map/ppermute | solution.py:20
  39.8 16.1 %collective-permute-start.3 = (bf16[64,1024]{1,0:T(8,128)(2,1)}, bf16[64,1024]{1,0:T(8,128)(2,1)S(1)}, u32[]{:S(2)}, u32[]{:S(2)}) collective-permute-start(bf16[64,1024]{1,0:T(8,128)(2,1)} %collective-permute-done.2), channel_id=1, source_target_pairs={{0,1},{1,0},{2,3},{3,2},{4,5},{5,4},{6,7},{7,6},{8,9},{9,8},{10,11... | collective-permute-start | bytes 393224 | tf_op jit(solution)/shard_map/ppermute | solution.py:30
  52.5 7.9 %collective-permute-start.5 = (bf16[64,1024]{1,0:T(8,128)(2,1)}, bf16[64,1024]{1,0:T(8,128)(2,1)S(1)}, u32[]{:S(2)}, u32[]{:S(2)}) collective-permute-start(bf16[64,1024]{1,0:T(8,128)(2,1)} %collective-permute-done.4), channel_id=1, source_target_pairs={{0,1},{1,0},{2,3},{3,2},{4,5},{5,4},{6,7},{7,6},{8,9},{9,8},{10,11... | collective-permute-start | bytes 393224 | tf_op jit(solution)/shard_map/ppermute | solution.py:30
  73.0 37.3 %copy-start.28 = (f32[2,8,64]{2,1,0:T(8,128)}, f32[2,8,64]{2,1,0:T(8,128)S(1)}, u32[]{:S(2)}) copy-start(f32[2,8,64]{2,1,0:T(8,128)S(1)} %copy_add_fusion.1) | copy-start | bytes 12292
  78.3 16.0 %collective-permute-start.13 = (bf16[128,1024]{1,0:T(8,128)(2,1)}, bf16[128,1024]{1,0:T(8,128)(2,1)}, u32[]{:S(2)}, u32[]{:S(2)}) collective-permute-start(bf16[128,1024]{1,0:T(8,128)(2,1)} %convolution_convert_fusion), channel_id=1, source_target_pairs={{0,12},{4,8},{8,4},{12,0},{1,13},{5,9},{9,5},{13,1},{2,14},{6,10},... | collective-permute-start | bytes 786440 | tf_op jit(solution)/shard_map/ppermute | solution.py:144
  79.4 26.5 %collective-permute-start.12 = (bf16[128,1024]{1,0:T(8,128)(2,1)}, bf16[128,1024]{1,0:T(8,128)(2,1)}, u32[]{:S(2)}, u32[]{:S(2)}) collective-permute-start(bf16[128,1024]{1,0:T(8,128)(2,1)} %convolution_convert_fusion.1), channel_id=1, source_target_pairs={{0,8},{4,12},{8,0},{12,4},{1,9},{5,13},{9,1},{13,5},{2,10},{6,14},... | collective-permute-start | bytes 786440 | tf_op jit(solution)/shard_map/ppermute | solution.py:144
  81.6 24.4 %collective-permute-start.11 = (bf16[128,1024]{1,0:T(8,128)(2,1)}, bf16[128,1024]{1,0:T(8,128)(2,1)}, u32[]{:S(2)}, u32[]{:S(2)}) collective-permute-start(bf16[128,1024]{1,0:T(8,128)(2,1)} %convolution_convert_fusion.2), channel_id=1, source_target_pairs={{0,4},{4,0},{8,12},{12,8},{1,5},{5,1},{9,13},{13,9},{2,6},{6,2},{1... | collective-permute-start | bytes 786440 | tf_op jit(solution)/shard_map/ppermute | solution.py:144
  88.8 17.1 %copy-start.20 = (bf16[128,1024]{1,0:T(8,128)(2,1)S(1)}, bf16[128,1024]{1,0:T(8,128)(2,1)}, u32[]{:S(2)}) copy-start(bf16[128,1024]{1,0:T(8,128)(2,1)} %dynamic-slice_bitcast_fusion) | copy-start | bytes 786436
  91.3 70.7 %collective-permute-start.19 = (bf16[512,1024]{1,0:T(8,128)(2,1)}, bf16[512,1024]{1,0:T(8,128)(2,1)}, u32[]{:S(2)}, u32[]{:S(2)}) collective-permute-start(bf16[512,1024]{1,0:T(8,128)(2,1)} %bitcast_select_fusion.1), channel_id=1, source_target_pairs={{0,2},{2,0},{1,3},{3,1},{4,6},{6,4},{5,7},{7,5},{8,10},{10,8},{9,1... | collective-permute-start | bytes 3145736 | tf_op jit(solution)/shard_map/ppermute | solution.py:30
  94.2 13.4 %copy-start.3 = (f32[2,8,64,192]{3,2,1,0:T(8,128)S(1)}, f32[2,8,64,192]{3,2,1,0:T(8,128)}, u32[]{:S(2)}) copy-start(f32[2,8,64,192]{3,2,1,0:T(8,128)} %copy-done.2) | copy-start | bytes 2359300
  94.2 13.4 %copy-start.26 = (bf16[48,8,8,128]{3,2,1,0:T(8,128)(2,1)S(1)}, bf16[48,8,8,128]{3,2,1,0:T(8,128)(2,1)}, u32[]{:S(2)}) copy-start(bf16[48,8,8,128]{3,2,1,0:T(8,128)(2,1)} %copy-done.25) | copy-start | bytes 2359300
  115.6 24.2 %collective-permute-start.18 = (bf16[2,1,32,1024]{3,0,2,1:T(2,128)(2,1)}, bf16[2,1,32,1024]{3,0,2,1:T(2,128)(2,1)}, u32[]{:S(2)}, u32[]{:S(2)}) collective-permute-start(bf16[2,1,32,1024]{3,0,2,1:T(2,128)(2,1)} %get-tuple-element.24), channel_id=1, source_target_pairs={{0,12},{4,8},{8,4},{12,0},{1,13},{5,9},{9,5},{13,1},{2,14},{6,10},... | collective-permute-start | bytes 393224 | tf_op jit(solution)/shard_map/ppermute | solution.py:220
  117.8 29.7 %collective-permute-start.17 = (bf16[2,1,32,1024]{3,0,2,1:T(2,128)(2,1)S(1)}, bf16[2,1,32,1024]{3,0,2,1:T(2,128)(2,1)}, u32[]{:S(2)}, u32[]{:S(2)}) collective-permute-start(bf16[2,1,32,1024]{3,0,2,1:T(2,128)(2,1)S(1)} %get-tuple-element.23), channel_id=1, source_target_pairs={{0,8},{4,12},{8,0},{12,4},{1,9},{5,13},{9,1},{13,5},{2,10},{6,14},... | collective-permute-start | bytes 393224 | tf_op jit(solution)/shard_map/ppermute | solution.py:220
  119.1 31.3 %collective-permute-start.16 = (bf16[2,1,64,1024]{3,2,0,1:T(8,128)(2,1)}, bf16[2,1,64,1024]{3,2,0,1:T(8,128)(2,1)}, u32[]{:S(2)}, u32[]{:S(2)}) collective-permute-start(bf16[2,1,64,1024]{3,2,0,1:T(8,128)(2,1)} %bitcast.249), channel_id=1, source_target_pairs={{0,4},{4,0},{8,12},{12,8},{1,5},{5,1},{9,13},{13,9},{2,6},{6,2},{1... | collective-permute-start | bytes 786440 | tf_op jit(solution)/shard_map/ppermute | solution.py:220
  136.9 8.6 %copy-start.5 = (bf16[2,1,4,64,1024]{4,3,2,0,1:T(8,128)(2,1)}, bf16[2,1,4,64,1024]{4,3,2,0,1:T(8,128)(2,1)S(1)}, u32[]{:S(2)}) copy-start(bf16[2,1,4,64,1024]{4,3,2,0,1:T(8,128)(2,1)S(1)} %maximum_convert_fusion) | copy-start | bytes 3145732
  138.0 20.8 %collective-permute-start.15 = (bf16[2,1,128,1024]{3,2,1,0:T(8,128)(2,1)}, bf16[2,1,128,1024]{3,2,1,0:T(8,128)(2,1)}, u32[]{:S(2)}, u32[]{:S(2)}) collective-permute-start(bf16[2,1,128,1024]{3,2,1,0:T(8,128)(2,1)} %get-tuple-element.22), channel_id=1, source_target_pairs={{4,0},{8,4},{12,8},{5,1},{9,5},{13,9},{6,2},{10,6},{14,10},{7,3},{... | collective-permute-start | bytes 1572872 | tf_op jit(solution)/shard_map/ppermute | solution.py:22
  139.8 18.9 %collective-permute-start.14 = (bf16[2,1,128,1024]{3,2,1,0:T(8,128)(2,1)}, bf16[2,1,128,1024]{3,2,1,0:T(8,128)(2,1)}, u32[]{:S(2)}, u32[]{:S(2)}) collective-permute-start(bf16[2,1,128,1024]{3,2,1,0:T(8,128)(2,1)} %get-tuple-element.21), channel_id=1, source_target_pairs={{0,4},{4,8},{8,12},{1,5},{5,9},{9,13},{2,6},{6,10},{10,14},{3,7},{... | collective-permute-start | bytes 1572872 | tf_op jit(solution)/shard_map/ppermute | solution.py:20
  150.4 8.4 %copy-start.12 = (f32[2,1,2,64,1024]{4,3,2,0,1:T(8,128)S(1)}, f32[2,1,2,64,1024]{4,3,2,0,1:T(8,128)}, u32[]{:S(2)}) copy-start(f32[2,1,2,64,1024]{4,3,2,0,1:T(8,128)} %slice.82) | copy-start | bytes 3145732
  (22 other events, 80.5 us)
Sparse Core Ops, SparseCore 0:
  91.9 59.2 all-gather.2

commit v16 on v10

--- a/solution.py
+++ b/solution.py
@@ -138,8 +138,12 @@
     feat_docs = jnp.take(jnp.stack(feat_list, axis=0), feat_order, axis=0).reshape(
         seq_count * cot_rows.shape[0], feat_count
     )
-    feat_docs = lax.all_gather(feat_docs, "dp", axis=0, tiled=True)
-    whole_output = lax.all_gather(out_rows, ("dp", "seq"), axis=0, tiled=True)
+    dp_count = lax.axis_size("dp")
+    feat_docs = lax.all_gather(feat_docs, "dp", axis=0, tiled=False)
+    feat_docs = jnp.swapaxes(
+        feat_docs.reshape(dp_count, seq_count, cot_rows.shape[0], feat_count), 0, 1
+    ).reshape(dp_count * seq_count * cot_rows.shape[0], feat_count)
+    whole_output = lax.all_gather(out_rows, ("seq", "dp"), axis=0, tiled=True)
     weight_grad = jnp.einsum(
         "tc,tw->cw", feat_docs, whole_output, preferred_element_type=jnp.float32
     )

time: 172 us -> 175 us (1.017)
  local copies, waits for them, and re-layouts: 36.5 us -> 39.6 us
    transpose x0 -> x1, local copies, waits for them, and re-layouts: none -> 3.12 us  [shards(): jnp.swapaxes(feat_docs.reshape(dp_count, seq_count, cot_rows.shape[0], fe...]
  transfers between devices with their start and end apart: 20 -> 20, of which waited for: 6 -> 6; matrix products, arithmetic and copies ran while one was open for 48% -> 49% of each run, Pallas kernels for 0% -> 0%
where the time goes in v16:
time: 175 us; the launch traced here: 174 us
  local copies, waits for them, and re-layouts  39.6 us (23%)
  waiting for transfers between devices  38.2 us (22%)
  other arithmetic  33.7 us (19%)
  starting transfers between devices  25.1 us (14%)
  matrix products  22.8 us (13%)
  between operations  14.8 us (8%)
    ppermute x2, waiting for transfers between devices, extended(): lax.ppermute(tail, axis, [(i, (i + 1) % count) for i in range(ends)])  14.1 us
    ppermute x3, waiting for transfers between devices, shards(): lax.ppermute(lax.dynamic_slice_in_dim(sent, core * half, half, axis=0), '...  9.79 us
    ppermute x5, waiting for transfers between devices, swapped(): lax.ppermute(shard, axis, [(i, i ^ 1 << stride) for i in range(lax.axis_s...  9.23 us
    dot_general x1, matrix products, shards(): jnp.einsum('tc,tw->cw', feat_docs, whole_output, preferred_element_type=j...  6.77 us
    dot_general x3, matrix products, shards(): part = jnp.dot(got, out_weight, preferred_element_type=jnp.float32)  6.51 us
    ppermute x2, starting transfers between devices, extended(): lax.ppermute(head, axis, [((i + 1) % count, i) for i in range(ends)])  5.93 us
    unnamed x59, local copies, waits for them, and re-layouts  5.58 us
    scatter-add x1, other arithmetic, place_blocks(): return holder.at[:, chosen_doc].add(grad_doc)  5.38 us
  transfers between devices with their start and end apart: 20, of which 6 were waited for; matrix products, arithmetic and copies ran while one was open for 49% of the time, Pallas kernels for 0%

profile of v16, /device:TPU:30, one launch (start us, length us, event | category | flops | bytes accessed | tf_op | source)
XLA Modules:
  0.0 174.1 jit_solution(7170238478015297264)
XLA Ops:
  7.2 2.0 %pad_maximum_fusion.5 = bf16[2,1,128,1024]{3,2,1,0:T(8,128)(2,1)} fusion(bf16[1,1,128,1024]{3,2,1,0:T(8,128)(2,1)} %bitcast.255, bf16[1,1,128,1024]{3,2,1,0:T(8,128)(2,1)} %bitcast.257), kind=kLoop, calls=%fused_computation.50 | loop fusion | flops 262144 | bytes 1048576 | tf_op jit(solution)/shard_map/stack | solution.py:58
  9.3 3.1 %collective-permute-start.1 = (bf16[2,1,128,1024]{3,2,1,0:T(8,128)(2,1)}, bf16[2,1,128,1024]{3,2,1,0:T(8,128)(2,1)}, u32[]{:S(2)}, u32[]{:S(2)}) collective-permute-start(bf16[2,1,128,1024]{3,2,1,0:T(8,128)(2,1)} %pad_maximum_fusion.5), channel_id=1, source_target_pairs={{4,0},{8,4},{12,8},{5,1},{9,5},{13,9},{6,2},{10,6},{14,10},{7,3},{... | collective-permute-start | bytes 1572872 | tf_op jit(solution)/shard_map/ppermute | solution.py:22
  13.8 2.0 %dynamic-slice_bitcast_fusion.2 = (bf16[64,1024]{1,0:T(8,128)(2,1)}, bf16[64,1024]{1,0:T(8,128)(2,1)}, bf16[64,1024]{1,0:T(8,128)(2,1)}) fusion(bf16[1,128,4096]{2,1,0:T(8,128)(2,1)} %param.11, s32[]{:T(128)S(6)} %select_n.146, s32[]{:T(128)S(6)} %select_n.148, s32[]{:T(128)S(6)} %select_n.154, s32[]{:T(128)S(6)} %select_n.151), kind=kLoop, calls=%fused_computation.121 | loop fusion | bytes 786448 | tf_op jit(solution)/shard_map/dynamic_slice | solution.py:124
  15.8 2.4 %collective-permute-start.10 = (bf16[64,1024]{1,0:T(8,128)(2,1)}, bf16[64,1024]{1,0:T(8,128)(2,1)}, u32[]{:S(2)}, u32[]{:S(2)}) collective-permute-start(bf16[64,1024]{1,0:T(8,128)(2,1)} %get-tuple-element.16), channel_id=1, source_target_pairs={{0,12},{4,8},{8,4},{12,0},{1,13},{5,9},{9,5},{13,1},{2,14},{6,10},... | collective-permute-start | bytes 393224 | tf_op jit(solution)/shard_map/ppermute | solution.py:123
  18.2 1.7 collective-permute-start.7
  26.1 5.3 %collective-permute-done.10 = bf16[64,1024]{1,0:T(8,128)(2,1)} collective-permute-done((bf16[64,1024]{1,0:T(8,128)(2,1)}, bf16[64,1024]{1,0:T(8,128)(2,1)}, u32[]{:S(2)}, u32[]{:S(2)}) %collective-permute-start.10) | collective-permute-done | bytes 131104 | tf_op jit(solution)/shard_map/ppermute | solution.py:123
  33.9 4.5 %collective-permute-done.7 = bf16[64,1024]{1,0:T(8,128)(2,1)} collective-permute-done((bf16[64,1024]{1,0:T(8,128)(2,1)}, bf16[64,1024]{1,0:T(8,128)(2,1)}, u32[]{:S(2)}, u32[]{:S(2)}) %collective-permute-start.7) | collective-permute-done | bytes 131104 | tf_op jit(solution)/shard_map/ppermute | solution.py:123
  38.4 1.7 collective-permute-start.2
  40.5 2.2 %convolution_convert_fusion = bf16[128,1024]{1,0:T(8,128)(2,1)} fusion(bf16[1024,1024]{1,0:T(8,128)(2,1)S(1)} %copy-done, bf16[64,1024]{1,0:T(8,128)(2,1)} %collective-permute-done.11, bf16[64,1024]{1,0:T(8,128)(2,1)} %collective-permute-done.10, pred[]{:T(512)S(6)} %eq.9), kind=kOutput, calls=%fused_computation.22 | convolution fusion | flops 269746176 | bytes 2621441 | tf_op jit(solution)/shard_map/dot_general | solution.py:132
  43.2 2.1 %convolution_convert_fusion.1 = bf16[128,1024]{1,0:T(8,128)(2,1)} fusion(bf16[1024,1024]{1,0:T(8,128)(2,1)S(1)} %copy-done, bf16[64,1024]{1,0:T(8,128)(2,1)S(1)} %collective-permute-done.8, bf16[64,1024]{1,0:T(8,128)(2,1)} %collective-permute-done.7, pred[]{:T(512)S(6)} %eq.9), kind=kOutput, calls=%fused_computation.23 | convolution fusion | flops 269746176 | bytes 2621441 | tf_op jit(solution)/shard_map/dot_general | solution.py:132
  47.6 1.5 collective-permute-start.9
  50.2 2.8 %gather_fusion = bf16[4,128,1024]{2,1,0:T(8,128)(2,1)} fusion(bf16[4,128,1024]{2,1,0:T(8,128)(2,1)} %pad_maximum_fusion.2, s32[1024]{0:T(1024)S(1)} %pad_clamp_fusion), kind=kCustom, calls=%fused_computation | custom fusion | bytes 2097168 | tf_op jit(solution)/shard_map/jit(_take)/gather | solution.py:138
  53.0 2.4 %bitcast_select_fusion = bf16[1,512,1024]{2,1,0:T(8,128)(2,1)} fusion(pred[512]{0:T(512)(128)(4,1)S(1)} %broadcast_bitcast_fusion, bf16[1,512,1024]{2,1,0:T(8,128)(2,1)} %bitcast.250), kind=kLoop, calls=%fused_computation.35 | loop fusion | flops 524288 | bytes 2097664 | tf_op jit(solution)/shard_map/jit(_take)/select_n | solution.py:138
  55.7 2.1 %convolution_convert_fusion.2 = bf16[128,1024]{1,0:T(8,128)(2,1)} fusion(bf16[1024,1024]{1,0:T(8,128)(2,1)S(1)} %copy-done, bf16[64,1024]{1,0:T(8,128)(2,1)} %copy-done.20, bf16[64,1024]{1,0:T(8,128)(2,1)S(1)} %collective-permute-done.4, pred[]{:T(512)S(6)} %eq.9), kind=kOutput, calls=%fused_computation.24 | convolution fusion | flops 269746176 | bytes 2621441 | tf_op jit(solution)/shard_map/dot_general | solution.py:132
  57.8 2.6 %collective-permute-start.6 = (bf16[128,1024]{1,0:T(8,128)(2,1)}, bf16[128,1024]{1,0:T(8,128)(2,1)}, u32[]{:S(2)}, u32[]{:S(2)}) collective-permute-start(bf16[128,1024]{1,0:T(8,128)(2,1)} %convolution_convert_fusion.2), channel_id=1, source_target_pairs={{0,4},{4,0},{8,12},{12,8},{1,5},{5,1},{9,13},{13,9},{2,6},{6,2},{1... | collective-permute-start | bytes 786440 | tf_op jit(solution)/shard_map/ppermute | solution.py:133
  61.7 1.8 %gather_fusion.1 = bf16[6,2,64,1024]{3,2,1,0:T(8,128)(2,1)} fusion(bf16[1,2,6,64,1024]{4,3,2,1,0:T(8,128)(2,1)S(1)} %bitcast.240, s32[6]{0:T(128)S(1)} %reshape.813), kind=kCustom, calls=%fused_computation.1 | custom fusion | bytes 3145776 | tf_op jit(solution)/shard_map/vmap()/gather | solution.py:41
  63.5 1.7 copy.205
  74.6 9.2 %collective-permute-done.3 = bf16[2,1,64,1024]{3,2,1,0:T(8,128)(2,1)S(1)} collective-permute-done((bf16[2,1,64,1024]{3,2,1,0:T(8,128)(2,1)S(1)}, bf16[2,1,64,1024]{3,2,1,0:T(8,128)(2,1)S(1)}, u32[]{:S(2)}, u32[]{:S(2)}) %collective-permute-start.3) | collective-permute-done | bytes 262176 | tf_op jit(solution)/shard_map/ppermute | solution.py:30
  86.7 1.6 multiply_reduce_fusion
  98.0 3.4 %collective-permute-start.15 = (bf16[2,1,64,1024]{3,2,0,1:T(8,128)(2,1)}, bf16[2,1,64,1024]{3,2,0,1:T(8,128)(2,1)}, u32[]{:S(2)}, u32[]{:S(2)}) collective-permute-start(bf16[2,1,64,1024]{3,2,0,1:T(8,128)(2,1)} %bitcast.224), channel_id=1, source_target_pairs={{0,4},{4,0},{8,12},{12,8},{1,5},{5,1},{9,13},{13,9},{2,6},{6,2},{1... | collective-permute-start | bytes 786440 | tf_op jit(solution)/shard_map/ppermute | solution.py:207
  105.7 3.1 %pad_maximum_fusion = f32[1,2,2,3,64,1024]{5,0,4,3,2,1:T(1,128)S(1)} fusion(f32[1,1,2,3,64,1024]{5,0,4,3,2,1:T(1,128)S(1)} %bitcast.242, f32[1,1,2,3,64,1024]{5,0,4,3,2,1:T(1,128)S(1)} %bitcast.243), kind=kLoop, calls=%fused_computation.3 | loop fusion | flops 786432 | bytes 6291456 | tf_op jit(solution)/shard_map/stack | solution.py:185
  108.7 2.4 %copy.270 = f32[1,2,2,3,64,1024]{5,4,1,3,2,0:T(8,128)} copy(f32[1,2,2,3,64,1024]{5,0,4,3,2,1:T(1,128)S(1)} %pad_maximum_fusion) | data formatting | bytes 6291456 | tf_op jit(solution)/shard_map/stack | solution.py:185
  111.7 5.4 %scatter_fusion = f32[2,6,64,1024]{3,2,1,0:T(8,128)S(1)} fusion(f32[2,6,64,1024]{3,2,1,0:T(8,128)S(1)} %broadcast.241, s32[6]{0:T(128)S(1)} %copy-done.25, f32[6,2,64,1024]{3,2,1,0:T(8,128)} %bitcast.231), kind=kCustom, calls=%fused_computation.2 | custom fusion | flops 786432 | bytes 9437208 | tf_op jit(solution)/shard_map/vmap()/scatter-add | solution.py:46
  119.4 2.8 %collective-permute-start.14 = (bf16[2,1,128,1024]{3,2,1,0:T(8,128)(2,1)}, bf16[2,1,128,1024]{3,2,1,0:T(8,128)(2,1)}, u32[]{:S(2)}, u32[]{:S(2)}) collective-permute-start(bf16[2,1,128,1024]{3,2,1,0:T(8,128)(2,1)} %get-tuple-element.12), channel_id=1, source_target_pairs={{4,0},{8,4},{12,8},{5,1},{9,5},{13,9},{6,2},{10,6},{14,10},{7,3},{... | collective-permute-start | bytes 1572872 | tf_op jit(solution)/shard_map/ppermute | solution.py:22
  122.2 1.5 collective-permute-start.13
  125.2 1.8 %convert_element_type.198 = bf16[1,128,1024]{2,1,0:T(8,128)(2,1)} reshape(bf16[1,2,64,8,128]{4,3,2,1,0:T(8,128)(2,1)} %copy-done.13) | data formatting | bytes 524288 | tf_op jit(solution)/shard_map/convert_element_type | solution.py:109
  133.4 1.8 %div.44 = f32[2,1,128,1024]{3,2,1,0:T(8,128)} reshape(f32[2,64,2,1024]{3,2,1,0:T(2,128)S(1)} %broadcast_in_dim.33) | data formatting | bytes 2097152 | tf_op jit(solution)/shard_map/div | solution.py:212
  135.2 4.9 %collective-permute-done.14 = bf16[2,1,128,1024]{3,2,1,0:T(8,128)(2,1)} collective-permute-done((bf16[2,1,128,1024]{3,2,1,0:T(8,128)(2,1)}, bf16[2,1,128,1024]{3,2,1,0:T(8,128)(2,1)}, u32[]{:S(2)}, u32[]{:S(2)}) %collective-permute-start.14) | collective-permute-done | bytes 524320 | tf_op jit(solution)/shard_map/ppermute | solution.py:22
  140.2 14.1 %collective-permute-done.13 = bf16[2,1,128,1024]{3,2,1,0:T(8,128)(2,1)} collective-permute-done((bf16[2,1,128,1024]{3,2,1,0:T(8,128)(2,1)}, bf16[2,1,128,1024]{3,2,1,0:T(8,128)(2,1)}, u32[]{:S(2)}, u32[]{:S(2)}) %collective-permute-start.13) | collective-permute-done | bytes 524320 | tf_op jit(solution)/shard_map/ppermute | solution.py:20
  154.3 2.3 %fusion.11 = bf16[2,1,128,1024]{3,2,1,0:T(8,128)(2,1)S(1)} fusion(f32[2,1,128,1024]{3,2,1,0:T(8,128)} %div.48, f32[2,1,128,1024]{3,2,1,0:T(8,128)} %div.44, f32[2,1,128,1024]{3,2,1,0:T(8,128)S(1)} %bitcast.252, bf16[2,1,128,1024]{3,2,1,0:T(8,128)(2,1)} %collective-permute-done.14, bf16[2,1,256,1024]{3,2,1,0:T(8,128)(2,1)S(1)} %bitcast.233, ...), kind=kLoop, calls=%fused_computation.30 | loop fusion | flops 4456448 | bytes 5767168 | tf_op jit(solution)/shard_map/convert.1
  157.4 3.1 %copy.253 = bf16[4,2,128,1024]{3,2,1,0:T(8,128)(2,1)} copy(bf16[4,2,128,1024]{3,2,0,1:T(8,128)(2,1)} %bitcast.268) | data formatting | bytes 4194304 | tf_op jit(solution)/shard_map/transpose | solution.py:143
  160.5 6.8 %fusion.75 = f32[1024,1024]{1,0:T(8,128)} fusion(bf16[1024,1024]{1,0:T(8,128)(2,1)} %bitcast.269, bf16[1024,1024]{1,0:T(8,128)(2,1)} %all-gather.5.cloned.1.call-done), kind=kOutput, calls=%fused_computation.150 | convolution fusion | flops 2147483648 | bytes 8388608 | tf_op jit(solution)/shard_map/tc,tw->cw/dot_general | solution.py:147
  (166 shorter events, 53.1 us)
Async XLA Ops:
  7.2 17.7 %copy-start = (bf16[1024,1024]{1,0:T(8,128)(2,1)S(1)}, bf16[1024,1024]{1,0:T(8,128)(2,1)}, u32[]{:S(2)}) copy-start(bf16[1024,1024]{1,0:T(8,128)(2,1)} %param.10) | copy-start | bytes 6291460
  7.2 14.1 %copy-start.10 = (bf16[1,128,1024]{2,1,0:T(8,128)(2,1)S(1)}, bf16[1,128,1024]{2,1,0:T(8,128)(2,1)}, u32[]{:S(2)}) copy-start(bf16[1,128,1024]{2,1,0:T(8,128)(2,1)} %param.7) | copy-start | bytes 786436
  7.2 14.2 %copy-start.26 = (s32[1,2,2]{2,1,0:T(2,128)S(1)}, s32[1,2,2]{2,1,0:T(2,128)}, u32[]{:S(2)}) copy-start(s32[1,2,2]{2,1,0:T(2,128)} %param.9) | copy-start | bytes 52
  7.2 150.2 %all-gather.3.cloned.1.call-start = ((), (), s32[]{:S(2)}) async-start(), calls=%async_computation | async-start | bytes 3145728 | tf_op jit(solution)/shard_map/all_gather | solution.py:142
  9.3 48.5 %collective-permute-start.1 = (bf16[2,1,128,1024]{3,2,1,0:T(8,128)(2,1)}, bf16[2,1,128,1024]{3,2,1,0:T(8,128)(2,1)}, u32[]{:S(2)}, u32[]{:S(2)}) collective-permute-start(bf16[2,1,128,1024]{3,2,1,0:T(8,128)(2,1)} %pad_maximum_fusion.5), channel_id=1, source_target_pairs={{4,0},{8,4},{12,8},{5,1},{9,5},{13,9},{6,2},{10,6},{14,10},{7,3},{... | collective-permute-start | bytes 1572872 | tf_op jit(solution)/shard_map/ppermute | solution.py:22
  12.4 47.9 %collective-permute-start = (bf16[2,1,128,1024]{3,2,1,0:T(8,128)(2,1)}, bf16[2,1,128,1024]{3,2,1,0:T(8,128)(2,1)}, u32[]{:S(2)}, u32[]{:S(2)}) collective-permute-start(bf16[2,1,128,1024]{3,2,1,0:T(8,128)(2,1)} %pad_maximum_fusion.5), channel_id=1, source_target_pairs={{0,4},{4,8},{8,12},{1,5},{5,9},{9,13},{2,6},{6,10},{10,14},{3,7},{... | collective-permute-start | bytes 1572872 | tf_op jit(solution)/shard_map/ppermute | solution.py:20
  15.8 15.6 %collective-permute-start.10 = (bf16[64,1024]{1,0:T(8,128)(2,1)}, bf16[64,1024]{1,0:T(8,128)(2,1)}, u32[]{:S(2)}, u32[]{:S(2)}) collective-permute-start(bf16[64,1024]{1,0:T(8,128)(2,1)} %get-tuple-element.16), channel_id=1, source_target_pairs={{0,12},{4,8},{8,4},{12,0},{1,13},{5,9},{9,5},{13,1},{2,14},{6,10},... | collective-permute-start | bytes 393224 | tf_op jit(solution)/shard_map/ppermute | solution.py:123
  18.2 20.2 %collective-permute-start.7 = (bf16[64,1024]{1,0:T(8,128)(2,1)}, bf16[64,1024]{1,0:T(8,128)(2,1)}, u32[]{:S(2)}, u32[]{:S(2)}) collective-permute-start(bf16[64,1024]{1,0:T(8,128)(2,1)} %get-tuple-element.17), channel_id=1, source_target_pairs={{0,8},{4,12},{8,0},{12,4},{1,9},{5,13},{9,1},{13,5},{2,10},{6,14},... | collective-permute-start | bytes 393224 | tf_op jit(solution)/shard_map/ppermute | solution.py:123
  19.9 20.1 %collective-permute-start.4 = (bf16[64,1024]{1,0:T(8,128)(2,1)}, bf16[64,1024]{1,0:T(8,128)(2,1)S(1)}, u32[]{:S(2)}, u32[]{:S(2)}) collective-permute-start(bf16[64,1024]{1,0:T(8,128)(2,1)} %get-tuple-element.15), channel_id=1, source_target_pairs={{0,4},{4,0},{8,12},{12,8},{1,5},{5,1},{9,13},{13,9},{2,6},{6,2},{1... | collective-permute-start | bytes 393224 | tf_op jit(solution)/shard_map/ppermute | solution.py:123
  31.4 8.8 %collective-permute-start.11 = (bf16[64,1024]{1,0:T(8,128)(2,1)}, bf16[64,1024]{1,0:T(8,128)(2,1)}, u32[]{:S(2)}, u32[]{:S(2)}) collective-permute-start(bf16[64,1024]{1,0:T(8,128)(2,1)} %collective-permute-done.10), channel_id=1, source_target_pairs={{0,1},{1,0},{2,3},{3,2},{4,5},{5,4},{6,7},{7,6},{8,9},{9,8},{10,11... | collective-permute-start | bytes 393224 | tf_op jit(solution)/shard_map/ppermute | solution.py:30
  38.4 27.0 %collective-permute-start.2 = (f32[2,1,64,1024]{3,2,1,0:T(8,128)}, f32[2,1,64,1024]{3,2,1,0:T(8,128)}, u32[]{:S(2)}, u32[]{:S(2)}) collective-permute-start(f32[2,1,64,1024]{3,2,1,0:T(8,128)} %get-tuple-element.25), channel_id=1, source_target_pairs={{0,4},{4,0},{8,12},{12,8},{1,5},{5,1},{9,13},{13,9},{2,6},{6,2},{1... | collective-permute-start | bytes 1572872 | tf_op jit(solution)/shard_map/ppermute | solution.py:30
  40.0 2.8 %collective-permute-start.8 = (bf16[64,1024]{1,0:T(8,128)(2,1)}, bf16[64,1024]{1,0:T(8,128)(2,1)S(1)}, u32[]{:S(2)}, u32[]{:S(2)}) collective-permute-start(bf16[64,1024]{1,0:T(8,128)(2,1)} %collective-permute-done.7), channel_id=1, source_target_pairs={{0,1},{1,0},{2,3},{3,2},{4,5},{5,4},{6,7},{7,6},{8,9},{9,8},{10,11... | collective-permute-start | bytes 393224 | tf_op jit(solution)/shard_map/ppermute | solution.py:30
  40.2 7.3 %collective-permute-start.5 = (bf16[64,1024]{1,0:T(8,128)(2,1)S(1)}, bf16[64,1024]{1,0:T(8,128)(2,1)S(1)}, u32[]{:S(2)}, u32[]{:S(2)}) collective-permute-start(bf16[64,1024]{1,0:T(8,128)(2,1)S(1)} %collective-permute-done.4), channel_id=1, source_target_pairs={{0,1},{1,0},{2,3},{3,2},{4,5},{5,4},{6,7},{7,6},{8,9},{9,8},{10,11... | collective-permute-start | bytes 393224 | tf_op jit(solution)/shard_map/ppermute | solution.py:30
  42.8 27.9 %collective-permute-start.12 = (bf16[128,1024]{1,0:T(8,128)(2,1)}, bf16[128,1024]{1,0:T(8,128)(2,1)}, u32[]{:S(2)}, u32[]{:S(2)}) collective-permute-start(bf16[128,1024]{1,0:T(8,128)(2,1)} %convolution_convert_fusion), channel_id=1, source_target_pairs={{0,12},{4,8},{8,4},{12,0},{1,13},{5,9},{9,5},{13,1},{2,14},{6,10},... | collective-permute-start | bytes 786440 | tf_op jit(solution)/shard_map/ppermute | solution.py:133
  47.6 23.1 %collective-permute-start.9 = (bf16[128,1024]{1,0:T(8,128)(2,1)}, bf16[128,1024]{1,0:T(8,128)(2,1)}, u32[]{:S(2)}, u32[]{:S(2)}) collective-permute-start(bf16[128,1024]{1,0:T(8,128)(2,1)} %convolution_convert_fusion.1), channel_id=1, source_target_pairs={{0,8},{4,12},{8,0},{12,4},{1,9},{5,13},{9,1},{13,5},{2,10},{6,14},... | collective-permute-start | bytes 786440 | tf_op jit(solution)/shard_map/ppermute | solution.py:133
  55.5 105.0 %all-gather.5.cloned.1.call-start = ((), (), s32[]{:S(2)}) async-start(), calls=%async_computation.1 | async-start | bytes 2359296 | tf_op jit(solution)/shard_map/all_gather | solution.py:146
  57.8 12.9 %collective-permute-start.6 = (bf16[128,1024]{1,0:T(8,128)(2,1)}, bf16[128,1024]{1,0:T(8,128)(2,1)}, u32[]{:S(2)}, u32[]{:S(2)}) collective-permute-start(bf16[128,1024]{1,0:T(8,128)(2,1)} %convolution_convert_fusion.2), channel_id=1, source_target_pairs={{0,4},{4,0},{8,12},{12,8},{1,5},{5,1},{9,13},{13,9},{2,6},{6,2},{1... | collective-permute-start | bytes 786440 | tf_op jit(solution)/shard_map/ppermute | solution.py:133
  68.0 5.9 %copy-start.4 = (bf16[48,8,8,128]{3,2,1,0:T(8,128)(2,1)}, bf16[48,8,8,128]{3,2,1,0:T(8,128)(2,1)S(1)}, u32[]{:S(2)}) copy-start(bf16[48,8,8,128]{3,2,1,0:T(8,128)(2,1)S(1)} %copy.271) | copy-start | bytes 2359300
  70.0 13.8 %collective-permute-start.3 = (bf16[2,1,64,1024]{3,2,1,0:T(8,128)(2,1)S(1)}, bf16[2,1,64,1024]{3,2,1,0:T(8,128)(2,1)S(1)}, u32[]{:S(2)}, u32[]{:S(2)}) collective-permute-start(bf16[2,1,64,1024]{3,2,1,0:T(8,128)(2,1)S(1)} %fusion.21), channel_id=1, source_target_pairs={{0,8},{4,12},{8,0},{12,4},{1,9},{5,13},{9,1},{13,5},{2,10},{6,14},... | collective-permute-start | bytes 786440 | tf_op jit(solution)/shard_map/ppermute | solution.py:30
  72.8 11.3 %copy-start.17 = (bf16[2,64,8,128]{3,1,0,2:T(8,128)(2,1)S(1)}, bf16[2,64,8,128]{3,1,0,2:T(8,128)(2,1)}, u32[]{:S(2)}) copy-start(bf16[2,64,8,128]{3,1,0,2:T(8,128)(2,1)} %copy.216) | copy-start | bytes 786436
  94.3 7.1 %copy-start.22 = (f32[2,8,64]{2,1,0:T(8,128)S(1)}, f32[2,8,64]{2,1,0:T(8,128)}, u32[]{:S(2)}) copy-start(f32[2,8,64]{2,1,0:T(8,128)} %copy-done.21) | copy-start | bytes 12292
  95.7 33.3 %collective-permute-start.17 = (bf16[2,1,32,1024]{3,0,2,1:T(2,128)(2,1)}, bf16[2,1,32,1024]{3,0,2,1:T(2,128)(2,1)}, u32[]{:S(2)}, u32[]{:S(2)}) collective-permute-start(bf16[2,1,32,1024]{3,0,2,1:T(2,128)(2,1)} %get-tuple-element.14), channel_id=1, source_target_pairs={{0,12},{4,8},{8,4},{12,0},{1,13},{5,9},{9,5},{13,1},{2,14},{6,10},... | collective-permute-start | bytes 393224 | tf_op jit(solution)/shard_map/ppermute | solution.py:207
  96.7 32.3 %collective-permute-start.16 = (bf16[2,1,32,1024]{3,0,2,1:T(2,128)(2,1)S(1)}, bf16[2,1,32,1024]{3,0,2,1:T(2,128)(2,1)}, u32[]{:S(2)}, u32[]{:S(2)}) collective-permute-start(bf16[2,1,32,1024]{3,0,2,1:T(2,128)(2,1)S(1)} %get-tuple-element.13), channel_id=1, source_target_pairs={{0,8},{4,12},{8,0},{12,4},{1,9},{5,13},{9,1},{13,5},{2,10},{6,14},... | collective-permute-start | bytes 393224 | tf_op jit(solution)/shard_map/ppermute | solution.py:207
  98.0 33.9 %collective-permute-start.15 = (bf16[2,1,64,1024]{3,2,0,1:T(8,128)(2,1)}, bf16[2,1,64,1024]{3,2,0,1:T(8,128)(2,1)}, u32[]{:S(2)}, u32[]{:S(2)}) collective-permute-start(bf16[2,1,64,1024]{3,2,0,1:T(8,128)(2,1)} %bitcast.224), channel_id=1, source_target_pairs={{0,4},{4,0},{8,12},{12,8},{1,5},{5,1},{9,13},{13,9},{2,6},{6,2},{1... | collective-permute-start | bytes 786440 | tf_op jit(solution)/shard_map/ppermute | solution.py:207
  117.3 6.5 %copy-start.5 = (bf16[48,8,8,128]{3,2,1,0:T(8,128)(2,1)S(1)}, bf16[48,8,8,128]{3,2,1,0:T(8,128)(2,1)}, u32[]{:S(2)}) copy-start(bf16[48,8,8,128]{3,2,1,0:T(8,128)(2,1)} %copy-done.4) | copy-start | bytes 2359300
  117.3 6.5 %copy-start.7 = (bf16[2,8,64,192]{3,2,1,0:T(8,128)(2,1)S(1)}, bf16[2,8,64,192]{3,2,1,0:T(8,128)(2,1)}, u32[]{:S(2)}) copy-start(bf16[2,8,64,192]{3,2,1,0:T(8,128)(2,1)} %copy-done.6) | copy-start | bytes 1179652
  117.4 6.8 %copy-start.12 = (bf16[1,1,128,1024]{2,3,1,0:T(8,128)(2,1)S(1)}, bf16[1,1,128,1024]{2,3,1,0:T(8,128)(2,1)}, u32[]{:S(2)}) copy-start(bf16[1,1,128,1024]{2,3,1,0:T(8,128)(2,1)} %copy-done.11) | copy-start | bytes 786436
  119.4 20.7 %collective-permute-start.14 = (bf16[2,1,128,1024]{3,2,1,0:T(8,128)(2,1)}, bf16[2,1,128,1024]{3,2,1,0:T(8,128)(2,1)}, u32[]{:S(2)}, u32[]{:S(2)}) collective-permute-start(bf16[2,1,128,1024]{3,2,1,0:T(8,128)(2,1)} %get-tuple-element.12), channel_id=1, source_target_pairs={{4,0},{8,4},{12,8},{5,1},{9,5},{13,9},{6,2},{10,6},{14,10},{7,3},{... | collective-permute-start | bytes 1572872 | tf_op jit(solution)/shard_map/ppermute | solution.py:22
  122.2 32.0 %collective-permute-start.13 = (bf16[2,1,128,1024]{3,2,1,0:T(8,128)(2,1)}, bf16[2,1,128,1024]{3,2,1,0:T(8,128)(2,1)}, u32[]{:S(2)}, u32[]{:S(2)}) collective-permute-start(bf16[2,1,128,1024]{3,2,1,0:T(8,128)(2,1)} %get-tuple-element.11), channel_id=1, source_target_pairs={{0,4},{4,8},{8,12},{1,5},{5,9},{9,13},{2,6},{6,10},{10,14},{3,7},{... | collective-permute-start | bytes 1572872 | tf_op jit(solution)/shard_map/ppermute | solution.py:20
  131.9 22.4 %copy-start.3 = (bf16[2,1,4,64,1024]{4,3,2,0,1:T(8,128)(2,1)S(1)}, bf16[2,1,4,64,1024]{4,3,2,0,1:T(8,128)(2,1)}, u32[]{:S(2)}) copy-start(bf16[2,1,4,64,1024]{4,3,2,0,1:T(8,128)(2,1)} %copy-done.2) | copy-start | bytes 3145732
  131.9 22.4 %copy-start.8 = (f32[2,1,2,64,1024]{4,3,2,0,1:T(8,128)S(1)}, f32[2,1,2,64,1024]{4,3,2,0,1:T(8,128)}, u32[]{:S(2)}) copy-start(f32[2,1,2,64,1024]{4,3,2,0,1:T(8,128)} %slice.78) | copy-start | bytes 3145732
  160.5 6.8 %copy-start.1 = (bf16[1024,1024]{1,0:T(8,128)(2,1)S(1)}, bf16[1024,1024]{1,0:T(8,128)(2,1)}, u32[]{:S(2)}) copy-start(bf16[1024,1024]{1,0:T(8,128)(2,1)} %param.10) | copy-start | bytes 6291460
  (15 other events, 29.6 us)
Sparse Core Ops, SparseCore 0:
  55.6 34.1 all-gather.2
  94.1 58.6 all-gather.4

commit v17 on v10

--- a/solution.py
+++ b/solution.py
@@ -60,8 +60,17 @@
     blocks_six = padded.reshape(2, doc_count, 6, block, head_cols)
     local_ids = jnp.arange(2, dtype=jnp.int32)[None, :, None]
     chosen = jnp.concatenate([local_ids, local_ids + pattern], axis=2) + 2
-    near_pair = jax.vmap(pick_blocks, in_axes=(1, 0), out_axes=1)(blocks_six, chosen)
-    near_pair = near_pair.reshape(2, doc_count, 2, near_width, head_cols)
+    candidates = [[b + p + 2 for p in (-2, -1, 1, 2)] for b in range(2)]
+    picked = []
+    for b in range(2):
+        picked.append(blocks_six[:, :, b + 2])
+        for n in range(1, NEAR + 1):
+            index = chosen[:, b, n][None, :, None, None]
+            acc = jnp.zeros_like(blocks_six[:, :, 0])
+            for j in candidates[b]:
+                acc = jnp.where(index == j, blocks_six[:, :, j], acc)
+            picked.append(acc)
+    near_pair = jnp.stack(picked, axis=2).reshape(2, doc_count, 2, near_width, head_cols)
     pooled = pool_pairs(key_value.astype(jnp.float32))
     siblings = []
     own_level = pooled
@@ -181,7 +190,18 @@
     near_rows = jnp.stack([near_key_rows, near_value_rows]).reshape(
         2, doc_count, 2, NEAR + 1, block, head_cols
     )
-    back_six = jax.vmap(place_blocks, in_axes=(1, 0), out_axes=1)(near_rows, chosen)
+    slots = []
+    for j in range(6):
+        total = jnp.zeros_like(near_rows[:, :, 0, 0])
+        for b in range(2):
+            if j == b + 2:
+                total = total + near_rows[:, :, b, 0]
+            if j in candidates[b]:
+                for n in range(1, NEAR + 1):
+                    index = chosen[:, b, n][None, :, None, None]
+                    total = total + jnp.where(index == j, near_rows[:, :, b, n], 0.0)
+        slots.append(total)
+    back_six = jnp.stack(slots, axis=2)
     rims = jnp.concatenate([back_six[:, :, 0:2], back_six[:, :, 4:6]], axis=2).reshape(
         2, doc_count, 2 * tok_count, head_cols
     )

time: 172 us -> 184 us (1.070)
  the two profiles are of different devices: /device:TPU:30 before, /device:TPU:6 now
where the time goes in v17:
time: 184 us; the launch traced here: 181 us
  waiting for transfers between devices  41.5 us (23%)
  starting transfers between devices  33.4 us (18%)
  other arithmetic  32.3 us (18%)
  local copies, waits for them, and re-layouts  26.3 us (14%)
  between operations  25.2 us (14%)
  matrix products  22.2 us (12%)
    all_gather x1, waiting for transfers between devices, shards(): whole_output = lax.all_gather(out_rows, ('dp', 'seq'), axis=0, tiled=True)  18.5 us
    ppermute x5, waiting for transfers between devices, swapped(): lax.ppermute(shard, axis, [(i, i ^ 1 << stride) for i in range(lax.axis_s...  16.9 us
    ppermute x2, starting transfers between devices, extended(): lax.ppermute(tail, axis, [(i, (i + 1) % count) for i in range(ends)])  10.7 us
    ppermute x5, starting transfers between devices, swapped(): lax.ppermute(shard, axis, [(i, i ^ 1 << stride) for i in range(lax.axis_s...  7.17 us
    dot_general x1, matrix products, shards(): jnp.einsum('tc,tw->cw', feat_docs, whole_output, preferred_element_type=j...  6.77 us
    another operation x4, other arithmetic  4.96 us
    add x4, other arithmetic, shards(): total = total + jnp.where(index == j, near_rows[:, :, b, n], 0.0)  4.88 us
    unnamed x53, local copies, waits for them, and re-layouts  4.75 us
  transfers between devices with their start and end apart: 20, of which 6 were waited for; matrix products, arithmetic and copies ran while one was open for 38% of the time, Pallas kernels for 0%

profile of v17, /device:TPU:6, one launch (start us, length us, event | category | flops | bytes accessed | tf_op | source)
XLA Modules:
  0.0 180.8 jit_solution(15519559694278356967)
XLA Ops:
  7.3 2.0 %pad_maximum_fusion.6 = bf16[2,1,128,1024]{3,2,1,0:T(8,128)(2,1)} fusion(bf16[1,1,128,1024]{3,2,1,0:T(8,128)(2,1)} %bitcast.265, bf16[1,1,128,1024]{3,2,1,0:T(8,128)(2,1)} %bitcast.267), kind=kLoop, calls=%fused_computation.67 | loop fusion | flops 262144 | bytes 1048576 | tf_op jit(solution)/shard_map/stack | solution.py:58
  9.3 1.3 collective-permute-start.1
  10.6 5.4 %collective-permute-start = (bf16[2,1,128,1024]{3,2,1,0:T(8,128)(2,1)}, bf16[2,1,128,1024]{3,2,1,0:T(8,128)(2,1)}, u32[]{:S(2)}, u32[]{:S(2)}) collective-permute-start(bf16[2,1,128,1024]{3,2,1,0:T(8,128)(2,1)} %pad_maximum_fusion.6), channel_id=1, source_target_pairs={{0,4},{4,8},{8,12},{1,5},{5,9},{9,13},{2,6},{6,10},{10,14},{3,7},{... | collective-permute-start | bytes 1572872 | tf_op jit(solution)/shard_map/ppermute | solution.py:20
  15.9 1.9 %dynamic-slice_bitcast_fusion.2 = (bf16[64,1024]{1,0:T(8,128)(2,1)S(1)}, bf16[64,1024]{1,0:T(8,128)(2,1)S(1)}, bf16[64,1024]{1,0:T(8,128)(2,1)}) fusion(bf16[1,128,4096]{2,1,0:T(8,128)(2,1)} %param.11, s32[]{:T(128)S(6)} %select_n.448, s32[]{:T(128)S(6)} %select_n.450, s32[]{:T(128)S(6)} %select_n.456, s32[]{:T(128)S(6)} %select_n.453), kind=kLoop, calls=%fused_computation.149 | loop fusion | bytes 786448 | tf_op jit(solution)/shard_map/dynamic_slice | solution.py:133
  17.9 1.5 collective-permute-start.10
  20.5 1.8 collective-permute-start.4
  22.5 1.4 convert_reduce_fusion
  28.1 3.1 %collective-permute-done.10 = bf16[64,1024]{1,0:T(8,128)(2,1)S(1)} collective-permute-done((bf16[64,1024]{1,0:T(8,128)(2,1)S(1)}, bf16[64,1024]{1,0:T(8,128)(2,1)S(1)}, u32[]{:S(2)}, u32[]{:S(2)}) %collective-permute-start.10) | collective-permute-done | bytes 131104 | tf_op jit(solution)/shard_map/ppermute | solution.py:132
  42.4 6.6 %collective-permute-start.2 = (f32[2,1,64,1024]{3,2,1,0:T(8,128)}, f32[2,1,64,1024]{3,2,1,0:T(8,128)}, u32[]{:S(2)}, u32[]{:S(2)}) collective-permute-start(f32[2,1,64,1024]{3,2,1,0:T(8,128)} %get-tuple-element.31), channel_id=1, source_target_pairs={{0,4},{4,0},{8,12},{12,8},{1,5},{5,1},{9,13},{13,9},{2,6},{6,2},{1... | collective-permute-start | bytes 1572872 | tf_op jit(solution)/shard_map/ppermute | solution.py:30
  50.6 3.4 %collective-permute-start.12 = (bf16[128,1024]{1,0:T(8,128)(2,1)}, bf16[128,1024]{1,0:T(8,128)(2,1)}, u32[]{:S(2)}, u32[]{:S(2)}) collective-permute-start(bf16[128,1024]{1,0:T(8,128)(2,1)} %convolution_convert_fusion), channel_id=1, source_target_pairs={{0,12},{4,8},{8,4},{12,0},{1,13},{5,9},{9,5},{13,1},{2,14},{6,10},... | collective-permute-start | bytes 786440 | tf_op jit(solution)/shard_map/ppermute | solution.py:142
  57.0 1.8 %gather_fusion = bf16[4,128,1024]{2,1,0:T(8,128)(2,1)S(1)} fusion(bf16[4,128,1024]{2,1,0:T(8,128)(2,1)} %pad_maximum_fusion.2, s32[1024]{0:T(1024)S(1)} %pad_clamp_fusion), kind=kCustom, calls=%fused_computation | custom fusion | bytes 2097168 | tf_op jit(solution)/shard_map/jit(_take)/gather | solution.py:147
  60.4 2.1 %convolution_convert_fusion.2 = bf16[128,1024]{1,0:T(8,128)(2,1)} fusion(bf16[1024,1024]{1,0:T(8,128)(2,1)S(1)} %copy-done, bf16[64,1024]{1,0:T(8,128)(2,1)} %copy-done.17, bf16[64,1024]{1,0:T(8,128)(2,1)S(1)} %collective-permute-done.4, pred[]{:T(512)S(6)} %eq.105), kind=kOutput, calls=%fused_computation.31 | convolution fusion | flops 269746176 | bytes 2621441 | tf_op jit(solution)/shard_map/dot_general | solution.py:141
  63.0 1.3 pad_maximum_fusion
  65.4 7.4 %collective-permute-done.2 = f32[2,1,64,1024]{3,2,1,0:T(8,128)} collective-permute-done((f32[2,1,64,1024]{3,2,1,0:T(8,128)}, f32[2,1,64,1024]{3,2,1,0:T(8,128)}, u32[]{:S(2)}, u32[]{:S(2)}) %collective-permute-start.2) | collective-permute-done | bytes 524320 | tf_op jit(solution)/shard_map/ppermute | solution.py:30
  72.8 1.4 maximum_select_fusion
  82.4 9.5 %collective-permute-done.3 = bf16[2,1,64,1024]{3,2,1,0:T(8,128)(2,1)S(1)} collective-permute-done((bf16[2,1,64,1024]{3,2,1,0:T(8,128)(2,1)S(1)}, bf16[2,1,64,1024]{3,2,1,0:T(8,128)(2,1)S(1)}, u32[]{:S(2)}, u32[]{:S(2)}) %collective-permute-start.3) | collective-permute-done | bytes 262176 | tf_op jit(solution)/shard_map/ppermute | solution.py:30
  95.3 2.8 %multiply_reduce_fusion = (f32[2,8,64]{2,1,0:T(8,128)S(1)}, f32[2,8,64,192]{3,2,1,0:T(8,128)}) fusion(f32[2,8,64]{2,1,0:T(8,128)S(1)} %copy_add_fusion.1, f32[2,8,64,192]{3,2,1,0:T(8,128)S(1)} %get-tuple-element.37, f32[2,8,64]{2,1,0:T(8,128)S(1)} %copy_maximum_fusion, bf16[2,192,8,128]{3,2,1,0:T(8,128)(2,1)} %bitcast.281, ...), kind=kOutput, calls=%fused_computation.45 | convolution fusion | flops 51117056 | bytes 2633728 | tf_op jit(solution)/shard_map/dbqhe,dbkhe->dbhqk/dot_general | solution.py:156
  102.9 1.3 copy.266
  108.4 3.2 %collective-permute-start.15 = (bf16[2,1,64,1024]{3,2,0,1:T(8,128)(2,1)}, bf16[2,1,64,1024]{3,2,0,1:T(8,128)(2,1)}, u32[]{:S(2)}, u32[]{:S(2)}) collective-permute-start(bf16[2,1,64,1024]{3,2,0,1:T(8,128)(2,1)} %bitcast.232), channel_id=1, source_target_pairs={{0,4},{4,0},{8,12},{12,8},{1,5},{5,1},{9,13},{13,9},{2,6},{6,2},{1... | collective-permute-start | bytes 786440 | tf_op jit(solution)/shard_map/ppermute | solution.py:223
  112.4 2.1 %convolution_bitcast_fusion = f32[1,2,192,8,128]{4,2,3,1,0:T(8,128)} fusion(bf16[2,64,8,128]{3,2,1,0:T(8,128)(2,1)S(1)} %bitcast.277, f32[2,8,64,192]{3,2,1,0:T(8,128)S(1)} %get-tuple-element.37, f32[2,8,64]{2,1,0:T(8,128)S(1)} %copy-done.19, f32[2,8,64]{2,1,0:T(8,128)S(1)} %copy_maximum_fusion), kind=kOutput, calls=%fused_computation.14 | convolution fusion | flops 50921472 | bytes 2629632 | tf_op jit(solution)/shard_map/dbhqk,dbqhe->dbkhe/dot_general | solution.py:180
  119.3 1.4 add_bitcast_fusion.2
  121.6 2.0 %maximum_convert_fusion = bf16[2,1,4,64,1024]{4,0,3,2,1:T(2,128)(2,1)S(1)} fusion(bf16[2,1,1,64,1024]{4,0,3,2,1:T(2,128)(2,1)S(1)} %get-tuple-element.18, bf16[2,1,1,64,1024]{4,0,3,2,1:T(2,128)(2,1)S(1)} %get-tuple-element.17, bf16[2,1,1,64,1024]{4,0,3,2,1:T(2,128)(2,1)S(1)} %get-tuple-element.8, bf16[2,1,1,64,1024]{4,0,3,2,1:T(2,128)(2,1)S(1)} %get-tuple-element.5), kind=kLoop, calls=%fused_computation.11 | loop fusion | flops 1572864 | bytes 2097152 | tf_op jit(solution)/shard_map/convert_element_type | solution.py:208
  125.0 1.3 collective-permute-start.14
  126.3 5.4 %collective-permute-start.13 = (bf16[2,1,128,1024]{3,2,1,0:T(8,128)(2,1)}, bf16[2,1,128,1024]{3,2,1,0:T(8,128)(2,1)}, u32[]{:S(2)}, u32[]{:S(2)}) collective-permute-start(bf16[2,1,128,1024]{3,2,1,0:T(8,128)(2,1)} %get-tuple-element.15), channel_id=1, source_target_pairs={{0,4},{4,8},{8,12},{1,5},{5,9},{9,13},{2,6},{6,10},{10,14},{3,7},{... | collective-permute-start | bytes 1572872 | tf_op jit(solution)/shard_map/ppermute | solution.py:20
  132.3 1.5 add_bitcast_fusion.4
  133.8 1.5 pad_maximum_fusion.1
  138.7 1.3 div.48
  141.4 1.7 div.44
  143.1 1.8 %collective-permute-done.14 = bf16[2,1,128,1024]{3,2,1,0:T(8,128)(2,1)} collective-permute-done((bf16[2,1,128,1024]{3,2,1,0:T(8,128)(2,1)}, bf16[2,1,128,1024]{3,2,1,0:T(8,128)(2,1)}, u32[]{:S(2)}, u32[]{:S(2)}) %collective-permute-start.14) | collective-permute-done | bytes 524320 | tf_op jit(solution)/shard_map/ppermute | solution.py:22
  144.9 2.9 %fusion.11 = bf16[2,1,128,1024]{3,2,1,0:T(8,128)(2,1)S(1)} fusion(f32[2,1,128,1024]{3,2,1,0:T(8,128)} %div.48, f32[2,1,128,1024]{3,2,1,0:T(8,128)} %div.44, f32[2,1,128,1024]{3,0,2,1:T(2,128)} %bitcast.262, bf16[2,1,128,1024]{3,2,1,0:T(8,128)(2,1)} %collective-permute-done.14, bf16[2,1,256,1024]{3,2,1,0:T(8,128)(2,1)S(1)} %copy.259, ...), kind=kLoop, calls=%fused_computation.37 | loop fusion | flops 4456448 | bytes 5767168 | tf_op jit(solution)/shard_map/convert.1
  148.7 18.5 %all-gather.5.cloned.1.call-done = bf16[1024,1024]{1,0:T(8,128)(2,1)} async-done(((bf16[128,1024]{1,0:T(8,128)(2,1)}), bf16[1024,1024]{1,0:T(8,128)(2,1)}) %all-gather.5.cloned.1.call-update) | async-done | bytes 2097168 | tf_op jit(solution)/shard_map/all_gather | solution.py:151
  167.2 6.8 %fusion.86 = f32[1024,1024]{1,0:T(8,128)} fusion(bf16[1024,1024]{1,0:T(8,128)(2,1)} %all-gather.3.cloned.1.call-done, bf16[1024,1024]{1,0:T(8,128)(2,1)} %all-gather.5.cloned.1.call-done), kind=kOutput, calls=%fused_computation.173 | convolution fusion | flops 2147483648 | bytes 8388608 | tf_op jit(solution)/shard_map/tc,tw->cw/dot_general | solution.py:152
  (158 shorter events, 48.4 us)
Async XLA Ops:
  7.2 19.0 %copy-start = (bf16[1024,1024]{1,0:T(8,128)(2,1)S(1)}, bf16[1024,1024]{1,0:T(8,128)(2,1)}, u32[]{:S(2)}) copy-start(bf16[1024,1024]{1,0:T(8,128)(2,1)} %param.10) | copy-start | bytes 6291460
  7.2 15.1 %copy-start.2 = (bf16[1,128,1024]{2,1,0:T(8,128)(2,1)S(1)}, bf16[1,128,1024]{2,1,0:T(8,128)(2,1)}, u32[]{:S(2)}) copy-start(bf16[1,128,1024]{2,1,0:T(8,128)(2,1)} %param.8) | copy-start | bytes 786436
  7.2 15.2 %copy-start.4 = (bf16[1,128,1024]{2,1,0:T(8,128)(2,1)S(1)}, bf16[1,128,1024]{2,1,0:T(8,128)(2,1)}, u32[]{:S(2)}) copy-start(bf16[1,128,1024]{2,1,0:T(8,128)(2,1)} %param.7) | copy-start | bytes 786436
  7.2 15.3 %copy-start.22 = (s32[1,2,2]{2,1,0:T(2,128)S(1)}, s32[1,2,2]{2,1,0:T(2,128)}, u32[]{:S(2)}) copy-start(s32[1,2,2]{2,1,0:T(2,128)} %param.9) | copy-start | bytes 52
  7.2 141.5 %all-gather.3.cloned.1.call-start = ((), (), s32[]{:S(2)}) async-start(), calls=%async_computation | async-start | bytes 3145728 | tf_op jit(solution)/shard_map/all_gather | solution.py:150
  9.3 53.2 %collective-permute-start.1 = (bf16[2,1,128,1024]{3,2,1,0:T(8,128)(2,1)}, bf16[2,1,128,1024]{3,2,1,0:T(8,128)(2,1)}, u32[]{:S(2)}, u32[]{:S(2)}) collective-permute-start(bf16[2,1,128,1024]{3,2,1,0:T(8,128)(2,1)} %pad_maximum_fusion.6), channel_id=1, source_target_pairs={{4,0},{8,4},{12,8},{5,1},{9,5},{13,9},{6,2},{10,6},{14,10},{7,3},{... | collective-permute-start | bytes 1572872 | tf_op jit(solution)/shard_map/ppermute | solution.py:22
  10.6 52.4 %collective-permute-start = (bf16[2,1,128,1024]{3,2,1,0:T(8,128)(2,1)}, bf16[2,1,128,1024]{3,2,1,0:T(8,128)(2,1)}, u32[]{:S(2)}, u32[]{:S(2)}) collective-permute-start(bf16[2,1,128,1024]{3,2,1,0:T(8,128)(2,1)} %pad_maximum_fusion.6), channel_id=1, source_target_pairs={{0,4},{4,8},{8,12},{1,5},{5,9},{9,13},{2,6},{6,10},{10,14},{3,7},{... | collective-permute-start | bytes 1572872 | tf_op jit(solution)/shard_map/ppermute | solution.py:20
  17.9 13.3 %collective-permute-start.10 = (bf16[64,1024]{1,0:T(8,128)(2,1)S(1)}, bf16[64,1024]{1,0:T(8,128)(2,1)S(1)}, u32[]{:S(2)}, u32[]{:S(2)}) collective-permute-start(bf16[64,1024]{1,0:T(8,128)(2,1)S(1)} %get-tuple-element.22), channel_id=1, source_target_pairs={{0,12},{4,8},{8,4},{12,0},{1,13},{5,9},{9,5},{13,1},{2,14},{6,10},... | collective-permute-start | bytes 393224 | tf_op jit(solution)/shard_map/ppermute | solution.py:132
  19.3 23.0 %collective-permute-start.7 = (bf16[64,1024]{1,0:T(8,128)(2,1)}, bf16[64,1024]{1,0:T(8,128)(2,1)S(1)}, u32[]{:S(2)}, u32[]{:S(2)}) collective-permute-start(bf16[64,1024]{1,0:T(8,128)(2,1)} %get-tuple-element.23), channel_id=1, source_target_pairs={{0,8},{4,12},{8,0},{12,4},{1,9},{5,13},{9,1},{13,5},{2,10},{6,14},... | collective-permute-start | bytes 393224 | tf_op jit(solution)/shard_map/ppermute | solution.py:132
  20.5 28.5 %collective-permute-start.4 = (bf16[64,1024]{1,0:T(8,128)(2,1)S(1)}, bf16[64,1024]{1,0:T(8,128)(2,1)S(1)}, u32[]{:S(2)}, u32[]{:S(2)}) collective-permute-start(bf16[64,1024]{1,0:T(8,128)(2,1)S(1)} %get-tuple-element.21), channel_id=1, source_target_pairs={{0,4},{4,0},{8,12},{12,8},{1,5},{5,1},{9,13},{13,9},{2,6},{6,2},{1... | collective-permute-start | bytes 393224 | tf_op jit(solution)/shard_map/ppermute | solution.py:132
  26.1 15.5 %copy-start.16 = (bf16[1,128,1024]{2,1,0:T(8,128)(2,1)S(1)}, bf16[1,128,1024]{2,1,0:T(8,128)(2,1)}, u32[]{:S(2)}) copy-start(bf16[1,128,1024]{2,1,0:T(8,128)(2,1)} %param.6) | copy-start | bytes 786436
  31.1 18.0 %collective-permute-start.11 = (bf16[64,1024]{1,0:T(8,128)(2,1)S(1)}, bf16[64,1024]{1,0:T(8,128)(2,1)S(1)}, u32[]{:S(2)}, u32[]{:S(2)}) collective-permute-start(bf16[64,1024]{1,0:T(8,128)(2,1)S(1)} %collective-permute-done.10), channel_id=1, source_target_pairs={{0,1},{1,0},{2,3},{3,2},{4,5},{5,4},{6,7},{7,6},{8,9},{9,8},{10,11... | collective-permute-start | bytes 393224 | tf_op jit(solution)/shard_map/ppermute | solution.py:30
  42.4 30.4 %collective-permute-start.2 = (f32[2,1,64,1024]{3,2,1,0:T(8,128)}, f32[2,1,64,1024]{3,2,1,0:T(8,128)}, u32[]{:S(2)}, u32[]{:S(2)}) collective-permute-start(f32[2,1,64,1024]{3,2,1,0:T(8,128)} %get-tuple-element.31), channel_id=1, source_target_pairs={{0,4},{4,0},{8,12},{12,8},{1,5},{5,1},{9,13},{13,9},{2,6},{6,2},{1... | collective-permute-start | bytes 1572872 | tf_op jit(solution)/shard_map/ppermute | solution.py:30
  49.0 1.7 collective-permute-start.8
  49.2 6.1 %collective-permute-start.5 = (bf16[64,1024]{1,0:T(8,128)(2,1)S(1)}, bf16[64,1024]{1,0:T(8,128)(2,1)S(1)}, u32[]{:S(2)}, u32[]{:S(2)}) collective-permute-start(bf16[64,1024]{1,0:T(8,128)(2,1)S(1)} %collective-permute-done.4), channel_id=1, source_target_pairs={{0,1},{1,0},{2,3},{3,2},{4,5},{5,4},{6,7},{7,6},{8,9},{9,8},{10,11... | collective-permute-start | bytes 393224 | tf_op jit(solution)/shard_map/ppermute | solution.py:30
  50.6 26.8 %collective-permute-start.12 = (bf16[128,1024]{1,0:T(8,128)(2,1)}, bf16[128,1024]{1,0:T(8,128)(2,1)}, u32[]{:S(2)}, u32[]{:S(2)}) collective-permute-start(bf16[128,1024]{1,0:T(8,128)(2,1)} %convolution_convert_fusion), channel_id=1, source_target_pairs={{0,12},{4,8},{8,4},{12,0},{1,13},{5,9},{9,5},{13,1},{2,14},{6,10},... | collective-permute-start | bytes 786440 | tf_op jit(solution)/shard_map/ppermute | solution.py:142
  55.3 22.2 %collective-permute-start.9 = (bf16[128,1024]{1,0:T(8,128)(2,1)}, bf16[128,1024]{1,0:T(8,128)(2,1)}, u32[]{:S(2)}, u32[]{:S(2)}) collective-permute-start(bf16[128,1024]{1,0:T(8,128)(2,1)} %convolution_convert_fusion.1), channel_id=1, source_target_pairs={{0,8},{4,12},{8,0},{12,4},{1,9},{5,13},{9,1},{13,5},{2,10},{6,14},... | collective-permute-start | bytes 786440 | tf_op jit(solution)/shard_map/ppermute | solution.py:142
  60.2 107.0 %all-gather.5.cloned.1.call-start = ((), (), s32[]{:S(2)}) async-start(), calls=%async_computation.1 | async-start | bytes 2359296 | tf_op jit(solution)/shard_map/all_gather | solution.py:151
  62.5 16.1 %collective-permute-start.6 = (bf16[128,1024]{1,0:T(8,128)(2,1)}, bf16[128,1024]{1,0:T(8,128)(2,1)S(1)}, u32[]{:S(2)}, u32[]{:S(2)}) collective-permute-start(bf16[128,1024]{1,0:T(8,128)(2,1)} %convolution_convert_fusion.2), channel_id=1, source_target_pairs={{0,4},{4,0},{8,12},{12,8},{1,5},{5,1},{9,13},{13,9},{2,6},{6,2},{1... | collective-permute-start | bytes 786440 | tf_op jit(solution)/shard_map/ppermute | solution.py:142
  65.2 7.6 %copy-start.9 = (f32[2,1,64,1024]{3,2,0,1:T(8,128)S(1)}, f32[2,1,64,1024]{3,2,0,1:T(8,128)}, u32[]{:S(2)}) copy-start(f32[2,1,64,1024]{3,2,0,1:T(8,128)} %get-tuple-element.30) | copy-start | bytes 1572868
  77.4 14.5 %collective-permute-start.3 = (bf16[2,1,64,1024]{3,2,1,0:T(8,128)(2,1)S(1)}, bf16[2,1,64,1024]{3,2,1,0:T(8,128)(2,1)S(1)}, u32[]{:S(2)}, u32[]{:S(2)}) collective-permute-start(bf16[2,1,64,1024]{3,2,1,0:T(8,128)(2,1)S(1)} %fusion.29), channel_id=1, source_target_pairs={{0,8},{4,12},{8,0},{12,4},{1,9},{5,13},{9,1},{13,5},{2,10},{6,14},... | collective-permute-start | bytes 786440 | tf_op jit(solution)/shard_map/ppermute | solution.py:30
  79.8 15.4 %copy-start.6 = (bf16[16,8,8,128]{3,2,1,0:T(8,128)(2,1)}, bf16[16,8,8,128]{3,2,1,0:T(8,128)(2,1)S(1)}, u32[]{:S(2)}) copy-start(bf16[16,8,8,128]{3,2,1,0:T(8,128)(2,1)S(1)} %copy.288) | copy-start | bytes 786436
  81.7 11.1 %copy-start.13 = (bf16[2,64,8,128]{3,1,0,2:T(8,128)(2,1)S(1)}, bf16[2,64,8,128]{3,1,0,2:T(8,128)(2,1)}, u32[]{:S(2)}) copy-start(bf16[2,64,8,128]{3,1,0,2:T(8,128)(2,1)} %copy.235) | copy-start | bytes 786436
  95.3 4.7 %copy-start.18 = (f32[2,8,64]{2,1,0:T(8,128)}, f32[2,8,64]{2,1,0:T(8,128)S(1)}, u32[]{:S(2)}) copy-start(f32[2,8,64]{2,1,0:T(8,128)S(1)} %copy_add_fusion.1) | copy-start | bytes 12292
  104.8 7.5 %copy-start.8 = (bf16[16,8,8,128]{3,2,1,0:T(8,128)(2,1)S(1)}, bf16[16,8,8,128]{3,2,1,0:T(8,128)(2,1)}, u32[]{:S(2)}) copy-start(bf16[16,8,8,128]{3,2,1,0:T(8,128)(2,1)} %copy-done.6) | copy-start | bytes 786436
  104.8 7.5 %copy-start.19 = (f32[2,8,64]{2,1,0:T(8,128)S(1)}, f32[2,8,64]{2,1,0:T(8,128)}, u32[]{:S(2)}) copy-start(f32[2,8,64]{2,1,0:T(8,128)} %copy-done.18) | copy-start | bytes 12292
  106.0 31.2 %collective-permute-start.17 = (bf16[2,1,32,1024]{3,0,2,1:T(2,128)(2,1)}, bf16[2,1,32,1024]{3,0,2,1:T(2,128)(2,1)}, u32[]{:S(2)}, u32[]{:S(2)}) collective-permute-start(bf16[2,1,32,1024]{3,0,2,1:T(2,128)(2,1)} %get-tuple-element.20), channel_id=1, source_target_pairs={{0,12},{4,8},{8,4},{12,0},{1,13},{5,9},{9,5},{13,1},{2,14},{6,10},... | collective-permute-start | bytes 393224 | tf_op jit(solution)/shard_map/ppermute | solution.py:223
  107.2 30.0 %collective-permute-start.16 = (bf16[2,1,32,1024]{3,0,2,1:T(2,128)(2,1)S(1)}, bf16[2,1,32,1024]{3,0,2,1:T(2,128)(2,1)}, u32[]{:S(2)}, u32[]{:S(2)}) collective-permute-start(bf16[2,1,32,1024]{3,0,2,1:T(2,128)(2,1)S(1)} %get-tuple-element.19), channel_id=1, source_target_pairs={{0,8},{4,12},{8,0},{12,4},{1,9},{5,13},{9,1},{13,5},{2,10},{6,14},... | collective-permute-start | bytes 393224 | tf_op jit(solution)/shard_map/ppermute | solution.py:223
  108.4 31.6 %collective-permute-start.15 = (bf16[2,1,64,1024]{3,2,0,1:T(8,128)(2,1)}, bf16[2,1,64,1024]{3,2,0,1:T(8,128)(2,1)}, u32[]{:S(2)}, u32[]{:S(2)}) collective-permute-start(bf16[2,1,64,1024]{3,2,0,1:T(8,128)(2,1)} %bitcast.232), channel_id=1, source_target_pairs={{0,4},{4,0},{8,12},{12,8},{1,5},{5,1},{9,13},{13,9},{2,6},{6,2},{1... | collective-permute-start | bytes 786440 | tf_op jit(solution)/shard_map/ppermute | solution.py:223
  125.0 19.9 %collective-permute-start.14 = (bf16[2,1,128,1024]{3,2,1,0:T(8,128)(2,1)}, bf16[2,1,128,1024]{3,2,1,0:T(8,128)(2,1)}, u32[]{:S(2)}, u32[]{:S(2)}) collective-permute-start(bf16[2,1,128,1024]{3,2,1,0:T(8,128)(2,1)} %get-tuple-element.16), channel_id=1, source_target_pairs={{4,0},{8,4},{12,8},{5,1},{9,5},{13,9},{6,2},{10,6},{14,10},{7,3},{... | collective-permute-start | bytes 1572872 | tf_op jit(solution)/shard_map/ppermute | solution.py:22
  126.3 18.7 %collective-permute-start.13 = (bf16[2,1,128,1024]{3,2,1,0:T(8,128)(2,1)}, bf16[2,1,128,1024]{3,2,1,0:T(8,128)(2,1)}, u32[]{:S(2)}, u32[]{:S(2)}) collective-permute-start(bf16[2,1,128,1024]{3,2,1,0:T(8,128)(2,1)} %get-tuple-element.15), channel_id=1, source_target_pairs={{0,4},{4,8},{8,12},{1,5},{5,9},{9,13},{2,6},{6,10},{10,14},{3,7},{... | collective-permute-start | bytes 1572872 | tf_op jit(solution)/shard_map/ppermute | solution.py:20
  167.2 6.8 %copy-start.1 = (bf16[1024,1024]{1,0:T(8,128)(2,1)S(1)}, bf16[1024,1024]{1,0:T(8,128)(2,1)}, u32[]{:S(2)}) copy-start(bf16[1024,1024]{1,0:T(8,128)(2,1)} %param.10) | copy-start | bytes 6291460
  (11 other events, 20.4 us)
Sparse Core Ops, SparseCore 0:
  60.3 32.1 all-gather.2
  115.1 52.1 all-gather.4

commit v18 on v17

--- a/solution.py
+++ b/solution.py
@@ -60,17 +60,8 @@
     blocks_six = padded.reshape(2, doc_count, 6, block, head_cols)
     local_ids = jnp.arange(2, dtype=jnp.int32)[None, :, None]
     chosen = jnp.concatenate([local_ids, local_ids + pattern], axis=2) + 2
-    candidates = [[b + p + 2 for p in (-2, -1, 1, 2)] for b in range(2)]
-    picked = []
-    for b in range(2):
-        picked.append(blocks_six[:, :, b + 2])
-        for n in range(1, NEAR + 1):
-            index = chosen[:, b, n][None, :, None, None]
-            acc = jnp.zeros_like(blocks_six[:, :, 0])
-            for j in candidates[b]:
-                acc = jnp.where(index == j, blocks_six[:, :, j], acc)
-            picked.append(acc)
-    near_pair = jnp.stack(picked, axis=2).reshape(2, doc_count, 2, near_width, head_cols)
+    near_pair = jax.vmap(pick_blocks, in_axes=(1, 0), out_axes=1)(blocks_six, chosen)
+    near_pair = near_pair.reshape(2, doc_count, 2, near_width, head_cols)
     pooled = pool_pairs(key_value.astype(jnp.float32))
     siblings = []
     own_level = pooled
@@ -190,6 +181,7 @@
     near_rows = jnp.stack([near_key_rows, near_value_rows]).reshape(
         2, doc_count, 2, NEAR + 1, block, head_cols
     )
+    candidates = [[b + p + 2 for p in (-2, -1, 1, 2)] for b in range(2)]
     slots = []
     for j in range(6):
         total = jnp.zeros_like(near_rows[:, :, 0, 0])

time: 184 us -> 183 us (level)
  local copies, waits for them, and re-layouts: 26.3 us -> 31 us
  waiting for transfers between devices: 41.5 us -> 37.4 us
  other arithmetic: 32.3 us -> 30.4 us
    gather x0 -> x4, local copies, waits for them, and re-layouts: none -> 3.59 us  [pick_blocks(): return blocks_doc[:, chosen_doc]]
    ppermute x5, waiting for transfers between devices: 16.9 us -> 14.3 us  [swapped(): lax.ppermute(shard, axis, [(i, i ^ 1 << stride) for i in range(lax.axis_s...]
    another operation x5 -> x4, other arithmetic: 5.14 us -> 4.49 us
    unnamed x53 -> x59, local copies, waits for them, and re-layouts: 4.75 us -> 4.93 us
  transfers between devices with their start and end apart: 20 -> 20, of which waited for: 6 -> 6; matrix products, arithmetic and copies ran while one was open for 38% -> 40% of each run, Pallas kernels for 0% -> 0%
where the time goes in v18:
time: 183 us; the launch traced here: 180 us
  waiting for transfers between devices  37.4 us (20%)
  starting transfers between devices  33.4 us (18%)
  local copies, waits for them, and re-layouts  31 us (17%)
  other arithmetic  30.4 us (17%)
  between operations  25.1 us (14%)
  matrix products  22.9 us (13%)
    all_gather x1, waiting for transfers between devices, shards(): whole_output = lax.all_gather(out_rows, ('dp', 'seq'), axis=0, tiled=True)  18.4 us
    ppermute x5, waiting for transfers between devices, swapped(): lax.ppermute(shard, axis, [(i, i ^ 1 << stride) for i in range(lax.axis_s...  14.3 us
    ppermute x2, starting transfers between devices, extended(): lax.ppermute(tail, axis, [(i, (i + 1) % count) for i in range(ends)])  10.7 us
    ppermute x5, starting transfers between devices, swapped(): lax.ppermute(shard, axis, [(i, i ^ 1 << stride) for i in range(lax.axis_s...  7.16 us
    dot_general x1, matrix products, shards(): jnp.einsum('tc,tw->cw', feat_docs, whole_output, preferred_element_type=j...  6.77 us
    add x4, other arithmetic, shards(): total = total + jnp.where(index == j, near_rows[:, :, b, n], 0.0)  5.05 us
    unnamed x59, local copies, waits for them, and re-layouts  4.93 us
    another operation x4, other arithmetic  4.49 us
  transfers between devices with their start and end apart: 20, of which 6 were waited for; matrix products, arithmetic and copies ran while one was open for 40% of the time, Pallas kernels for 0%

profile of v18, /device:TPU:6, one launch (start us, length us, event | category | flops | bytes accessed | tf_op | source)
XLA Modules:
  0.0 180.2 jit_solution(10669001912645839245)
XLA Ops:
  7.2 2.0 %pad_maximum_fusion.6 = bf16[2,1,128,1024]{3,2,1,0:T(8,128)(2,1)} fusion(bf16[1,1,128,1024]{3,2,1,0:T(8,128)(2,1)} %bitcast.264, bf16[1,1,128,1024]{3,2,1,0:T(8,128)(2,1)} %bitcast.266), kind=kLoop, calls=%fused_computation.68 | loop fusion | flops 262144 | bytes 1048576 | tf_op jit(solution)/shard_map/stack | solution.py:58
  9.3 1.3 collective-permute-start.1
  10.6 5.3 %collective-permute-start = (bf16[2,1,128,1024]{3,2,1,0:T(8,128)(2,1)}, bf16[2,1,128,1024]{3,2,1,0:T(8,128)(2,1)}, u32[]{:S(2)}, u32[]{:S(2)}) collective-permute-start(bf16[2,1,128,1024]{3,2,1,0:T(8,128)(2,1)} %pad_maximum_fusion.6), channel_id=1, source_target_pairs={{0,4},{4,8},{8,12},{1,5},{5,9},{9,13},{2,6},{6,10},{10,14},{3,7},{... | collective-permute-start | bytes 1572872 | tf_op jit(solution)/shard_map/ppermute | solution.py:20
  15.9 1.9 %dynamic-slice_bitcast_fusion.2 = (bf16[64,1024]{1,0:T(8,128)(2,1)S(1)}, bf16[64,1024]{1,0:T(8,128)(2,1)S(1)}, bf16[64,1024]{1,0:T(8,128)(2,1)}) fusion(bf16[1,128,4096]{2,1,0:T(8,128)(2,1)} %param.11, s32[]{:T(128)S(6)} %select_n.348, s32[]{:T(128)S(6)} %select_n.350, s32[]{:T(128)S(6)} %select_n.356, s32[]{:T(128)S(6)} %select_n.353), kind=kLoop, calls=%fused_computation.144 | loop fusion | bytes 786448 | tf_op jit(solution)/shard_map/dynamic_slice | solution.py:124
  17.8 1.5 collective-permute-start.10
  20.5 1.7 collective-permute-start.4
  23.4 1.4 convert_reduce_fusion
  29.1 2.0 %collective-permute-done.10 = bf16[64,1024]{1,0:T(8,128)(2,1)S(1)} collective-permute-done((bf16[64,1024]{1,0:T(8,128)(2,1)S(1)}, bf16[64,1024]{1,0:T(8,128)(2,1)S(1)}, u32[]{:S(2)}, u32[]{:S(2)}) %collective-permute-start.10) | collective-permute-done | bytes 131104 | tf_op jit(solution)/shard_map/ppermute | solution.py:123
  42.4 6.6 %collective-permute-start.2 = (f32[2,1,64,1024]{3,2,1,0:T(8,128)}, f32[2,1,64,1024]{3,2,1,0:T(8,128)}, u32[]{:S(2)}, u32[]{:S(2)}) collective-permute-start(f32[2,1,64,1024]{3,2,1,0:T(8,128)} %get-tuple-element.31), channel_id=1, source_target_pairs={{0,4},{4,0},{8,12},{12,8},{1,5},{5,1},{9,13},{13,9},{2,6},{6,2},{1... | collective-permute-start | bytes 1572872 | tf_op jit(solution)/shard_map/ppermute | solution.py:30
  50.7 3.4 %collective-permute-start.12 = (bf16[128,1024]{1,0:T(8,128)(2,1)}, bf16[128,1024]{1,0:T(8,128)(2,1)}, u32[]{:S(2)}, u32[]{:S(2)}) collective-permute-start(bf16[128,1024]{1,0:T(8,128)(2,1)} %convolution_convert_fusion), channel_id=1, source_target_pairs={{0,12},{4,8},{8,4},{12,0},{1,13},{5,9},{9,5},{13,1},{2,14},{6,10},... | collective-permute-start | bytes 786440 | tf_op jit(solution)/shard_map/ppermute | solution.py:133
  57.1 1.8 %gather_fusion = bf16[4,128,1024]{2,1,0:T(8,128)(2,1)S(1)} fusion(bf16[4,128,1024]{2,1,0:T(8,128)(2,1)} %pad_maximum_fusion.2, s32[1024]{0:T(1024)S(1)} %pad_clamp_fusion), kind=kCustom, calls=%fused_computation | custom fusion | bytes 2097168 | tf_op jit(solution)/shard_map/jit(_take)/gather | solution.py:138
  60.4 2.1 %convolution_convert_fusion.2 = bf16[128,1024]{1,0:T(8,128)(2,1)} fusion(bf16[1024,1024]{1,0:T(8,128)(2,1)S(1)} %copy-done, bf16[64,1024]{1,0:T(8,128)(2,1)} %copy-done.21, bf16[64,1024]{1,0:T(8,128)(2,1)S(1)} %collective-permute-done.4, pred[]{:T(512)S(6)} %eq.73), kind=kOutput, calls=%fused_computation.32 | convolution fusion | flops 269746176 | bytes 2621441 | tf_op jit(solution)/shard_map/dot_general | solution.py:132
  63.1 1.3 pad_maximum_fusion
  64.4 1.8 %gather_fusion.1 = bf16[6,2,64,1024]{3,2,1,0:T(8,128)(2,1)} fusion(bf16[1,2,6,64,1024]{4,3,2,1,0:T(8,128)(2,1)S(1)} %bitcast.251, s32[6]{0:T(128)S(1)} %reshape.1212), kind=kCustom, calls=%fused_computation.1 | custom fusion | bytes 3145776 | tf_op jit(solution)/shard_map/vmap()/gather | solution.py:41
  66.2 1.7 copy.205
  68.1 4.7 %collective-permute-done.2 = f32[2,1,64,1024]{3,2,1,0:T(8,128)} collective-permute-done((f32[2,1,64,1024]{3,2,1,0:T(8,128)}, f32[2,1,64,1024]{3,2,1,0:T(8,128)}, u32[]{:S(2)}, u32[]{:S(2)}) %collective-permute-start.2) | collective-permute-done | bytes 524320 | tf_op jit(solution)/shard_map/ppermute | solution.py:30
  72.8 1.5 maximum_select_fusion
  82.5 9.5 %collective-permute-done.3 = bf16[2,1,64,1024]{3,2,1,0:T(8,128)(2,1)S(1)} collective-permute-done((bf16[2,1,64,1024]{3,2,1,0:T(8,128)(2,1)S(1)}, bf16[2,1,64,1024]{3,2,1,0:T(8,128)(2,1)S(1)}, u32[]{:S(2)}, u32[]{:S(2)}) %collective-permute-start.3) | collective-permute-done | bytes 262176 | tf_op jit(solution)/shard_map/ppermute | solution.py:30
  95.4 2.8 %multiply_reduce_fusion = (f32[2,8,64]{2,1,0:T(8,128)S(1)}, f32[2,8,64,192]{3,2,1,0:T(8,128)}) fusion(f32[2,8,64]{2,1,0:T(8,128)S(1)} %copy_add_fusion.1, f32[2,8,64,192]{3,2,1,0:T(8,128)S(1)} %get-tuple-element.39, f32[2,8,64]{2,1,0:T(8,128)S(1)} %copy_maximum_fusion, bf16[2,192,8,128]{3,2,1,0:T(8,128)(2,1)} %bitcast.280, ...), kind=kOutput, calls=%fused_computation.46 | convolution fusion | flops 51117056 | bytes 2633728 | tf_op jit(solution)/shard_map/dbqhe,dbkhe->dbhqk/dot_general | solution.py:147
  108.1 3.2 %collective-permute-start.15 = (bf16[2,1,64,1024]{3,2,0,1:T(8,128)(2,1)}, bf16[2,1,64,1024]{3,2,0,1:T(8,128)(2,1)}, u32[]{:S(2)}, u32[]{:S(2)}) collective-permute-start(bf16[2,1,64,1024]{3,2,0,1:T(8,128)(2,1)} %bitcast.235), channel_id=1, source_target_pairs={{0,4},{4,0},{8,12},{12,8},{1,5},{5,1},{9,13},{13,9},{2,6},{6,2},{1... | collective-permute-start | bytes 786440 | tf_op jit(solution)/shard_map/ppermute | solution.py:215
  112.1 2.1 %convolution_bitcast_fusion = f32[1,2,192,8,128]{4,2,3,1,0:T(8,128)} fusion(bf16[2,64,8,128]{3,2,1,0:T(8,128)(2,1)S(1)} %bitcast.276, f32[2,8,64,192]{3,2,1,0:T(8,128)S(1)} %get-tuple-element.39, f32[2,8,64]{2,1,0:T(8,128)S(1)} %copy-done.23, f32[2,8,64]{2,1,0:T(8,128)S(1)} %copy_maximum_fusion), kind=kOutput, calls=%fused_computation.15 | convolution fusion | flops 50921472 | bytes 2629632 | tf_op jit(solution)/shard_map/dbhqk,dbqhe->dbkhe/dot_general | solution.py:171
  119.3 1.4 add_bitcast_fusion.2
  121.6 2.0 %maximum_convert_fusion = bf16[2,1,4,64,1024]{4,0,3,2,1:T(2,128)(2,1)S(1)} fusion(bf16[2,1,1,64,1024]{4,0,3,2,1:T(2,128)(2,1)S(1)} %get-tuple-element.18, bf16[2,1,1,64,1024]{4,0,3,2,1:T(2,128)(2,1)S(1)} %get-tuple-element.17, bf16[2,1,1,64,1024]{4,0,3,2,1:T(2,128)(2,1)S(1)} %get-tuple-element.8, bf16[2,1,1,64,1024]{4,0,3,2,1:T(2,128)(2,1)S(1)} %get-tuple-element.5), kind=kLoop, calls=%fused_computation.12 | loop fusion | flops 1572864 | bytes 2097152 | tf_op jit(solution)/shard_map/convert_element_type | solution.py:200
  124.9 1.3 collective-permute-start.14
  126.2 5.4 %collective-permute-start.13 = (bf16[2,1,128,1024]{3,2,1,0:T(8,128)(2,1)}, bf16[2,1,128,1024]{3,2,1,0:T(8,128)(2,1)}, u32[]{:S(2)}, u32[]{:S(2)}) collective-permute-start(bf16[2,1,128,1024]{3,2,1,0:T(8,128)(2,1)} %get-tuple-element.15), channel_id=1, source_target_pairs={{0,4},{4,8},{8,12},{1,5},{5,9},{9,13},{2,6},{6,10},{10,14},{3,7},{... | collective-permute-start | bytes 1572872 | tf_op jit(solution)/shard_map/ppermute | solution.py:20
  133.0 1.5 add_bitcast_fusion.4
  138.9 1.3 div.48
  141.6 1.7 div.44
  143.3 1.6 collective-permute-done.14
  144.9 2.4 %fusion.11 = bf16[2,1,128,1024]{3,2,1,0:T(8,128)(2,1)S(1)} fusion(f32[2,1,128,1024]{3,2,1,0:T(8,128)} %div.48, f32[2,1,128,1024]{3,2,1,0:T(8,128)} %div.44, f32[2,1,128,1024]{3,0,2,1:T(2,128)S(1)} %bitcast.261, bf16[2,1,128,1024]{3,2,1,0:T(8,128)(2,1)} %collective-permute-done.14, bf16[2,1,256,1024]{3,2,1,0:T(8,128)(2,1)S(1)} %copy.240, ...), kind=kLoop, calls=%fused_computation.38 | loop fusion | flops 4456448 | bytes 5767168 | tf_op jit(solution)/shard_map/convert.1
  148.2 18.4 %all-gather.5.cloned.1.call-done = bf16[1024,1024]{1,0:T(8,128)(2,1)} async-done(((bf16[128,1024]{1,0:T(8,128)(2,1)}), bf16[1024,1024]{1,0:T(8,128)(2,1)}) %all-gather.5.cloned.1.call-update) | async-done | bytes 2097168 | tf_op jit(solution)/shard_map/all_gather | solution.py:142
  166.6 6.8 %fusion.91 = f32[1024,1024]{1,0:T(8,128)} fusion(bf16[1024,1024]{1,0:T(8,128)(2,1)} %all-gather.3.cloned.1.call-done, bf16[1024,1024]{1,0:T(8,128)(2,1)} %all-gather.5.cloned.1.call-done), kind=kOutput, calls=%fused_computation.178 | convolution fusion | flops 2147483648 | bytes 8388608 | tf_op jit(solution)/shard_map/tc,tw->cw/dot_general | solution.py:143
  (167 shorter events, 51.5 us)
Async XLA Ops:
  7.2 20.7 %copy-start = (bf16[1024,1024]{1,0:T(8,128)(2,1)S(1)}, bf16[1024,1024]{1,0:T(8,128)(2,1)}, u32[]{:S(2)}) copy-start(bf16[1024,1024]{1,0:T(8,128)(2,1)} %param.10) | copy-start | bytes 6291460
  7.2 16.1 %copy-start.5 = (bf16[1,128,1024]{2,1,0:T(8,128)(2,1)S(1)}, bf16[1,128,1024]{2,1,0:T(8,128)(2,1)}, u32[]{:S(2)}) copy-start(bf16[1,128,1024]{2,1,0:T(8,128)(2,1)} %param.7) | copy-start | bytes 786436
  7.2 16.2 %copy-start.26 = (s32[1,2,2]{2,1,0:T(2,128)S(1)}, s32[1,2,2]{2,1,0:T(2,128)}, u32[]{:S(2)}) copy-start(s32[1,2,2]{2,1,0:T(2,128)} %param.9) | copy-start | bytes 52
  7.2 141.0 %all-gather.3.cloned.1.call-start = ((), (), s32[]{:S(2)}) async-start(), calls=%async_computation | async-start | bytes 3145728 | tf_op jit(solution)/shard_map/all_gather | solution.py:141
  9.3 53.3 %collective-permute-start.1 = (bf16[2,1,128,1024]{3,2,1,0:T(8,128)(2,1)}, bf16[2,1,128,1024]{3,2,1,0:T(8,128)(2,1)}, u32[]{:S(2)}, u32[]{:S(2)}) collective-permute-start(bf16[2,1,128,1024]{3,2,1,0:T(8,128)(2,1)} %pad_maximum_fusion.6), channel_id=1, source_target_pairs={{4,0},{8,4},{12,8},{5,1},{9,5},{13,9},{6,2},{10,6},{14,10},{7,3},{... | collective-permute-start | bytes 1572872 | tf_op jit(solution)/shard_map/ppermute | solution.py:22
  10.6 52.5 %collective-permute-start = (bf16[2,1,128,1024]{3,2,1,0:T(8,128)(2,1)}, bf16[2,1,128,1024]{3,2,1,0:T(8,128)(2,1)}, u32[]{:S(2)}, u32[]{:S(2)}) collective-permute-start(bf16[2,1,128,1024]{3,2,1,0:T(8,128)(2,1)} %pad_maximum_fusion.6), channel_id=1, source_target_pairs={{0,4},{4,8},{8,12},{1,5},{5,9},{9,13},{2,6},{6,10},{10,14},{3,7},{... | collective-permute-start | bytes 1572872 | tf_op jit(solution)/shard_map/ppermute | solution.py:20
  17.8 13.3 %collective-permute-start.10 = (bf16[64,1024]{1,0:T(8,128)(2,1)S(1)}, bf16[64,1024]{1,0:T(8,128)(2,1)S(1)}, u32[]{:S(2)}, u32[]{:S(2)}) collective-permute-start(bf16[64,1024]{1,0:T(8,128)(2,1)S(1)} %get-tuple-element.22), channel_id=1, source_target_pairs={{0,12},{4,8},{8,4},{12,0},{1,13},{5,9},{9,5},{13,1},{2,14},{6,10},... | collective-permute-start | bytes 393224 | tf_op jit(solution)/shard_map/ppermute | solution.py:123
  19.3 23.1 %collective-permute-start.7 = (bf16[64,1024]{1,0:T(8,128)(2,1)}, bf16[64,1024]{1,0:T(8,128)(2,1)S(1)}, u32[]{:S(2)}, u32[]{:S(2)}) collective-permute-start(bf16[64,1024]{1,0:T(8,128)(2,1)} %get-tuple-element.23), channel_id=1, source_target_pairs={{0,8},{4,12},{8,0},{12,4},{1,9},{5,13},{9,1},{13,5},{2,10},{6,14},... | collective-permute-start | bytes 393224 | tf_op jit(solution)/shard_map/ppermute | solution.py:123
  20.5 28.5 %collective-permute-start.4 = (bf16[64,1024]{1,0:T(8,128)(2,1)S(1)}, bf16[64,1024]{1,0:T(8,128)(2,1)S(1)}, u32[]{:S(2)}, u32[]{:S(2)}) collective-permute-start(bf16[64,1024]{1,0:T(8,128)(2,1)S(1)} %get-tuple-element.21), channel_id=1, source_target_pairs={{0,4},{4,0},{8,12},{12,8},{1,5},{5,1},{9,13},{13,9},{2,6},{6,2},{1... | collective-permute-start | bytes 393224 | tf_op jit(solution)/shard_map/ppermute | solution.py:123
  26.0 15.6 %copy-start.20 = (bf16[1,128,1024]{2,1,0:T(8,128)(2,1)S(1)}, bf16[1,128,1024]{2,1,0:T(8,128)(2,1)}, u32[]{:S(2)}) copy-start(bf16[1,128,1024]{2,1,0:T(8,128)(2,1)} %param.6) | copy-start | bytes 786436
  31.1 18.1 %collective-permute-start.11 = (bf16[64,1024]{1,0:T(8,128)(2,1)S(1)}, bf16[64,1024]{1,0:T(8,128)(2,1)S(1)}, u32[]{:S(2)}, u32[]{:S(2)}) collective-permute-start(bf16[64,1024]{1,0:T(8,128)(2,1)S(1)} %collective-permute-done.10), channel_id=1, source_target_pairs={{0,1},{1,0},{2,3},{3,2},{4,5},{5,4},{6,7},{7,6},{8,9},{9,8},{10,11... | collective-permute-start | bytes 393224 | tf_op jit(solution)/shard_map/ppermute | solution.py:30
  42.4 30.4 %collective-permute-start.2 = (f32[2,1,64,1024]{3,2,1,0:T(8,128)}, f32[2,1,64,1024]{3,2,1,0:T(8,128)}, u32[]{:S(2)}, u32[]{:S(2)}) collective-permute-start(f32[2,1,64,1024]{3,2,1,0:T(8,128)} %get-tuple-element.31), channel_id=1, source_target_pairs={{0,4},{4,0},{8,12},{12,8},{1,5},{5,1},{9,13},{13,9},{2,6},{6,2},{1... | collective-permute-start | bytes 1572872 | tf_op jit(solution)/shard_map/ppermute | solution.py:30
  49.0 1.7 collective-permute-start.8
  49.2 6.1 %collective-permute-start.5 = (bf16[64,1024]{1,0:T(8,128)(2,1)S(1)}, bf16[64,1024]{1,0:T(8,128)(2,1)S(1)}, u32[]{:S(2)}, u32[]{:S(2)}) collective-permute-start(bf16[64,1024]{1,0:T(8,128)(2,1)S(1)} %collective-permute-done.4), channel_id=1, source_target_pairs={{0,1},{1,0},{2,3},{3,2},{4,5},{5,4},{6,7},{7,6},{8,9},{9,8},{10,11... | collective-permute-start | bytes 393224 | tf_op jit(solution)/shard_map/ppermute | solution.py:30
  50.7 26.9 %collective-permute-start.12 = (bf16[128,1024]{1,0:T(8,128)(2,1)}, bf16[128,1024]{1,0:T(8,128)(2,1)}, u32[]{:S(2)}, u32[]{:S(2)}) collective-permute-start(bf16[128,1024]{1,0:T(8,128)(2,1)} %convolution_convert_fusion), channel_id=1, source_target_pairs={{0,12},{4,8},{8,4},{12,0},{1,13},{5,9},{9,5},{13,1},{2,14},{6,10},... | collective-permute-start | bytes 786440 | tf_op jit(solution)/shard_map/ppermute | solution.py:133
  55.3 22.2 %collective-permute-start.9 = (bf16[128,1024]{1,0:T(8,128)(2,1)}, bf16[128,1024]{1,0:T(8,128)(2,1)}, u32[]{:S(2)}, u32[]{:S(2)}) collective-permute-start(bf16[128,1024]{1,0:T(8,128)(2,1)} %convolution_convert_fusion.1), channel_id=1, source_target_pairs={{0,8},{4,12},{8,0},{12,4},{1,9},{5,13},{9,1},{13,5},{2,10},{6,14},... | collective-permute-start | bytes 786440 | tf_op jit(solution)/shard_map/ppermute | solution.py:133
  60.2 106.4 %all-gather.5.cloned.1.call-start = ((), (), s32[]{:S(2)}) async-start(), calls=%async_computation.1 | async-start | bytes 2359296 | tf_op jit(solution)/shard_map/all_gather | solution.py:142
  62.5 16.1 %collective-permute-start.6 = (bf16[128,1024]{1,0:T(8,128)(2,1)}, bf16[128,1024]{1,0:T(8,128)(2,1)S(1)}, u32[]{:S(2)}, u32[]{:S(2)}) collective-permute-start(bf16[128,1024]{1,0:T(8,128)(2,1)} %convolution_convert_fusion.2), channel_id=1, source_target_pairs={{0,4},{4,0},{8,12},{12,8},{1,5},{5,1},{9,13},{13,9},{2,6},{6,2},{1... | collective-permute-start | bytes 786440 | tf_op jit(solution)/shard_map/ppermute | solution.py:133
  67.9 4.9 %copy-start.12 = (f32[2,1,64,1024]{3,2,0,1:T(8,128)S(1)}, f32[2,1,64,1024]{3,2,0,1:T(8,128)}, u32[]{:S(2)}) copy-start(f32[2,1,64,1024]{3,2,0,1:T(8,128)} %get-tuple-element.30) | copy-start | bytes 1572868
  77.5 14.5 %collective-permute-start.3 = (bf16[2,1,64,1024]{3,2,1,0:T(8,128)(2,1)S(1)}, bf16[2,1,64,1024]{3,2,1,0:T(8,128)(2,1)S(1)}, u32[]{:S(2)}, u32[]{:S(2)}) collective-permute-start(bf16[2,1,64,1024]{3,2,1,0:T(8,128)(2,1)S(1)} %fusion.29), channel_id=1, source_target_pairs={{0,8},{4,12},{8,0},{12,4},{1,9},{5,13},{9,1},{13,5},{2,10},{6,14},... | collective-permute-start | bytes 786440 | tf_op jit(solution)/shard_map/ppermute | solution.py:30
  79.9 15.5 %copy-start.9 = (bf16[16,8,8,128]{3,2,1,0:T(8,128)(2,1)}, bf16[16,8,8,128]{3,2,1,0:T(8,128)(2,1)S(1)}, u32[]{:S(2)}) copy-start(bf16[16,8,8,128]{3,2,1,0:T(8,128)(2,1)S(1)} %copy.270) | copy-start | bytes 786436
  80.7 12.3 %copy-start.17 = (bf16[2,64,8,128]{3,1,0,2:T(8,128)(2,1)S(1)}, bf16[2,64,8,128]{3,1,0,2:T(8,128)(2,1)}, u32[]{:S(2)}) copy-start(bf16[2,64,8,128]{3,1,0,2:T(8,128)(2,1)} %copy.216) | copy-start | bytes 786436
  101.5 9.7 %copy-start.7 = (bf16[1,2,64,8,128]{4,3,2,1,0:T(8,128)(2,1)}, bf16[1,2,64,8,128]{4,3,2,1,0:T(8,128)(2,1)S(1)}, u32[]{:S(2)}) copy-start(bf16[1,2,64,8,128]{4,3,2,1,0:T(8,128)(2,1)S(1)} %copy.225) | copy-start | bytes 786436
  104.5 7.6 %copy-start.11 = (bf16[16,8,8,128]{3,2,1,0:T(8,128)(2,1)S(1)}, bf16[16,8,8,128]{3,2,1,0:T(8,128)(2,1)}, u32[]{:S(2)}) copy-start(bf16[16,8,8,128]{3,2,1,0:T(8,128)(2,1)} %copy-done.9) | copy-start | bytes 786436
  104.5 7.6 %copy-start.23 = (f32[2,8,64]{2,1,0:T(8,128)S(1)}, f32[2,8,64]{2,1,0:T(8,128)}, u32[]{:S(2)}) copy-start(f32[2,8,64]{2,1,0:T(8,128)} %copy-done.22) | copy-start | bytes 12292
  105.7 31.7 %collective-permute-start.17 = (bf16[2,1,32,1024]{3,0,2,1:T(2,128)(2,1)}, bf16[2,1,32,1024]{3,0,2,1:T(2,128)(2,1)}, u32[]{:S(2)}, u32[]{:S(2)}) collective-permute-start(bf16[2,1,32,1024]{3,0,2,1:T(2,128)(2,1)} %get-tuple-element.20), channel_id=1, source_target_pairs={{0,12},{4,8},{8,4},{12,0},{1,13},{5,9},{9,5},{13,1},{2,14},{6,10},... | collective-permute-start | bytes 393224 | tf_op jit(solution)/shard_map/ppermute | solution.py:215
  106.8 30.5 %collective-permute-start.16 = (bf16[2,1,32,1024]{3,0,2,1:T(2,128)(2,1)S(1)}, bf16[2,1,32,1024]{3,0,2,1:T(2,128)(2,1)}, u32[]{:S(2)}, u32[]{:S(2)}) collective-permute-start(bf16[2,1,32,1024]{3,0,2,1:T(2,128)(2,1)S(1)} %get-tuple-element.19), channel_id=1, source_target_pairs={{0,8},{4,12},{8,0},{12,4},{1,9},{5,13},{9,1},{13,5},{2,10},{6,14},... | collective-permute-start | bytes 393224 | tf_op jit(solution)/shard_map/ppermute | solution.py:215
  108.1 32.1 %collective-permute-start.15 = (bf16[2,1,64,1024]{3,2,0,1:T(8,128)(2,1)}, bf16[2,1,64,1024]{3,2,0,1:T(8,128)(2,1)}, u32[]{:S(2)}, u32[]{:S(2)}) collective-permute-start(bf16[2,1,64,1024]{3,2,0,1:T(8,128)(2,1)} %bitcast.235), channel_id=1, source_target_pairs={{0,4},{4,0},{8,12},{12,8},{1,5},{5,1},{9,13},{13,9},{2,6},{6,2},{1... | collective-permute-start | bytes 786440 | tf_op jit(solution)/shard_map/ppermute | solution.py:215
  123.6 8.0 %copy-start.3 = (bf16[2,8,64,192]{3,2,1,0:T(8,128)(2,1)S(1)}, bf16[2,8,64,192]{3,2,1,0:T(8,128)(2,1)}, u32[]{:S(2)}) copy-start(bf16[2,8,64,192]{3,2,1,0:T(8,128)(2,1)} %copy-done.2) | copy-start | bytes 1179652
  124.9 20.0 %collective-permute-start.14 = (bf16[2,1,128,1024]{3,2,1,0:T(8,128)(2,1)}, bf16[2,1,128,1024]{3,2,1,0:T(8,128)(2,1)}, u32[]{:S(2)}, u32[]{:S(2)}) collective-permute-start(bf16[2,1,128,1024]{3,2,1,0:T(8,128)(2,1)} %get-tuple-element.16), channel_id=1, source_target_pairs={{4,0},{8,4},{12,8},{5,1},{9,5},{13,9},{6,2},{10,6},{14,10},{7,3},{... | collective-permute-start | bytes 1572872 | tf_op jit(solution)/shard_map/ppermute | solution.py:22
  126.2 18.7 %collective-permute-start.13 = (bf16[2,1,128,1024]{3,2,1,0:T(8,128)(2,1)}, bf16[2,1,128,1024]{3,2,1,0:T(8,128)(2,1)}, u32[]{:S(2)}, u32[]{:S(2)}) collective-permute-start(bf16[2,1,128,1024]{3,2,1,0:T(8,128)(2,1)} %get-tuple-element.15), channel_id=1, source_target_pairs={{0,4},{4,8},{8,12},{1,5},{5,9},{9,13},{2,6},{6,10},{10,14},{3,7},{... | collective-permute-start | bytes 1572872 | tf_op jit(solution)/shard_map/ppermute | solution.py:20
  166.6 6.8 %copy-start.1 = (bf16[1024,1024]{1,0:T(8,128)(2,1)S(1)}, bf16[1024,1024]{1,0:T(8,128)(2,1)}, u32[]{:S(2)}) copy-start(bf16[1024,1024]{1,0:T(8,128)(2,1)} %param.10) | copy-start | bytes 6291460
  (15 other events, 31.2 us)
Sparse Core Ops, SparseCore 0:
  60.3 32.1 all-gather.2
  114.8 51.7 all-gather.4

commit v19 on v10

--- a/solution.py
+++ b/solution.py
@@ -139,10 +139,19 @@
         seq_count * cot_rows.shape[0], feat_count
     )
     feat_docs = lax.all_gather(feat_docs, "dp", axis=0, tiled=True)
-    whole_output = lax.all_gather(out_rows, ("dp", "seq"), axis=0, tiled=True)
-    weight_grad = jnp.einsum(
-        "tc,tw->cw", feat_docs, whole_output, preferred_element_type=jnp.float32
-    )
+    chunk_rows = out_rows.shape[0]
+    feat_chunks = feat_docs.reshape(-1, chunk_rows, feat_count)
+    split = chunk_rows // 2
+    weight_grad = None
+    for lo, hi in ((0, split), (split, chunk_rows)):
+        gathered = lax.all_gather(out_rows[lo:hi], ("dp", "seq"), axis=0, tiled=True)
+        part = jnp.einsum(
+            "tc,tw->cw",
+            feat_chunks[:, lo:hi].reshape(-1, feat_count),
+            gathered,
+            preferred_element_type=jnp.float32,
+        )
+        weight_grad = part if weight_grad is None else weight_grad + part
     grad_heads = attn_grad.reshape(doc_count, 2, block, heads, HEAD_DIM)
     prob_near = jnp.einsum(
         "dbqhe,dbkhe->dbhqk", grad_heads, near_v, preferred_element_type=jnp.float32

time: 172 us -> 202 us (1.17)
  the two profiles are of different devices: /device:TPU:30 before, /device:TPU:6 now
where the time goes in v19:
time: 202 us; the launch traced here: 198 us
  waiting for transfers between devices  54.7 us (27%)
  local copies, waits for them, and re-layouts  39.5 us (20%)
  other arithmetic  34.5 us (17%)
  starting transfers between devices  29.5 us (15%)
  matrix products  25.6 us (13%)
  between operations  14.4 us (7%)
    all_gather x2, waiting for transfers between devices, shards(): lax.all_gather(out_rows[lo:hi], ('dp', 'seq'), axis=0, tiled=True)  28.7 us
    ppermute x5, waiting for transfers between devices, swapped(): lax.ppermute(shard, axis, [(i, i ^ 1 << stride) for i in range(lax.axis_s...  12.8 us
    ppermute x2, starting transfers between devices, extended(): lax.ppermute(tail, axis, [(i, (i + 1) % count) for i in range(ends)])  10.7 us
    dot_general x2, matrix products, shards(): jnp.einsum('tc,tw->cw', feat_chunks[:, lo:hi].reshape(-1, feat_count), ga...  10.5 us
    scatter-add x1, other arithmetic, place_blocks(): return holder.at[:, chosen_doc].add(grad_doc)  8.48 us
    ppermute x3, waiting for transfers between devices, shards(): lax.ppermute(lax.dynamic_slice_in_dim(sent, core * half, half, axis=0), '...  7.23 us
    another operation x4, other arithmetic  4.65 us
    ppermute x2, waiting for transfers between devices, extended(): lax.ppermute(head, axis, [((i + 1) % count, i) for i in range(ends)])  4.52 us
  transfers between devices with their start and end apart: 21, of which 8 were waited for; matrix products, arithmetic and copies ran while one was open for 46% of the time, Pallas kernels for 0%

profile of v19, /device:TPU:6, one launch (start us, length us, event | category | flops | bytes accessed | tf_op | source)
XLA Modules:
  0.0 198.3 jit_solution(2672313903539891174)
XLA Ops:
  7.2 2.0 %pad_maximum_fusion.5 = bf16[2,1,128,1024]{3,2,1,0:T(8,128)(2,1)} fusion(bf16[1,1,128,1024]{3,2,1,0:T(8,128)(2,1)} %bitcast.255, bf16[1,1,128,1024]{3,2,1,0:T(8,128)(2,1)} %bitcast.257), kind=kLoop, calls=%fused_computation.54 | loop fusion | flops 262144 | bytes 1048576 | tf_op jit(solution)/shard_map/stack | solution.py:58
  10.6 5.3 %collective-permute-start = (bf16[2,1,128,1024]{3,2,1,0:T(8,128)(2,1)}, bf16[2,1,128,1024]{3,2,1,0:T(8,128)(2,1)}, u32[]{:S(2)}, u32[]{:S(2)}) collective-permute-start(bf16[2,1,128,1024]{3,2,1,0:T(8,128)(2,1)} %pad_maximum_fusion.5), channel_id=1, source_target_pairs={{0,4},{4,8},{8,12},{1,5},{5,9},{9,13},{2,6},{6,10},{10,14},{3,7},{... | collective-permute-start | bytes 1572872 | tf_op jit(solution)/shard_map/ppermute | solution.py:20
  15.9 1.9 dynamic-slice_bitcast_fusion.2
  17.8 1.5 collective-permute-start.10
  20.5 1.7 collective-permute-start.4
  28.5 2.6 %collective-permute-done.10 = bf16[64,1024]{1,0:T(8,128)(2,1)S(1)} collective-permute-done((bf16[64,1024]{1,0:T(8,128)(2,1)S(1)}, bf16[64,1024]{1,0:T(8,128)(2,1)S(1)}, u32[]{:S(2)}, u32[]{:S(2)}) %collective-permute-start.10) | collective-permute-done | bytes 131104 | tf_op jit(solution)/shard_map/ppermute | solution.py:123
  32.7 4.6 %collective-permute-done.7 = bf16[64,1024]{1,0:T(8,128)(2,1)S(1)} collective-permute-done((bf16[64,1024]{1,0:T(8,128)(2,1)}, bf16[64,1024]{1,0:T(8,128)(2,1)S(1)}, u32[]{:S(2)}, u32[]{:S(2)}) %collective-permute-start.7) | collective-permute-done | bytes 131104 | tf_op jit(solution)/shard_map/ppermute | solution.py:123
  37.3 2.0 %collective-permute-start.2 = (f32[2,1,64,1024]{3,2,1,0:T(8,128)}, f32[2,1,64,1024]{3,2,1,0:T(8,128)}, u32[]{:S(2)}, u32[]{:S(2)}) collective-permute-start(f32[2,1,64,1024]{3,2,1,0:T(8,128)} %get-tuple-element.27), channel_id=1, source_target_pairs={{0,4},{4,0},{8,12},{12,8},{1,5},{5,1},{9,13},{13,9},{2,6},{6,2},{1... | collective-permute-start | bytes 1572872 | tf_op jit(solution)/shard_map/ppermute | solution.py:30
  40.9 3.4 %collective-permute-start.12 = (bf16[128,1024]{1,0:T(8,128)(2,1)}, bf16[128,1024]{1,0:T(8,128)(2,1)}, u32[]{:S(2)}, u32[]{:S(2)}) collective-permute-start(bf16[128,1024]{1,0:T(8,128)(2,1)} %convolution_convert_fusion), channel_id=1, source_target_pairs={{0,12},{4,8},{8,4},{12,0},{1,13},{5,9},{9,5},{13,1},{2,14},{6,10},... | collective-permute-start | bytes 786440 | tf_op jit(solution)/shard_map/ppermute | solution.py:133
  47.4 1.8 gather_fusion
  50.7 2.1 %convolution_convert_fusion.2 = bf16[128,1024]{1,0:T(8,128)(2,1)} fusion(bf16[1024,1024]{1,0:T(8,128)(2,1)S(1)} %copy-done, bf16[64,1024]{1,0:T(8,128)(2,1)} %copy-done.19, bf16[64,1024]{1,0:T(8,128)(2,1)S(1)} %collective-permute-done.4, pred[]{:T(512)S(6)} %eq.9), kind=kOutput, calls=%fused_computation.25 | convolution fusion | flops 269746176 | bytes 2621441 | tf_op jit(solution)/shard_map/dot_general | solution.py:132
  54.7 1.8 gather_fusion.1
  56.5 1.7 copy.198
  58.3 4.1 %collective-permute-done.2 = f32[2,1,64,1024]{3,2,1,0:T(8,128)} collective-permute-done((f32[2,1,64,1024]{3,2,1,0:T(8,128)}, f32[2,1,64,1024]{3,2,1,0:T(8,128)}, u32[]{:S(2)}, u32[]{:S(2)}) %collective-permute-start.2) | collective-permute-done | bytes 524320 | tf_op jit(solution)/shard_map/ppermute | solution.py:30
  72.8 8.7 %collective-permute-done.3 = bf16[2,1,64,1024]{3,2,1,0:T(8,128)(2,1)S(1)} collective-permute-done((bf16[2,1,64,1024]{3,2,1,0:T(8,128)(2,1)S(1)}, bf16[2,1,64,1024]{3,2,1,0:T(8,128)(2,1)S(1)}, u32[]{:S(2)}, u32[]{:S(2)}) %collective-permute-start.3) | collective-permute-done | bytes 262176 | tf_op jit(solution)/shard_map/ppermute | solution.py:30
  84.9 2.8 %multiply_reduce_fusion = (f32[2,8,64]{2,1,0:T(8,128)S(1)}, f32[2,8,64,192]{3,2,1,0:T(8,128)}) fusion(f32[2,8,64]{2,1,0:T(8,128)S(1)} %copy_add_fusion.1, f32[2,8,64,192]{3,2,1,0:T(8,128)S(1)} %get-tuple-element.31, f32[2,8,64]{2,1,0:T(8,128)S(1)} %copy_maximum_fusion, bf16[2,192,8,128]{3,2,1,0:T(8,128)(2,1)} %bitcast.270, ...), kind=kOutput, calls=%fused_computation.41 | convolution fusion | flops 51117056 | bytes 2633728 | tf_op jit(solution)/shard_map/dbqhe,dbkhe->dbhqk/dot_general | solution.py:156
  96.7 2.1 %convolution_bitcast_fusion = f32[1,2,192,8,128]{4,2,3,1,0:T(8,128)} fusion(bf16[2,64,8,128]{3,2,1,0:T(8,128)(2,1)S(1)} %bitcast.266, f32[2,8,64,192]{3,2,1,0:T(8,128)S(1)} %get-tuple-element.31, f32[2,8,64]{2,1,0:T(8,128)S(1)} %copy-done.21, f32[2,8,64]{2,1,0:T(8,128)S(1)} %copy_maximum_fusion), kind=kOutput, calls=%fused_computation.8 | convolution fusion | flops 50921472 | bytes 2629632 | tf_op jit(solution)/shard_map/dbhqk,dbqhe->dbkhe/dot_general | solution.py:180
  100.3 4.2 %collective-permute-start.15 = (bf16[2,1,64,1024]{3,2,0,1:T(8,128)(2,1)}, bf16[2,1,64,1024]{3,2,0,1:T(8,128)(2,1)}, u32[]{:S(2)}, u32[]{:S(2)}) collective-permute-start(bf16[2,1,64,1024]{3,2,0,1:T(8,128)(2,1)} %bitcast.224), channel_id=1, source_target_pairs={{0,4},{4,0},{8,12},{12,8},{1,5},{5,1},{9,13},{13,9},{2,6},{6,2},{1... | collective-permute-start | bytes 786440 | tf_op jit(solution)/shard_map/ppermute | solution.py:212
  107.3 3.1 %pad_maximum_fusion = f32[1,2,2,3,64,1024]{5,0,4,3,2,1:T(1,128)S(1)} fusion(f32[1,1,2,3,64,1024]{5,0,4,3,2,1:T(1,128)S(1)} %bitcast.242, f32[1,1,2,3,64,1024]{5,0,4,3,2,1:T(1,128)S(1)} %bitcast.243), kind=kLoop, calls=%fused_computation.3 | loop fusion | flops 786432 | bytes 6291456 | tf_op jit(solution)/shard_map/stack | solution.py:190
  110.3 2.4 %copy.261 = f32[1,2,2,3,64,1024]{5,4,1,3,2,0:T(8,128)} copy(f32[1,2,2,3,64,1024]{5,0,4,3,2,1:T(1,128)S(1)} %pad_maximum_fusion) | data formatting | bytes 6291456 | tf_op jit(solution)/shard_map/stack | solution.py:190
  112.7 2.1 %broadcast.223 = f32[2,6,64,1024]{3,2,1,0:T(8,128)} broadcast(f32[]{:T(128)} %constant.103.clone.1), dimensions={} | broadcast | bytes 3145732 | tf_op jit(solution)/shard_map/vmap()/broadcast_in_dim;vmap()/broadcast_in_dim | solution.py:46
  114.7 8.5 %scatter_fusion = f32[2,6,64,1024]{3,2,1,0:T(8,128)} fusion(f32[2,6,64,1024]{3,2,1,0:T(8,128)} %broadcast.223, s32[6]{0:T(128)S(1)} %copy-done.24, f32[6,2,64,1024]{3,2,1,0:T(8,128)} %bitcast.230), kind=kCustom, calls=%fused_computation.2 | custom fusion | flops 786432 | bytes 9437208 | tf_op jit(solution)/shard_map/vmap()/scatter-add | solution.py:46
  123.2 1.7 fusion.74
  127.5 5.4 %collective-permute-start.13 = (bf16[2,1,128,1024]{3,2,1,0:T(8,128)(2,1)}, bf16[2,1,128,1024]{3,2,1,0:T(8,128)(2,1)}, u32[]{:S(2)}, u32[]{:S(2)}) collective-permute-start(bf16[2,1,128,1024]{3,2,1,0:T(8,128)(2,1)} %get-tuple-element.13), channel_id=1, source_target_pairs={{0,4},{4,8},{8,12},{1,5},{5,9},{9,13},{2,6},{6,10},{10,14},{3,7},{... | collective-permute-start | bytes 1572872 | tf_op jit(solution)/shard_map/ppermute | solution.py:20
  133.6 2.3 %slice.102 = f32[2,1,2,64,1024]{4,3,2,0,1:T(8,128)} slice(f32[2,1,6,64,1024]{4,3,2,0,1:T(8,128)} %bitcast.226), slice={[0:2], [0:1], [2:4], [0:64], [0:1024]} | slice | bytes 2097152 | tf_op jit(solution)/shard_map/slice | solution.py:200
  141.1 1.7 div.44
  142.8 4.5 %collective-permute-done.14 = bf16[2,1,128,1024]{3,2,1,0:T(8,128)(2,1)} collective-permute-done((bf16[2,1,128,1024]{3,2,1,0:T(8,128)(2,1)}, bf16[2,1,128,1024]{3,2,1,0:T(8,128)(2,1)}, u32[]{:S(2)}, u32[]{:S(2)}) %collective-permute-start.14) | collective-permute-done | bytes 524320 | tf_op jit(solution)/shard_map/ppermute | solution.py:22
  147.4 2.6 %fusion.11 = bf16[2,1,128,1024]{3,2,1,0:T(8,128)(2,1)S(1)} fusion(f32[2,1,128,1024]{3,2,1,0:T(8,128)} %div.48, f32[2,1,128,1024]{3,2,1,0:T(8,128)} %div.44, f32[2,1,128,1024]{3,2,1,0:T(8,128)} %bitcast.252, bf16[2,1,128,1024]{3,2,1,0:T(8,128)(2,1)} %collective-permute-done.14, bf16[2,1,256,1024]{3,2,1,0:T(8,128)(2,1)S(1)} %bitcast.232, ...), kind=kLoop, calls=%fused_computation.31 | loop fusion | flops 4456448 | bytes 5767168 | tf_op jit(solution)/shard_map/convert.1
  150.8 1.8 fusion.75
  152.6 4.5 %fusion.13 = f32[1024,1024]{1,0:T(8,128)} fusion(bf16[512,1024]{1,0:T(8,128)(2,1)S(1)} %bitcast.244, bf16[1,512,1024]{2,1,0:T(8,128)(2,1)} %all-gather.8.cloned.1.call-done), kind=kOutput, calls=%fused_computation.37 | convolution fusion | flops 1073741824 | bytes 6291456 | tf_op jit(solution)/shard_map/tc,tw->cw/dot_general | solution.py:148
  157.1 28.7 %all-gather.10.cloned.1.call-done = bf16[1,512,1024]{2,1,0:T(8,128)(2,1)} async-done(((bf16[1,64,1024]{2,1,0:T(8,128)(2,1)}), bf16[1,512,1024]{2,1,0:T(8,128)(2,1)}) %all-gather.10.cloned.1.call-update) | async-done | bytes 1048592 | tf_op jit(solution)/shard_map/all_gather | solution.py:147
  185.8 6.0 %convolution_add_fusion = f32[1024,1024]{1,0:T(8,128)} fusion(f32[1024,1024]{1,0:T(8,128)} %fusion.13, bf16[512,1024]{1,0:T(8,128)(2,1)S(1)} %bitcast.233, bf16[1,512,1024]{2,1,0:T(8,128)(2,1)} %all-gather.10.cloned.1.call-done), kind=kOutput, calls=%fused_computation.4 | convolution fusion | flops 1074790400 | bytes 10485760 | tf_op jit(solution)/shard_map/tc,tw->cw/dot_general | solution.py:148
  (168 shorter events, 54.4 us)
Async XLA Ops:
  7.2 20.0 %copy-start = (bf16[1024,1024]{1,0:T(8,128)(2,1)S(1)}, bf16[1024,1024]{1,0:T(8,128)(2,1)}, u32[]{:S(2)}) copy-start(bf16[1024,1024]{1,0:T(8,128)(2,1)} %param.10) | copy-start | bytes 6291460
  7.2 16.1 %copy-start.3 = (bf16[1,128,1024]{2,1,0:T(8,128)(2,1)S(1)}, bf16[1,128,1024]{2,1,0:T(8,128)(2,1)}, u32[]{:S(2)}) copy-start(bf16[1,128,1024]{2,1,0:T(8,128)(2,1)} %param.7) | copy-start | bytes 786436
  7.2 16.2 %copy-start.25 = (s32[1,2,2]{2,1,0:T(2,128)S(1)}, s32[1,2,2]{2,1,0:T(2,128)}, u32[]{:S(2)}) copy-start(s32[1,2,2]{2,1,0:T(2,128)} %param.9) | copy-start | bytes 52
  7.2 143.6 %all-gather.6.cloned.1.call-start = ((), (), s32[]{:S(2)}) async-start(), calls=%async_computation | async-start | bytes 3145728 | tf_op jit(solution)/shard_map/all_gather | solution.py:141
  9.3 43.5 %collective-permute-start.1 = (bf16[2,1,128,1024]{3,2,1,0:T(8,128)(2,1)}, bf16[2,1,128,1024]{3,2,1,0:T(8,128)(2,1)}, u32[]{:S(2)}, u32[]{:S(2)}) collective-permute-start(bf16[2,1,128,1024]{3,2,1,0:T(8,128)(2,1)} %pad_maximum_fusion.5), channel_id=1, source_target_pairs={{4,0},{8,4},{12,8},{5,1},{9,5},{13,9},{6,2},{10,6},{14,10},{7,3},{... | collective-permute-start | bytes 1572872 | tf_op jit(solution)/shard_map/ppermute | solution.py:22
  10.6 42.7 %collective-permute-start = (bf16[2,1,128,1024]{3,2,1,0:T(8,128)(2,1)}, bf16[2,1,128,1024]{3,2,1,0:T(8,128)(2,1)}, u32[]{:S(2)}, u32[]{:S(2)}) collective-permute-start(bf16[2,1,128,1024]{3,2,1,0:T(8,128)(2,1)} %pad_maximum_fusion.5), channel_id=1, source_target_pairs={{0,4},{4,8},{8,12},{1,5},{5,9},{9,13},{2,6},{6,10},{10,14},{3,7},{... | collective-permute-start | bytes 1572872 | tf_op jit(solution)/shard_map/ppermute | solution.py:20
  17.8 13.3 %collective-permute-start.10 = (bf16[64,1024]{1,0:T(8,128)(2,1)S(1)}, bf16[64,1024]{1,0:T(8,128)(2,1)S(1)}, u32[]{:S(2)}, u32[]{:S(2)}) collective-permute-start(bf16[64,1024]{1,0:T(8,128)(2,1)S(1)} %get-tuple-element.18), channel_id=1, source_target_pairs={{0,12},{4,8},{8,4},{12,0},{1,13},{5,9},{9,5},{13,1},{2,14},{6,10},... | collective-permute-start | bytes 393224 | tf_op jit(solution)/shard_map/ppermute | solution.py:123
  19.3 18.0 %collective-permute-start.7 = (bf16[64,1024]{1,0:T(8,128)(2,1)}, bf16[64,1024]{1,0:T(8,128)(2,1)S(1)}, u32[]{:S(2)}, u32[]{:S(2)}) collective-permute-start(bf16[64,1024]{1,0:T(8,128)(2,1)} %get-tuple-element.19), channel_id=1, source_target_pairs={{0,8},{4,12},{8,0},{12,4},{1,9},{5,13},{9,1},{13,5},{2,10},{6,14},... | collective-permute-start | bytes 393224 | tf_op jit(solution)/shard_map/ppermute | solution.py:123
  20.5 18.8 %collective-permute-start.4 = (bf16[64,1024]{1,0:T(8,128)(2,1)S(1)}, bf16[64,1024]{1,0:T(8,128)(2,1)S(1)}, u32[]{:S(2)}, u32[]{:S(2)}) collective-permute-start(bf16[64,1024]{1,0:T(8,128)(2,1)S(1)} %get-tuple-element.17), channel_id=1, source_target_pairs={{0,4},{4,0},{8,12},{12,8},{1,5},{5,1},{9,13},{13,9},{2,6},{6,2},{1... | collective-permute-start | bytes 393224 | tf_op jit(solution)/shard_map/ppermute | solution.py:123
  31.1 8.4 %collective-permute-start.11 = (bf16[64,1024]{1,0:T(8,128)(2,1)S(1)}, bf16[64,1024]{1,0:T(8,128)(2,1)S(1)}, u32[]{:S(2)}, u32[]{:S(2)}) collective-permute-start(bf16[64,1024]{1,0:T(8,128)(2,1)S(1)} %collective-permute-done.10), channel_id=1, source_target_pairs={{0,1},{1,0},{2,3},{3,2},{4,5},{5,4},{6,7},{7,6},{8,9},{9,8},{10,11... | collective-permute-start | bytes 393224 | tf_op jit(solution)/shard_map/ppermute | solution.py:30
  37.3 25.1 %collective-permute-start.2 = (f32[2,1,64,1024]{3,2,1,0:T(8,128)}, f32[2,1,64,1024]{3,2,1,0:T(8,128)}, u32[]{:S(2)}, u32[]{:S(2)}) collective-permute-start(f32[2,1,64,1024]{3,2,1,0:T(8,128)} %get-tuple-element.27), channel_id=1, source_target_pairs={{0,4},{4,0},{8,12},{12,8},{1,5},{5,1},{9,13},{13,9},{2,6},{6,2},{1... | collective-permute-start | bytes 1572872 | tf_op jit(solution)/shard_map/ppermute | solution.py:30
  39.3 1.7 collective-permute-start.8
  39.5 6.1 %collective-permute-start.5 = (bf16[64,1024]{1,0:T(8,128)(2,1)S(1)}, bf16[64,1024]{1,0:T(8,128)(2,1)S(1)}, u32[]{:S(2)}, u32[]{:S(2)}) collective-permute-start(bf16[64,1024]{1,0:T(8,128)(2,1)S(1)} %collective-permute-done.4), channel_id=1, source_target_pairs={{0,1},{1,0},{2,3},{3,2},{4,5},{5,4},{6,7},{7,6},{8,9},{9,8},{10,11... | collective-permute-start | bytes 393224 | tf_op jit(solution)/shard_map/ppermute | solution.py:30
  40.9 26.5 %collective-permute-start.12 = (bf16[128,1024]{1,0:T(8,128)(2,1)}, bf16[128,1024]{1,0:T(8,128)(2,1)}, u32[]{:S(2)}, u32[]{:S(2)}) collective-permute-start(bf16[128,1024]{1,0:T(8,128)(2,1)} %convolution_convert_fusion), channel_id=1, source_target_pairs={{0,12},{4,8},{8,4},{12,0},{1,13},{5,9},{9,5},{13,1},{2,14},{6,10},... | collective-permute-start | bytes 786440 | tf_op jit(solution)/shard_map/ppermute | solution.py:133
  45.6 22.3 %collective-permute-start.9 = (bf16[128,1024]{1,0:T(8,128)(2,1)}, bf16[128,1024]{1,0:T(8,128)(2,1)}, u32[]{:S(2)}, u32[]{:S(2)}) collective-permute-start(bf16[128,1024]{1,0:T(8,128)(2,1)} %convolution_convert_fusion.1), channel_id=1, source_target_pairs={{0,8},{4,12},{8,0},{12,4},{1,9},{5,13},{9,1},{13,5},{2,10},{6,14},... | collective-permute-start | bytes 786440 | tf_op jit(solution)/shard_map/ppermute | solution.py:133
  50.5 102.1 %all-gather.8.cloned.1.call-start = ((), (), s32[]{:S(2)}) async-start(), calls=%async_computation.1 | async-start | bytes 1179648 | tf_op jit(solution)/shard_map/all_gather | solution.py:147
  52.8 16.1 %collective-permute-start.6 = (bf16[128,1024]{1,0:T(8,128)(2,1)}, bf16[128,1024]{1,0:T(8,128)(2,1)S(1)}, u32[]{:S(2)}, u32[]{:S(2)}) collective-permute-start(bf16[128,1024]{1,0:T(8,128)(2,1)} %convolution_convert_fusion.2), channel_id=1, source_target_pairs={{0,4},{4,0},{8,12},{12,8},{1,5},{5,1},{9,13},{13,9},{2,6},{6,2},{1... | collective-permute-start | bytes 786440 | tf_op jit(solution)/shard_map/ppermute | solution.py:133
  67.0 14.5 %collective-permute-start.3 = (bf16[2,1,64,1024]{3,2,1,0:T(8,128)(2,1)S(1)}, bf16[2,1,64,1024]{3,2,1,0:T(8,128)(2,1)S(1)}, u32[]{:S(2)}, u32[]{:S(2)}) collective-permute-start(bf16[2,1,64,1024]{3,2,1,0:T(8,128)(2,1)S(1)} %fusion.24), channel_id=1, source_target_pairs={{0,8},{4,12},{8,0},{12,4},{1,9},{5,13},{9,1},{13,5},{2,10},{6,14},... | collective-permute-start | bytes 786440 | tf_op jit(solution)/shard_map/ppermute | solution.py:30
  70.2 14.7 %copy-start.7 = (bf16[16,8,8,128]{3,2,1,0:T(8,128)(2,1)}, bf16[16,8,8,128]{3,2,1,0:T(8,128)(2,1)S(1)}, u32[]{:S(2)}) copy-start(bf16[16,8,8,128]{3,2,1,0:T(8,128)(2,1)S(1)} %copy.265) | copy-start | bytes 786436
  71.0 11.4 %copy-start.15 = (bf16[2,64,8,128]{3,1,0,2:T(8,128)(2,1)S(1)}, bf16[2,64,8,128]{3,1,0,2:T(8,128)(2,1)}, u32[]{:S(2)}) copy-start(bf16[2,64,8,128]{3,1,0,2:T(8,128)(2,1)} %copy.209) | copy-start | bytes 786436
  82.4 5.3 %copy-start.5 = (bf16[1,1,128,1024]{2,3,1,0:T(8,128)(2,1)}, bf16[1,1,128,1024]{2,3,1,0:T(8,128)(2,1)S(1)}, u32[]{:S(2)}) copy-start(bf16[1,1,128,1024]{2,3,1,0:T(8,128)(2,1)S(1)} %copy.207) | copy-start | bytes 786436
  95.7 41.2 %collective-permute-start.17 = (bf16[2,1,32,1024]{3,0,2,1:T(2,128)(2,1)}, bf16[2,1,32,1024]{3,0,2,1:T(2,128)(2,1)}, u32[]{:S(2)}, u32[]{:S(2)}) collective-permute-start(bf16[2,1,32,1024]{3,0,2,1:T(2,128)(2,1)} %get-tuple-element.16), channel_id=1, source_target_pairs={{0,12},{4,8},{8,4},{12,0},{1,13},{5,9},{9,5},{13,1},{2,14},{6,10},... | collective-permute-start | bytes 393224 | tf_op jit(solution)/shard_map/ppermute | solution.py:212
  95.9 41.0 %collective-permute-start.16 = (bf16[2,1,32,1024]{3,0,2,1:T(2,128)(2,1)S(1)}, bf16[2,1,32,1024]{3,0,2,1:T(2,128)(2,1)}, u32[]{:S(2)}, u32[]{:S(2)}) collective-permute-start(bf16[2,1,32,1024]{3,0,2,1:T(2,128)(2,1)S(1)} %get-tuple-element.15), channel_id=1, source_target_pairs={{0,8},{4,12},{8,0},{12,4},{1,9},{5,13},{9,1},{13,5},{2,10},{6,14},... | collective-permute-start | bytes 393224 | tf_op jit(solution)/shard_map/ppermute | solution.py:212
  98.7 87.1 %all-gather.10.cloned.1.call-start = ((), (), s32[]{:S(2)}) async-start(), calls=%async_computation.2 | async-start | bytes 1179648 | tf_op jit(solution)/shard_map/all_gather | solution.py:147
  99.0 5.5 %copy-start.12 = (f32[1,2,192,8,128]{4,2,3,1,0:T(8,128)S(1)}, f32[1,2,192,8,128]{4,2,3,1,0:T(8,128)}, u32[]{:S(2)}) copy-start(f32[1,2,192,8,128]{4,2,3,1,0:T(8,128)} %convolution_bitcast_fusion) | copy-start | bytes 4718596
  99.5 5.9 %copy-start.13 = (f32[2,8,64,192]{3,2,1,0:T(8,128)S(1)}, f32[2,8,64,192]{3,2,1,0:T(8,128)}, u32[]{:S(2)}) copy-start(f32[2,8,64,192]{3,2,1,0:T(8,128)} %get-tuple-element.33) | copy-start | bytes 2359300
  99.5 5.9 %copy-start.23 = (f32[2,8,64]{2,1,0:T(8,128)S(1)}, f32[2,8,64]{2,1,0:T(8,128)}, u32[]{:S(2)}) copy-start(f32[2,8,64]{2,1,0:T(8,128)} %copy-done.22) | copy-start | bytes 12292
  100.3 39.5 %collective-permute-start.15 = (bf16[2,1,64,1024]{3,2,0,1:T(8,128)(2,1)}, bf16[2,1,64,1024]{3,2,0,1:T(8,128)(2,1)}, u32[]{:S(2)}, u32[]{:S(2)}) collective-permute-start(bf16[2,1,64,1024]{3,2,0,1:T(8,128)(2,1)} %bitcast.224), channel_id=1, source_target_pairs={{0,4},{4,0},{8,12},{12,8},{1,5},{5,1},{9,13},{13,9},{2,6},{6,2},{1... | collective-permute-start | bytes 786440 | tf_op jit(solution)/shard_map/ppermute | solution.py:212
  125.0 8.2 %copy-start.6 = (bf16[1,1,128,1024]{2,3,1,0:T(8,128)(2,1)S(1)}, bf16[1,1,128,1024]{2,3,1,0:T(8,128)(2,1)}, u32[]{:S(2)}) copy-start(bf16[1,1,128,1024]{2,3,1,0:T(8,128)(2,1)} %copy-done.5) | copy-start | bytes 786436
  126.2 21.2 %collective-permute-start.14 = (bf16[2,1,128,1024]{3,2,1,0:T(8,128)(2,1)}, bf16[2,1,128,1024]{3,2,1,0:T(8,128)(2,1)}, u32[]{:S(2)}, u32[]{:S(2)}) collective-permute-start(bf16[2,1,128,1024]{3,2,1,0:T(8,128)(2,1)} %get-tuple-element.14), channel_id=1, source_target_pairs={{4,0},{8,4},{12,8},{5,1},{9,5},{13,9},{6,2},{10,6},{14,10},{7,3},{... | collective-permute-start | bytes 1572872 | tf_op jit(solution)/shard_map/ppermute | solution.py:22
  127.5 19.9 %collective-permute-start.13 = (bf16[2,1,128,1024]{3,2,1,0:T(8,128)(2,1)}, bf16[2,1,128,1024]{3,2,1,0:T(8,128)(2,1)}, u32[]{:S(2)}, u32[]{:S(2)}) collective-permute-start(bf16[2,1,128,1024]{3,2,1,0:T(8,128)(2,1)} %get-tuple-element.13), channel_id=1, source_target_pairs={{0,4},{4,8},{8,12},{1,5},{5,9},{9,13},{2,6},{6,10},{10,14},{3,7},{... | collective-permute-start | bytes 1572872 | tf_op jit(solution)/shard_map/ppermute | solution.py:20
  185.8 6.0 %copy-start.1 = (bf16[1024,1024]{1,0:T(8,128)(2,1)S(1)}, bf16[1024,1024]{1,0:T(8,128)(2,1)}, u32[]{:S(2)}) copy-start(bf16[1024,1024]{1,0:T(8,128)(2,1)} %param.10) | copy-start | bytes 6291460
  (15 other events, 39.8 us)
Sparse Core Ops, SparseCore 0:
  50.6 32.1 all-gather.5
  98.9 45.0 all-gather.7
  146.1 39.6 all-gather.9

commit v20 on v10

--- a/solution.py
+++ b/solution.py
@@ -138,7 +138,14 @@
     feat_docs = jnp.take(jnp.stack(feat_list, axis=0), feat_order, axis=0).reshape(
         seq_count * cot_rows.shape[0], feat_count
     )
-    feat_docs = lax.all_gather(feat_docs, "dp", axis=0, tiled=True)
+    if lax.axis_size("dp") == 2:
+        feat_docs = jnp.take(
+            jnp.stack([feat_docs, swapped(feat_docs, "dp", 0)], axis=0),
+            jnp.arange(2, dtype=jnp.int32) ^ lax.axis_index("dp"),
+            axis=0,
+        ).reshape(2 * feat_docs.shape[0], feat_count)
+    else:
+        feat_docs = lax.all_gather(feat_docs, "dp", axis=0, tiled=True)
     whole_output = lax.all_gather(out_rows, ("dp", "seq"), axis=0, tiled=True)
     weight_grad = jnp.einsum(
         "tc,tw->cw", feat_docs, whole_output, preferred_element_type=jnp.float32

time: 172 us -> 177 us (1.029)
  the two profiles are of different devices: /device:TPU:30 before, /device:TPU:6 now
where the time goes in v20:
time: 177 us; the launch traced here: 175 us
  other arithmetic  38 us (21%)
  waiting for transfers between devices  35.7 us (20%)
  local copies, waits for them, and re-layouts  33.1 us (19%)
  starting transfers between devices  30.2 us (17%)
  matrix products  22.7 us (13%)
  between operations  14.8 us (8%)
    ppermute x6, waiting for transfers between devices, swapped(): lax.ppermute(shard, axis, [(i, i ^ 1 << stride) for i in range(lax.axis_s...  15.3 us
    ppermute x2, waiting for transfers between devices, extended(): lax.ppermute(head, axis, [((i + 1) % count, i) for i in range(ends)])  13.1 us
    ppermute x2, starting transfers between devices, extended(): lax.ppermute(tail, axis, [(i, (i + 1) % count) for i in range(ends)])  10.7 us
    dot_general x1, matrix products, shards(): jnp.einsum('tc,tw->cw', feat_docs, whole_output, preferred_element_type=j...  6.77 us
    ppermute x3, waiting for transfers between devices, shards(): lax.ppermute(lax.dynamic_slice_in_dim(sent, core * half, half, axis=0), '...  5.95 us
    scatter-add x1, other arithmetic, place_blocks(): return holder.at[:, chosen_doc].add(grad_doc)  5.59 us
    unnamed x75, local copies, waits for them, and re-layouts  4.65 us
    another operation x4, other arithmetic  4.65 us
  transfers between devices with their start and end apart: 20, of which 6 were waited for; matrix products, arithmetic and copies ran while one was open for 47% of the time, Pallas kernels for 0%

profile of v20, /device:TPU:6, one launch (start us, length us, event | category | flops | bytes accessed | tf_op | source)
XLA Modules:
  0.0 174.5 jit_solution(11013407313710990897)
XLA Ops:
  7.2 2.0 %pad_maximum_fusion.6 = bf16[2,1,128,1024]{3,2,1,0:T(8,128)(2,1)} fusion(bf16[1,1,128,1024]{3,2,1,0:T(8,128)(2,1)} %bitcast.258, bf16[1,1,128,1024]{3,2,1,0:T(8,128)(2,1)} %bitcast.260), kind=kLoop, calls=%fused_computation.54 | loop fusion | flops 262144 | bytes 1048576 | tf_op jit(solution)/shard_map/stack | solution.py:58
  10.6 5.4 %collective-permute-start = (bf16[2,1,128,1024]{3,2,1,0:T(8,128)(2,1)}, bf16[2,1,128,1024]{3,2,1,0:T(8,128)(2,1)}, u32[]{:S(2)}, u32[]{:S(2)}) collective-permute-start(bf16[2,1,128,1024]{3,2,1,0:T(8,128)(2,1)} %pad_maximum_fusion.6), channel_id=1, source_target_pairs={{0,4},{4,8},{8,12},{1,5},{5,9},{9,13},{2,6},{6,10},{10,14},{3,7},{... | collective-permute-start | bytes 1572872 | tf_op jit(solution)/shard_map/ppermute | solution.py:20
  15.9 2.0 %dynamic-slice_bitcast_fusion.2 = (bf16[64,1024]{1,0:T(8,128)(2,1)}, bf16[64,1024]{1,0:T(8,128)(2,1)S(1)}, bf16[64,1024]{1,0:T(8,128)(2,1)}) fusion(bf16[1,128,4096]{2,1,0:T(8,128)(2,1)} %param.11, s32[]{:T(128)S(6)} %select_n.170, s32[]{:T(128)S(6)} %select_n.172, s32[]{:T(128)S(6)} %select_n.178, s32[]{:T(128)S(6)} %select_n.175), kind=kLoop, calls=%fused_computation.125 | loop fusion | bytes 786448 | tf_op jit(solution)/shard_map/dynamic_slice | solution.py:124
  17.9 1.4 collective-permute-start.10
  20.5 1.8 %collective-permute-start.4 = (bf16[64,1024]{1,0:T(8,128)(2,1)}, bf16[64,1024]{1,0:T(8,128)(2,1)S(1)}, u32[]{:S(2)}, u32[]{:S(2)}) collective-permute-start(bf16[64,1024]{1,0:T(8,128)(2,1)} %get-tuple-element.15), channel_id=1, source_target_pairs={{0,4},{4,0},{8,12},{12,8},{1,5},{5,1},{9,13},{13,9},{2,6},{6,2},{1... | collective-permute-start | bytes 393224 | tf_op jit(solution)/shard_map/ppermute | solution.py:123
  23.6 1.4 convert_reduce_fusion
  28.6 2.6 %collective-permute-done.10 = bf16[64,1024]{1,0:T(8,128)(2,1)S(1)} collective-permute-done((bf16[64,1024]{1,0:T(8,128)(2,1)S(1)}, bf16[64,1024]{1,0:T(8,128)(2,1)S(1)}, u32[]{:S(2)}, u32[]{:S(2)}) %collective-permute-start.10) | collective-permute-done | bytes 131104 | tf_op jit(solution)/shard_map/ppermute | solution.py:123
  33.9 3.4 %collective-permute-done.7 = bf16[64,1024]{1,0:T(8,128)(2,1)S(1)} collective-permute-done((bf16[64,1024]{1,0:T(8,128)(2,1)}, bf16[64,1024]{1,0:T(8,128)(2,1)S(1)}, u32[]{:S(2)}, u32[]{:S(2)}) %collective-permute-start.7) | collective-permute-done | bytes 131104 | tf_op jit(solution)/shard_map/ppermute | solution.py:123
  37.3 3.1 %collective-permute-start.2 = (f32[2,1,64,1024]{3,2,1,0:T(8,128)}, f32[2,1,64,1024]{3,2,1,0:T(8,128)}, u32[]{:S(2)}, u32[]{:S(2)}) collective-permute-start(f32[2,1,64,1024]{3,2,1,0:T(8,128)} %get-tuple-element.25), channel_id=1, source_target_pairs={{0,4},{4,0},{8,12},{12,8},{1,5},{5,1},{9,13},{13,9},{2,6},{6,2},{1... | collective-permute-start | bytes 1572872 | tf_op jit(solution)/shard_map/ppermute | solution.py:30
  42.1 3.4 %collective-permute-start.12 = (bf16[128,1024]{1,0:T(8,128)(2,1)}, bf16[128,1024]{1,0:T(8,128)(2,1)}, u32[]{:S(2)}, u32[]{:S(2)}) collective-permute-start(bf16[128,1024]{1,0:T(8,128)(2,1)} %convolution_convert_fusion), channel_id=1, source_target_pairs={{0,12},{4,8},{8,4},{12,0},{1,13},{5,9},{9,5},{13,1},{2,14},{6,10},... | collective-permute-start | bytes 786440 | tf_op jit(solution)/shard_map/ppermute | solution.py:133
  48.6 1.8 %gather_fusion = bf16[4,128,1024]{2,1,0:T(8,128)(2,1)S(1)} fusion(bf16[4,128,1024]{2,1,0:T(8,128)(2,1)} %pad_maximum_fusion.3, s32[1024]{0:T(1024)S(1)} %pad_clamp_fusion.1), kind=kCustom, calls=%fused_computation | custom fusion | bytes 2097168 | tf_op jit(solution)/shard_map/jit(_take)/gather | solution.py:138
  50.4 2.1 %convolution_convert_fusion.2 = bf16[128,1024]{1,0:T(8,128)(2,1)} fusion(bf16[1024,1024]{1,0:T(8,128)(2,1)S(1)} %copy-done, bf16[64,1024]{1,0:T(8,128)(2,1)} %copy-done.27, bf16[64,1024]{1,0:T(8,128)(2,1)S(1)} %collective-permute-done.4, pred[]{:T(512)S(6)} %eq.9), kind=kOutput, calls=%fused_computation.27 | convolution fusion | flops 269746176 | bytes 2621441 | tf_op jit(solution)/shard_map/dot_general | solution.py:132
  55.9 1.3 pad_maximum_fusion.2
  58.2 6.1 %collective-permute-done.2 = f32[2,1,64,1024]{3,2,1,0:T(8,128)} collective-permute-done((f32[2,1,64,1024]{3,2,1,0:T(8,128)}, f32[2,1,64,1024]{3,2,1,0:T(8,128)}, u32[]{:S(2)}, u32[]{:S(2)}) %collective-permute-start.2) | collective-permute-done | bytes 524320 | tf_op jit(solution)/shard_map/ppermute | solution.py:30
  64.3 1.4 maximum_select_fusion
  74.1 9.3 %collective-permute-done.3 = bf16[2,1,64,1024]{3,2,1,0:T(8,128)(2,1)S(1)} collective-permute-done((bf16[2,1,64,1024]{3,2,1,0:T(8,128)(2,1)S(1)}, bf16[2,1,64,1024]{3,2,1,0:T(8,128)(2,1)S(1)}, u32[]{:S(2)}, u32[]{:S(2)}) %collective-permute-start.3) | collective-permute-done | bytes 262176 | tf_op jit(solution)/shard_map/ppermute | solution.py:30
  86.9 1.6 multiply_reduce_fusion
  88.6 2.2 %convolution_bitcast_fusion = f32[1,2,192,8,128]{4,2,3,1,0:T(8,128)} fusion(bf16[2,64,8,128]{3,2,1,0:T(8,128)(2,1)S(1)} %bitcast.269, f32[2,8,64,192]{3,2,1,0:T(8,128)S(1)} %get-tuple-element.27, f32[2,8,64]{2,1,0:T(8,128)S(1)} %copy_add_fusion.1, f32[2,8,64]{2,1,0:T(8,128)S(1)} %copy_maximum_fusion), kind=kOutput, calls=%fused_computation.10 | convolution fusion | flops 50921472 | bytes 2629632 | tf_op jit(solution)/shard_map/dbhqk,dbqhe->dbkhe/dot_general | solution.py:178
  98.8 3.3 %collective-permute-start.15 = (bf16[2,1,64,1024]{3,2,0,1:T(8,128)(2,1)}, bf16[2,1,64,1024]{3,2,0,1:T(8,128)(2,1)}, u32[]{:S(2)}, u32[]{:S(2)}) collective-permute-start(bf16[2,1,64,1024]{3,2,0,1:T(8,128)(2,1)} %bitcast.227), channel_id=1, source_target_pairs={{0,4},{4,0},{8,12},{12,8},{1,5},{5,1},{9,13},{13,9},{2,6},{6,2},{1... | collective-permute-start | bytes 786440 | tf_op jit(solution)/shard_map/ppermute | solution.py:210
  105.0 3.1 %pad_maximum_fusion = f32[1,2,2,3,64,1024]{5,0,4,3,2,1:T(1,128)S(1)} fusion(f32[1,1,2,3,64,1024]{5,0,4,3,2,1:T(1,128)S(1)} %bitcast.246, f32[1,1,2,3,64,1024]{5,0,4,3,2,1:T(1,128)S(1)} %bitcast.247), kind=kLoop, calls=%fused_computation.4 | loop fusion | flops 786432 | bytes 6291456 | tf_op jit(solution)/shard_map/stack | solution.py:188
  108.0 2.4 %copy.266 = f32[1,2,2,3,64,1024]{5,4,1,3,2,0:T(8,128)} copy(f32[1,2,2,3,64,1024]{5,0,4,3,2,1:T(1,128)S(1)} %pad_maximum_fusion) | data formatting | bytes 6291456 | tf_op jit(solution)/shard_map/stack | solution.py:188
  111.1 5.6 %scatter_fusion = f32[2,6,64,1024]{3,2,1,0:T(8,128)S(1)} fusion(f32[2,6,64,1024]{3,2,1,0:T(8,128)S(1)} %broadcast.288, s32[6]{0:T(128)S(1)} %copy-done.33, f32[6,2,64,1024]{3,2,1,0:T(8,128)} %bitcast.234), kind=kCustom, calls=%fused_computation.3 | custom fusion | flops 786432 | bytes 9437208 | tf_op jit(solution)/shard_map/vmap()/scatter-add | solution.py:46
  116.7 1.7 convolution_bitcast_fusion.1
  125.9 5.3 %collective-permute-start.13 = (bf16[2,1,128,1024]{3,2,1,0:T(8,128)(2,1)}, bf16[2,1,128,1024]{3,2,1,0:T(8,128)(2,1)}, u32[]{:S(2)}, u32[]{:S(2)}) collective-permute-start(bf16[2,1,128,1024]{3,2,1,0:T(8,128)(2,1)} %get-tuple-element.11), channel_id=1, source_target_pairs={{0,4},{4,8},{8,12},{1,5},{5,9},{9,13},{2,6},{6,10},{10,14},{3,7},{... | collective-permute-start | bytes 1572872 | tf_op jit(solution)/shard_map/ppermute | solution.py:20
  132.8 1.5 div.48
  135.7 1.7 div.44
  137.4 2.7 %pad_maximum_fusion.1 = bf16[2,512,1024]{2,1,0:T(8,128)(2,1)} fusion(bf16[1,512,1024]{2,1,0:T(8,128)(2,1)} %bitcast.93, bf16[1,512,1024]{2,1,0:T(8,128)(2,1)S(1)} %copy-done.6), kind=kLoop, calls=%fused_computation.6 | loop fusion | flops 1048576 | bytes 4194304 | tf_op jit(solution)/shard_map/stack | solution.py:143
  140.2 2.5 %gather_fusion.1 = bf16[2,512,1024]{2,1,0:T(8,128)(2,1)S(1)} fusion(bf16[2,512,1024]{2,1,0:T(8,128)(2,1)} %pad_maximum_fusion.1, s32[1024]{0:T(1024)} %pad_clamp_fusion), kind=kCustom, calls=%fused_computation.1 | custom fusion | bytes 4194312 | tf_op jit(solution)/shard_map/jit(_take)/gather | solution.py:142
  142.7 13.1 %collective-permute-done.14 = bf16[2,1,128,1024]{3,2,1,0:T(8,128)(2,1)} collective-permute-done((bf16[2,1,128,1024]{3,2,1,0:T(8,128)(2,1)}, bf16[2,1,128,1024]{3,2,1,0:T(8,128)(2,1)}, u32[]{:S(2)}, u32[]{:S(2)}) %collective-permute-start.14) | collective-permute-done | bytes 524320 | tf_op jit(solution)/shard_map/ppermute | solution.py:22
  155.8 2.6 %fusion.11 = bf16[2,1,128,1024]{3,2,1,0:T(8,128)(2,1)S(1)} fusion(f32[2,1,128,1024]{3,2,1,0:T(8,128)} %div.48, f32[2,1,128,1024]{3,2,1,0:T(8,128)} %div.44, f32[2,1,128,1024]{3,2,1,0:T(8,128)} %bitcast.255, bf16[2,1,128,1024]{3,2,1,0:T(8,128)(2,1)} %collective-permute-done.14, bf16[2,1,256,1024]{3,2,1,0:T(8,128)(2,1)S(1)} %bitcast.237, ...), kind=kLoop, calls=%fused_computation.33 | loop fusion | flops 4456448 | bytes 5767168 | tf_op jit(solution)/shard_map/convert.1
  159.2 1.7 bitcast_select_fusion
  160.9 6.8 %fusion.76 = f32[1024,1024]{1,0:T(8,128)} fusion(bf16[1024,1024]{1,0:T(8,128)(2,1)} %bitcast_select_fusion, bf16[1024,1024]{1,0:T(8,128)(2,1)} %all-gather.2.cloned.1.call-done), kind=kOutput, calls=%fused_computation.159 | convolution fusion | flops 2147483648 | bytes 8388608 | tf_op jit(solution)/shard_map/tc,tw->cw/dot_general | solution.py:150
  (189 shorter events, 53.4 us)
Async XLA Ops:
  7.2 20.1 %copy-start = (bf16[1024,1024]{1,0:T(8,128)(2,1)S(1)}, bf16[1024,1024]{1,0:T(8,128)(2,1)}, u32[]{:S(2)}) copy-start(bf16[1024,1024]{1,0:T(8,128)(2,1)} %param.10) | copy-start | bytes 6291460
  7.2 16.2 %copy-start.10 = (bf16[1,128,1024]{2,1,0:T(8,128)(2,1)S(1)}, bf16[1,128,1024]{2,1,0:T(8,128)(2,1)}, u32[]{:S(2)}) copy-start(bf16[1,128,1024]{2,1,0:T(8,128)(2,1)} %param.7) | copy-start | bytes 786436
  7.2 16.3 %copy-start.34 = (s32[1,2,2]{2,1,0:T(2,128)S(1)}, s32[1,2,2]{2,1,0:T(2,128)}, u32[]{:S(2)}) copy-start(s32[1,2,2]{2,1,0:T(2,128)} %param.9) | copy-start | bytes 52
  7.2 153.7 %all-gather.2.cloned.1.call-start = ((), (), s32[]{:S(2)}) async-start(), calls=%async_computation | async-start | bytes 2359296 | tf_op jit(solution)/shard_map/all_gather | solution.py:149
  9.3 45.6 %collective-permute-start.1 = (bf16[2,1,128,1024]{3,2,1,0:T(8,128)(2,1)}, bf16[2,1,128,1024]{3,2,1,0:T(8,128)(2,1)}, u32[]{:S(2)}, u32[]{:S(2)}) collective-permute-start(bf16[2,1,128,1024]{3,2,1,0:T(8,128)(2,1)} %pad_maximum_fusion.6), channel_id=1, source_target_pairs={{4,0},{8,4},{12,8},{5,1},{9,5},{13,9},{6,2},{10,6},{14,10},{7,3},{... | collective-permute-start | bytes 1572872 | tf_op jit(solution)/shard_map/ppermute | solution.py:22
  10.6 44.8 %collective-permute-start = (bf16[2,1,128,1024]{3,2,1,0:T(8,128)(2,1)}, bf16[2,1,128,1024]{3,2,1,0:T(8,128)(2,1)}, u32[]{:S(2)}, u32[]{:S(2)}) collective-permute-start(bf16[2,1,128,1024]{3,2,1,0:T(8,128)(2,1)} %pad_maximum_fusion.6), channel_id=1, source_target_pairs={{0,4},{4,8},{8,12},{1,5},{5,9},{9,13},{2,6},{6,10},{10,14},{3,7},{... | collective-permute-start | bytes 1572872 | tf_op jit(solution)/shard_map/ppermute | solution.py:20
  17.9 13.2 %collective-permute-start.10 = (bf16[64,1024]{1,0:T(8,128)(2,1)S(1)}, bf16[64,1024]{1,0:T(8,128)(2,1)S(1)}, u32[]{:S(2)}, u32[]{:S(2)}) collective-permute-start(bf16[64,1024]{1,0:T(8,128)(2,1)S(1)} %get-tuple-element.16), channel_id=1, source_target_pairs={{0,12},{4,8},{8,4},{12,0},{1,13},{5,9},{9,5},{13,1},{2,14},{6,10},... | collective-permute-start | bytes 393224 | tf_op jit(solution)/shard_map/ppermute | solution.py:123
  19.4 17.9 %collective-permute-start.7 = (bf16[64,1024]{1,0:T(8,128)(2,1)}, bf16[64,1024]{1,0:T(8,128)(2,1)S(1)}, u32[]{:S(2)}, u32[]{:S(2)}) collective-permute-start(bf16[64,1024]{1,0:T(8,128)(2,1)} %get-tuple-element.17), channel_id=1, source_target_pairs={{0,8},{4,12},{8,0},{12,4},{1,9},{5,13},{9,1},{13,5},{2,10},{6,14},... | collective-permute-start | bytes 393224 | tf_op jit(solution)/shard_map/ppermute | solution.py:123
  20.5 19.9 %collective-permute-start.4 = (bf16[64,1024]{1,0:T(8,128)(2,1)}, bf16[64,1024]{1,0:T(8,128)(2,1)S(1)}, u32[]{:S(2)}, u32[]{:S(2)}) collective-permute-start(bf16[64,1024]{1,0:T(8,128)(2,1)} %get-tuple-element.15), channel_id=1, source_target_pairs={{0,4},{4,0},{8,12},{12,8},{1,5},{5,1},{9,13},{13,9},{2,6},{6,2},{1... | collective-permute-start | bytes 393224 | tf_op jit(solution)/shard_map/ppermute | solution.py:123
  26.2 5.1 %copy-start.26 = (bf16[1,128,1024]{2,1,0:T(8,128)(2,1)S(1)}, bf16[1,128,1024]{2,1,0:T(8,128)(2,1)}, u32[]{:S(2)}) copy-start(bf16[1,128,1024]{2,1,0:T(8,128)(2,1)} %param.6) | copy-start | bytes 786436
  31.1 9.5 %collective-permute-start.11 = (bf16[64,1024]{1,0:T(8,128)(2,1)S(1)}, bf16[64,1024]{1,0:T(8,128)(2,1)S(1)}, u32[]{:S(2)}, u32[]{:S(2)}) collective-permute-start(bf16[64,1024]{1,0:T(8,128)(2,1)S(1)} %collective-permute-done.10), channel_id=1, source_target_pairs={{0,1},{1,0},{2,3},{3,2},{4,5},{5,4},{6,7},{7,6},{8,9},{9,8},{10,11... | collective-permute-start | bytes 393224 | tf_op jit(solution)/shard_map/ppermute | solution.py:30
  37.3 27.0 %collective-permute-start.2 = (f32[2,1,64,1024]{3,2,1,0:T(8,128)}, f32[2,1,64,1024]{3,2,1,0:T(8,128)}, u32[]{:S(2)}, u32[]{:S(2)}) collective-permute-start(f32[2,1,64,1024]{3,2,1,0:T(8,128)} %get-tuple-element.25), channel_id=1, source_target_pairs={{0,4},{4,0},{8,12},{12,8},{1,5},{5,1},{9,13},{13,9},{2,6},{6,2},{1... | collective-permute-start | bytes 1572872 | tf_op jit(solution)/shard_map/ppermute | solution.py:30
  40.4 1.7 collective-permute-start.8
  40.7 6.1 %collective-permute-start.5 = (bf16[64,1024]{1,0:T(8,128)(2,1)S(1)}, bf16[64,1024]{1,0:T(8,128)(2,1)S(1)}, u32[]{:S(2)}, u32[]{:S(2)}) collective-permute-start(bf16[64,1024]{1,0:T(8,128)(2,1)S(1)} %collective-permute-done.4), channel_id=1, source_target_pairs={{0,1},{1,0},{2,3},{3,2},{4,5},{5,4},{6,7},{7,6},{8,9},{9,8},{10,11... | collective-permute-start | bytes 393224 | tf_op jit(solution)/shard_map/ppermute | solution.py:30
  42.1 26.8 %collective-permute-start.12 = (bf16[128,1024]{1,0:T(8,128)(2,1)}, bf16[128,1024]{1,0:T(8,128)(2,1)}, u32[]{:S(2)}, u32[]{:S(2)}) collective-permute-start(bf16[128,1024]{1,0:T(8,128)(2,1)} %convolution_convert_fusion), channel_id=1, source_target_pairs={{0,12},{4,8},{8,4},{12,0},{1,13},{5,9},{9,5},{13,1},{2,14},{6,10},... | collective-permute-start | bytes 786440 | tf_op jit(solution)/shard_map/ppermute | solution.py:133
  46.8 22.2 %collective-permute-start.9 = (bf16[128,1024]{1,0:T(8,128)(2,1)}, bf16[128,1024]{1,0:T(8,128)(2,1)}, u32[]{:S(2)}, u32[]{:S(2)}) collective-permute-start(bf16[128,1024]{1,0:T(8,128)(2,1)} %convolution_convert_fusion.1), channel_id=1, source_target_pairs={{0,8},{4,12},{8,0},{12,4},{1,9},{5,13},{9,1},{13,5},{2,10},{6,14},... | collective-permute-start | bytes 786440 | tf_op jit(solution)/shard_map/ppermute | solution.py:133
  54.9 15.3 %collective-permute-start.6 = (bf16[128,1024]{1,0:T(8,128)(2,1)}, bf16[128,1024]{1,0:T(8,128)(2,1)}, u32[]{:S(2)}, u32[]{:S(2)}) collective-permute-start(bf16[128,1024]{1,0:T(8,128)(2,1)} %convolution_convert_fusion.2), channel_id=1, source_target_pairs={{0,4},{4,0},{8,12},{12,8},{1,5},{5,1},{9,13},{13,9},{2,6},{6,2},{1... | collective-permute-start | bytes 786440 | tf_op jit(solution)/shard_map/ppermute | solution.py:133
  55.3 82.1 %collective-permute-start.18 = (bf16[512,1024]{1,0:T(8,128)(2,1)}, bf16[512,1024]{1,0:T(8,128)(2,1)}, u32[]{:S(2)}, u32[]{:S(2)}) collective-permute-start(bf16[512,1024]{1,0:T(8,128)(2,1)} %bitcast_select_fusion.1), channel_id=1, source_target_pairs={{0,2},{2,0},{1,3},{3,1},{4,6},{6,4},{5,7},{7,5},{8,10},{10,8},{9,1... | collective-permute-start | bytes 3145736 | tf_op jit(solution)/shard_map/ppermute | solution.py:30
  58.0 6.2 %copy-start.16 = (f32[2,1,64,1024]{3,2,0,1:T(8,128)S(1)}, f32[2,1,64,1024]{3,2,0,1:T(8,128)}, u32[]{:S(2)}) copy-start(f32[2,1,64,1024]{3,2,0,1:T(8,128)} %get-tuple-element.24) | copy-start | bytes 1572868
  66.9 17.7 %copy-start.4 = (bf16[48,8,8,128]{3,2,1,0:T(8,128)(2,1)}, bf16[48,8,8,128]{3,2,1,0:T(8,128)(2,1)S(1)}, u32[]{:S(2)}) copy-start(bf16[48,8,8,128]{3,2,1,0:T(8,128)(2,1)S(1)} %copy.267) | copy-start | bytes 2359300
  68.8 14.5 %collective-permute-start.3 = (bf16[2,1,64,1024]{3,2,1,0:T(8,128)(2,1)S(1)}, bf16[2,1,64,1024]{3,2,1,0:T(8,128)(2,1)S(1)}, u32[]{:S(2)}, u32[]{:S(2)}) collective-permute-start(bf16[2,1,64,1024]{3,2,1,0:T(8,128)(2,1)S(1)} %fusion.21), channel_id=1, source_target_pairs={{0,8},{4,12},{8,0},{12,4},{1,9},{5,13},{9,1},{13,5},{2,10},{6,14},... | collective-permute-start | bytes 786440 | tf_op jit(solution)/shard_map/ppermute | solution.py:30
  72.3 12.1 %copy-start.21 = (bf16[2,64,8,128]{3,1,0,2:T(8,128)(2,1)S(1)}, bf16[2,64,8,128]{3,1,0,2:T(8,128)(2,1)}, u32[]{:S(2)}) copy-start(bf16[2,64,8,128]{3,1,0,2:T(8,128)(2,1)} %copy.213) | copy-start | bytes 786436
  95.7 30.3 %collective-permute-start.17 = (bf16[2,1,32,1024]{3,0,2,1:T(2,128)(2,1)}, bf16[2,1,32,1024]{3,0,2,1:T(2,128)(2,1)}, u32[]{:S(2)}, u32[]{:S(2)}) collective-permute-start(bf16[2,1,32,1024]{3,0,2,1:T(2,128)(2,1)} %get-tuple-element.14), channel_id=1, source_target_pairs={{0,12},{4,8},{8,4},{12,0},{1,13},{5,9},{9,5},{13,1},{2,14},{6,10},... | collective-permute-start | bytes 393224 | tf_op jit(solution)/shard_map/ppermute | solution.py:210
  96.7 34.5 %collective-permute-start.16 = (bf16[2,1,32,1024]{3,0,2,1:T(2,128)(2,1)S(1)}, bf16[2,1,32,1024]{3,0,2,1:T(2,128)(2,1)}, u32[]{:S(2)}, u32[]{:S(2)}) collective-permute-start(bf16[2,1,32,1024]{3,0,2,1:T(2,128)(2,1)S(1)} %get-tuple-element.13), channel_id=1, source_target_pairs={{0,8},{4,12},{8,0},{12,4},{1,9},{5,13},{9,1},{13,5},{2,10},{6,14},... | collective-permute-start | bytes 393224 | tf_op jit(solution)/shard_map/ppermute | solution.py:210
  98.0 5.0 %copy-start.20 = (f32[2,8,64,192]{3,2,1,0:T(8,128)S(1)}, f32[2,8,64,192]{3,2,1,0:T(8,128)}, u32[]{:S(2)}) copy-start(f32[2,8,64,192]{3,2,1,0:T(8,128)} %get-tuple-element.29) | copy-start | bytes 2359300
  98.0 5.0 %copy-start.29 = (f32[2,8,64]{2,1,0:T(8,128)S(1)}, f32[2,8,64]{2,1,0:T(8,128)}, u32[]{:S(2)}) copy-start(f32[2,8,64]{2,1,0:T(8,128)} %copy-done.28) | copy-start | bytes 12292
  98.0 5.0 %copy-start.31 = (f32[2,8,64]{2,1,0:T(8,128)S(1)}, f32[2,8,64]{2,1,0:T(8,128)}, u32[]{:S(2)}) copy-start(f32[2,8,64]{2,1,0:T(8,128)} %copy-done.30) | copy-start | bytes 12292
  98.8 35.4 %collective-permute-start.15 = (bf16[2,1,64,1024]{3,2,0,1:T(8,128)(2,1)}, bf16[2,1,64,1024]{3,2,0,1:T(8,128)(2,1)}, u32[]{:S(2)}, u32[]{:S(2)}) collective-permute-start(bf16[2,1,64,1024]{3,2,0,1:T(8,128)(2,1)} %bitcast.227), channel_id=1, source_target_pairs={{0,4},{4,0},{8,12},{12,8},{1,5},{5,1},{9,13},{13,9},{2,6},{6,2},{1... | collective-permute-start | bytes 786440 | tf_op jit(solution)/shard_map/ppermute | solution.py:210
  124.6 31.2 %collective-permute-start.14 = (bf16[2,1,128,1024]{3,2,1,0:T(8,128)(2,1)}, bf16[2,1,128,1024]{3,2,1,0:T(8,128)(2,1)}, u32[]{:S(2)}, u32[]{:S(2)}) collective-permute-start(bf16[2,1,128,1024]{3,2,1,0:T(8,128)(2,1)} %get-tuple-element.12), channel_id=1, source_target_pairs={{4,0},{8,4},{12,8},{5,1},{9,5},{13,9},{6,2},{10,6},{14,10},{7,3},{... | collective-permute-start | bytes 1572872 | tf_op jit(solution)/shard_map/ppermute | solution.py:22
  125.9 29.9 %collective-permute-start.13 = (bf16[2,1,128,1024]{3,2,1,0:T(8,128)(2,1)}, bf16[2,1,128,1024]{3,2,1,0:T(8,128)(2,1)}, u32[]{:S(2)}, u32[]{:S(2)}) collective-permute-start(bf16[2,1,128,1024]{3,2,1,0:T(8,128)(2,1)} %get-tuple-element.11), channel_id=1, source_target_pairs={{0,4},{4,8},{8,12},{1,5},{5,9},{9,13},{2,6},{6,10},{10,14},{3,7},{... | collective-permute-start | bytes 1572872 | tf_op jit(solution)/shard_map/ppermute | solution.py:20
  140.2 15.6 %copy-start.3 = (bf16[2,1,4,64,1024]{4,3,2,0,1:T(8,128)(2,1)S(1)}, bf16[2,1,4,64,1024]{4,3,2,0,1:T(8,128)(2,1)}, u32[]{:S(2)}) copy-start(bf16[2,1,4,64,1024]{4,3,2,0,1:T(8,128)(2,1)} %copy-done.2) | copy-start | bytes 3145732
  160.9 6.8 %copy-start.1 = (bf16[1024,1024]{1,0:T(8,128)(2,1)S(1)}, bf16[1024,1024]{1,0:T(8,128)(2,1)}, u32[]{:S(2)}) copy-start(bf16[1024,1024]{1,0:T(8,128)(2,1)} %param.10) | copy-start | bytes 6291460
  (23 other events, 52.0 us)
Sparse Core Ops, SparseCore 0:
  97.6 57.0 all-gather.1

commit v21 on v10

--- a/solution.py
+++ b/solution.py
@@ -124,10 +124,11 @@
             lax.dynamic_slice_in_dim(sent, core * half, half, axis=0), "seq", pairs
         )
         other_half = swapped(got_half, "head", 0)
-        got = jnp.where(
-            core == 0,
-            jnp.concatenate([got_half, other_half], axis=0),
-            jnp.concatenate([other_half, got_half], axis=0),
+        got = lax.dynamic_update_slice_in_dim(
+            lax.dynamic_update_slice_in_dim(jnp.zeros_like(sent), got_half, core * half, axis=0),
+            other_half,
+            (1 - core) * half,
+            axis=0,
         )
         part = jnp.dot(got, out_weight, preferred_element_type=jnp.float32)
         back = lax.ppermute(part.astype(jnp.bfloat16), "seq", pairs)

time: 172 us -> 173 us (level)
  the two profiles are of different devices: /device:TPU:30 before, /device:TPU:6 now
where the time goes in v21:
time: 173 us; the launch traced here: 170 us
  waiting for transfers between devices  38.4 us (22%)
  local copies, waits for them, and re-layouts  37.6 us (22%)
  other arithmetic  30.3 us (18%)
  starting transfers between devices  29.4 us (17%)
  matrix products  19.8 us (11%)
  between operations  14.7 us (8%)
    ppermute x3, waiting for transfers between devices, shards(): lax.ppermute(lax.dynamic_slice_in_dim(sent, core * half, half, axis=0), '...  16 us
    ppermute x2, waiting for transfers between devices, extended(): lax.ppermute(head, axis, [((i + 1) % count, i) for i in range(ends)])  13.3 us
    ppermute x2, starting transfers between devices, extended(): lax.ppermute(tail, axis, [(i, (i + 1) % count) for i in range(ends)])  10.7 us
    ppermute x3, waiting for transfers between devices, shards(): back = lax.ppermute(part.astype(jnp.bfloat16), 'seq', pairs)  8.02 us
    dot_general x1, matrix products, shards(): jnp.einsum('tc,tw->cw', feat_docs, whole_output, preferred_element_type=j...  6.77 us
    scatter-add x1, other arithmetic, place_blocks(): return holder.at[:, chosen_doc].add(grad_doc)  5.37 us
    unnamed x61, local copies, waits for them, and re-layouts  4.75 us
    ppermute x3, starting transfers between devices, shards(): back = lax.ppermute(part.astype(jnp.bfloat16), 'seq', pairs)  4.45 us
  transfers between devices with their start and end apart: 20, of which 6 were waited for; matrix products, arithmetic and copies ran while one was open for 45% of the time, Pallas kernels for 0%

profile of v21, /device:TPU:6, one launch (start us, length us, event | category | flops | bytes accessed | tf_op | source)
XLA Modules:
  0.0 170.2 jit_solution(4400657463081127013)
XLA Ops:
  7.2 2.0 %pad_maximum_fusion.5 = bf16[2,1,128,1024]{3,2,1,0:T(8,128)(2,1)} fusion(bf16[1,1,128,1024]{3,2,1,0:T(8,128)(2,1)} %bitcast.249, bf16[1,1,128,1024]{3,2,1,0:T(8,128)(2,1)} %bitcast.251), kind=kLoop, calls=%fused_computation.50 | loop fusion | flops 262144 | bytes 1048576 | tf_op jit(solution)/shard_map/stack | solution.py:58
  9.3 1.3 collective-permute-start.1
  10.5 5.4 %collective-permute-start = (bf16[2,1,128,1024]{3,2,1,0:T(8,128)(2,1)}, bf16[2,1,128,1024]{3,2,1,0:T(8,128)(2,1)}, u32[]{:S(2)}, u32[]{:S(2)}) collective-permute-start(bf16[2,1,128,1024]{3,2,1,0:T(8,128)(2,1)} %pad_maximum_fusion.5), channel_id=1, source_target_pairs={{0,4},{4,8},{8,12},{1,5},{5,9},{9,13},{2,6},{6,10},{10,14},{3,7},{... | collective-permute-start | bytes 1572872 | tf_op jit(solution)/shard_map/ppermute | solution.py:20
  18.0 1.4 convert_reduce_fusion
  21.1 2.1 %dynamic-slice_bitcast_fusion.2 = (bf16[64,1024]{1,0:T(8,128)(2,1)}, bf16[64,1024]{1,0:T(8,128)(2,1)}, bf16[64,1024]{1,0:T(8,128)(2,1)}) fusion(bf16[1,128,4096]{2,1,0:T(8,128)(2,1)} %param.11, s32[]{:T(128)S(6)} %select_n.102, s32[]{:T(128)S(6)} %select_n.104, s32[]{:T(128)S(6)} %select_n.109, s32[]{:T(128)S(6)} %select_n.107), kind=kLoop, calls=%fused_computation.97 | loop fusion | bytes 786448 | tf_op jit(solution)/shard_map/dynamic_slice | solution.py:124
  23.2 3.3 %collective-permute-start.10 = (bf16[64,1024]{1,0:T(8,128)(2,1)}, bf16[64,1024]{1,0:T(8,128)(2,1)}, u32[]{:S(2)}, u32[]{:S(2)}) collective-permute-start(bf16[64,1024]{1,0:T(8,128)(2,1)} %get-tuple-element.16), channel_id=1, source_target_pairs={{0,12},{4,8},{8,4},{12,0},{1,13},{5,9},{9,5},{13,1},{2,14},{6,10},... | collective-permute-start | bytes 393224 | tf_op jit(solution)/shard_map/ppermute | solution.py:123
  30.5 11.9 %collective-permute-done.10 = bf16[64,1024]{1,0:T(8,128)(2,1)} collective-permute-done((bf16[64,1024]{1,0:T(8,128)(2,1)}, bf16[64,1024]{1,0:T(8,128)(2,1)}, u32[]{:S(2)}, u32[]{:S(2)}) %collective-permute-start.10) | collective-permute-done | bytes 131104 | tf_op jit(solution)/shard_map/ppermute | solution.py:123
  43.3 1.3 collective-permute-done.7
  44.6 2.9 %collective-permute-done.4 = bf16[64,1024]{1,0:T(8,128)(2,1)S(1)} collective-permute-done((bf16[64,1024]{1,0:T(8,128)(2,1)}, bf16[64,1024]{1,0:T(8,128)(2,1)S(1)}, u32[]{:S(2)}, u32[]{:S(2)}) %collective-permute-start.4) | collective-permute-done | bytes 131104 | tf_op jit(solution)/shard_map/ppermute | solution.py:123
  49.3 3.8 %collective-permute-start.12 = (bf16[128,1024]{1,0:T(8,128)(2,1)}, bf16[128,1024]{1,0:T(8,128)(2,1)}, u32[]{:S(2)}, u32[]{:S(2)}) collective-permute-start(bf16[128,1024]{1,0:T(8,128)(2,1)} %convolution_convert_fusion), channel_id=1, source_target_pairs={{0,12},{4,8},{8,4},{12,0},{1,13},{5,9},{9,5},{13,1},{2,14},{6,10},... | collective-permute-start | bytes 786440 | tf_op jit(solution)/shard_map/ppermute | solution.py:134
  55.4 2.8 %gather_fusion = bf16[4,128,1024]{2,1,0:T(8,128)(2,1)} fusion(bf16[4,128,1024]{2,1,0:T(8,128)(2,1)} %pad_maximum_fusion.2, s32[1024]{0:T(1024)S(1)} %pad_clamp_fusion), kind=kCustom, calls=%fused_computation | custom fusion | bytes 2097168 | tf_op jit(solution)/shard_map/jit(_take)/gather | solution.py:139
  61.6 1.3 pad_maximum_fusion.1
  63.0 1.8 %gather_fusion.1 = bf16[6,2,64,1024]{3,2,1,0:T(8,128)(2,1)} fusion(bf16[1,2,6,64,1024]{4,3,2,1,0:T(8,128)(2,1)S(1)} %bitcast.235, s32[6]{0:T(128)S(1)} %reshape.611), kind=kCustom, calls=%fused_computation.1 | custom fusion | bytes 3145776 | tf_op jit(solution)/shard_map/vmap()/gather | solution.py:41
  64.8 1.6 copy.202
  66.5 1.4 maximum_select_fusion
  71.1 2.4 %collective-permute-start.3 = (bf16[2,1,64,1024]{3,2,1,0:T(8,128)(2,1)S(1)}, bf16[2,1,64,1024]{3,2,1,0:T(8,128)(2,1)S(1)}, u32[]{:S(2)}, u32[]{:S(2)}) collective-permute-start(bf16[2,1,64,1024]{3,2,1,0:T(8,128)(2,1)S(1)} %fusion.21), channel_id=1, source_target_pairs={{0,8},{4,12},{8,0},{12,4},{1,9},{5,13},{9,1},{13,5},{2,10},{6,14},... | collective-permute-start | bytes 786440 | tf_op jit(solution)/shard_map/ppermute | solution.py:30
  73.5 8.0 %collective-permute-done.9 = bf16[128,1024]{1,0:T(8,128)(2,1)} collective-permute-done((bf16[128,1024]{1,0:T(8,128)(2,1)}, bf16[128,1024]{1,0:T(8,128)(2,1)}, u32[]{:S(2)}, u32[]{:S(2)}) %collective-permute-start.9) | collective-permute-done | bytes 262176 | tf_op jit(solution)/shard_map/ppermute | solution.py:134
  89.3 1.6 multiply_reduce_fusion
  94.5 1.3 copy.245
  98.3 2.6 %collective-permute-start.17 = (bf16[2,1,32,1024]{3,0,2,1:T(2,128)(2,1)}, bf16[2,1,32,1024]{3,0,2,1:T(2,128)(2,1)}, u32[]{:S(2)}, u32[]{:S(2)}) collective-permute-start(bf16[2,1,32,1024]{3,0,2,1:T(2,128)(2,1)} %get-tuple-element.14), channel_id=1, source_target_pairs={{0,12},{4,8},{8,4},{12,0},{1,13},{5,9},{9,5},{13,1},{2,14},{6,10},... | collective-permute-start | bytes 393224 | tf_op jit(solution)/shard_map/ppermute | solution.py:204
  102.2 1.7 %collective-permute-start.15 = (bf16[2,1,64,1024]{3,2,0,1:T(8,128)(2,1)}, bf16[2,1,64,1024]{3,2,0,1:T(8,128)(2,1)}, u32[]{:S(2)}, u32[]{:S(2)}) collective-permute-start(bf16[2,1,64,1024]{3,2,0,1:T(8,128)(2,1)} %bitcast.220), channel_id=1, source_target_pairs={{0,4},{4,0},{8,12},{12,8},{1,5},{5,1},{9,13},{13,9},{2,6},{6,2},{1... | collective-permute-start | bytes 786440 | tf_op jit(solution)/shard_map/ppermute | solution.py:204
  108.3 3.1 %pad_maximum_fusion = f32[1,2,2,3,64,1024]{5,0,4,3,2,1:T(1,128)S(1)} fusion(f32[1,1,2,3,64,1024]{5,0,4,3,2,1:T(1,128)S(1)} %bitcast.237, f32[1,1,2,3,64,1024]{5,0,4,3,2,1:T(1,128)S(1)} %bitcast.238), kind=kLoop, calls=%fused_computation.3 | loop fusion | flops 786432 | bytes 6291456 | tf_op jit(solution)/shard_map/stack | solution.py:182
  111.3 2.4 %copy.266 = f32[1,2,2,3,64,1024]{5,4,1,3,2,0:T(8,128)} copy(f32[1,2,2,3,64,1024]{5,0,4,3,2,1:T(1,128)S(1)} %pad_maximum_fusion) | data formatting | bytes 6291456 | tf_op jit(solution)/shard_map/stack | solution.py:182
  114.3 5.4 %scatter_fusion = f32[2,6,64,1024]{3,2,1,0:T(8,128)S(1)} fusion(f32[2,6,64,1024]{3,2,1,0:T(8,128)S(1)} %broadcast.206, s32[6]{0:T(128)S(1)} %copy-done.26, f32[6,2,64,1024]{3,2,1,0:T(8,128)} %bitcast.226), kind=kCustom, calls=%fused_computation.2 | custom fusion | flops 786432 | bytes 9437208 | tf_op jit(solution)/shard_map/vmap()/scatter-add | solution.py:46
  122.1 1.3 collective-permute-start.14
  123.4 5.3 %collective-permute-start.13 = (bf16[2,1,128,1024]{3,2,1,0:T(8,128)(2,1)}, bf16[2,1,128,1024]{3,2,1,0:T(8,128)(2,1)}, u32[]{:S(2)}, u32[]{:S(2)}) collective-permute-start(bf16[2,1,128,1024]{3,2,1,0:T(8,128)(2,1)} %get-tuple-element.11), channel_id=1, source_target_pairs={{0,4},{4,8},{8,12},{1,5},{5,9},{9,13},{2,6},{6,10},{10,14},{3,7},{... | collective-permute-start | bytes 1572872 | tf_op jit(solution)/shard_map/ppermute | solution.py:20
  130.2 1.8 %convert_element_type.198 = bf16[1,128,1024]{2,1,0:T(8,128)(2,1)} reshape(bf16[1,2,64,8,128]{4,3,2,1,0:T(8,128)(2,1)} %copy-done.14) | data formatting | bytes 524288 | tf_op jit(solution)/shard_map/convert_element_type | solution.py:109
  135.5 1.3 div.48
  138.4 1.8 %div.44 = f32[2,1,128,1024]{3,2,1,0:T(8,128)} reshape(f32[2,64,2,1024]{3,2,1,0:T(2,128)S(1)} %broadcast_in_dim.33) | data formatting | bytes 2097152 | tf_op jit(solution)/shard_map/div | solution.py:209
  140.2 13.3 %collective-permute-done.14 = bf16[2,1,128,1024]{3,2,1,0:T(8,128)(2,1)} collective-permute-done((bf16[2,1,128,1024]{3,2,1,0:T(8,128)(2,1)}, bf16[2,1,128,1024]{3,2,1,0:T(8,128)(2,1)}, u32[]{:S(2)}, u32[]{:S(2)}) %collective-permute-start.14) | collective-permute-done | bytes 524320 | tf_op jit(solution)/shard_map/ppermute | solution.py:22
  153.5 2.3 %fusion.11 = bf16[2,1,128,1024]{3,2,1,0:T(8,128)(2,1)S(1)} fusion(f32[2,1,128,1024]{3,2,1,0:T(8,128)} %div.48, f32[2,1,128,1024]{3,2,1,0:T(8,128)} %div.44, f32[2,1,128,1024]{3,2,1,0:T(8,128)S(1)} %bitcast.246, bf16[2,1,128,1024]{3,2,1,0:T(8,128)(2,1)} %collective-permute-done.14, bf16[2,1,256,1024]{3,2,1,0:T(8,128)(2,1)S(1)} %bitcast.228, ...), kind=kLoop, calls=%fused_computation.30 | loop fusion | flops 4456448 | bytes 5767168 | tf_op jit(solution)/shard_map/convert.1
  156.6 6.8 %fusion.54 = f32[1024,1024]{1,0:T(8,128)} fusion(bf16[1024,1024]{1,0:T(8,128)(2,1)} %all-gather.3.cloned.1.call-done, bf16[1024,1024]{1,0:T(8,128)(2,1)} %all-gather.5.cloned.1.call-done), kind=kOutput, calls=%fused_computation.129 | convolution fusion | flops 2147483648 | bytes 8388608 | tf_op jit(solution)/shard_map/tc,tw->cw/dot_general | solution.py:144
  (173 shorter events, 49.0 us)
Async XLA Ops:
  7.2 20.5 %copy-start = (bf16[1024,1024]{1,0:T(8,128)(2,1)S(1)}, bf16[1024,1024]{1,0:T(8,128)(2,1)}, u32[]{:S(2)}) copy-start(bf16[1024,1024]{1,0:T(8,128)(2,1)} %param.10) | copy-start | bytes 6291460
  7.2 149.4 %all-gather.3.cloned.1.call-start = ((), (), s32[]{:S(2)}) async-start(), calls=%async_computation | async-start | bytes 3145728 | tf_op jit(solution)/shard_map/all_gather | solution.py:142
  9.3 51.7 %collective-permute-start.1 = (bf16[2,1,128,1024]{3,2,1,0:T(8,128)(2,1)}, bf16[2,1,128,1024]{3,2,1,0:T(8,128)(2,1)}, u32[]{:S(2)}, u32[]{:S(2)}) collective-permute-start(bf16[2,1,128,1024]{3,2,1,0:T(8,128)(2,1)} %pad_maximum_fusion.5), channel_id=1, source_target_pairs={{4,0},{8,4},{12,8},{5,1},{9,5},{13,9},{6,2},{10,6},{14,10},{7,3},{... | collective-permute-start | bytes 1572872 | tf_op jit(solution)/shard_map/ppermute | solution.py:22
  10.5 51.1 %collective-permute-start = (bf16[2,1,128,1024]{3,2,1,0:T(8,128)(2,1)}, bf16[2,1,128,1024]{3,2,1,0:T(8,128)(2,1)}, u32[]{:S(2)}, u32[]{:S(2)}) collective-permute-start(bf16[2,1,128,1024]{3,2,1,0:T(8,128)(2,1)} %pad_maximum_fusion.5), channel_id=1, source_target_pairs={{0,4},{4,8},{8,12},{1,5},{5,9},{9,13},{2,6},{6,10},{10,14},{3,7},{... | collective-permute-start | bytes 1572872 | tf_op jit(solution)/shard_map/ppermute | solution.py:20
  17.0 9.5 %copy-start.27 = (s32[1,2,2]{2,1,0:T(2,128)S(1)}, s32[1,2,2]{2,1,0:T(2,128)}, u32[]{:S(2)}) copy-start(s32[1,2,2]{2,1,0:T(2,128)} %param.9) | copy-start | bytes 52
  20.4 46.1 %collective-permute-start.2 = (f32[2,1,64,1024]{3,2,1,0:T(8,128)}, f32[2,1,64,1024]{3,2,1,0:T(8,128)}, u32[]{:S(2)}, u32[]{:S(2)}) collective-permute-start(f32[2,1,64,1024]{3,2,1,0:T(8,128)} %get-tuple-element.25), channel_id=1, source_target_pairs={{0,4},{4,0},{8,12},{12,8},{1,5},{5,1},{9,13},{13,9},{2,6},{6,2},{1... | collective-permute-start | bytes 1572872 | tf_op jit(solution)/shard_map/ppermute | solution.py:30
  21.1 7.9 %copy-start.21 = (bf16[1,128,1024]{2,1,0:T(8,128)(2,1)S(1)}, bf16[1,128,1024]{2,1,0:T(8,128)(2,1)}, u32[]{:S(2)}) copy-start(bf16[1,128,1024]{2,1,0:T(8,128)(2,1)} %param.6) | copy-start | bytes 786436
  23.2 19.1 %collective-permute-start.10 = (bf16[64,1024]{1,0:T(8,128)(2,1)}, bf16[64,1024]{1,0:T(8,128)(2,1)}, u32[]{:S(2)}, u32[]{:S(2)}) collective-permute-start(bf16[64,1024]{1,0:T(8,128)(2,1)} %get-tuple-element.16), channel_id=1, source_target_pairs={{0,12},{4,8},{8,4},{12,0},{1,13},{5,9},{9,5},{13,1},{2,14},{6,10},... | collective-permute-start | bytes 393224 | tf_op jit(solution)/shard_map/ppermute | solution.py:123
  26.5 18.1 %collective-permute-start.7 = (bf16[64,1024]{1,0:T(8,128)(2,1)}, bf16[64,1024]{1,0:T(8,128)(2,1)S(1)}, u32[]{:S(2)}, u32[]{:S(2)}) collective-permute-start(bf16[64,1024]{1,0:T(8,128)(2,1)} %get-tuple-element.17), channel_id=1, source_target_pairs={{0,8},{4,12},{8,0},{12,4},{1,9},{5,13},{9,1},{13,5},{2,10},{6,14},... | collective-permute-start | bytes 393224 | tf_op jit(solution)/shard_map/ppermute | solution.py:123
  42.3 5.2 %collective-permute-start.4 = (bf16[64,1024]{1,0:T(8,128)(2,1)}, bf16[64,1024]{1,0:T(8,128)(2,1)S(1)}, u32[]{:S(2)}, u32[]{:S(2)}) collective-permute-start(bf16[64,1024]{1,0:T(8,128)(2,1)} %get-tuple-element.15), channel_id=1, source_target_pairs={{0,4},{4,0},{8,12},{12,8},{1,5},{5,1},{9,13},{13,9},{2,6},{6,2},{1... | collective-permute-start | bytes 393224 | tf_op jit(solution)/shard_map/ppermute | solution.py:123
  44.6 3.0 %collective-permute-start.11 = (bf16[64,1024]{1,0:T(8,128)(2,1)}, bf16[64,1024]{1,0:T(8,128)(2,1)S(1)}, u32[]{:S(2)}, u32[]{:S(2)}) collective-permute-start(bf16[64,1024]{1,0:T(8,128)(2,1)} %collective-permute-done.10), channel_id=1, source_target_pairs={{0,1},{1,0},{2,3},{3,2},{4,5},{5,4},{6,7},{7,6},{8,9},{9,8},{10,11... | collective-permute-start | bytes 393224 | tf_op jit(solution)/shard_map/ppermute | solution.py:30
  47.5 1.8 %collective-permute-start.8 = (bf16[64,1024]{1,0:T(8,128)(2,1)S(1)}, bf16[64,1024]{1,0:T(8,128)(2,1)S(1)}, u32[]{:S(2)}, u32[]{:S(2)}) collective-permute-start(bf16[64,1024]{1,0:T(8,128)(2,1)S(1)} %collective-permute-done.7), channel_id=1, source_target_pairs={{0,1},{1,0},{2,3},{3,2},{4,5},{5,4},{6,7},{7,6},{8,9},{9,8},{10,11... | collective-permute-start | bytes 393224 | tf_op jit(solution)/shard_map/ppermute | solution.py:30
  47.6 6.7 %collective-permute-start.5 = (bf16[64,1024]{1,0:T(8,128)(2,1)S(1)}, bf16[64,1024]{1,0:T(8,128)(2,1)S(1)}, u32[]{:S(2)}, u32[]{:S(2)}) collective-permute-start(bf16[64,1024]{1,0:T(8,128)(2,1)S(1)} %collective-permute-done.4), channel_id=1, source_target_pairs={{0,1},{1,0},{2,3},{3,2},{4,5},{5,4},{6,7},{7,6},{8,9},{9,8},{10,11... | collective-permute-start | bytes 393224 | tf_op jit(solution)/shard_map/ppermute | solution.py:30
  49.3 24.2 %collective-permute-start.12 = (bf16[128,1024]{1,0:T(8,128)(2,1)}, bf16[128,1024]{1,0:T(8,128)(2,1)}, u32[]{:S(2)}, u32[]{:S(2)}) collective-permute-start(bf16[128,1024]{1,0:T(8,128)(2,1)} %convolution_convert_fusion), channel_id=1, source_target_pairs={{0,12},{4,8},{8,4},{12,0},{1,13},{5,9},{9,5},{13,1},{2,14},{6,10},... | collective-permute-start | bytes 786440 | tf_op jit(solution)/shard_map/ppermute | solution.py:134
  54.3 27.3 %collective-permute-start.9 = (bf16[128,1024]{1,0:T(8,128)(2,1)}, bf16[128,1024]{1,0:T(8,128)(2,1)}, u32[]{:S(2)}, u32[]{:S(2)}) collective-permute-start(bf16[128,1024]{1,0:T(8,128)(2,1)} %convolution_convert_fusion.1), channel_id=1, source_target_pairs={{0,8},{4,12},{8,0},{12,4},{1,9},{5,13},{9,1},{13,5},{2,10},{6,14},... | collective-permute-start | bytes 786440 | tf_op jit(solution)/shard_map/ppermute | solution.py:134
  60.7 95.9 %all-gather.5.cloned.1.call-start = ((), (), s32[]{:S(2)}) async-start(), calls=%async_computation.1 | async-start | bytes 2359296 | tf_op jit(solution)/shard_map/all_gather | solution.py:143
  60.9 20.6 %collective-permute-start.6 = (bf16[128,1024]{1,0:T(8,128)(2,1)}, bf16[128,1024]{1,0:T(8,128)(2,1)}, u32[]{:S(2)}, u32[]{:S(2)}) collective-permute-start(bf16[128,1024]{1,0:T(8,128)(2,1)} %convolution_convert_fusion.2), channel_id=1, source_target_pairs={{0,4},{4,0},{8,12},{12,8},{1,5},{5,1},{9,13},{13,9},{2,6},{6,2},{1... | collective-permute-start | bytes 786440 | tf_op jit(solution)/shard_map/ppermute | solution.py:134
  69.1 15.6 %copy-start.4 = (bf16[48,8,8,128]{3,2,1,0:T(8,128)(2,1)}, bf16[48,8,8,128]{3,2,1,0:T(8,128)(2,1)S(1)}, u32[]{:S(2)}) copy-start(bf16[48,8,8,128]{3,2,1,0:T(8,128)(2,1)S(1)} %copy.267) | copy-start | bytes 2359300
  69.2 12.4 %copy-start.15 = (f32[128,1024]{1,0:T(8,128)S(1)}, f32[128,1024]{1,0:T(8,128)}, u32[]{:S(2)}) copy-start(f32[128,1024]{1,0:T(8,128)} %fusion.30) | copy-start | bytes 1572868
  71.1 15.3 %collective-permute-start.3 = (bf16[2,1,64,1024]{3,2,1,0:T(8,128)(2,1)S(1)}, bf16[2,1,64,1024]{3,2,1,0:T(8,128)(2,1)S(1)}, u32[]{:S(2)}, u32[]{:S(2)}) collective-permute-start(bf16[2,1,64,1024]{3,2,1,0:T(8,128)(2,1)S(1)} %fusion.21), channel_id=1, source_target_pairs={{0,8},{4,12},{8,0},{12,4},{1,9},{5,13},{9,1},{13,5},{2,10},{6,14},... | collective-permute-start | bytes 786440 | tf_op jit(solution)/shard_map/ppermute | solution.py:30
  96.9 7.1 %copy-start.23 = (f32[2,8,64]{2,1,0:T(8,128)S(1)}, f32[2,8,64]{2,1,0:T(8,128)}, u32[]{:S(2)}) copy-start(f32[2,8,64]{2,1,0:T(8,128)} %copy-done.22) | copy-start | bytes 12292
  98.3 35.7 %collective-permute-start.17 = (bf16[2,1,32,1024]{3,0,2,1:T(2,128)(2,1)}, bf16[2,1,32,1024]{3,0,2,1:T(2,128)(2,1)}, u32[]{:S(2)}, u32[]{:S(2)}) collective-permute-start(bf16[2,1,32,1024]{3,0,2,1:T(2,128)(2,1)} %get-tuple-element.14), channel_id=1, source_target_pairs={{0,12},{4,8},{8,4},{12,0},{1,13},{5,9},{9,5},{13,1},{2,14},{6,10},... | collective-permute-start | bytes 393224 | tf_op jit(solution)/shard_map/ppermute | solution.py:204
  101.0 33.0 %collective-permute-start.16 = (bf16[2,1,32,1024]{3,0,2,1:T(2,128)(2,1)S(1)}, bf16[2,1,32,1024]{3,0,2,1:T(2,128)(2,1)}, u32[]{:S(2)}, u32[]{:S(2)}) collective-permute-start(bf16[2,1,32,1024]{3,0,2,1:T(2,128)(2,1)S(1)} %get-tuple-element.13), channel_id=1, source_target_pairs={{0,8},{4,12},{8,0},{12,4},{1,9},{5,13},{9,1},{13,5},{2,10},{6,14},... | collective-permute-start | bytes 393224 | tf_op jit(solution)/shard_map/ppermute | solution.py:204
  102.2 34.7 %collective-permute-start.15 = (bf16[2,1,64,1024]{3,2,0,1:T(8,128)(2,1)}, bf16[2,1,64,1024]{3,2,0,1:T(8,128)(2,1)}, u32[]{:S(2)}, u32[]{:S(2)}) collective-permute-start(bf16[2,1,64,1024]{3,2,0,1:T(8,128)(2,1)} %bitcast.220), channel_id=1, source_target_pairs={{0,4},{4,0},{8,12},{12,8},{1,5},{5,1},{9,13},{13,9},{2,6},{6,2},{1... | collective-permute-start | bytes 786440 | tf_op jit(solution)/shard_map/ppermute | solution.py:204
  119.9 8.8 %copy-start.5 = (bf16[48,8,8,128]{3,2,1,0:T(8,128)(2,1)S(1)}, bf16[48,8,8,128]{3,2,1,0:T(8,128)(2,1)}, u32[]{:S(2)}) copy-start(bf16[48,8,8,128]{3,2,1,0:T(8,128)(2,1)} %copy-done.4) | copy-start | bytes 2359300
  119.9 8.8 %copy-start.7 = (bf16[2,8,64,192]{3,2,1,0:T(8,128)(2,1)S(1)}, bf16[2,8,64,192]{3,2,1,0:T(8,128)(2,1)}, u32[]{:S(2)}) copy-start(bf16[2,8,64,192]{3,2,1,0:T(8,128)(2,1)} %copy-done.6) | copy-start | bytes 1179652
  120.0 9.1 %copy-start.13 = (bf16[1,1,128,1024]{2,3,1,0:T(8,128)(2,1)S(1)}, bf16[1,1,128,1024]{2,3,1,0:T(8,128)(2,1)}, u32[]{:S(2)}) copy-start(bf16[1,1,128,1024]{2,3,1,0:T(8,128)(2,1)} %copy-done.12) | copy-start | bytes 786436
  122.1 31.4 %collective-permute-start.14 = (bf16[2,1,128,1024]{3,2,1,0:T(8,128)(2,1)}, bf16[2,1,128,1024]{3,2,1,0:T(8,128)(2,1)}, u32[]{:S(2)}, u32[]{:S(2)}) collective-permute-start(bf16[2,1,128,1024]{3,2,1,0:T(8,128)(2,1)} %get-tuple-element.12), channel_id=1, source_target_pairs={{4,0},{8,4},{12,8},{5,1},{9,5},{13,9},{6,2},{10,6},{14,10},{7,3},{... | collective-permute-start | bytes 1572872 | tf_op jit(solution)/shard_map/ppermute | solution.py:22
  123.4 30.1 %collective-permute-start.13 = (bf16[2,1,128,1024]{3,2,1,0:T(8,128)(2,1)}, bf16[2,1,128,1024]{3,2,1,0:T(8,128)(2,1)}, u32[]{:S(2)}, u32[]{:S(2)}) collective-permute-start(bf16[2,1,128,1024]{3,2,1,0:T(8,128)(2,1)} %get-tuple-element.11), channel_id=1, source_target_pairs={{0,4},{4,8},{8,12},{1,5},{5,9},{9,13},{2,6},{6,10},{10,14},{3,7},{... | collective-permute-start | bytes 1572872 | tf_op jit(solution)/shard_map/ppermute | solution.py:20
  136.9 16.6 %copy-start.3 = (bf16[2,1,4,64,1024]{4,3,2,0,1:T(8,128)(2,1)S(1)}, bf16[2,1,4,64,1024]{4,3,2,0,1:T(8,128)(2,1)}, u32[]{:S(2)}) copy-start(bf16[2,1,4,64,1024]{4,3,2,0,1:T(8,128)(2,1)} %copy-done.2) | copy-start | bytes 3145732
  136.9 16.6 %copy-start.9 = (f32[2,1,2,64,1024]{4,3,2,0,1:T(8,128)S(1)}, f32[2,1,2,64,1024]{4,3,2,0,1:T(8,128)}, u32[]{:S(2)}) copy-start(f32[2,1,2,64,1024]{4,3,2,0,1:T(8,128)} %slice.78) | copy-start | bytes 3145732
  156.6 6.8 %copy-start.1 = (bf16[1024,1024]{1,0:T(8,128)(2,1)S(1)}, bf16[1024,1024]{1,0:T(8,128)(2,1)}, u32[]{:S(2)}) copy-start(bf16[1024,1024]{1,0:T(8,128)(2,1)} %param.10) | copy-start | bytes 6291460
  (16 other events, 29.3 us)
Sparse Core Ops, SparseCore 0:
  60.8 32.6 all-gather.2
  96.7 58.1 all-gather.4
